TPU v7x, 32 devices: a whole 2x2x4 slice. The times are simulated.
32 devices in a mesh: lat: 8 (over y, x, core), lon: 4 (over z).
Axes of the slice: x: 2, y: 2, z: 4, core: 2. Of those that a mesh axis runs over, the one named last changes fastest.
Arguments:
- grad_output: bfloat16 [64, 720, 128], P('lat', 'lon'), may hold values from -6 to 6
- band_rows: int32 [8], replicated, may hold values from 1 to 8, 60 in all
- legendre: float32 [192, 360, 64], P('lat'), may hold values from -0.75 to 0.75
- quad_weights: float32 [64], replicated, may hold values from 0.3 to 3
- spectral_filter: float32 [2, 360, 128], replicated, may hold values from -6 to 6
- disco_kernel: float32 [64, 9, 9], replicated, may hold values from -2 to 2
- disco_weight: bfloat16 [128, 9, 128], replicated, may hold values from -0.1875 to 0.1875
Outputs:
- grad_input: bfloat16 [64, 720, 128], P('lat', 'lon')
Inputs may be any that keep to these rules, and one draw needn't show every extreme that they name: Bands follow each other from north to south; the live rows of band b fill its first band_rows[b] slots, and all bands together hold 60 rows.
All inputs are finite; a program needn't handle non-finite values.
Results may differ from a plain program's by a relative error of at most 0.0048.
Values may be sent and summed in bfloat16 or wider, within the bound.
No kernel may reach another device: no remote copies, remote signals or barrier semaphores. Data moves between devices by JAX's collectives and lax.ppermute only.
A program may use at most 64 MiB of HBM per device.

v0:
```python
import jax
import jax.numpy as jnp
from jax import lax
from jax.sharding import PartitionSpec as P

highest = lax.Precision.HIGHEST
tripled = lax.Precision.HIGH


def padded(array, sides, width):
    for axis, dim in sides:
        devices, length = (lax.axis_size(axis), array.shape[dim])
        up = [(i, (i + 1) % devices) for i in range(devices)]
        down = [(j, i) for i, j in up]
        last = lax.slice_in_dim(array, length - width, length, axis=dim)
        first = lax.slice_in_dim(array, 0, width, axis=dim)
        before = lax.ppermute(last, axis, up)
        after = lax.ppermute(first, axis, down)
        array = jnp.concatenate([before, array, after], axis=dim)
    return array


def make_trig(mode_count, point_count):
    wavenumber = lax.broadcasted_iota(jnp.int32, (point_count, mode_count), 1)
    position = lax.broadcasted_iota(jnp.int32, (point_count, mode_count), 0)
    angles = (wavenumber * position % point_count).astype(jnp.float32) * (
        2.0 * jnp.pi / point_count
    )
    scaled = jnp.stack([jnp.cos(angles), -jnp.sin(angles)], axis=2) * point_count ** (-0.5)
    return scaled.reshape(point_count, 2 * mode_count)


def tap_products(source_field, kernel_rows, disco_weight):
    row_count, lon_count, channels = source_field.shape
    kernel_kinds = disco_weight.shape[1]
    mixtures = jnp.dot(
        source_field.reshape(row_count * lon_count, channels),
        disco_weight.reshape(channels, kernel_kinds * channels),
        preferred_element_type=jnp.float32,
    )
    mixtures = mixtures.reshape(row_count, lon_count, kernel_kinds, channels)
    return jnp.einsum("rnkc,rtk->rntc", mixtures, kernel_rows, precision=highest).astype(
        jnp.bfloat16
    )


def last_live(band_block, live_rows):
    last_slice = lax.dynamic_slice_in_dim(band_block, live_rows - 1, 1, 0)
    return lax.dynamic_update_slice_in_dim(band_block, last_slice, band_block.shape[0] - 1, 0)


def combine_taps(from_above, from_level, from_below, lon_count):
    summed = jnp.zeros((from_level.shape[0], lon_count, from_level.shape[3]), jnp.float32)
    for row_step, source in ((1, from_above), (0, from_level), (-1, from_below)):
        for col_step in (-1, 0, 1):
            tap_index = 3 * (row_step + 1) + col_step + 1
            summed = summed + source[
                :, 1 - col_step : 1 - col_step + lon_count, tap_index, :
            ].astype(jnp.float32)
    return summed


def on_device(
    grad_output, band_rows, legendre, quad_weights, spectral_filter, disco_kernel, disco_weight
):
    row_count, lon_count, channels = grad_output.shape
    band_index = lax.axis_index("lat")
    band_total = lax.axis_size("lat")
    lon_index = lax.axis_index("lon")
    point_count = lon_count * lax.axis_size("lon")
    mode_count = legendre.shape[0] * band_total
    chan_share = channels // lax.axis_size("lon")
    slot_ids = jnp.arange(row_count, dtype=jnp.int32)
    live_rows = band_rows[band_index]
    live_slot = slot_ids < live_rows
    masked = jnp.where(live_slot[:, None, None], grad_output, jnp.zeros_like(grad_output))
    trig_table = make_trig(mode_count, point_count)
    portion = lax.all_to_all(masked, "lon", split_axis=2, concat_axis=1, tiled=True)
    spectra = jnp.einsum("rnc,nk->rkc", portion.astype(jnp.float32), trig_table, precision=tripled)
    spectra = spectra.reshape(portion.shape[0], mode_count, 2, portion.shape[2]).astype(
        jnp.bfloat16
    )
    columns = lax.all_to_all(spectra, "lat", split_axis=1, concat_axis=0, tiled=True)
    coefficients = jnp.einsum(
        "mls,smpc->lmpc", legendre, columns.astype(jnp.float32), precision=highest
    )
    filter_slice = lax.dynamic_slice_in_dim(spectral_filter, lon_index * chan_share, chan_share, 2)
    filter_real = filter_slice[0][:, None, :]
    filter_imag = filter_slice[1][:, None, :]
    real_part = coefficients[:, :, 0, :]
    imag_part = coefficients[:, :, 1, :]
    filtered = jnp.stack(
        [
            filter_real * real_part + filter_imag * imag_part,
            filter_real * imag_part - filter_imag * real_part,
        ],
        axis=2,
    )
    returned = jnp.einsum("mls,lmpc->smpc", legendre, filtered, precision=highest)
    returned = (returned * quad_weights[:, None, None, None]).astype(jnp.bfloat16)
    portion = lax.all_to_all(returned, "lat", split_axis=0, concat_axis=1, tiled=True)
    flat_modes = portion.reshape(portion.shape[0], 2 * mode_count, portion.shape[3]).astype(
        jnp.float32
    )
    spectral_rows = jnp.einsum("rkc,nk->rnc", flat_modes, trig_table, precision=tripled).astype(
        jnp.bfloat16
    )
    spectral = lax.all_to_all(spectral_rows, "lon", split_axis=1, concat_axis=2, tiled=True)
    extended_input = padded(last_live(masked, live_rows), (("lat", 0), ("lon", 1)), 1)
    above_band = jnp.maximum(band_index - 1, 0)
    above_row = above_band * row_count + band_rows[above_band] - 1
    level_rows = band_index * row_count + jnp.where(
        slot_ids == row_count - 1, live_rows - 1, slot_ids
    )
    below_row = jnp.minimum(band_index + 1, band_total - 1) * row_count
    row_index = jnp.concatenate([above_row[None], level_rows, below_row[None]])
    row_index = jnp.clip(row_index, 0, disco_kernel.shape[0] - 1)
    kernel_rows = disco_kernel[row_index]
    extended = tap_products(extended_input, kernel_rows, disco_weight)
    top_rim = jnp.where(band_index > 0, extended[0], jnp.zeros_like(extended[0]))
    bottom_rim = jnp.where(
        band_index < band_total - 1, extended[row_count + 1], jnp.zeros_like(extended[0])
    )
    from_above = jnp.concatenate([top_rim[None], extended[1:row_count]], axis=0)
    from_level = extended[1 : row_count + 1]
    below_live = (slot_ids + 1 < live_rows)[:, None, None, None]
    from_below = jnp.where(below_live, extended[2 : row_count + 2], bottom_rim[None])
    disco_term = combine_taps(from_above, from_level, from_below, lon_count)
    summed = masked.astype(jnp.float32) + disco_term + spectral.astype(jnp.float32)
    return jnp.where(live_slot[:, None, None], summed, 0.0).astype(jnp.bfloat16)


def solution(mesh):
    placed = (P("lat", "lon", None), P(), P("lat", None, None), P(), P(), P(), P())
    return jax.shard_map(
        on_device, mesh=mesh, in_specs=placed, out_specs=P("lat", "lon", None), check_vma=False
    )
```

profile of v0, /device:TPU:0, one launch (start us, length us, event | category | flops | bytes accessed | tf_op | source)
XLA Modules:
  0.0 158.5 jit_solution(16150966369396686081)
XLA Ops:
  0.0 1.4 fusion.46
  1.4 1.2 add_compare_fusion
  2.6 0.5 copy-done.6
  3.1 1.1 broadcast_select_fusion.2
  4.2 1.3 copy.114
  5.5 6.3 %all-to-all-start = ((bf16[8,180,128]{1,0,2:T(8,128)(2,1)}), bf16[8,180,128]{1,0,2:T(8,128)(2,1)}, u32[]{:S(2)}, u32[]{:S(2)}) async-start(bf16[8,180,128]{1,0,2:T(8,128)(2,1)} %copy.114), calls=%async_computation | async-start | bytes 1048576 | tf_op jit(solution)/shard_map/all_to_all | solution.py:78
  13.1 0.7 constant_dynamic-slice_fusion
  13.9 0.0 collective-permute-start
  13.9 3.4 %dynamic_update_slice.3 = bf16[8,180,128]{2,0,1:T(8,128)(2,1)S(1)} dynamic-update-slice(bf16[8,180,128]{2,0,1:T(8,128)(2,1)S(1)} %broadcast_select_fusion.2, bf16[1,180,128]{2,0,1:T(2,128)(2,1)} %constant_dynamic-slice_fusion, s32[]{:T(128)} %constant.14.clone.1, s32[]{:T(128)} %constant.19.clone.1, s32[]{:T(128)} %constant.19.clone.1) | dynamic-update-slice | bytes 92164 | tf_op jit(solution)/shard_map/dynamic_update_slice | solution.py:49
  17.3 0.0 copy-start.1
  17.3 0.7 slice.87
  18.1 2.6 %collective-permute-start.1 = (bf16[1,180,128]{2,0,1:T(2,128)(2,1)}, bf16[1,180,128]{2,0,1:T(2,128)(2,1)S(1)}, u32[]{:S(2)}, u32[]{:S(2)}) collective-permute-start(bf16[1,180,128]{2,0,1:T(2,128)(2,1)} %slice.87), channel_id=1, source_target_pairs={{4,0},{8,4},{12,8},{16,12},{20,16},{24,20},{28,24},{0,28},{5,1},{9... | collective-permute-start | bytes 138248 | tf_op jit(solution)/shard_map/ppermute | solution.py:18
  20.7 3.2 %sine_negate_fusion = (f32[720,192,1]{0,1,2:T(8,128)S(1)}, f32[720,192,1]{0,1,2:T(8,128)}) fusion(), kind=kLoop, calls=%fused_computation.32 | loop fusion | flops 1382400 | bytes 1105920 | tf_op jit(solution)/shard_map/neg | solution.py:29
  24.5 2.2 %maximum_multiply_fusion = f32[720,192,2]{0,1,2:T(8,128)} fusion(f32[720,192,1]{0,1,2:T(8,128)S(1)} %get-tuple-element.15, f32[720,192,1]{0,1,2:T(8,128)} %get-tuple-element.16), kind=kLoop, calls=%fused_computation.19 | loop fusion | flops 552960 | bytes 2211840 | tf_op jit(solution)/shard_map/mul | solution.py:29
  26.7 1.9 %dynamic-slice_bitcast_fusion.1 = (f32[360,32]{1,0:T(8,128)}, f32[360,32]{1,0:T(8,128)}) fusion(f32[2,360,128]{2,1,0:T(8,128)} %param.11, s32[]{:T(128)S(6)} %select_n.89, s32[]{:T(128)S(6)} %add.137), kind=kLoop, calls=%fused_computation.46 | loop fusion | bytes 184328 | tf_op jit(solution)/shard_map/mul | solution.py:94
  28.7 0.1 fusion.43
  28.8 0.6 pad_maximum_fusion.3
  29.4 3.8 %collective-permute-start.3 = (bf16[10,1,128]{2,0,1:T(8,128)(2,1)}, bf16[10,1,128]{2,0,1:T(8,128)(2,1)S(1)}, u32[]{:S(2)}, u32[]{:S(2)}) collective-permute-start(bf16[10,1,128]{2,0,1:T(8,128)(2,1)} %get-tuple-element.10), channel_id=1, source_target_pairs={{1,0},{2,1},{3,2},{0,3},{5,4},{6,5},{7,6},{4,7},{9,8},{10,9},{11,1... | collective-permute-start | bytes 7688 | tf_op jit(solution)/shard_map/ppermute | solution.py:18
  33.3 3.2 %copy.112 = f32[720,192,2]{0,2,1:T(2,128)} copy(f32[720,192,2]{0,1,2:T(8,128)} %maximum_multiply_fusion) | data formatting | bytes 2211840 | tf_op jit(solution)/shard_map/mul | solution.py:29
  36.5 2.1 %mul.120 = f32[720,384]{0,1:T(8,128)S(1)} reshape(f32[720,192,2]{0,2,1:T(2,128)} %copy.112) | data formatting | bytes 2211840 | tf_op jit(solution)/shard_map/mul | solution.py:29
  38.6 1.6 %copy.121 = f32[360,32]{0,1:T(8,128)} copy(f32[360,32]{1,0:T(8,128)} %get-tuple-element.12) | data formatting | bytes 92160 | tf_op jit(solution)/shard_map/mul | solution.py:94
  40.2 1.6 %copy.113 = f32[360,32]{0,1:T(8,128)} copy(f32[360,32]{1,0:T(8,128)} %get-tuple-element.11) | data formatting | bytes 92160 | tf_op jit(solution)/shard_map/mul | solution.py:94
  41.9 1.8 %copy.106 = bf16[128,9,128]{0,2,1:T(8,128)(2,1)} copy(bf16[128,9,128]{2,0,1:T(8,128)(2,1)} %param.13) | data formatting | bytes 589824 | tf_op args[6]
  43.7 2.0 %copy.105 = f32[64,9,9]{2,1,0:T(8,128)} copy(f32[64,9,9]{0,2,1:T(8,128)} %param.12) | data formatting | bytes 41472 | tf_op args[5]
  45.7 2.2 %gather_fusion = f32[10,9,9]{2,1,0:T(8,128)} fusion(f32[64,9,9]{2,1,0:T(8,128)} %copy.105, s32[1024]{0:T(1024)S(1)} %pad_clamp_fusion), kind=kCustom, calls=%fused_computation | custom fusion | bytes 6520 | tf_op jit(solution)/shard_map/gather | solution.py:118
  47.9 2.4 %maximum_bitcast_fusion = bf16[10,182,128,1]{2,0,1,3:T(8,128)(2,1)} fusion(bf16[10,1,128]{2,0,1:T(8,128)(2,1)S(1)} %collective-permute-done.3, bf16[1,180,128]{2,0,1:T(2,128)(2,1)} %copy-done.3, bf16[8,180,128]{2,0,1:T(8,128)(2,1)} %copy-done.1, bf16[1,180,128]{2,0,1:T(2,128)(2,1)} %copy-done.2, bf16[10,1,128]{2,0,1:T(8,128)(2,1)S(1)} %collective-permute-done.2), kind=kLoop, calls=%fused_computation.24 | loop fusion | flops 2329600 | bytes 931840 | tf_op jit(solution)/shard_map/concatenate | solution.py:19
  50.3 2.3 %copy.116 = bf16[8,4,180,32]{2,1,3,0:T(4,128)(2,1)} copy(bf16[8,4,180,32]{2,0,3,1:T(8,128)(2,1)} %bitcast.20) | data formatting | bytes 737280 | tf_op jit(solution)/shard_map/all_to_all | solution.py:78
  52.6 2.2 %all_to_all.47 = bf16[8,720,32]{1,2,0:T(8,128)(2,1)} reshape(bf16[8,4,180,32]{2,1,3,0:T(4,128)(2,1)} %copy.116) | data formatting | bytes 737280 | tf_op jit(solution)/shard_map/all_to_all | solution.py:78
  54.8 1.6 fusion.47
  56.4 0.7 convert_bitcast_fusion.1
  57.1 2.3 %copy.118 = bf16[8,384,32]{2,0,1:T(8,128)(2,1)} copy(bf16[8,384,32]{1,2,0:T(8,128)(2,1)} %convert_bitcast_fusion.1) | data formatting | bytes 393216 | tf_op jit(solution)/shard_map/convert_element_type | solution.py:80
  59.3 2.5 %reshape.186 = bf16[8,2,6144]{2,1,0:T(2,128)(2,1)} reshape(bf16[192,2,8,32]{3,2,1,0:T(8,128)(2,1)} %bitcast.114) | data formatting | bytes 393216
  61.9 4.2 %all-to-all-start.1 = ((bf16[8,2,6144]{2,1,0:T(2,128)(2,1)}), bf16[8,2,6144]{2,1,0:T(2,128)(2,1)}, u32[]{:S(2)}, u32[]{:S(2)}) async-start(bf16[8,2,6144]{2,1,0:T(2,128)(2,1)} %reshape.186), calls=%async_computation.1 | async-start | bytes 393216 | tf_op jit(solution)/shard_map/all_to_all | solution.py:83
  66.1 5.9 %fusion.38 = f32[10,182,9,128]{3,1,2,0:T(8,128)} fusion(bf16[10,182,128,1]{2,0,1,3:T(8,128)(2,1)} %maximum_bitcast_fusion, bf16[128,9,128]{0,2,1:T(8,128)(2,1)} %copy.106), kind=kOutput, calls=%fused_computation.38 | convolution fusion | flops 536739840 | bytes 9147392 | tf_op jit(solution)/shard_map/dot_general | solution.py:36
  72.0 0.1 all-to-all-done.1
  72.1 2.3 %reshape.187 = bf16[192,2,8,32]{3,2,1,0:T(8,128)(2,1)} reshape(bf16[8,2,6144]{2,1,0:T(2,128)(2,1)} %all-to-all-done.1) | data formatting | bytes 393216
  74.4 1.3 copy.119
  75.8 1.5 fusion.10
  77.3 0.0 copy-start.8
  77.3 0.3 multiply_add_fusion
  77.6 0.3 copy-done.8
  77.9 3.6 %fusion.23 = bf16[64,24,2,32]{0,3,2,1:T(8,128)(2,1)} fusion(f32[24,360,64]{1,2,0:T(8,128)S(1)} %copy-done, f32[360,24,1,32]{0,3,2,1:T(8,128)S(1)} %get-tuple-element.8, f32[360,24,1,32]{0,3,2,1:T(8,128)S(1)} %get-tuple-element.7, f32[64]{0:T(128)S(1)} %copy-done.8), kind=kOutput, calls=%fused_computation.18 | convolution fusion | flops 425422848 | bytes 4620544 | tf_op jit(solution)/shard_map/mls,lmpc->smpc/dot_general | solution.py:99
  81.6 3.1 %copy.122 = bf16[64,24,2,32]{3,2,1,0:T(2,128)(2,1)} copy(bf16[64,24,2,32]{0,3,2,1:T(8,128)(2,1)} %fusion.23) | data formatting | bytes 393216 | tf_op jit(solution)/shard_map/convert_element_type | solution.py:100
  84.7 2.5 %reshape.188 = bf16[8,2,6144]{2,1,0:T(2,128)(2,1)} reshape(bf16[64,24,2,32]{3,2,1,0:T(2,128)(2,1)} %copy.122) | data formatting | bytes 393216
  87.3 4.2 %all-to-all-start.2 = ((bf16[8,2,6144]{2,1,0:T(2,128)(2,1)}), bf16[8,2,6144]{2,1,0:T(2,128)(2,1)}, u32[]{:S(2)}, u32[]{:S(2)}) async-start(bf16[8,2,6144]{2,1,0:T(2,128)(2,1)} %reshape.188), calls=%async_computation.2 | async-start | bytes 393216 | tf_op jit(solution)/shard_map/all_to_all | solution.py:101
  91.5 17.3 %fusion = bf16[10,9,182,128]{3,1,2,0:T(8,128)(2,1)S(1)} fusion(f32[10,182,9,128]{3,1,2,0:T(8,128)} %fusion.38, f32[10,9,9]{2,1,0:T(8,128)} %gather_fusion), kind=kOutput, calls=%fused_computation.1 | convolution fusion | flops 226437120 | bytes 12583080 | tf_op jit(solution)/shard_map/rnkc,rtk->rntc/dot_general | solution.py:42
  108.8 5.8 %copy.149 = bf16[10,9,182,128]{3,0,1,2:T(8,128)(2,1)} copy(bf16[10,9,182,128]{3,1,2,0:T(8,128)(2,1)S(1)} %fusion) | data formatting | bytes 8386560 | tf_op jit(solution)/shard_map/rnkc,rtk->rntc/dot_general | solution.py:42
  114.7 2.2 %reshape.189 = bf16[64,24,2,32]{3,2,1,0:T(2,128)(2,1)} reshape(bf16[8,2,6144]{2,1,0:T(2,128)(2,1)} %all-to-all-done.2) | data formatting | bytes 393216
  116.9 1.2 copy.123
  118.1 1.1 copy.124
  119.2 2.2 %copy.126 = bf16[8,384,32]{1,2,0:T(8,128)(2,1)} copy(bf16[8,384,32]{2,0,1:T(8,128)(2,1)} %bitcast.113) | data formatting | bytes 393216 | tf_op jit(solution)/shard_map/reshape | solution.py:102
  121.4 1.5 fusion.48
  123.0 1.9 %copy.127 = bf16[8,720,32]{2,0,1:T(8,128)(2,1)} copy(bf16[8,720,32]{1,2,0:T(8,128)(2,1)S(1)} %convert_bitcast_fusion) | data formatting | bytes 737280 | tf_op jit(solution)/shard_map/convert_element_type | solution.py:105
  124.9 2.9 %reshape.190 = bf16[4,2,23040]{2,1,0:T(2,128)(2,1)} reshape(bf16[720,8,32]{2,1,0:T(8,128)(2,1)} %bitcast.107) | data formatting | bytes 737280
  127.7 5.1 %all-to-all-start.3 = ((bf16[4,2,23040]{2,1,0:T(2,128)(2,1)}), bf16[4,2,23040]{2,1,0:T(2,128)(2,1)S(1)}, u32[]{:S(2)}, u32[]{:S(2)}) async-start(bf16[4,2,23040]{2,1,0:T(2,128)(2,1)} %reshape.190), calls=%async_computation.3 | async-start | bytes 737280 | tf_op jit(solution)/shard_map/all_to_all | solution.py:108
  132.8 4.6 %broadcast_select_fusion.1 = (bf16[1,182,9,128]{3,0,2,1:T(2,128)(2,1)}, bf16[1,182,9,128]{3,0,2,1:T(2,128)(2,1)S(1)}) fusion(pred[]{:T(512)S(6)} %gt.3, bf16[10,182,9,128]{3,0,2,1:T(8,128)(2,1)} %bitcast.103, pred[]{:T(512)S(6)} %lt.55), kind=kLoop, calls=%fused_computation.15 | loop fusion | flops 419328 | bytes 1677314 | tf_op jit(solution)/shard_map/jit(_where)/select_n | solution.py:120
  137.4 4.6 %slice.89 = bf16[7,182,9,128]{3,0,2,1:T(8,128)(2,1)} slice(bf16[10,182,9,128]{3,0,2,1:T(8,128)(2,1)} %bitcast.104), slice={[1:8], [0:182], [0:9], [0:128]} | slice | bytes 5870592 | tf_op jit(solution)/shard_map/slice | solution.py:124
  142.0 0.1 copy.150
  142.1 0.5 copy-done.9
  142.6 6.2 %slice_select_fusion = bf16[8,182,9,128]{3,0,2,1:T(8,128)(2,1)} fusion(bf16[10,182,9,128]{3,0,2,1:T(8,128)(2,1)} %bitcast.105, pred[8]{0:T(512)(128)(4,1)S(1)} %copy-done.9, bf16[182,9,128]{2,1,0:T(8,128)(2,1)S(1)} %bitcast.116), kind=kLoop, calls=%fused_computation.5 | loop fusion | flops 1677312 | bytes 7128584 | tf_op jit(solution)/shard_map/jit(_where)/select_n | solution.py:127
  148.8 1.7 %reshape.191 = bf16[720,8,32]{2,1,0:T(8,128)(2,1)} reshape(bf16[4,2,23040]{2,1,0:T(2,128)(2,1)S(1)} %all-to-all-done.3) | data formatting | bytes 737280
  150.5 2.1 %copy.128 = f32[8,4,180,32]{2,3,1,0:T(8,128)S(1)} copy(bf16[8,4,180,32]{3,0,2,1:T(8,128)(2,1)} %bitcast.108) | data formatting | bytes 1105920 | tf_op jit(solution)/shard_map/convert_element_type | solution.py:129
  152.6 1.2 copy.129
  153.9 4.7 %fusion.31 = bf16[8,180,128]{2,0,1:T(8,128)(2,1)} fusion(f32[8,180,128]{2,0,1:T(8,128)} %copy.129, bf16[8,182,9,128]{3,0,2,1:T(8,128)(2,1)} %slice_select_fusion, bf16[10,182,9,128]{3,0,2,1:T(8,128)(2,1)} %bitcast.106, bf16[7,182,9,128]{3,0,2,1:T(8,128)(2,1)} %slice.89, bf16[1,182,9,128]{3,0,2,1:T(2,128)(2,1)} %get-tuple-element.5, ...), kind=kLoop, calls=%fused_computation.29 | loop fusion | flops 5898240 | bytes 7041032 | tf_op jit(solution)/shard_map/convert_element_type | solution.py:130
  (26 shorter events, 0.1 us)
Async XLA Ops:
  0.0 75.8 %copy-start = (f32[24,360,64]{1,2,0:T(8,128)S(1)}, f32[24,360,64]{1,2,0:T(8,128)}, u32[]{:S(2)}) copy-start(f32[24,360,64]{1,2,0:T(8,128)} %param.9) | copy-start | bytes 6635524
  2.6 0.5 copy-start.6
  5.5 44.8 %all-to-all-start = ((bf16[8,180,128]{1,0,2:T(8,128)(2,1)}), bf16[8,180,128]{1,0,2:T(8,128)(2,1)}, u32[]{:S(2)}, u32[]{:S(2)}) async-start(bf16[8,180,128]{1,0,2:T(8,128)(2,1)} %copy.114), calls=%async_computation | async-start | bytes 1048576 | tf_op jit(solution)/shard_map/all_to_all | solution.py:78
  13.9 14.9 %collective-permute-start = (bf16[1,180,128]{2,0,1:T(2,128)(2,1)}, bf16[1,180,128]{2,0,1:T(2,128)(2,1)S(1)}, u32[]{:S(2)}, u32[]{:S(2)}) collective-permute-start(bf16[1,180,128]{2,0,1:T(2,128)(2,1)} %constant_dynamic-slice_fusion), channel_id=1, source_target_pairs={{0,4},{4,8},{8,12},{12,16},{16,20},{20,24},{24,28},{28,0},{1,5},{5... | collective-permute-start | bytes 138248 | tf_op jit(solution)/shard_map/ppermute | solution.py:17
  17.3 11.5 %copy-start.1 = (bf16[8,180,128]{2,0,1:T(8,128)(2,1)}, bf16[8,180,128]{2,0,1:T(8,128)(2,1)S(1)}, u32[]{:S(2)}) copy-start(bf16[8,180,128]{2,0,1:T(8,128)(2,1)S(1)} %dynamic_update_slice.3) | copy-start | bytes 1105924
  18.1 10.7 %collective-permute-start.1 = (bf16[1,180,128]{2,0,1:T(2,128)(2,1)}, bf16[1,180,128]{2,0,1:T(2,128)(2,1)S(1)}, u32[]{:S(2)}, u32[]{:S(2)}) collective-permute-start(bf16[1,180,128]{2,0,1:T(2,128)(2,1)} %slice.87), channel_id=1, source_target_pairs={{4,0},{8,4},{12,8},{16,12},{20,16},{24,20},{28,24},{0,28},{5,1},{9... | collective-permute-start | bytes 138248 | tf_op jit(solution)/shard_map/ppermute | solution.py:18
  28.7 4.5 %copy-start.3 = (bf16[1,180,128]{2,0,1:T(2,128)(2,1)}, bf16[1,180,128]{2,0,1:T(2,128)(2,1)S(1)}, u32[]{:S(2)}) copy-start(bf16[1,180,128]{2,0,1:T(2,128)(2,1)S(1)} %collective-permute-done.1) | copy-start | bytes 138244
  28.8 4.5 %copy-start.2 = (bf16[1,180,128]{2,0,1:T(2,128)(2,1)}, bf16[1,180,128]{2,0,1:T(2,128)(2,1)S(1)}, u32[]{:S(2)}) copy-start(bf16[1,180,128]{2,0,1:T(2,128)(2,1)S(1)} %collective-permute-done) | copy-start | bytes 138244
  29.4 18.5 %collective-permute-start.3 = (bf16[10,1,128]{2,0,1:T(8,128)(2,1)}, bf16[10,1,128]{2,0,1:T(8,128)(2,1)S(1)}, u32[]{:S(2)}, u32[]{:S(2)}) collective-permute-start(bf16[10,1,128]{2,0,1:T(8,128)(2,1)} %get-tuple-element.10), channel_id=1, source_target_pairs={{1,0},{2,1},{3,2},{0,3},{5,4},{6,5},{7,6},{4,7},{9,8},{10,9},{11,1... | collective-permute-start | bytes 7688 | tf_op jit(solution)/shard_map/ppermute | solution.py:18
  33.2 14.7 %collective-permute-start.2 = (bf16[10,1,128]{2,0,1:T(8,128)(2,1)S(1)}, bf16[10,1,128]{2,0,1:T(8,128)(2,1)S(1)}, u32[]{:S(2)}, u32[]{:S(2)}) collective-permute-start(bf16[10,1,128]{2,0,1:T(8,128)(2,1)S(1)} %get-tuple-element.9), channel_id=1, source_target_pairs={{0,1},{1,2},{2,3},{3,0},{4,5},{5,6},{6,7},{7,4},{8,9},{9,10},{10,1... | collective-permute-start | bytes 7688 | tf_op jit(solution)/shard_map/ppermute | solution.py:17
  61.9 10.3 %all-to-all-start.1 = ((bf16[8,2,6144]{2,1,0:T(2,128)(2,1)}), bf16[8,2,6144]{2,1,0:T(2,128)(2,1)}, u32[]{:S(2)}, u32[]{:S(2)}) async-start(bf16[8,2,6144]{2,1,0:T(2,128)(2,1)} %reshape.186), calls=%async_computation.1 | async-start | bytes 393216 | tf_op jit(solution)/shard_map/all_to_all | solution.py:83
  75.8 1.5 copy-start.4
  75.8 1.5 copy-start.5
  77.3 0.7 copy-start.8
  87.3 27.4 %all-to-all-start.2 = ((bf16[8,2,6144]{2,1,0:T(2,128)(2,1)}), bf16[8,2,6144]{2,1,0:T(2,128)(2,1)}, u32[]{:S(2)}, u32[]{:S(2)}) async-start(bf16[8,2,6144]{2,1,0:T(2,128)(2,1)} %reshape.188), calls=%async_computation.2 | async-start | bytes 393216 | tf_op jit(solution)/shard_map/all_to_all | solution.py:101
  127.7 21.1 %all-to-all-start.3 = ((bf16[4,2,23040]{2,1,0:T(2,128)(2,1)}), bf16[4,2,23040]{2,1,0:T(2,128)(2,1)S(1)}, u32[]{:S(2)}, u32[]{:S(2)}) async-start(bf16[4,2,23040]{2,1,0:T(2,128)(2,1)} %reshape.190), calls=%async_computation.3 | async-start | bytes 737280 | tf_op jit(solution)/shard_map/all_to_all | solution.py:108
  142.0 0.6 copy-start.9
  152.6 1.2 copy-start.7
where the time goes:
time: 160 us; the launch traced here: 159 us
  local copies, waits for them, and re-layouts  71.1 us (44%)
  matrix products  31.4 us (20%)
  other arithmetic  27.4 us (17%)
  starting transfers between devices  26.3 us (16%)
  between operations  2.12 us (1%)
    unnamed x28, local copies, waits for them, and re-layouts  19.3 us
    dot_general x1, matrix products, tap_products(): jnp.einsum('rnkc,rtk->rntc', mixtures, kernel_rows, precision=highest)  17.3 us
    ppermute x2, starting transfers between devices, padded(): after = lax.ppermute(first, axis, down)  6.46 us
    all_to_all x1, starting transfers between devices, on_device(): lax.all_to_all(masked, 'lon', split_axis=2, concat_axis=1, tiled=True)  6.32 us
    select_n x1, other arithmetic, on_device(): jnp.where(below_live, extended[2:row_count + 2], bottom_rim[None])  6.21 us
    dot_general x1, matrix products, tap_products(): jnp.dot(source_field.reshape(row_count * lon_count, channels), disco_weig...  5.91 us
    dot_general x1, local copies, waits for them, and re-layouts, tap_products(): jnp.einsum('rnkc,rtk->rntc', mixtures, kernel_rows, precision=highest)  5.83 us
    mul x2, local copies, waits for them, and re-layouts, make_trig(): jnp.stack([jnp.cos(angles), -jnp.sin(angles)], axis=2)  5.3 us
  transfers between devices with their start and end apart: 8, of which 1 were waited for; matrix products, arithmetic and copies ran while one was open for 47% of the time, Pallas kernels for 0%

commit v1 on v0

v1 whole, which is shorter than its diff:
```python
import jax
import jax.numpy as jnp
from jax import lax
from jax.experimental import pallas as pl
from jax.experimental.pallas import tpu as pltpu
from jax.sharding import PartitionSpec as P

highest = lax.Precision.HIGHEST
tripled = lax.Precision.HIGH


def make_trig(mode_count, point_count):
    wavenumber = lax.broadcasted_iota(jnp.int32, (point_count, mode_count), 1)
    position = lax.broadcasted_iota(jnp.int32, (point_count, mode_count), 0)
    angles = (wavenumber * position % point_count).astype(jnp.float32) * (
        2.0 * jnp.pi / point_count
    )
    scaled = jnp.stack([jnp.cos(angles), -jnp.sin(angles)], axis=2) * point_count ** (-0.5)
    return scaled.reshape(point_count, 2 * mode_count)


CHUNK = 64


def round_up(value, step):
    return -(-value // step) * step


def disco_body(src_ref, coef_ref, ext_ref, w_ref, out_ref, mix_ref):
    row_total = ext_ref.shape[0]
    slot_total = out_ref.shape[0]
    kinds = w_ref.shape[1] // w_ref.shape[0]
    channels = w_ref.shape[0]
    for r in range(row_total):
        mix_ref[r] = jnp.dot(ext_ref[r], w_ref[...], preferred_element_type=jnp.float32)

    def slot_step(s, carry):
        for c0 in range(0, out_ref.shape[1], CHUNK):
            acc = jnp.zeros((CHUNK, channels), jnp.float32)
            for a_i in range(3):
                row = src_ref[s * 3 + a_i]
                for b_i in range(3):
                    for k in range(kinds):
                        coef = coef_ref[((s * 3 + a_i) * 3 + b_i) * kinds + k]
                        acc = acc + coef * mix_ref[
                            row, pl.ds(c0 + 2 - b_i, CHUNK), pl.ds(k * channels, channels)
                        ]
            out_ref[s, pl.ds(c0, CHUNK), :] = acc
        return carry

    lax.fori_loop(0, slot_total, slot_step, 0)


def disco_apply(src, coef, ext, weight_flat, slot_total, lon_count):
    row_total, lon_pad, channels = ext.shape
    out_rows = round_up(lon_count, CHUNK)
    smem = pltpu.MemorySpace.SMEM if hasattr(pltpu, "MemorySpace") else pltpu.SMEM
    return pl.pallas_call(
        disco_body,
        out_shape=jax.ShapeDtypeStruct((slot_total, out_rows, channels), jnp.float32),
        in_specs=[
            pl.BlockSpec(memory_space=smem),
            pl.BlockSpec(memory_space=smem),
            pl.BlockSpec(memory_space=pltpu.VMEM),
            pl.BlockSpec(memory_space=pltpu.VMEM),
        ],
        out_specs=pl.BlockSpec(memory_space=pltpu.VMEM),
        scratch_shapes=[pltpu.VMEM((row_total, lon_pad, weight_flat.shape[1]), jnp.float32)],
    )(src, coef, ext, weight_flat)


def disco_tables(band_rows, disco_kernel, band_index, band_total, row_count):
    slot_ids = jnp.arange(row_count, dtype=jnp.int32)
    live_rows = band_rows[band_index]
    has_next = slot_ids + 1 < live_rows
    prev_band = jnp.maximum(band_index - 1, 0)
    next_band = jnp.minimum(band_index + 1, band_total - 1)
    base = band_index * row_count
    up_src = jnp.where(slot_ids == 0, 0, slot_ids)
    down_src = jnp.where(has_next, slot_ids + 2, row_count + 1)
    src = jnp.stack([up_src, slot_ids + 1, down_src], axis=1)
    up_row = jnp.where(
        slot_ids == 0, prev_band * row_count + band_rows[prev_band] - 1, base + slot_ids - 1
    )
    down_row = jnp.where(has_next, base + slot_ids + 1, next_band * row_count)
    kernel_row = jnp.stack([up_row, base + slot_ids, down_row], axis=1)
    kernel_row = jnp.clip(kernel_row, 0, disco_kernel.shape[0] - 1)
    up_ok = (slot_ids > 0) | (band_index > 0)
    down_ok = has_next | (band_index < band_total - 1)
    valid = jnp.stack([up_ok, jnp.ones_like(up_ok), down_ok], axis=1)
    gathered = disco_kernel[kernel_row]
    gathered = gathered.reshape(row_count, 3, 3, 3, disco_kernel.shape[2])
    coef = jnp.stack([gathered[:, 0, 2], gathered[:, 1, 1], gathered[:, 2, 0]], axis=1)
    coef = jnp.where(valid[:, :, None, None], coef, 0.0)
    return src.reshape(-1).astype(jnp.int32), coef.reshape(-1).astype(jnp.float32)


def halo_extend(masked, live_rows):
    row_count, lon_count, channels = masked.shape
    lat_total = lax.axis_size("lat")
    lon_total = lax.axis_size("lon")
    lat_up = [(i, (i + 1) % lat_total) for i in range(lat_total)]
    lat_down = [(j, i) for i, j in lat_up]
    lon_up = [(i, (i + 1) % lon_total) for i in range(lon_total)]
    lon_down = [(j, i) for i, j in lon_up]
    last_row = lax.dynamic_slice_in_dim(masked, live_rows - 1, 1, 0)
    from_above = lax.ppermute(last_row, "lat", lat_up)
    from_below = lax.ppermute(masked[0:1], "lat", lat_down)
    rows = jnp.concatenate([from_above, masked, from_below], axis=0)
    from_left = lax.ppermute(rows[:, lon_count - 1 : lon_count], "lon", lon_up)
    from_right = lax.ppermute(rows[:, 0:1], "lon", lon_down)
    lon_pad = round_up(round_up(lon_count, CHUNK) + 2, 16)
    pad = jnp.zeros((row_count + 2, lon_pad - lon_count - 2, channels), masked.dtype)
    return jnp.concatenate([from_left, rows, from_right, pad], axis=1)


def on_device(
    grad_output, band_rows, legendre, quad_weights, spectral_filter, disco_kernel, disco_weight
):
    row_count, lon_count, channels = grad_output.shape
    band_index = lax.axis_index("lat")
    band_total = lax.axis_size("lat")
    lon_index = lax.axis_index("lon")
    point_count = lon_count * lax.axis_size("lon")
    mode_count = legendre.shape[0] * band_total
    chan_share = channels // lax.axis_size("lon")
    slot_ids = jnp.arange(row_count, dtype=jnp.int32)
    live_rows = band_rows[band_index]
    live_slot = slot_ids < live_rows
    masked = jnp.where(live_slot[:, None, None], grad_output, jnp.zeros_like(grad_output))
    trig_table = make_trig(mode_count, point_count)
    portion = lax.all_to_all(masked, "lon", split_axis=2, concat_axis=1, tiled=True)
    spectra = jnp.einsum("rnc,nk->rkc", portion.astype(jnp.float32), trig_table, precision=tripled)
    spectra = spectra.reshape(portion.shape[0], mode_count, 2, portion.shape[2]).astype(
        jnp.bfloat16
    )
    columns = lax.all_to_all(spectra, "lat", split_axis=1, concat_axis=0, tiled=True)
    coefficients = jnp.einsum(
        "mls,smpc->lmpc", legendre, columns.astype(jnp.float32), precision=highest
    )
    filter_slice = lax.dynamic_slice_in_dim(spectral_filter, lon_index * chan_share, chan_share, 2)
    filter_real = filter_slice[0][:, None, :]
    filter_imag = filter_slice[1][:, None, :]
    real_part = coefficients[:, :, 0, :]
    imag_part = coefficients[:, :, 1, :]
    filtered = jnp.stack(
        [
            filter_real * real_part + filter_imag * imag_part,
            filter_real * imag_part - filter_imag * real_part,
        ],
        axis=2,
    )
    returned = jnp.einsum("mls,lmpc->smpc", legendre, filtered, precision=highest)
    returned = (returned * quad_weights[:, None, None, None]).astype(jnp.bfloat16)
    portion = lax.all_to_all(returned, "lat", split_axis=0, concat_axis=1, tiled=True)
    flat_modes = portion.reshape(portion.shape[0], 2 * mode_count, portion.shape[3]).astype(
        jnp.float32
    )
    spectral_rows = jnp.einsum("rkc,nk->rnc", flat_modes, trig_table, precision=tripled).astype(
        jnp.bfloat16
    )
    spectral = lax.all_to_all(spectral_rows, "lon", split_axis=1, concat_axis=2, tiled=True)
    ext = halo_extend(masked, live_rows)
    src_rows, coef = disco_tables(band_rows, disco_kernel, band_index, band_total, row_count)
    weight_flat = disco_weight.reshape(channels, -1)
    disco_full = disco_apply(src_rows, coef, ext, weight_flat, row_count, lon_count)
    disco_term = disco_full[:, :lon_count, :]
    summed = masked.astype(jnp.float32) + disco_term + spectral.astype(jnp.float32)
    return jnp.where(live_slot[:, None, None], summed, 0.0).astype(jnp.bfloat16)


def solution(mesh):
    placed = (P("lat", "lon", None), P(), P("lat", None, None), P(), P(), P(), P())
    return jax.shard_map(
        on_device, mesh=mesh, in_specs=placed, out_specs=P("lat", "lon", None), check_vma=False
    )
```

time: 160 us -> 142 us (0.89)
  matrix products: 31.4 us -> 8.22 us
  Pallas kernels: 0 us -> 13.9 us
  waiting for transfers between devices: 0.17 us -> 11.5 us
  other arithmetic: 27.4 us -> 17.2 us
  local copies, waits for them, and re-layouts: 71.1 us -> 62.2 us
    dot_general x2 -> x0, matrix products: 23.2 us -> none  [the longest x1 17.3 us: tap_products(): jnp.einsum('rnkc,rtk->rntc', mixtures, kernel_rows, precision=highest)]
    pallas_call x0 -> x1, Pallas kernels: none -> 13.9 us  [disco_apply(): pl.pallas_call(disco_body, out_shape=jax.ShapeDtypeStruct((slot_total, ou...]
    select_n x3, other arithmetic: 10.9 us -> 2.63 us  [the longest x1 1.42 us: disco_tables(): coef = jnp.where(valid[:, :, None, None], coef, 0.0)]
    dot_general x1 -> x0, local copies, waits for them, and re-layouts: 5.83 us -> none  [tap_products(): jnp.einsum('rnkc,rtk->rntc', mixtures, kernel_rows, precision=highest)]
    all_to_all x1, waiting for transfers between devices: 0.01 us -> 4.83 us  [on_device(): lax.all_to_all(returned, 'lat', split_axis=0, concat_axis=1, tiled=True)]
    all_to_all x1, waiting for transfers between devices: 0.15 us -> 4.88 us  [on_device(): lax.all_to_all(spectra, 'lat', split_axis=1, concat_axis=0, tiled=True)]
    slice x2 -> x1, local copies, waits for them, and re-layouts: 5.32 us -> 1.48 us  [disco_tables(): gathered[:, 0, 2]]
    dynamic_update_slice x1 -> x0, local copies, waits for them, and re-layouts: 3.41 us -> none  [last_live(): lax.dynamic_update_slice_in_dim(band_block, last_slice, band_block.shape[...]
  transfers between devices with their start and end apart: 8 -> 8, of which waited for: 1 -> 3; matrix products, arithmetic and copies ran while one was open for 47% -> 52% of each run, Pallas kernels for 0% -> 10%
where the time goes in v1:
time: 142 us; the launch traced here: 140 us
  local copies, waits for them, and re-layouts  62.2 us (44%)
  starting transfers between devices  24.8 us (17%)
  other arithmetic  17.2 us (12%)
  Pallas kernels  13.9 us (10%)
  waiting for transfers between devices  11.5 us (8%)
  matrix products  8.22 us (6%)
  between operations  2.08 us (1%)
    unnamed x26, local copies, waits for them, and re-layouts  17.7 us
    pallas_call x1, Pallas kernels, disco_apply(): pl.pallas_call(disco_body, out_shape=jax.ShapeDtypeStruct((slot_total, ou...  13.9 us
    all_to_all x1, starting transfers between devices, on_device(): lax.all_to_all(masked, 'lon', split_axis=2, concat_axis=1, tiled=True)  6.32 us
    all_to_all x1, waiting for transfers between devices, on_device(): lax.all_to_all(spectra, 'lat', split_axis=1, concat_axis=0, tiled=True)  4.88 us
    all_to_all x1, waiting for transfers between devices, on_device(): lax.all_to_all(returned, 'lat', split_axis=0, concat_axis=1, tiled=True)  4.83 us
    all_to_all x1, starting transfers between devices, on_device(): lax.all_to_all(spectral_rows, 'lon', split_axis=1, concat_axis=2, tiled=T...  4.81 us
    all_to_all x2, local copies, waits for them, and re-layouts, on_device(): lax.all_to_all(masked, 'lon', split_axis=2, concat_axis=1, tiled=True)  4.49 us
    all_to_all x1, starting transfers between devices, on_device(): lax.all_to_all(spectra, 'lat', split_axis=1, concat_axis=0, tiled=True)  4.2 us
  transfers between devices with their start and end apart: 8, of which 3 were waited for; matrix products, arithmetic and copies ran while one was open for 52% of the time, Pallas kernels for 10%

profile of v1, /device:TPU:0, one launch (start us, length us, event | category | flops | bytes accessed | tf_op | source)
XLA Modules:
  0.0 139.9 jit_solution(2506125797998433265)
XLA Ops:
  0.0 1.5 %fusion.39 = (s32[1]{0:T(128)}, s32[1]{0:T(128)}) fusion(s32[8]{0:T(128)} %param.8, s32[]{:T(128)S(6)} %max.10, s32[]{:T(128)S(6)} %select_n.113), kind=kLoop, calls=%fused_computation.59 | loop fusion | bytes 24 | tf_op jit(solution)/shard_map/dynamic_slice | solution.py:83
  1.5 0.6 iota_compare_fusion
  2.1 1.1 copy_select_fusion
  3.2 1.2 copy.83
  4.4 6.3 %all-to-all-start = ((bf16[8,180,128]{1,0,2:T(8,128)(2,1)}), bf16[8,180,128]{1,0,2:T(8,128)(2,1)}, u32[]{:S(2)}, u32[]{:S(2)}) async-start(bf16[8,180,128]{1,0,2:T(8,128)(2,1)} %copy.83), calls=%async_computation | async-start | bytes 1048576 | tf_op jit(solution)/shard_map/all_to_all | solution.py:132
  12.0 0.6 constant_dynamic-slice_fusion
  12.6 1.6 %collective-permute-start.1 = (bf16[1,180,128]{2,1,0:T(8,128)(2,1)}, bf16[1,180,128]{2,1,0:T(8,128)(2,1)}, u32[]{:S(2)}, u32[]{:S(2)}) collective-permute-start(bf16[1,180,128]{2,1,0:T(8,128)(2,1)} %get-tuple-element.10), channel_id=1, source_target_pairs={{4,0},{8,4},{12,8},{16,12},{20,16},{24,20},{28,24},{0,28},{5,1},{9... | collective-permute-start | bytes 138248 | tf_op jit(solution)/shard_map/ppermute | solution.py:108
  14.2 3.2 %sine_negate_fusion = (f32[720,192,1]{0,1,2:T(8,128)S(1)}, f32[720,192,1]{0,1,2:T(8,128)}) fusion(), kind=kLoop, calls=%fused_computation.23 | loop fusion | flops 1382400 | bytes 1105920 | tf_op jit(solution)/shard_map/neg | solution.py:18
  17.5 1.2 maximum_multiply_fusion
  18.6 1.9 %copy.81 = f32[720,192,2]{0,2,1:T(2,128)} copy(f32[720,192,2]{0,1,2:T(8,128)S(1)} %maximum_multiply_fusion) | data formatting | bytes 2211840 | tf_op jit(solution)/shard_map/mul | solution.py:18
  20.6 2.1 %mul.120 = f32[720,384]{0,1:T(8,128)S(1)} reshape(f32[720,192,2]{0,2,1:T(2,128)} %copy.81) | data formatting | bytes 2211840 | tf_op jit(solution)/shard_map/mul | solution.py:18
  22.7 1.9 %dynamic-slice_bitcast_fusion.1 = (f32[360,32]{1,0:T(8,128)}, f32[360,32]{1,0:T(8,128)}) fusion(f32[2,360,128]{2,1,0:T(8,128)} %param.11, s32[]{:T(128)S(6)} %select_n.124, s32[]{:T(128)S(6)} %add.196), kind=kLoop, calls=%fused_computation.34 | loop fusion | bytes 184328 | tf_op jit(solution)/shard_map/mul | solution.py:148
  24.6 1.6 %copy.90 = f32[360,32]{0,1:T(8,128)} copy(f32[360,32]{1,0:T(8,128)} %get-tuple-element.12) | data formatting | bytes 92160 | tf_op jit(solution)/shard_map/mul | solution.py:148
  26.2 1.6 %copy.82 = f32[360,32]{0,1:T(8,128)} copy(f32[360,32]{1,0:T(8,128)} %get-tuple-element.11) | data formatting | bytes 92160 | tf_op jit(solution)/shard_map/mul | solution.py:148
  27.9 2.0 %copy.75 = f32[64,9,9]{2,1,0:T(8,128)} copy(f32[64,9,9]{0,2,1:T(8,128)} %param.12) | data formatting | bytes 41472 | tf_op args[5]
  30.4 0.6 fusion.35
  31.3 2.3 %gather_fusion = f32[24,9,9]{2,1,0:T(8,128)} fusion(f32[64,9,9]{2,1,0:T(8,128)} %copy.75, s32[1024]{0:T(1024)S(1)} %pad_clamp_fusion), kind=kCustom, calls=%fused_computation | custom fusion | bytes 15648 | tf_op jit(solution)/shard_map/gather | solution.py:91
  33.6 1.6 %copy.76 = f32[24,9,9]{2,0,1:T(8,128)} copy(f32[24,9,9]{2,1,0:T(8,128)} %gather_fusion) | data formatting | bytes 15552 | tf_op jit(solution)/shard_map/gather | solution.py:91
  35.2 1.6 %reshape.208 = f32[8,3,3,3,9]{4,1,0,3,2:T(4,128)} reshape(f32[24,9,9]{2,0,1:T(8,128)} %copy.76) | data formatting | bytes 15552 | tf_op jit(solution)/shard_map/reshape | solution.py:92
  36.8 0.7 pad.20.clone
  37.4 1.2 compare_select_fusion.2
  38.6 1.2 compare_or_fusion
  39.8 1.5 %fusion.38 = (f32[8,1,1,3,9]{4,1,0,3,2:T(1,128)S(1)}, f32[8,1,1,3,9]{4,1,0,3,2:T(1,128)}, f32[8,1,1,3,9]{4,1,0,3,2:T(1,128)}) fusion(f32[8,3,3,3,9]{4,1,0,3,2:T(4,128)} %reshape.208), kind=kLoop, calls=%fused_computation.58 | loop fusion | bytes 5184 | tf_op jit(solution)/shard_map/slice | solution.py:93
  41.3 2.3 %copy.85 = bf16[8,4,180,32]{2,1,3,0:T(4,128)(2,1)} copy(bf16[8,4,180,32]{2,0,3,1:T(8,128)(2,1)} %bitcast.12) | data formatting | bytes 737280 | tf_op jit(solution)/shard_map/all_to_all | solution.py:132
  43.6 2.2 %all_to_all.47 = bf16[8,720,32]{1,2,0:T(8,128)(2,1)} reshape(bf16[8,4,180,32]{2,1,3,0:T(4,128)(2,1)} %copy.85) | data formatting | bytes 737280 | tf_op jit(solution)/shard_map/all_to_all | solution.py:132
  45.8 1.6 %fusion.40 = f32[384,256]{0,1:S(1)} fusion(f32[720,384]{0,1:T(8,128)S(1)} %mul.120, bf16[720,256]{0,1:T(8,128)(2,1)} %bitcast.92), kind=kOutput, calls=%fused_computation.60 | convolution fusion | flops 424673280 | bytes 1867776
  47.4 0.7 convert_bitcast_fusion.1
  48.1 2.3 %copy.87 = bf16[8,384,32]{2,0,1:T(8,128)(2,1)} copy(bf16[8,384,32]{1,2,0:T(8,128)(2,1)} %convert_bitcast_fusion.1) | data formatting | bytes 393216 | tf_op jit(solution)/shard_map/convert_element_type | solution.py:134
  50.4 2.5 %reshape.229 = bf16[8,2,6144]{2,1,0:T(2,128)(2,1)} reshape(bf16[192,2,8,32]{3,2,1,0:T(8,128)(2,1)} %bitcast.90) | data formatting | bytes 393216
  52.9 4.2 %all-to-all-start.1 = ((bf16[8,2,6144]{2,1,0:T(2,128)(2,1)}), bf16[8,2,6144]{2,1,0:T(2,128)(2,1)}, u32[]{:S(2)}, u32[]{:S(2)}) async-start(bf16[8,2,6144]{2,1,0:T(2,128)(2,1)} %reshape.229), calls=%async_computation.1 | async-start | bytes 393216 | tf_op jit(solution)/shard_map/all_to_all | solution.py:137
  57.1 1.3 pad_add_fusion.1
  58.5 4.9 %all-to-all-done.1 = bf16[8,2,6144]{2,1,0:T(2,128)(2,1)} async-done(((bf16[8,2,6144]{2,1,0:T(2,128)(2,1)}), bf16[8,2,6144]{2,1,0:T(2,128)(2,1)}, u32[]{:S(2)}, u32[]{:S(2)}) %all-to-all-start.1) | async-done | bytes 196640 | tf_op jit(solution)/shard_map/all_to_all | solution.py:137
  63.3 2.3 %reshape.230 = bf16[192,2,8,32]{3,2,1,0:T(8,128)(2,1)} reshape(bf16[8,2,6144]{2,1,0:T(2,128)(2,1)} %all-to-all-done.1) | data formatting | bytes 393216
  65.6 1.3 copy.88
  67.0 1.5 %fusion.7 = f32[360,24,2,32]{0,3,2,1:T(8,128)S(1)} fusion(f32[24,360,64]{1,2,0:T(8,128)S(1)} %copy-done, bf16[64,24,2,32]{3,1,2,0:T(8,128)(2,1)S(1)} %bitcast.91), kind=kOutput, calls=%fused_computation.8 | convolution fusion | flops 424673280 | bytes 4620288 | tf_op jit(solution)/shard_map/mls,smpc->lmpc/dot_general | solution.py:138
  68.5 0.3 multiply_add_fusion
  69.1 3.6 %fusion.20 = bf16[64,24,2,32]{0,3,2,1:T(8,128)(2,1)} fusion(f32[24,360,64]{1,2,0:T(8,128)S(1)} %copy-done, f32[360,24,1,32]{0,3,2,1:T(8,128)S(1)} %get-tuple-element.6, f32[360,24,1,32]{0,3,2,1:T(8,128)S(1)} %get-tuple-element.5, f32[64]{0:T(128)S(1)} %copy-done.8), kind=kOutput, calls=%fused_computation.11 | convolution fusion | flops 425422848 | bytes 4620544 | tf_op jit(solution)/shard_map/mls,lmpc->smpc/dot_general | solution.py:153
  72.8 3.1 %copy.91 = bf16[64,24,2,32]{3,2,1,0:T(2,128)(2,1)} copy(bf16[64,24,2,32]{0,3,2,1:T(8,128)(2,1)} %fusion.20) | data formatting | bytes 393216 | tf_op jit(solution)/shard_map/convert_element_type | solution.py:154
  75.9 2.5 %reshape.231 = bf16[8,2,6144]{2,1,0:T(2,128)(2,1)} reshape(bf16[64,24,2,32]{3,2,1,0:T(2,128)(2,1)} %copy.91) | data formatting | bytes 393216
  78.4 4.0 %all-to-all-start.2 = ((bf16[8,2,6144]{2,1,0:T(2,128)(2,1)}), bf16[8,2,6144]{2,1,0:T(2,128)(2,1)}, u32[]{:S(2)}, u32[]{:S(2)}) async-start(bf16[8,2,6144]{2,1,0:T(2,128)(2,1)} %reshape.231), calls=%async_computation.2 | async-start | bytes 393216 | tf_op jit(solution)/shard_map/all_to_all | solution.py:155
  82.4 1.4 %maximum_select_fusion = f32[8,3,3,9]{3,0,2,1:T(8,128)} fusion(f32[8,1,3,9]{3,0,2,1:T(8,128)} %bitcast.97, f32[8,1,3,9]{3,0,2,1:T(8,128)} %bitcast.98, f32[8,1,3,9]{3,0,2,1:T(8,128)S(1)} %bitcast.96, pred[8,3]{0,1:T(4,128)(4,1)} %pad_add_fusion.1), kind=kLoop, calls=%fused_computation.35 | loop fusion | flops 1944 | bytes 5208 | tf_op jit(solution)/shard_map/jit(_where)/select_n | solution.py:94
  83.8 4.8 %all-to-all-done.2 = bf16[8,2,6144]{2,1,0:T(2,128)(2,1)} async-done(((bf16[8,2,6144]{2,1,0:T(2,128)(2,1)}), bf16[8,2,6144]{2,1,0:T(2,128)(2,1)}, u32[]{:S(2)}, u32[]{:S(2)}) %all-to-all-start.2) | async-done | bytes 196640 | tf_op jit(solution)/shard_map/all_to_all | solution.py:155
  88.7 2.3 %reshape.232 = bf16[64,24,2,32]{3,2,1,0:T(2,128)(2,1)} reshape(bf16[8,2,6144]{2,1,0:T(2,128)(2,1)} %all-to-all-done.2) | data formatting | bytes 393216
  90.9 1.2 copy.92
  92.2 1.1 copy.93
  93.3 2.2 %copy.95 = bf16[8,384,32]{1,2,0:T(8,128)(2,1)} copy(bf16[8,384,32]{2,0,1:T(8,128)(2,1)} %bitcast.89) | data formatting | bytes 393216 | tf_op jit(solution)/shard_map/reshape | solution.py:156
  95.5 1.5 %fusion.41 = f32[720,256]{0,1:S(1)} fusion(f32[720,384]{0,1:T(8,128)S(1)} %mul.120, bf16[384,256]{0,1:T(8,128)(2,1)} %bitcast.95), kind=kOutput, calls=%fused_computation.61 | convolution fusion | flops 424673280 | bytes 2039808
  97.1 1.8 %copy.96 = bf16[8,720,32]{2,0,1:T(8,128)(2,1)} copy(bf16[8,720,32]{1,2,0:T(8,128)(2,1)S(1)} %convert_bitcast_fusion) | data formatting | bytes 737280 | tf_op jit(solution)/shard_map/convert_element_type | solution.py:159
  98.9 2.9 %reshape.233 = bf16[4,2,23040]{2,1,0:T(2,128)(2,1)} reshape(bf16[720,8,32]{2,1,0:T(8,128)(2,1)} %bitcast.83) | data formatting | bytes 737280
  101.8 4.8 %all-to-all-start.3 = ((bf16[4,2,23040]{2,1,0:T(2,128)(2,1)}), bf16[4,2,23040]{2,1,0:T(2,128)(2,1)S(1)}, u32[]{:S(2)}, u32[]{:S(2)}) async-start(bf16[4,2,23040]{2,1,0:T(2,128)(2,1)} %reshape.233), calls=%async_computation.3 | async-start | bytes 737280 | tf_op jit(solution)/shard_map/all_to_all | solution.py:162
  106.7 0.7 pad_maximum_fusion.2
  107.4 3.9 %collective-permute-start.3 = (bf16[10,1,128]{2,1,0:T(2,128)(2,1)S(1)}, bf16[10,1,128]{2,1,0:T(2,128)(2,1)S(1)}, u32[]{:S(2)}, u32[]{:S(2)}) collective-permute-start(bf16[10,1,128]{2,1,0:T(2,128)(2,1)S(1)} %get-tuple-element.8), channel_id=1, source_target_pairs={{1,0},{2,1},{3,2},{0,3},{5,4},{6,5},{7,6},{4,7},{9,8},{10,9},{11,1... | collective-permute-start | bytes 7688 | tf_op jit(solution)/shard_map/ppermute | solution.py:111
  111.3 0.7 reshape.207.src_ref
  112.0 0.7 select_n.121.coef_ref
  112.8 1.2 copy.79
  114.0 0.9 copy.80.w_ref
  115.0 1.8 %collective-permute-done.2 = bf16[10,1,128]{2,1,0:T(2,128)(2,1)S(1)} collective-permute-done((bf16[10,1,128]{2,1,0:T(2,128)(2,1)S(1)}, bf16[10,1,128]{2,1,0:T(2,128)(2,1)S(1)}, u32[]{:S(2)}, u32[]{:S(2)}) %collective-permute-start.2) | collective-permute-done | bytes 2592 | tf_op jit(solution)/shard_map/ppermute | solution.py:110
  116.8 1.8 %maximum_maximum_fusion.ext_ref = bf16[10,208,128]{2,1,0:T(8,128)(2,1)} fusion(bf16[10,1,128]{2,1,0:T(2,128)(2,1)S(1)} %collective-permute-done.3, bf16[1,180,128]{2,1,0:T(8,128)(2,1)} %collective-permute-done.1, bf16[8,180,128]{2,1,0:T(8,128)(2,1)S(1)} %copy-done.2, bf16[1,180,128]{2,1,0:T(8,128)(2,1)} %collective-permute-done, ...), kind=kLoop, calls=%fused_computation.29 | loop fusion | flops 3194880 | bytes 998816 | tf_op jit(solution)/shard_map/concatenate | solution.py:114
  118.6 13.9 %shard_map.73 = f32[8,192,128]{2,1,0:T(8,128)} custom-call(s32[24]{0:T(128)} %reshape.207.src_ref, f32[648]{0:T(1024)} %select_n.121.coef_ref, bf16[10,208,128]{2,1,0:T(8,128)(2,1)} %maximum_maximum_fusion.ext_ref, bf16[128,1152]{1,0:T(8,128)(2,1)} %copy.80.w_ref), custom_call_target="tpu_custom_call" | custom-call | tf_op jit(solution)/shard_map/pallas_call | solution.py:58
  132.5 1.7 %reshape.234 = bf16[720,8,32]{2,1,0:T(8,128)(2,1)} reshape(bf16[4,2,23040]{2,1,0:T(2,128)(2,1)S(1)} %all-to-all-done.3) | data formatting | bytes 737280
  134.2 2.1 %copy.97 = f32[8,4,180,32]{2,3,1,0:T(8,128)S(1)} copy(bf16[8,4,180,32]{3,0,2,1:T(8,128)(2,1)} %bitcast.84) | data formatting | bytes 1105920 | tf_op jit(solution)/shard_map/convert_element_type | solution.py:168
  136.3 1.2 copy.98
  137.5 1.7 %fusion.28 = bf16[8,180,128]{2,1,0:T(8,128)(2,1)S(1)} fusion(f32[8,180,128]{2,1,0:T(8,128)} %copy.98, f32[8,192,128]{2,1,0:T(8,128)} %shard_map.73, pred[8]{0:T(512)(128)(4,1)S(1)} %iota_compare_fusion, bf16[8,180,128]{2,0,1:T(8,128)(2,1)} %param.7), kind=kLoop, calls=%fused_computation.20 | loop fusion | flops 1105920 | bytes 2211848 | tf_op jit(solution)/shard_map/convert_element_type | solution.py:169
  139.2 0.8 copy.99
  (37 shorter events, 0.8 us)
Async XLA Ops:
  0.0 66.9 %copy-start = (f32[24,360,64]{1,2,0:T(8,128)S(1)}, f32[24,360,64]{1,2,0:T(8,128)}, u32[]{:S(2)}) copy-start(f32[24,360,64]{1,2,0:T(8,128)} %param.9) | copy-start | bytes 6635524
  3.2 14.3 %copy-start.1 = (bf16[8,180,128]{2,1,0:T(8,128)(2,1)}, bf16[8,180,128]{2,1,0:T(8,128)(2,1)S(1)}, u32[]{:S(2)}) copy-start(bf16[8,180,128]{2,1,0:T(8,128)(2,1)S(1)} %copy_select_fusion) | copy-start | bytes 1105924
  4.4 36.9 %all-to-all-start = ((bf16[8,180,128]{1,0,2:T(8,128)(2,1)}), bf16[8,180,128]{1,0,2:T(8,128)(2,1)}, u32[]{:S(2)}, u32[]{:S(2)}) async-start(bf16[8,180,128]{1,0,2:T(8,128)(2,1)} %copy.83), calls=%async_computation | async-start | bytes 1048576 | tf_op jit(solution)/shard_map/all_to_all | solution.py:132
  12.6 94.0 %collective-permute-start.1 = (bf16[1,180,128]{2,1,0:T(8,128)(2,1)}, bf16[1,180,128]{2,1,0:T(8,128)(2,1)}, u32[]{:S(2)}, u32[]{:S(2)}) collective-permute-start(bf16[1,180,128]{2,1,0:T(8,128)(2,1)} %get-tuple-element.10), channel_id=1, source_target_pairs={{4,0},{8,4},{12,8},{16,12},{20,16},{24,20},{28,24},{0,28},{5,1},{9... | collective-permute-start | bytes 138248 | tf_op jit(solution)/shard_map/ppermute | solution.py:108
  14.2 92.4 %collective-permute-start = (bf16[1,180,128]{2,1,0:T(8,128)(2,1)}, bf16[1,180,128]{2,1,0:T(8,128)(2,1)}, u32[]{:S(2)}, u32[]{:S(2)}) collective-permute-start(bf16[1,180,128]{2,1,0:T(8,128)(2,1)} %get-tuple-element.9), channel_id=1, source_target_pairs={{0,4},{4,8},{8,12},{12,16},{16,20},{20,24},{24,28},{28,0},{1,5},{5... | collective-permute-start | bytes 138248 | tf_op jit(solution)/shard_map/ppermute | solution.py:107
  52.9 10.4 %all-to-all-start.1 = ((bf16[8,2,6144]{2,1,0:T(2,128)(2,1)}), bf16[8,2,6144]{2,1,0:T(2,128)(2,1)}, u32[]{:S(2)}, u32[]{:S(2)}) async-start(bf16[8,2,6144]{2,1,0:T(2,128)(2,1)} %reshape.229), calls=%async_computation.1 | async-start | bytes 393216 | tf_op jit(solution)/shard_map/all_to_all | solution.py:137
  67.0 1.5 %copy-start.3 = (f32[360,32]{0,1:T(8,128)S(1)}, f32[360,32]{0,1:T(8,128)}, u32[]{:S(2)}) copy-start(f32[360,32]{0,1:T(8,128)} %copy.90) | copy-start | bytes 138244
  67.0 1.5 %copy-start.4 = (f32[360,32]{0,1:T(8,128)S(1)}, f32[360,32]{0,1:T(8,128)}, u32[]{:S(2)}) copy-start(f32[360,32]{0,1:T(8,128)} %copy.82) | copy-start | bytes 138244
  68.5 0.7 copy-start.8
  78.4 10.3 %all-to-all-start.2 = ((bf16[8,2,6144]{2,1,0:T(2,128)(2,1)}), bf16[8,2,6144]{2,1,0:T(2,128)(2,1)}, u32[]{:S(2)}, u32[]{:S(2)}) async-start(bf16[8,2,6144]{2,1,0:T(2,128)(2,1)} %reshape.231), calls=%async_computation.2 | async-start | bytes 393216 | tf_op jit(solution)/shard_map/all_to_all | solution.py:155
  98.9 7.7 %copy-start.2 = (bf16[8,180,128]{2,1,0:T(8,128)(2,1)S(1)}, bf16[8,180,128]{2,1,0:T(8,128)(2,1)}, u32[]{:S(2)}) copy-start(bf16[8,180,128]{2,1,0:T(8,128)(2,1)} %copy-done.1) | copy-start | bytes 1105924
  98.9 12.3 %copy-start.6 = (s32[8,1]{0,1:T(1,128)S(1)}, s32[8,1]{0,1:T(1,128)}, u32[]{:S(2)}) copy-start(s32[8,1]{0,1:T(1,128)} %get-tuple-element.20) | copy-start | bytes 100
  98.9 12.3 %copy-start.7 = (s32[8,1]{0,1:T(1,128)S(1)}, s32[8,1]{0,1:T(1,128)}, u32[]{:S(2)}) copy-start(s32[8,1]{0,1:T(1,128)} %get-tuple-element.21) | copy-start | bytes 100
  98.9 13.1 %copy-start.5 = (f32[8,3,3,9]{3,0,2,1:T(8,128)S(1)}, f32[8,3,3,9]{3,0,2,1:T(8,128)}, u32[]{:S(2)}) copy-start(f32[8,3,3,9]{3,0,2,1:T(8,128)} %maximum_select_fusion) | copy-start | bytes 7780
  101.8 30.6 %all-to-all-start.3 = ((bf16[4,2,23040]{2,1,0:T(2,128)(2,1)}), bf16[4,2,23040]{2,1,0:T(2,128)(2,1)S(1)}, u32[]{:S(2)}, u32[]{:S(2)}) async-start(bf16[4,2,23040]{2,1,0:T(2,128)(2,1)} %reshape.233), calls=%async_computation.3 | async-start | bytes 737280 | tf_op jit(solution)/shard_map/all_to_all | solution.py:162
  107.4 7.6 %collective-permute-start.3 = (bf16[10,1,128]{2,1,0:T(2,128)(2,1)S(1)}, bf16[10,1,128]{2,1,0:T(2,128)(2,1)S(1)}, u32[]{:S(2)}, u32[]{:S(2)}) collective-permute-start(bf16[10,1,128]{2,1,0:T(2,128)(2,1)S(1)} %get-tuple-element.8), channel_id=1, source_target_pairs={{1,0},{2,1},{3,2},{0,3},{5,4},{6,5},{7,6},{4,7},{9,8},{10,9},{11,1... | collective-permute-start | bytes 7688 | tf_op jit(solution)/shard_map/ppermute | solution.py:111
  111.2 5.5 %collective-permute-start.2 = (bf16[10,1,128]{2,1,0:T(2,128)(2,1)S(1)}, bf16[10,1,128]{2,1,0:T(2,128)(2,1)S(1)}, u32[]{:S(2)}, u32[]{:S(2)}) collective-permute-start(bf16[10,1,128]{2,1,0:T(2,128)(2,1)S(1)} %get-tuple-element.7), channel_id=1, source_target_pairs={{0,1},{1,2},{2,3},{3,0},{4,5},{5,6},{6,7},{7,4},{8,9},{9,10},{10,1... | collective-permute-start | bytes 7688 | tf_op jit(solution)/shard_map/ppermute | solution.py:110

commit v2 on v1

--- a/solution.py
+++ b/solution.py
@@ -1,3 +1,5 @@
+import ml_dtypes
+import numpy as np
 import jax
 import jax.numpy as jnp
 from jax import lax
@@ -5,18 +7,39 @@
 from jax.experimental.pallas import tpu as pltpu
 from jax.sharding import PartitionSpec as P
 
-highest = lax.Precision.HIGHEST
-tripled = lax.Precision.HIGH
+
+def make_trig(mode_count, point_count):
+    step = next(d for d in range(int(point_count ** 0.5), 0, -1) if point_count % d == 0)
+    coarse = np.arange(point_count // step)[:, None] * step
+    fine = np.arange(step)[:, None]
+    wavenumber = np.arange(mode_count)[None, :]
+    coarse_angle = (wavenumber * coarse % point_count) * (2.0 * np.pi / point_count)
+    fine_angle = (wavenumber * fine % point_count) * (2.0 * np.pi / point_count)
+    scale = point_count ** (-0.5)
+    coarse_cos = jnp.asarray((np.cos(coarse_angle) * scale).astype(np.float32))[:, None, :]
+    coarse_sin = jnp.asarray((np.sin(coarse_angle) * scale).astype(np.float32))[:, None, :]
+    fine_cos = jnp.asarray(np.cos(fine_angle).astype(np.float32))[None, :, :]
+    fine_sin = jnp.asarray(np.sin(fine_angle).astype(np.float32))[None, :, :]
+    cosine = coarse_cos * fine_cos - coarse_sin * fine_sin
+    sine = coarse_sin * fine_cos + coarse_cos * fine_sin
+    table = jnp.stack([cosine, -sine], axis=3).reshape(point_count, 2 * mode_count)
+    return split_bf16(table)
 
 
-def make_trig(mode_count, point_count):
-    wavenumber = lax.broadcasted_iota(jnp.int32, (point_count, mode_count), 1)
-    position = lax.broadcasted_iota(jnp.int32, (point_count, mode_count), 0)
-    angles = (wavenumber * position % point_count).astype(jnp.float32) * (
-        2.0 * jnp.pi / point_count
-    )
-    scaled = jnp.stack([jnp.cos(angles), -jnp.sin(angles)], axis=2) * point_count ** (-0.5)
-    return scaled.reshape(point_count, 2 * mode_count)
+def split_bf16(values):
+    rounded = lax.reduce_precision(values, exponent_bits=8, mantissa_bits=7)
+    return rounded.astype(jnp.bfloat16), (values - rounded).astype(jnp.bfloat16)
+
+
+def dot_split(spec, left_parts, right_parts):
+    total = None
+    for lp in left_parts:
+        for rp in right_parts:
+            if lp is not left_parts[0] and rp is not right_parts[0]:
+                continue
+            term = jnp.einsum(spec, lp, rp, preferred_element_type=jnp.float32)
+            total = term if total is None else total + term
+    return total
 
 
 CHUNK = 64
@@ -128,16 +151,15 @@
     live_rows = band_rows[band_index]
     live_slot = slot_ids < live_rows
     masked = jnp.where(live_slot[:, None, None], grad_output, jnp.zeros_like(grad_output))
-    trig_table = make_trig(mode_count, point_count)
+    trig_parts = make_trig(mode_count, point_count)
     portion = lax.all_to_all(masked, "lon", split_axis=2, concat_axis=1, tiled=True)
-    spectra = jnp.einsum("rnc,nk->rkc", portion.astype(jnp.float32), trig_table, precision=tripled)
+    spectra = dot_split("rnc,nk->rkc", (portion,), trig_parts)
     spectra = spectra.reshape(portion.shape[0], mode_count, 2, portion.shape[2]).astype(
         jnp.bfloat16
     )
     columns = lax.all_to_all(spectra, "lat", split_axis=1, concat_axis=0, tiled=True)
-    coefficients = jnp.einsum(
-        "mls,smpc->lmpc", legendre, columns.astype(jnp.float32), precision=highest
-    )
+    legendre_parts = split_bf16(legendre)
+    coefficients = dot_split("mls,smpc->lmpc", legendre_parts, (columns,))
     filter_slice = lax.dynamic_slice_in_dim(spectral_filter, lon_index * chan_share, chan_share, 2)
     filter_real = filter_slice[0][:, None, :]
     filter_imag = filter_slice[1][:, None, :]
@@ -150,15 +172,11 @@
         ],
         axis=2,
     )
-    returned = jnp.einsum("mls,lmpc->smpc", legendre, filtered, precision=highest)
+    returned = dot_split("mls,lmpc->smpc", legendre_parts, split_bf16(filtered))
     returned = (returned * quad_weights[:, None, None, None]).astype(jnp.bfloat16)
     portion = lax.all_to_all(returned, "lat", split_axis=0, concat_axis=1, tiled=True)
-    flat_modes = portion.reshape(portion.shape[0], 2 * mode_count, portion.shape[3]).astype(
-        jnp.float32
-    )
-    spectral_rows = jnp.einsum("rkc,nk->rnc", flat_modes, trig_table, precision=tripled).astype(
-        jnp.bfloat16
-    )
+    flat_modes = portion.reshape(portion.shape[0], 2 * mode_count, portion.shape[3])
+    spectral_rows = dot_split("rkc,nk->rnc", (flat_modes,), trig_parts).astype(jnp.bfloat16)
     spectral = lax.all_to_all(spectral_rows, "lon", split_axis=1, concat_axis=2, tiled=True)
     ext = halo_extend(masked, live_rows)
     src_rows, coef = disco_tables(band_rows, disco_kernel, band_index, band_total, row_count)

time: 142 us -> 129 us (0.908)
  other arithmetic: 17.2 us -> 9.5 us
  local copies, waits for them, and re-layouts: 62.2 us -> 56.5 us
  waiting for transfers between devices: 11.5 us -> 14.5 us
  matrix products: 8.22 us -> 6.07 us
    convert_element_type x1 -> x5, local copies, waits for them, and re-layouts: 1.84 us -> 27.2 us  [the longest x2 12.9 us: split_bf16(): (values - rounded).astype(jnp.bfloat16)]
    unnamed x26 -> x36, local copies, waits for them, and re-layouts: 17.7 us -> 8.07 us
    mul x2 -> x0, local copies, waits for them, and re-layouts: 4.02 us -> none  [make_trig(): jnp.stack([jnp.cos(angles), -jnp.sin(angles)], axis=2)]
    all_to_all x1 -> x2, local copies, waits for them, and re-layouts: 1.34 us -> 4.85 us  [on_device(): lax.all_to_all(spectra, 'lat', split_axis=1, concat_axis=0, tiled=True)]
    gather x2, local copies, waits for them, and re-layouts: 3.89 us -> 0.62 us  [disco_tables(): gathered = disco_kernel[kernel_row]]
    neg x1 -> x0, other arithmetic: 3.23 us -> none  [make_trig(): -jnp.sin(angles)]
    all_to_all x2, local copies, waits for them, and re-layouts: 4.49 us -> 1.82 us  [on_device(): lax.all_to_all(masked, 'lon', split_axis=2, concat_axis=1, tiled=True)]
    mul x2, local copies, waits for them, and re-layouts: 3.56 us -> 1.3 us  [on_device(): filter_real * real_part + filter_imag * imag_part]
  transfers between devices with their start and end apart: 8 -> 8, of which waited for: 3 -> 3; matrix products, arithmetic and copies ran while one was open for 52% -> 48% of each run, Pallas kernels for 10% -> 11%
where the time goes in v2:
time: 129 us; the launch traced here: 128 us
  local copies, waits for them, and re-layouts  56.5 us (44%)
  starting transfers between devices  25.2 us (20%)
  waiting for transfers between devices  14.5 us (11%)
  Pallas kernels  13.9 us (11%)
  other arithmetic  9.5 us (7%)
  matrix products  6.07 us (5%)
  between operations  2.26 us (2%)
    pallas_call x1, Pallas kernels, disco_apply(): pl.pallas_call(disco_body, out_shape=jax.ShapeDtypeStruct((slot_total, ou...  13.9 us
    convert_element_type x2, local copies, waits for them, and re-layouts, split_bf16(): (values - rounded).astype(jnp.bfloat16)  12.9 us
    convert_element_type x2, local copies, waits for them, and re-layouts, split_bf16(): rounded.astype(jnp.bfloat16)  12.9 us
    unnamed x36, local copies, waits for them, and re-layouts  8.07 us
    all_to_all x1, starting transfers between devices, on_device(): lax.all_to_all(masked, 'lon', split_axis=2, concat_axis=1, tiled=True)  6.32 us
    all_to_all x1, waiting for transfers between devices, on_device(): lax.all_to_all(returned, 'lat', split_axis=0, concat_axis=1, tiled=True)  6.09 us
    all_to_all x1, waiting for transfers between devices, on_device(): lax.all_to_all(spectra, 'lat', split_axis=1, concat_axis=0, tiled=True)  5.91 us
    all_to_all x1, starting transfers between devices, on_device(): lax.all_to_all(spectral_rows, 'lon', split_axis=1, concat_axis=2, tiled=T...  5.09 us
  transfers between devices with their start and end apart: 8, of which 3 were waited for; matrix products, arithmetic and copies ran while one was open for 48% of the time, Pallas kernels for 11%

profile of v2, /device:TPU:0, one launch (start us, length us, event | category | flops | bytes accessed | tf_op | source)
XLA Modules:
  0.0 127.9 jit_solution(1444907293927851108)
XLA Ops:
  0.0 1.3 %fusion.27 = (s32[1]{0:T(128)}, s32[1]{0:T(128)}) fusion(s32[8]{0:T(128)} %param.12, s32[]{:T(128)S(6)} %max.10, s32[]{:T(128)S(6)} %select_n.93), kind=kLoop, calls=%fused_computation.64 | loop fusion | bytes 24 | tf_op jit(solution)/shard_map/dynamic_slice | solution.py:106
  1.3 0.6 iota_compare_fusion
  1.9 1.1 copy_select_fusion
  3.0 1.2 copy.97
  4.2 6.3 %all-to-all-start = ((bf16[8,180,128]{1,0,2:T(8,128)(2,1)}), bf16[8,180,128]{1,0,2:T(8,128)(2,1)}, u32[]{:S(2)}, u32[]{:S(2)}) async-start(bf16[8,180,128]{1,0,2:T(8,128)(2,1)} %copy.97), calls=%async_computation | async-start | bytes 1048576 | tf_op jit(solution)/shard_map/all_to_all | solution.py:155
  11.7 0.6 constant_dynamic-slice_fusion
  12.3 2.6 %collective-permute-start.1 = (bf16[1,180,128]{2,1,0:T(8,128)(2,1)}, bf16[1,180,128]{2,1,0:T(8,128)(2,1)}, u32[]{:S(2)}, u32[]{:S(2)}) collective-permute-start(bf16[1,180,128]{2,1,0:T(8,128)(2,1)} %get-tuple-element.12), channel_id=1, source_target_pairs={{4,0},{8,4},{12,8},{16,12},{20,16},{24,20},{28,24},{0,28},{5,1},{9... | collective-permute-start | bytes 138248 | tf_op jit(solution)/shard_map/ppermute | solution.py:131
  15.2 1.4 %fusion.2 = (bf16[30,24,192,2]{2,1,3,0:T(8,128)(2,1)}, bf16[30,24,192,2]{2,1,3,0:T(8,128)(2,1)}) fusion(f32[30,24,192,1]{2,1,3,0:T(8,128)S(1)} %get-tuple-element.19, f32[30,24,192,1]{2,1,3,0:T(8,128)S(1)} %get-tuple-element.18), kind=kLoop, calls=%fused_computation.11 | loop fusion | flops 1382400 | bytes 2211840 | tf_op jit(solution)/shard_map/convert_element_type | solution.py:31
  16.6 7.2 %copy.101 = bf16[30,24,192,2]{1,0,3,2:T(8,128)(2,1)S(1)} copy(bf16[30,24,192,2]{2,1,3,0:T(8,128)(2,1)} %get-tuple-element.7) | data formatting | bytes 1105920 | tf_op jit(solution)/shard_map/convert_element_type | solution.py:31
  23.8 5.7 %convert_element_type.87 = bf16[720,384]{0,1:T(8,128)(2,1)} reshape(bf16[30,24,192,2]{1,0,3,2:T(8,128)(2,1)S(1)} %copy.101) | data formatting | bytes 1105920 | tf_op jit(solution)/shard_map/convert_element_type | solution.py:31
  29.5 7.2 %copy.95 = bf16[30,24,192,2]{1,0,3,2:T(8,128)(2,1)S(1)} copy(bf16[30,24,192,2]{2,1,3,0:T(8,128)(2,1)} %get-tuple-element.8) | data formatting | bytes 1105920 | tf_op jit(solution)/shard_map/convert_element_type | solution.py:31
  36.7 5.7 %convert_element_type.85 = bf16[720,384]{0,1:T(8,128)(2,1)} reshape(bf16[30,24,192,2]{1,0,3,2:T(8,128)(2,1)S(1)} %copy.95) | data formatting | bytes 1105920 | tf_op jit(solution)/shard_map/convert_element_type | solution.py:31
  42.4 1.2 dynamic-slice_bitcast_fusion.1
  44.5 0.6 fusion.17
  45.2 0.3 copy.89
  45.6 0.6 gather_fusion
  46.3 0.6 compare_select_fusion.2
  47.0 0.6 compare_or_fusion
  47.6 1.4 %copy.99 = bf16[8,4,180,32]{2,1,3,0:T(4,128)(2,1)S(1)} copy(bf16[8,4,180,32]{2,0,3,1:T(8,128)(2,1)} %bitcast.12) | data formatting | bytes 737280 | tf_op jit(solution)/shard_map/all_to_all | solution.py:155
  49.0 0.4 all_to_all.47
  49.4 0.4 fusion.29
  49.8 0.3 copy-done.2
  50.1 0.4 fusion.28
  50.5 0.5 copy.103
  51.0 1.4 %reshape.223 = bf16[8,2,6144]{2,1,0:T(2,128)(2,1)} reshape(bf16[192,2,8,32]{3,2,1,0:T(8,128)(2,1)S(1)} %bitcast.106) | data formatting | bytes 393216
  52.4 3.6 %all-to-all-start.1 = ((bf16[8,2,6144]{2,1,0:T(2,128)(2,1)}), bf16[8,2,6144]{2,1,0:T(2,128)(2,1)S(1)}, u32[]{:S(2)}, u32[]{:S(2)}) async-start(bf16[8,2,6144]{2,1,0:T(2,128)(2,1)} %reshape.223), calls=%async_computation.1 | async-start | bytes 393216 | tf_op jit(solution)/shard_map/all_to_all | solution.py:160
  56.1 5.9 %all-to-all-done.1 = bf16[8,2,6144]{2,1,0:T(2,128)(2,1)S(1)} async-done(((bf16[8,2,6144]{2,1,0:T(2,128)(2,1)}), bf16[8,2,6144]{2,1,0:T(2,128)(2,1)S(1)}, u32[]{:S(2)}, u32[]{:S(2)}) %all-to-all-start.1) | async-done | bytes 196640 | tf_op jit(solution)/shard_map/all_to_all | solution.py:160
  62.0 1.3 reshape.224
  63.3 2.4 %copy.104 = bf16[8,8,24,2,32]{4,2,3,0,1:T(8,128)(2,1)} copy(bf16[8,8,24,2,32]{4,0,3,2,1:T(8,128)(2,1)} %bitcast.104) | data formatting | bytes 393216 | tf_op jit(solution)/shard_map/all_to_all | solution.py:160
  65.6 2.5 %copy.105 = bf16[64,24,2,32]{0,3,2,1:T(8,128)(2,1)} copy(bf16[64,24,2,32]{3,1,2,0:T(8,128)(2,1)} %bitcast.100) | data formatting | bytes 393216 | tf_op jit(solution)/shard_map/all_to_all | solution.py:160
  68.1 1.5 %fusion.24 = f32[24,2,32,360]{3,2,1,0:T(8,128)S(1)} fusion(bf16[64,24,2,32]{0,3,2,1:T(8,128)(2,1)} %copy.105, f32[24,360,64]{1,2,0:T(8,128)S(1)} %copy-done), kind=kOutput, calls=%fused_computation.62 | convolution fusion | flops 71884800 | bytes 4620288 | tf_op jit(solution)/shard_map/mls,smpc->lmpc/dot_general | solution.py:40
  69.7 0.5 add_bitcast_fusion
  70.2 0.3 multiply_add_fusion
  70.5 0.6 fusion.16
  71.1 0.6 convolution_add_fusion.1
  71.8 1.3 %fusion.5 = bf16[64,24,2,32]{0,3,2,1:T(8,128)(2,1)} fusion(f32[24,2,32,64]{3,2,1,0:T(8,128)S(1)} %convolution_add_fusion.1, f32[64]{0:T(128)S(1)} %copy-done.13, f32[24,360,64]{1,2,0:T(8,128)S(1)} %copy-done, f32[360,24,1,32]{0,3,2,1:T(8,128)S(1)} %get-tuple-element.6, f32[360,24,1,32]{0,3,2,1:T(8,128)S(1)} %get-tuple-element.5), kind=kOutput, calls=%fused_computation.17 | convolution fusion | flops 74391552 | bytes 5013760 | tf_op jit(solution)/shard_map/mls,lmpc->smpc/dot_general | solution.py:40
  73.1 2.3 %copy.108 = bf16[64,24,2,32]{3,2,1,0:T(2,128)(2,1)S(1)} copy(bf16[64,24,2,32]{0,3,2,1:T(8,128)(2,1)} %fusion.5) | data formatting | bytes 393216 | tf_op jit(solution)/shard_map/convert_element_type | solution.py:176
  75.4 1.4 %reshape.225 = bf16[8,2,6144]{2,1,0:T(2,128)(2,1)} reshape(bf16[64,24,2,32]{3,2,1,0:T(2,128)(2,1)S(1)} %copy.108) | data formatting | bytes 393216
  76.8 3.4 %all-to-all-start.2 = ((bf16[8,2,6144]{2,1,0:T(2,128)(2,1)}), bf16[8,2,6144]{2,1,0:T(2,128)(2,1)S(1)}, u32[]{:S(2)}, u32[]{:S(2)}) async-start(bf16[8,2,6144]{2,1,0:T(2,128)(2,1)} %reshape.225), calls=%async_computation.2 | async-start | bytes 393216 | tf_op jit(solution)/shard_map/all_to_all | solution.py:177
  80.3 6.1 %all-to-all-done.2 = bf16[8,2,6144]{2,1,0:T(2,128)(2,1)S(1)} async-done(((bf16[8,2,6144]{2,1,0:T(2,128)(2,1)}), bf16[8,2,6144]{2,1,0:T(2,128)(2,1)S(1)}, u32[]{:S(2)}, u32[]{:S(2)}) %all-to-all-start.2) | async-done | bytes 196640 | tf_op jit(solution)/shard_map/all_to_all | solution.py:177
  86.4 0.4 reshape.226
  86.9 0.2 copy.110
  87.1 0.5 copy.112
  87.6 0.4 fusion.31
  87.9 0.2 copy-done.3
  88.1 0.4 fusion.30
  88.6 1.4 %copy.115 = bf16[8,720,32]{2,0,1:T(8,128)(2,1)S(1)} copy(bf16[8,720,32]{1,2,0:T(8,128)(2,1)S(1)} %fusion.12) | data formatting | bytes 737280 | tf_op jit(solution)/shard_map/convert_element_type | solution.py:179
  90.0 1.8 %reshape.227 = bf16[4,2,23040]{2,1,0:T(2,128)(2,1)} reshape(bf16[720,8,32]{2,1,0:T(8,128)(2,1)S(1)} %bitcast.95) | data formatting | bytes 737280
  91.7 5.1 %all-to-all-start.3 = ((bf16[4,2,23040]{2,1,0:T(2,128)(2,1)}), bf16[4,2,23040]{2,1,0:T(2,128)(2,1)S(1)}, u32[]{:S(2)}, u32[]{:S(2)}) async-start(bf16[4,2,23040]{2,1,0:T(2,128)(2,1)} %reshape.227), calls=%async_computation.3 | async-start | bytes 737280 | tf_op jit(solution)/shard_map/all_to_all | solution.py:180
  96.8 0.7 pad_maximum_fusion.4
  97.5 2.1 %collective-permute-start.2 = (bf16[10,1,128]{2,1,0:T(2,128)(2,1)S(1)}, bf16[10,1,128]{2,1,0:T(2,128)(2,1)S(1)}, u32[]{:S(2)}, u32[]{:S(2)}) collective-permute-start(bf16[10,1,128]{2,1,0:T(2,128)(2,1)S(1)} %get-tuple-element.9), channel_id=1, source_target_pairs={{0,1},{1,2},{2,3},{3,0},{4,5},{5,6},{6,7},{7,4},{8,9},{9,10},{10,1... | collective-permute-start | bytes 7688 | tf_op jit(solution)/shard_map/ppermute | solution.py:133
  99.6 2.1 %collective-permute-start.3 = (bf16[10,1,128]{2,1,0:T(2,128)(2,1)S(1)}, bf16[10,1,128]{2,1,0:T(2,128)(2,1)S(1)}, u32[]{:S(2)}, u32[]{:S(2)}) collective-permute-start(bf16[10,1,128]{2,1,0:T(2,128)(2,1)S(1)} %get-tuple-element.10), channel_id=1, source_target_pairs={{1,0},{2,1},{3,2},{0,3},{5,4},{6,5},{7,6},{4,7},{9,8},{10,9},{11,1... | collective-permute-start | bytes 7688 | tf_op jit(solution)/shard_map/ppermute | solution.py:134
  101.7 0.7 select_n.101.coef_ref
  102.6 0.7 reshape.196.src_ref
  103.2 0.2 copy.93
  103.4 0.9 copy.94.w_ref
  104.4 2.5 %collective-permute-done.2 = bf16[10,1,128]{2,1,0:T(2,128)(2,1)S(1)} collective-permute-done((bf16[10,1,128]{2,1,0:T(2,128)(2,1)S(1)}, bf16[10,1,128]{2,1,0:T(2,128)(2,1)S(1)}, u32[]{:S(2)}, u32[]{:S(2)}) %collective-permute-start.2) | collective-permute-done | bytes 2592 | tf_op jit(solution)/shard_map/ppermute | solution.py:133
  107.0 1.8 %maximum_maximum_fusion.ext_ref = bf16[10,208,128]{2,1,0:T(8,128)(2,1)} fusion(bf16[10,1,128]{2,1,0:T(2,128)(2,1)S(1)} %collective-permute-done.3, bf16[1,180,128]{2,1,0:T(8,128)(2,1)} %collective-permute-done.1, bf16[8,180,128]{2,1,0:T(8,128)(2,1)S(1)} %copy_select_fusion, bf16[1,180,128]{2,1,0:T(8,128)(2,1)} %collective-permute-done, ...), kind=kLoop, calls=%fused_computation.29 | loop fusion | flops 3194880 | bytes 998816 | tf_op jit(solution)/shard_map/concatenate | solution.py:137
  108.8 13.9 %shard_map.109 = f32[8,192,128]{2,1,0:T(8,128)} custom-call(s32[24]{0:T(128)} %reshape.196.src_ref, f32[648]{0:T(1024)} %select_n.101.coef_ref, bf16[10,208,128]{2,1,0:T(8,128)(2,1)} %maximum_maximum_fusion.ext_ref, bf16[128,1152]{1,0:T(8,128)(2,1)} %copy.94.w_ref), custom_call_target="tpu_custom_call" | custom-call | tf_op jit(solution)/shard_map/pallas_call | solution.py:81
  122.7 0.8 reshape.228
  123.5 1.0 copy.116
  124.5 1.2 copy.117
  125.8 1.3 %fusion.11 = bf16[8,180,128]{2,1,0:T(8,128)(2,1)S(1)} fusion(f32[8,180,128]{2,1,0:T(8,128)} %copy.117, f32[8,192,128]{2,1,0:T(8,128)S(1)} %copy-done.5, pred[8]{0:T(512)(128)(4,1)S(1)} %iota_compare_fusion, bf16[8,180,128]{2,0,1:T(8,128)(2,1)S(1)} %copy-done.6), kind=kLoop, calls=%fused_computation.26 | loop fusion | flops 1105920 | bytes 2211848 | tf_op jit(solution)/shard_map/convert_element_type | solution.py:187
  127.1 0.8 copy.118
  (55 shorter events, 1.5 us)
Async XLA Ops:
  3.0 12.0 %copy-start.9 = (f32[30,192]{1,0:T(8,128)S(1)}, f32[30,192]{1,0:T(8,128)}, u32[]{:S(2)}) copy-start(f32[30,192]{1,0:T(8,128)} %constant.54.clone) | copy-start | bytes 69124
  3.0 12.0 %copy-start.10 = (f32[30,192]{1,0:T(8,128)S(1)}, f32[30,192]{1,0:T(8,128)}, u32[]{:S(2)}) copy-start(f32[30,192]{1,0:T(8,128)} %constant.55.clone) | copy-start | bytes 69124
  3.0 12.0 %copy-start.11 = (f32[24,192]{1,0:T(8,128)S(1)}, f32[24,192]{1,0:T(8,128)}, u32[]{:S(2)}) copy-start(f32[24,192]{1,0:T(8,128)} %constant.56.clone) | copy-start | bytes 55300
  3.0 12.0 %copy-start.12 = (f32[24,192]{1,0:T(8,128)S(1)}, f32[24,192]{1,0:T(8,128)}, u32[]{:S(2)}) copy-start(f32[24,192]{1,0:T(8,128)} %constant.57.clone) | copy-start | bytes 55300
  4.2 43.4 %all-to-all-start = ((bf16[8,180,128]{1,0,2:T(8,128)(2,1)}), bf16[8,180,128]{1,0,2:T(8,128)(2,1)}, u32[]{:S(2)}, u32[]{:S(2)}) async-start(bf16[8,180,128]{1,0,2:T(8,128)(2,1)} %copy.97), calls=%async_computation | async-start | bytes 1048576 | tf_op jit(solution)/shard_map/all_to_all | solution.py:155
  12.3 84.5 %collective-permute-start = (bf16[1,180,128]{2,1,0:T(8,128)(2,1)}, bf16[1,180,128]{2,1,0:T(8,128)(2,1)}, u32[]{:S(2)}, u32[]{:S(2)}) collective-permute-start(bf16[1,180,128]{2,1,0:T(8,128)(2,1)} %get-tuple-element.11), channel_id=1, source_target_pairs={{0,4},{4,8},{8,12},{12,16},{16,20},{20,24},{24,28},{28,0},{1,5},{5... | collective-permute-start | bytes 138248 | tf_op jit(solution)/shard_map/ppermute | solution.py:130
  12.3 84.5 %collective-permute-start.1 = (bf16[1,180,128]{2,1,0:T(8,128)(2,1)}, bf16[1,180,128]{2,1,0:T(8,128)(2,1)}, u32[]{:S(2)}, u32[]{:S(2)}) collective-permute-start(bf16[1,180,128]{2,1,0:T(8,128)(2,1)} %get-tuple-element.12), channel_id=1, source_target_pairs={{4,0},{8,4},{12,8},{16,12},{20,16},{24,20},{28,24},{0,28},{5,1},{9... | collective-permute-start | bytes 138248 | tf_op jit(solution)/shard_map/ppermute | solution.py:131
  42.4 2.9 %copy-start.8 = (f32[64,9,9]{0,2,1:T(8,128)S(1)}, f32[64,9,9]{0,2,1:T(8,128)}, u32[]{:S(2)}) copy-start(f32[64,9,9]{0,2,1:T(8,128)} %param.16) | copy-start | bytes 62212
  46.2 3.2 %copy-start.1 = (bf16[720,384]{0,1:T(8,128)(2,1)S(1)}, bf16[720,384]{0,1:T(8,128)(2,1)}, u32[]{:S(2)}) copy-start(bf16[720,384]{0,1:T(8,128)(2,1)} %convert_element_type.87) | copy-start | bytes 1658884
  49.0 1.1 copy-start.2
  52.4 9.6 %all-to-all-start.1 = ((bf16[8,2,6144]{2,1,0:T(2,128)(2,1)}), bf16[8,2,6144]{2,1,0:T(2,128)(2,1)S(1)}, u32[]{:S(2)}, u32[]{:S(2)}) async-start(bf16[8,2,6144]{2,1,0:T(2,128)(2,1)} %reshape.223), calls=%async_computation.1 | async-start | bytes 393216 | tf_op jit(solution)/shard_map/all_to_all | solution.py:160
  63.3 4.9 %copy-start = (f32[24,360,64]{1,2,0:T(8,128)S(1)}, f32[24,360,64]{1,2,0:T(8,128)}, u32[]{:S(2)}) copy-start(f32[24,360,64]{1,2,0:T(8,128)} %param.13) | copy-start | bytes 6635524
  68.1 1.5 %copy-start.4 = (bf16[64,24,2,32]{0,3,2,1:T(8,128)(2,1)S(1)}, bf16[64,24,2,32]{0,3,2,1:T(8,128)(2,1)}, u32[]{:S(2)}) copy-start(bf16[64,24,2,32]{0,3,2,1:T(8,128)(2,1)} %copy.105) | copy-start | bytes 589828
  71.1 0.7 copy-start.13
  76.8 9.6 %all-to-all-start.2 = ((bf16[8,2,6144]{2,1,0:T(2,128)(2,1)}), bf16[8,2,6144]{2,1,0:T(2,128)(2,1)S(1)}, u32[]{:S(2)}, u32[]{:S(2)}) async-start(bf16[8,2,6144]{2,1,0:T(2,128)(2,1)} %reshape.225), calls=%async_computation.2 | async-start | bytes 393216 | tf_op jit(solution)/shard_map/all_to_all | solution.py:177
  87.1 1.1 copy-start.3
  90.0 13.3 %copy-start.7 = (bf16[128,9,128]{2,0,1:T(8,128)(2,1)S(1)}, bf16[128,9,128]{2,0,1:T(8,128)(2,1)}, u32[]{:S(2)}) copy-start(bf16[128,9,128]{2,0,1:T(8,128)(2,1)} %param.17) | copy-start | bytes 884740
  91.7 30.9 %all-to-all-start.3 = ((bf16[4,2,23040]{2,1,0:T(2,128)(2,1)}), bf16[4,2,23040]{2,1,0:T(2,128)(2,1)S(1)}, u32[]{:S(2)}, u32[]{:S(2)}) async-start(bf16[4,2,23040]{2,1,0:T(2,128)(2,1)} %reshape.227), calls=%async_computation.3 | async-start | bytes 737280 | tf_op jit(solution)/shard_map/all_to_all | solution.py:180
  97.5 9.4 %collective-permute-start.2 = (bf16[10,1,128]{2,1,0:T(2,128)(2,1)S(1)}, bf16[10,1,128]{2,1,0:T(2,128)(2,1)S(1)}, u32[]{:S(2)}, u32[]{:S(2)}) collective-permute-start(bf16[10,1,128]{2,1,0:T(2,128)(2,1)S(1)} %get-tuple-element.9), channel_id=1, source_target_pairs={{0,1},{1,2},{2,3},{3,0},{4,5},{5,6},{6,7},{7,4},{8,9},{9,10},{10,1... | collective-permute-start | bytes 7688 | tf_op jit(solution)/shard_map/ppermute | solution.py:133
  99.6 7.3 %collective-permute-start.3 = (bf16[10,1,128]{2,1,0:T(2,128)(2,1)S(1)}, bf16[10,1,128]{2,1,0:T(2,128)(2,1)S(1)}, u32[]{:S(2)}, u32[]{:S(2)}) collective-permute-start(bf16[10,1,128]{2,1,0:T(2,128)(2,1)S(1)} %get-tuple-element.10), channel_id=1, source_target_pairs={{1,0},{2,1},{3,2},{0,3},{5,4},{6,5},{7,6},{4,7},{9,8},{10,9},{11,1... | collective-permute-start | bytes 7688 | tf_op jit(solution)/shard_map/ppermute | solution.py:134
  124.5 1.3 copy-start.5
  124.5 1.2 copy-start.6

commit v3 on v2

--- a/solution.py
+++ b/solution.py
@@ -158,8 +158,9 @@
         jnp.bfloat16
     )
     columns = lax.all_to_all(spectra, "lat", split_axis=1, concat_axis=0, tiled=True)
-    legendre_parts = split_bf16(legendre)
-    coefficients = dot_split("mls,smpc->lmpc", legendre_parts, (columns,))
+    coefficients = jnp.einsum(
+        "mls,smpc->lmpc", legendre, columns.astype(jnp.float32), precision=lax.Precision.HIGHEST
+    )
     filter_slice = lax.dynamic_slice_in_dim(spectral_filter, lon_index * chan_share, chan_share, 2)
     filter_real = filter_slice[0][:, None, :]
     filter_imag = filter_slice[1][:, None, :]
@@ -172,7 +173,7 @@
         ],
         axis=2,
     )
-    returned = dot_split("mls,lmpc->smpc", legendre_parts, split_bf16(filtered))
+    returned = jnp.einsum("mls,lmpc->smpc", legendre, filtered, precision=lax.Precision.HIGHEST)
     returned = (returned * quad_weights[:, None, None, None]).astype(jnp.bfloat16)
     portion = lax.all_to_all(returned, "lat", split_axis=0, concat_axis=1, tiled=True)
     flat_modes = portion.reshape(portion.shape[0], 2 * mode_count, portion.shape[3])

time: 129 us -> 148 us (1.15)
  local copies, waits for them, and re-layouts: 56.5 us -> 73 us
  other arithmetic: 9.5 us -> 12.5 us
  waiting for transfers between devices: 14.5 us -> 11.6 us
  matrix products: 6.07 us -> 7.7 us
    unnamed x36 -> x38, local copies, waits for them, and re-layouts: 8.07 us -> 16.3 us
    convert_element_type x2, local copies, waits for them, and re-layouts: 12.9 us -> 9.06 us  [split_bf16(): (values - rounded).astype(jnp.bfloat16)]
    all_to_all x2 -> x1, local copies, waits for them, and re-layouts: 4.85 us -> 1.34 us  [on_device(): lax.all_to_all(spectra, 'lat', split_axis=1, concat_axis=0, tiled=True)]
    convert_element_type x2, local copies, waits for them, and re-layouts: 2.26 us -> 5.4 us  [on_device(): spectral.astype(jnp.float32)]
    all_to_all x2, local copies, waits for them, and re-layouts: 1.82 us -> 4.47 us  [on_device(): lax.all_to_all(masked, 'lon', split_axis=2, concat_axis=1, tiled=True)]
    convert_element_type x2, local copies, waits for them, and re-layouts: 12.9 us -> 10.8 us  [split_bf16(): rounded.astype(jnp.bfloat16)]
    all_to_all x2, local copies, waits for them, and re-layouts: 0.31 us -> 2.33 us  [on_device(): lax.all_to_all(returned, 'lat', split_axis=0, concat_axis=1, tiled=True)]
    gather x2, local copies, waits for them, and re-layouts: 0.62 us -> 2.28 us  [disco_tables(): gathered = disco_kernel[kernel_row]]
  transfers between devices with their start and end apart: 8 -> 8, of which waited for: 3 -> 3; matrix products, arithmetic and copies ran while one was open for 48% -> 52% of each run, Pallas kernels for 11% -> 9%
where the time goes in v3:
time: 148 us; the launch traced here: 146 us
  local copies, waits for them, and re-layouts  73 us (49%)
  starting transfers between devices  25.2 us (17%)
  Pallas kernels  13.9 us (9%)
  other arithmetic  12.5 us (8%)
  waiting for transfers between devices  11.6 us (8%)
  matrix products  7.7 us (5%)
  between operations  2.23 us (2%)
    unnamed x38, local copies, waits for them, and re-layouts  16.3 us
    pallas_call x1, Pallas kernels, disco_apply(): pl.pallas_call(disco_body, out_shape=jax.ShapeDtypeStruct((slot_total, ou...  13.9 us
    convert_element_type x2, local copies, waits for them, and re-layouts, split_bf16(): rounded.astype(jnp.bfloat16)  10.8 us
    convert_element_type x2, local copies, waits for them, and re-layouts, split_bf16(): (values - rounded).astype(jnp.bfloat16)  9.06 us
    all_to_all x1, starting transfers between devices, on_device(): lax.all_to_all(masked, 'lon', split_axis=2, concat_axis=1, tiled=True)  6.32 us
    convert_element_type x2, local copies, waits for them, and re-layouts, on_device(): spectral.astype(jnp.float32)  5.4 us
    all_to_all x1, waiting for transfers between devices, on_device(): lax.all_to_all(spectra, 'lat', split_axis=1, concat_axis=0, tiled=True)  5.27 us
    all_to_all x1, starting transfers between devices, on_device(): lax.all_to_all(spectral_rows, 'lon', split_axis=1, concat_axis=2, tiled=T...  5.08 us
  transfers between devices with their start and end apart: 8, of which 3 were waited for; matrix products, arithmetic and copies ran while one was open for 52% of the time, Pallas kernels for 9%

profile of v3, /device:TPU:0, one launch (start us, length us, event | category | flops | bytes accessed | tf_op | source)
XLA Modules:
  0.0 146.1 jit_solution(12408564904528770350)
XLA Ops:
  0.0 1.5 %fusion.36 = (s32[1]{0:T(128)}, s32[1]{0:T(128)}) fusion(s32[8]{0:T(128)} %param.12, s32[]{:T(128)S(6)} %max.10, s32[]{:T(128)S(6)} %select_n.93), kind=kLoop, calls=%fused_computation.57 | loop fusion | bytes 24 | tf_op jit(solution)/shard_map/dynamic_slice | solution.py:106
  1.5 0.6 iota_compare_fusion
  2.1 1.1 copy_select_fusion
  3.2 1.2 copy.95
  4.4 6.3 %all-to-all-start = ((bf16[8,180,128]{1,0,2:T(8,128)(2,1)}), bf16[8,180,128]{1,0,2:T(8,128)(2,1)}, u32[]{:S(2)}, u32[]{:S(2)}) async-start(bf16[8,180,128]{1,0,2:T(8,128)(2,1)} %copy.95), calls=%async_computation | async-start | bytes 1048576 | tf_op jit(solution)/shard_map/all_to_all | solution.py:155
  12.0 0.7 constant_dynamic-slice_fusion
  12.6 2.6 %collective-permute-start.1 = (bf16[1,180,128]{2,1,0:T(8,128)(2,1)}, bf16[1,180,128]{2,1,0:T(8,128)(2,1)}, u32[]{:S(2)}, u32[]{:S(2)}) collective-permute-start(bf16[1,180,128]{2,1,0:T(8,128)(2,1)} %get-tuple-element.12), channel_id=1, source_target_pairs={{4,0},{8,4},{12,8},{16,12},{20,16},{24,20},{28,24},{0,28},{5,1},{9... | collective-permute-start | bytes 138248 | tf_op jit(solution)/shard_map/ppermute | solution.py:131
  15.5 1.1 fusion.10
  16.6 4.0 %copy.99 = bf16[30,24,192,2]{1,0,3,2:T(8,128)(2,1)} copy(bf16[30,24,192,2]{2,1,3,0:T(8,128)(2,1)S(1)} %get-tuple-element.7) | data formatting | bytes 1105920 | tf_op jit(solution)/shard_map/convert_element_type | solution.py:31
  20.6 5.1 %convert_element_type.76 = bf16[720,384]{0,1:T(8,128)(2,1)S(1)} reshape(bf16[30,24,192,2]{1,0,3,2:T(8,128)(2,1)} %copy.99) | data formatting | bytes 1105920 | tf_op jit(solution)/shard_map/convert_element_type | solution.py:31
  25.7 5.0 %copy.93 = bf16[30,24,192,2]{1,0,3,2:T(8,128)(2,1)} copy(bf16[30,24,192,2]{2,1,3,0:T(8,128)(2,1)} %get-tuple-element.8) | data formatting | bytes 1105920 | tf_op jit(solution)/shard_map/convert_element_type | solution.py:31
  30.7 5.8 %convert_element_type.74 = bf16[720,384]{0,1:T(8,128)(2,1)} reshape(bf16[30,24,192,2]{1,0,3,2:T(8,128)(2,1)} %copy.93) | data formatting | bytes 1105920 | tf_op jit(solution)/shard_map/convert_element_type | solution.py:31
  36.5 1.8 %dynamic-slice_bitcast_fusion.1 = (f32[360,32]{1,0:T(8,128)S(1)}, f32[360,32]{1,0:T(8,128)}) fusion(f32[2,360,128]{2,1,0:T(8,128)} %param.15, s32[]{:T(128)S(6)} %select_n.103, s32[]{:T(128)S(6)} %add.197), kind=kLoop, calls=%fused_computation.32 | loop fusion | bytes 184328 | tf_op jit(solution)/shard_map/mul | solution.py:171
  38.3 1.6 %copy.104 = f32[360,32]{0,1:T(8,128)} copy(f32[360,32]{1,0:T(8,128)} %get-tuple-element.14) | data formatting | bytes 92160 | tf_op jit(solution)/shard_map/mul | solution.py:171
  40.0 0.7 copy.94
  41.4 0.6 fusion.32
  42.2 1.9 %copy.87 = f32[64,9,9]{2,1,0:T(8,128)} copy(f32[64,9,9]{0,2,1:T(8,128)} %param.16) | data formatting | bytes 41472 | tf_op args[5]
  44.2 1.6 %gather_fusion = f32[24,9,9]{2,1,0:T(8,128)S(1)} fusion(f32[64,9,9]{2,1,0:T(8,128)} %copy.87, s32[1024]{0:T(1024)S(1)} %pad_clamp_fusion), kind=kCustom, calls=%fused_computation | custom fusion | bytes 15648 | tf_op jit(solution)/shard_map/gather | solution.py:114
  45.8 0.7 copy.88
  46.5 0.9 reshape.197
  47.4 0.6 pad.20.clone
  48.0 1.2 compare_select_fusion.2
  49.2 1.2 compare_or_fusion
  50.3 0.6 fusion.35
  51.0 2.2 %copy.97 = bf16[8,4,180,32]{2,1,3,0:T(4,128)(2,1)} copy(bf16[8,4,180,32]{2,0,3,1:T(8,128)(2,1)} %bitcast.12) | data formatting | bytes 737280 | tf_op jit(solution)/shard_map/all_to_all | solution.py:155
  53.2 2.2 %all_to_all.47 = bf16[8,720,32]{1,2,0:T(8,128)(2,1)} reshape(bf16[8,4,180,32]{2,1,3,0:T(4,128)(2,1)} %copy.97) | data formatting | bytes 737280 | tf_op jit(solution)/shard_map/all_to_all | solution.py:155
  55.5 1.5 fusion.38
  57.4 1.3 copy.101
  58.7 2.5 %reshape.222 = bf16[8,2,6144]{2,1,0:T(2,128)(2,1)} reshape(bf16[192,2,8,32]{3,2,1,0:T(8,128)(2,1)} %bitcast.105) | data formatting | bytes 393216
  61.2 3.6 %all-to-all-start.1 = ((bf16[8,2,6144]{2,1,0:T(2,128)(2,1)}), bf16[8,2,6144]{2,1,0:T(2,128)(2,1)S(1)}, u32[]{:S(2)}, u32[]{:S(2)}) async-start(bf16[8,2,6144]{2,1,0:T(2,128)(2,1)} %reshape.222), calls=%async_computation.1 | async-start | bytes 393216 | tf_op jit(solution)/shard_map/all_to_all | solution.py:160
  64.8 0.7 pad_add_fusion.1
  65.5 5.3 %all-to-all-done.1 = bf16[8,2,6144]{2,1,0:T(2,128)(2,1)S(1)} async-done(((bf16[8,2,6144]{2,1,0:T(2,128)(2,1)}), bf16[8,2,6144]{2,1,0:T(2,128)(2,1)S(1)}, u32[]{:S(2)}, u32[]{:S(2)}) %all-to-all-start.1) | async-done | bytes 196640 | tf_op jit(solution)/shard_map/all_to_all | solution.py:160
  70.8 1.2 reshape.223
  72.1 1.3 copy.102
  73.4 1.5 %fusion.7 = f32[360,24,2,32]{0,3,2,1:T(8,128)S(1)} fusion(f32[24,360,64]{1,2,0:T(8,128)S(1)} %copy-done, bf16[64,24,2,32]{3,1,2,0:T(8,128)(2,1)S(1)} %bitcast.106), kind=kOutput, calls=%fused_computation.10 | convolution fusion | flops 424673280 | bytes 4620288 | tf_op jit(solution)/shard_map/mls,smpc->lmpc/dot_general | solution.py:161
  75.6 3.6 %fusion.21 = bf16[64,24,2,32]{0,3,2,1:T(8,128)(2,1)} fusion(f32[24,360,64]{1,2,0:T(8,128)S(1)} %copy-done, f32[360,24,1,32]{0,3,2,1:T(8,128)S(1)} %get-tuple-element.6, f32[360,24,1,32]{0,3,2,1:T(8,128)S(1)} %get-tuple-element.5, f32[64]{0:T(128)S(1)} %copy-done.14), kind=kOutput, calls=%fused_computation.15 | convolution fusion | flops 425422848 | bytes 4620544 | tf_op jit(solution)/shard_map/mls,lmpc->smpc/dot_general | solution.py:176
  79.2 3.1 %copy.105 = bf16[64,24,2,32]{3,2,1,0:T(2,128)(2,1)} copy(bf16[64,24,2,32]{0,3,2,1:T(8,128)(2,1)} %fusion.21) | data formatting | bytes 393216 | tf_op jit(solution)/shard_map/convert_element_type | solution.py:177
  82.3 2.5 %reshape.224 = bf16[8,2,6144]{2,1,0:T(2,128)(2,1)} reshape(bf16[64,24,2,32]{3,2,1,0:T(2,128)(2,1)} %copy.105) | data formatting | bytes 393216
  84.9 3.4 %all-to-all-start.2 = ((bf16[8,2,6144]{2,1,0:T(2,128)(2,1)}), bf16[8,2,6144]{2,1,0:T(2,128)(2,1)S(1)}, u32[]{:S(2)}, u32[]{:S(2)}) async-start(bf16[8,2,6144]{2,1,0:T(2,128)(2,1)} %reshape.224), calls=%async_computation.2 | async-start | bytes 393216 | tf_op jit(solution)/shard_map/all_to_all | solution.py:178
  88.3 1.4 maximum_select_fusion
  89.7 4.8 %all-to-all-done.2 = bf16[8,2,6144]{2,1,0:T(2,128)(2,1)S(1)} async-done(((bf16[8,2,6144]{2,1,0:T(2,128)(2,1)}), bf16[8,2,6144]{2,1,0:T(2,128)(2,1)S(1)}, u32[]{:S(2)}, u32[]{:S(2)}) %all-to-all-start.2) | async-done | bytes 196640 | tf_op jit(solution)/shard_map/all_to_all | solution.py:178
  94.4 1.2 reshape.225
  95.7 1.2 copy.106
  96.9 1.1 copy.107
  98.0 1.5 %copy.109 = bf16[8,384,32]{1,2,0:T(8,128)(2,1)S(1)} copy(bf16[8,384,32]{2,0,1:T(8,128)(2,1)} %bitcast.104) | data formatting | bytes 393216 | tf_op jit(solution)/shard_map/reshape | solution.py:179
  99.9 0.7 copy-done.2
  101.1 1.9 %copy.112 = bf16[8,720,32]{2,0,1:T(8,128)(2,1)} copy(bf16[8,720,32]{1,2,0:T(8,128)(2,1)S(1)} %fusion.30) | data formatting | bytes 737280 | tf_op jit(solution)/shard_map/convert_element_type | solution.py:180
  103.0 2.9 %reshape.226 = bf16[4,2,23040]{2,1,0:T(2,128)(2,1)} reshape(bf16[720,8,32]{2,1,0:T(8,128)(2,1)} %bitcast.95) | data formatting | bytes 737280
  105.8 5.1 %all-to-all-start.3 = ((bf16[4,2,23040]{2,1,0:T(2,128)(2,1)}), bf16[4,2,23040]{2,1,0:T(2,128)(2,1)S(1)}, u32[]{:S(2)}, u32[]{:S(2)}) async-start(bf16[4,2,23040]{2,1,0:T(2,128)(2,1)} %reshape.226), calls=%async_computation.3 | async-start | bytes 737280 | tf_op jit(solution)/shard_map/all_to_all | solution.py:181
  110.9 0.7 pad_maximum_fusion.3
  111.6 2.1 %collective-permute-start.2 = (bf16[10,1,128]{2,1,0:T(2,128)(2,1)S(1)}, bf16[10,1,128]{2,1,0:T(2,128)(2,1)S(1)}, u32[]{:S(2)}, u32[]{:S(2)}) collective-permute-start(bf16[10,1,128]{2,1,0:T(2,128)(2,1)S(1)} %get-tuple-element.9), channel_id=1, source_target_pairs={{0,1},{1,2},{2,3},{3,0},{4,5},{5,6},{6,7},{7,4},{8,9},{9,10},{10,1... | collective-permute-start | bytes 7688 | tf_op jit(solution)/shard_map/ppermute | solution.py:133
  113.7 2.1 %collective-permute-start.3 = (bf16[10,1,128]{2,1,0:T(2,128)(2,1)S(1)}, bf16[10,1,128]{2,1,0:T(2,128)(2,1)S(1)}, u32[]{:S(2)}, u32[]{:S(2)}) collective-permute-start(bf16[10,1,128]{2,1,0:T(2,128)(2,1)S(1)} %get-tuple-element.10), channel_id=1, source_target_pairs={{1,0},{2,1},{3,2},{0,3},{5,4},{6,5},{7,6},{4,7},{9,8},{10,9},{11,1... | collective-permute-start | bytes 7688 | tf_op jit(solution)/shard_map/ppermute | solution.py:134
  115.8 0.7 select_n.101.coef_ref
  116.7 0.6 reshape.196.src_ref
  117.3 1.2 copy.91
  118.5 0.9 copy.92.w_ref
  119.5 1.6 %collective-permute-done.2 = bf16[10,1,128]{2,1,0:T(2,128)(2,1)S(1)} collective-permute-done((bf16[10,1,128]{2,1,0:T(2,128)(2,1)S(1)}, bf16[10,1,128]{2,1,0:T(2,128)(2,1)S(1)}, u32[]{:S(2)}, u32[]{:S(2)}) %collective-permute-start.2) | collective-permute-done | bytes 2592 | tf_op jit(solution)/shard_map/ppermute | solution.py:133
  121.0 1.8 %maximum_maximum_fusion.ext_ref = bf16[10,208,128]{2,1,0:T(8,128)(2,1)} fusion(bf16[10,1,128]{2,1,0:T(2,128)(2,1)S(1)} %collective-permute-done.3, bf16[1,180,128]{2,1,0:T(8,128)(2,1)} %collective-permute-done.1, bf16[8,180,128]{2,1,0:T(8,128)(2,1)S(1)} %copy_select_fusion, bf16[1,180,128]{2,1,0:T(8,128)(2,1)} %collective-permute-done, ...), kind=kLoop, calls=%fused_computation.26 | loop fusion | flops 3194880 | bytes 998816 | tf_op jit(solution)/shard_map/concatenate | solution.py:137
  122.9 13.9 %shard_map.109 = f32[8,192,128]{2,1,0:T(8,128)} custom-call(s32[24]{0:T(128)} %reshape.196.src_ref, f32[648]{0:T(1024)} %select_n.101.coef_ref, bf16[10,208,128]{2,1,0:T(8,128)(2,1)} %maximum_maximum_fusion.ext_ref, bf16[128,1152]{1,0:T(8,128)(2,1)} %copy.92.w_ref), custom_call_target="tpu_custom_call" | custom-call | tf_op jit(solution)/shard_map/pallas_call | solution.py:81
  136.7 1.7 %reshape.227 = bf16[720,8,32]{2,1,0:T(8,128)(2,1)} reshape(bf16[4,2,23040]{2,1,0:T(2,128)(2,1)S(1)} %all-to-all-done.3) | data formatting | bytes 737280
  138.4 2.9 %copy.113 = f32[8,4,180,32]{2,3,1,0:T(8,128)} copy(bf16[8,4,180,32]{3,0,2,1:T(8,128)(2,1)} %bitcast.96) | data formatting | bytes 1105920 | tf_op jit(solution)/shard_map/convert_element_type | solution.py:187
  141.3 2.5 %copy.114 = f32[8,180,128]{2,1,0:T(8,128)} copy(f32[8,180,128]{1,2,0:T(8,128)} %bitcast.97) | data formatting | bytes 1474560 | tf_op jit(solution)/shard_map/convert_element_type | solution.py:187
  143.8 1.4 fusion.29
  145.3 0.8 copy.115
  (53 shorter events, 2.5 us)
Async XLA Ops:
  0.0 73.4 %copy-start = (f32[24,360,64]{1,2,0:T(8,128)S(1)}, f32[24,360,64]{1,2,0:T(8,128)}, u32[]{:S(2)}) copy-start(f32[24,360,64]{1,2,0:T(8,128)} %param.13) | copy-start | bytes 6635524
  3.2 12.1 %copy-start.8 = (f32[30,192]{1,0:T(8,128)S(1)}, f32[30,192]{1,0:T(8,128)}, u32[]{:S(2)}) copy-start(f32[30,192]{1,0:T(8,128)} %constant.54.clone) | copy-start | bytes 69124
  3.2 12.1 %copy-start.9 = (f32[30,192]{1,0:T(8,128)S(1)}, f32[30,192]{1,0:T(8,128)}, u32[]{:S(2)}) copy-start(f32[30,192]{1,0:T(8,128)} %constant.55.clone) | copy-start | bytes 69124
  3.2 12.1 %copy-start.10 = (f32[24,192]{1,0:T(8,128)S(1)}, f32[24,192]{1,0:T(8,128)}, u32[]{:S(2)}) copy-start(f32[24,192]{1,0:T(8,128)} %constant.56.clone) | copy-start | bytes 55300
  3.2 12.1 %copy-start.11 = (f32[24,192]{1,0:T(8,128)S(1)}, f32[24,192]{1,0:T(8,128)}, u32[]{:S(2)}) copy-start(f32[24,192]{1,0:T(8,128)} %constant.57.clone) | copy-start | bytes 55300
  4.4 46.5 %all-to-all-start = ((bf16[8,180,128]{1,0,2:T(8,128)(2,1)}), bf16[8,180,128]{1,0,2:T(8,128)(2,1)}, u32[]{:S(2)}, u32[]{:S(2)}) async-start(bf16[8,180,128]{1,0,2:T(8,128)(2,1)} %copy.95), calls=%async_computation | async-start | bytes 1048576 | tf_op jit(solution)/shard_map/all_to_all | solution.py:155
  12.6 98.3 %collective-permute-start = (bf16[1,180,128]{2,1,0:T(8,128)(2,1)}, bf16[1,180,128]{2,1,0:T(8,128)(2,1)}, u32[]{:S(2)}, u32[]{:S(2)}) collective-permute-start(bf16[1,180,128]{2,1,0:T(8,128)(2,1)} %get-tuple-element.11), channel_id=1, source_target_pairs={{0,4},{4,8},{8,12},{12,16},{16,20},{20,24},{24,28},{28,0},{1,5},{5... | collective-permute-start | bytes 138248 | tf_op jit(solution)/shard_map/ppermute | solution.py:130
  12.6 98.3 %collective-permute-start.1 = (bf16[1,180,128]{2,1,0:T(8,128)(2,1)}, bf16[1,180,128]{2,1,0:T(8,128)(2,1)}, u32[]{:S(2)}, u32[]{:S(2)}) collective-permute-start(bf16[1,180,128]{2,1,0:T(8,128)(2,1)} %get-tuple-element.12), channel_id=1, source_target_pairs={{4,0},{8,4},{12,8},{16,12},{20,16},{24,20},{28,24},{0,28},{5,1},{9... | collective-permute-start | bytes 138248 | tf_op jit(solution)/shard_map/ppermute | solution.py:131
  55.5 1.5 %copy-start.1 = (bf16[720,384]{0,1:T(8,128)(2,1)S(1)}, bf16[720,384]{0,1:T(8,128)(2,1)}, u32[]{:S(2)}) copy-start(bf16[720,384]{0,1:T(8,128)(2,1)} %convert_element_type.74) | copy-start | bytes 1658884
  55.5 1.5 %copy-start.3 = (bf16[8,720,32]{1,2,0:T(8,128)(2,1)S(1)}, bf16[8,720,32]{1,2,0:T(8,128)(2,1)}, u32[]{:S(2)}) copy-start(bf16[8,720,32]{1,2,0:T(8,128)(2,1)} %all_to_all.47) | copy-start | bytes 1105924
  61.2 9.6 %all-to-all-start.1 = ((bf16[8,2,6144]{2,1,0:T(2,128)(2,1)}), bf16[8,2,6144]{2,1,0:T(2,128)(2,1)S(1)}, u32[]{:S(2)}, u32[]{:S(2)}) async-start(bf16[8,2,6144]{2,1,0:T(2,128)(2,1)} %reshape.222), calls=%async_computation.1 | async-start | bytes 393216 | tf_op jit(solution)/shard_map/all_to_all | solution.py:160
  73.4 1.5 %copy-start.5 = (f32[360,32]{0,1:T(8,128)S(1)}, f32[360,32]{0,1:T(8,128)}, u32[]{:S(2)}) copy-start(f32[360,32]{0,1:T(8,128)} %copy.104) | copy-start | bytes 138244
  73.4 1.5 %copy-start.6 = (f32[360,32]{0,1:T(8,128)S(1)}, f32[360,32]{0,1:T(8,128)}, u32[]{:S(2)}) copy-start(f32[360,32]{0,1:T(8,128)} %copy.94) | copy-start | bytes 138244
  74.9 0.7 copy-start.14
  84.9 9.6 %all-to-all-start.2 = ((bf16[8,2,6144]{2,1,0:T(2,128)(2,1)}), bf16[8,2,6144]{2,1,0:T(2,128)(2,1)S(1)}, u32[]{:S(2)}, u32[]{:S(2)}) async-start(bf16[8,2,6144]{2,1,0:T(2,128)(2,1)} %reshape.224), calls=%async_computation.2 | async-start | bytes 393216 | tf_op jit(solution)/shard_map/all_to_all | solution.py:178
  99.6 1.1 copy-start.2
  103.0 12.8 %copy-start.12 = (s32[8,1]{0,1:T(1,128)S(1)}, s32[8,1]{0,1:T(1,128)}, u32[]{:S(2)}) copy-start(s32[8,1]{0,1:T(1,128)} %get-tuple-element.22) | copy-start | bytes 100
  103.0 12.8 %copy-start.13 = (s32[8,1]{0,1:T(1,128)S(1)}, s32[8,1]{0,1:T(1,128)}, u32[]{:S(2)}) copy-start(s32[8,1]{0,1:T(1,128)} %get-tuple-element.23) | copy-start | bytes 100
  103.0 12.9 %copy-start.7 = (f32[8,3,3,9]{3,0,2,1:T(8,128)S(1)}, f32[8,3,3,9]{3,0,2,1:T(8,128)}, u32[]{:S(2)}) copy-start(f32[8,3,3,9]{3,0,2,1:T(8,128)} %maximum_select_fusion) | copy-start | bytes 7780
  105.8 30.9 %all-to-all-start.3 = ((bf16[4,2,23040]{2,1,0:T(2,128)(2,1)}), bf16[4,2,23040]{2,1,0:T(2,128)(2,1)S(1)}, u32[]{:S(2)}, u32[]{:S(2)}) async-start(bf16[4,2,23040]{2,1,0:T(2,128)(2,1)} %reshape.226), calls=%async_computation.3 | async-start | bytes 737280 | tf_op jit(solution)/shard_map/all_to_all | solution.py:181
  111.6 9.4 %collective-permute-start.2 = (bf16[10,1,128]{2,1,0:T(2,128)(2,1)S(1)}, bf16[10,1,128]{2,1,0:T(2,128)(2,1)S(1)}, u32[]{:S(2)}, u32[]{:S(2)}) collective-permute-start(bf16[10,1,128]{2,1,0:T(2,128)(2,1)S(1)} %get-tuple-element.9), channel_id=1, source_target_pairs={{0,1},{1,2},{2,3},{3,0},{4,5},{5,6},{6,7},{7,4},{8,9},{9,10},{10,1... | collective-permute-start | bytes 7688 | tf_op jit(solution)/shard_map/ppermute | solution.py:133
  113.7 7.3 %collective-permute-start.3 = (bf16[10,1,128]{2,1,0:T(2,128)(2,1)S(1)}, bf16[10,1,128]{2,1,0:T(2,128)(2,1)S(1)}, u32[]{:S(2)}, u32[]{:S(2)}) collective-permute-start(bf16[10,1,128]{2,1,0:T(2,128)(2,1)S(1)} %get-tuple-element.10), channel_id=1, source_target_pairs={{1,0},{2,1},{3,2},{0,3},{5,4},{6,5},{7,6},{4,7},{9,8},{10,9},{11,1... | collective-permute-start | bytes 7688 | tf_op jit(solution)/shard_map/ppermute | solution.py:134
  141.3 2.5 %copy-start.4 = (f32[8,192,128]{2,1,0:T(8,128)S(1)}, f32[8,192,128]{2,1,0:T(8,128)}, u32[]{:S(2)}) copy-start(f32[8,192,128]{2,1,0:T(8,128)} %shard_map.109) | copy-start | bytes 2359300

commit v4 on v2

--- a/solution.py
+++ b/solution.py
@@ -9,7 +9,7 @@
 
 
 def make_trig(mode_count, point_count):
-    step = next(d for d in range(int(point_count ** 0.5), 0, -1) if point_count % d == 0)
+    step = 16 if point_count % 16 == 0 else 1
     coarse = np.arange(point_count // step)[:, None] * step
     fine = np.arange(step)[:, None]
     wavenumber = np.arange(mode_count)[None, :]
@@ -21,9 +21,10 @@
     fine_cos = jnp.asarray(np.cos(fine_angle).astype(np.float32))[None, :, :]
     fine_sin = jnp.asarray(np.sin(fine_angle).astype(np.float32))[None, :, :]
     cosine = coarse_cos * fine_cos - coarse_sin * fine_sin
-    sine = coarse_sin * fine_cos + coarse_cos * fine_sin
-    table = jnp.stack([cosine, -sine], axis=3).reshape(point_count, 2 * mode_count)
-    return split_bf16(table)
+    minus_sine = -(coarse_sin * fine_cos + coarse_cos * fine_sin)
+    return tuple(
+        split_bf16(part.reshape(point_count, mode_count)) for part in (cosine, minus_sine)
+    )
 
 
 def split_bf16(values):
@@ -153,30 +154,33 @@
     masked = jnp.where(live_slot[:, None, None], grad_output, jnp.zeros_like(grad_output))
     trig_parts = make_trig(mode_count, point_count)
     portion = lax.all_to_all(masked, "lon", split_axis=2, concat_axis=1, tiled=True)
-    spectra = dot_split("rnc,nk->rkc", (portion,), trig_parts)
-    spectra = spectra.reshape(portion.shape[0], mode_count, 2, portion.shape[2]).astype(
-        jnp.bfloat16
+    spectra = jnp.stack(
+        [dot_split("rnc,nk->rkc", (portion,), parts).astype(jnp.bfloat16) for parts in trig_parts],
+        axis=1,
     )
-    columns = lax.all_to_all(spectra, "lat", split_axis=1, concat_axis=0, tiled=True)
+    columns = lax.all_to_all(spectra, "lat", split_axis=2, concat_axis=0, tiled=True)
     legendre_parts = split_bf16(legendre)
-    coefficients = dot_split("mls,smpc->lmpc", legendre_parts, (columns,))
+    coefficients = dot_split("mls,spmc->lpmc", legendre_parts, (columns,))
     filter_slice = lax.dynamic_slice_in_dim(spectral_filter, lon_index * chan_share, chan_share, 2)
     filter_real = filter_slice[0][:, None, :]
     filter_imag = filter_slice[1][:, None, :]
-    real_part = coefficients[:, :, 0, :]
-    imag_part = coefficients[:, :, 1, :]
+    real_part = coefficients[:, 0]
+    imag_part = coefficients[:, 1]
     filtered = jnp.stack(
         [
             filter_real * real_part + filter_imag * imag_part,
             filter_real * imag_part - filter_imag * real_part,
         ],
-        axis=2,
+        axis=1,
     )
-    returned = dot_split("mls,lmpc->smpc", legendre_parts, split_bf16(filtered))
+    returned = dot_split("mls,lpmc->spmc", legendre_parts, split_bf16(filtered))
     returned = (returned * quad_weights[:, None, None, None]).astype(jnp.bfloat16)
-    portion = lax.all_to_all(returned, "lat", split_axis=0, concat_axis=1, tiled=True)
-    flat_modes = portion.reshape(portion.shape[0], 2 * mode_count, portion.shape[3])
-    spectral_rows = dot_split("rkc,nk->rnc", (flat_modes,), trig_parts).astype(jnp.bfloat16)
+    portion = lax.all_to_all(returned, "lat", split_axis=0, concat_axis=2, tiled=True)
+    spectral_rows = None
+    for p, parts in enumerate(trig_parts):
+        term = dot_split("rkc,nk->rnc", (portion[:, p],), parts)
+        spectral_rows = term if spectral_rows is None else spectral_rows + term
+    spectral_rows = spectral_rows.astype(jnp.bfloat16)
     spectral = lax.all_to_all(spectral_rows, "lon", split_axis=1, concat_axis=2, tiled=True)
     ext = halo_extend(masked, live_rows)
     src_rows, coef = disco_tables(band_rows, disco_kernel, band_index, band_total, row_count)

time: 129 us -> 103 us (0.80)
  local copies, waits for them, and re-layouts: 56.5 us -> 29.2 us
  waiting for transfers between devices: 14.5 us -> 18.5 us
  starting transfers between devices: 25.2 us -> 23.7 us
    convert_element_type x6 -> x1, local copies, waits for them, and re-layouts: 27.6 us -> 1.37 us  [on_device(): spectral_rows = spectral_rows.astype(jnp.bfloat16)]
    all_to_all x1, waiting for transfers between devices: 0.01 us -> 3.4 us  [on_device(): lax.all_to_all(masked, 'lon', split_axis=2, concat_axis=1, tiled=True)]
    dot_general x5, matrix products: 4.59 us -> 2.75 us  [dot_split(): term = jnp.einsum(spec, lp, rp, preferred_element_type=jnp.float32)]
    all_to_all x1, starting transfers between devices: 5.09 us -> 3.46 us  [on_device(): lax.all_to_all(spectral_rows, 'lon', split_axis=1, concat_axis=2, tiled=T...]
    convert_element_type x1, local copies, waits for them, and re-layouts: 2.29 us -> 0.77 us  [on_device(): (returned * quad_weights[:, None, None, None]).astype(jnp.bfloat16)]
    all_to_all x4 -> x5, local copies, waits for them, and re-layouts: 5.16 us -> 5.74 us  [the longest x2 4.1 us: on_device(): lax.all_to_all(spectra, 'lat', split_axis=2, concat_axis=0, tiled=True)]
    unnamed x36 -> x54, local copies, waits for them, and re-layouts: 8.07 us -> 8.63 us
  transfers between devices with their start and end apart: 8 -> 8, of which waited for: 3 -> 4; matrix products, arithmetic and copies ran while one was open for 48% -> 32% of each run, Pallas kernels for 11% -> 14%
where the time goes in v4:
time: 103 us; the launch traced here: 102 us
  local copies, waits for them, and re-layouts  29.2 us (28%)
  starting transfers between devices  23.7 us (23%)
  waiting for transfers between devices  18.5 us (18%)
  Pallas kernels  13.9 us (13%)
  other arithmetic  9.28 us (9%)
  matrix products  5 us (5%)
  between operations  2.52 us (2%)
    pallas_call x1, Pallas kernels, disco_apply(): pl.pallas_call(disco_body, out_shape=jax.ShapeDtypeStruct((slot_total, ou...  13.9 us
    unnamed x54, local copies, waits for them, and re-layouts  8.63 us
    all_to_all x1, starting transfers between devices, on_device(): lax.all_to_all(masked, 'lon', split_axis=2, concat_axis=1, tiled=True)  6.45 us
    all_to_all x1, waiting for transfers between devices, on_device(): lax.all_to_all(spectra, 'lat', split_axis=2, concat_axis=0, tiled=True)  6.16 us
    all_to_all x1, waiting for transfers between devices, on_device(): lax.all_to_all(returned, 'lat', split_axis=0, concat_axis=2, tiled=True)  5.88 us
    all_to_all x2, local copies, waits for them, and re-layouts, on_device(): lax.all_to_all(spectra, 'lat', split_axis=2, concat_axis=0, tiled=True)  4.1 us
    all_to_all x1, starting transfers between devices, on_device(): lax.all_to_all(spectra, 'lat', split_axis=2, concat_axis=0, tiled=True)  3.72 us
    all_to_all x1, starting transfers between devices, on_device(): lax.all_to_all(returned, 'lat', split_axis=0, concat_axis=2, tiled=True)  3.57 us
  transfers between devices with their start and end apart: 8, of which 4 were waited for; matrix products, arithmetic and copies ran while one was open for 32% of the time, Pallas kernels for 14%

profile of v4, /device:TPU:0, one launch (start us, length us, event | category | flops | bytes accessed | tf_op | source)
XLA Modules:
  0.0 102.1 jit_solution(13030572581893976936)
XLA Ops:
  0.0 1.4 %fusion.30 = (s32[1]{0:T(128)}, s32[1]{0:T(128)}) fusion(s32[8]{0:T(128)} %param.12, s32[]{:T(128)S(6)} %max.10, s32[]{:T(128)S(6)} %select_n.93), kind=kLoop, calls=%fused_computation.70 | loop fusion | bytes 24 | tf_op jit(solution)/shard_map/dynamic_slice | solution.py:107
  1.4 0.6 iota_compare_fusion
  2.0 1.1 %copy_select_fusion = bf16[8,180,128]{2,1,0:T(8,128)(2,1)S(1)} fusion(bf16[8,180,128]{2,0,1:T(8,128)(2,1)} %param.11, pred[8]{0:T(512)(128)(4,1)S(1)} %iota_compare_fusion), kind=kLoop, calls=%fused_computation.33 | loop fusion | flops 184320 | bytes 737288 | tf_op jit(solution)/shard_map/jit(_where)/select_n | solution.py:154
  3.1 1.2 %copy.103 = bf16[8,180,128]{1,0,2:T(8,128)(2,1)} copy(bf16[8,180,128]{2,1,0:T(8,128)(2,1)S(1)} %copy_select_fusion) | data formatting | bytes 737280 | tf_op jit(solution)/shard_map/jit(_where)/select_n | solution.py:154
  4.3 6.4 %all-to-all-start = ((bf16[8,180,128]{1,0,2:T(8,128)(2,1)}), bf16[8,180,128]{1,0,2:T(8,128)(2,1)S(1)}, u32[]{:S(2)}, u32[]{:S(2)}) async-start(bf16[8,180,128]{1,0,2:T(8,128)(2,1)} %copy.103), calls=%async_computation | async-start | bytes 1048576 | tf_op jit(solution)/shard_map/all_to_all | solution.py:156
  12.0 0.6 constant_dynamic-slice_fusion
  12.7 2.6 %collective-permute-start.1 = (bf16[1,180,128]{2,1,0:T(8,128)(2,1)}, bf16[1,180,128]{2,1,0:T(8,128)(2,1)}, u32[]{:S(2)}, u32[]{:S(2)}) collective-permute-start(bf16[1,180,128]{2,1,0:T(8,128)(2,1)} %get-tuple-element.10), channel_id=1, source_target_pairs={{4,0},{8,4},{12,8},{16,12},{20,16},{24,20},{28,24},{0,28},{5,1},{9... | collective-permute-start | bytes 138248 | tf_op jit(solution)/shard_map/ppermute | solution.py:132
  15.3 1.2 %compare_select_fusion.2 = (s32[8,1]{0,1:T(1,128)}, s32[8,1]{0,1:T(1,128)}) fusion(s32[]{:T(128)} %bitcast), kind=kLoop, calls=%fused_computation.49 | loop fusion | flops 48 | bytes 68 | tf_op jit(solution)/shard_map/jit(_where)/select_n | solution.py:103
  16.9 0.7 copy.115
  18.3 0.6 fusion.19
  19.1 0.3 copy.96
  19.4 0.6 gather_fusion
  20.2 0.6 compare_or_fusion
  20.8 0.6 fusion.29
  21.5 0.4 fusion.11
  21.9 3.4 %all-to-all-done = bf16[8,180,128]{1,0,2:T(8,128)(2,1)S(1)} async-done(((bf16[8,180,128]{1,0,2:T(8,128)(2,1)}), bf16[8,180,128]{1,0,2:T(8,128)(2,1)S(1)}, u32[]{:S(2)}, u32[]{:S(2)}) %all-to-all-start) | async-done | bytes 368672 | tf_op jit(solution)/shard_map/all_to_all | solution.py:156
  25.3 0.4 copy.105
  25.7 0.4 all_to_all.49
  26.1 0.3 fusion.36
  26.3 0.3 fusion.37
  26.9 0.3 fusion.35
  27.3 0.7 copy.110
  28.0 1.4 %reshape.271 = bf16[8,2,6144]{2,1,0:T(2,128)(2,1)} reshape(bf16[192,2,8,32]{3,2,1,0:T(8,128)(2,1)S(1)} %bitcast.155) | data formatting | bytes 393216
  29.4 3.7 %all-to-all-start.1 = ((bf16[8,2,6144]{2,1,0:T(2,128)(2,1)}), bf16[8,2,6144]{2,1,0:T(2,128)(2,1)S(1)}, u32[]{:S(2)}, u32[]{:S(2)}) async-start(bf16[8,2,6144]{2,1,0:T(2,128)(2,1)} %reshape.271), calls=%async_computation.1 | async-start | bytes 393216 | tf_op jit(solution)/shard_map/all_to_all | solution.py:161
  33.2 6.2 %all-to-all-done.1 = bf16[8,2,6144]{2,1,0:T(2,128)(2,1)S(1)} async-done(((bf16[8,2,6144]{2,1,0:T(2,128)(2,1)}), bf16[8,2,6144]{2,1,0:T(2,128)(2,1)S(1)}, u32[]{:S(2)}, u32[]{:S(2)}) %all-to-all-start.1) | async-done | bytes 196640 | tf_op jit(solution)/shard_map/all_to_all | solution.py:161
  39.4 1.3 %reshape.272 = bf16[192,2,8,32]{3,2,1,0:T(8,128)(2,1)} reshape(bf16[8,2,6144]{2,1,0:T(2,128)(2,1)S(1)} %all-to-all-done.1) | data formatting | bytes 393216
  40.6 2.4 %copy.112 = bf16[8,8,2,24,32]{4,3,2,1,0:T(8,128)(2,1)} copy(bf16[8,8,2,24,32]{4,1,2,3,0:T(8,128)(2,1)} %bitcast.152) | data formatting | bytes 393216 | tf_op jit(solution)/shard_map/all_to_all | solution.py:161
  43.0 1.7 %copy.113 = bf16[64,2,24,32]{0,3,1,2:T(8,128)(2,1)S(1)} copy(bf16[64,2,24,32]{3,2,1,0:T(8,128)(2,1)} %bitcast.151) | data formatting | bytes 393216 | tf_op jit(solution)/shard_map/all_to_all | solution.py:161
  44.7 0.5 fusion.26
  45.2 0.5 add_bitcast_fusion
  45.7 0.3 copy-done.11
  46.0 0.3 multiply_add_fusion
  46.3 0.6 fusion.18
  47.0 0.6 convolution_add_fusion.1
  47.6 0.6 fusion.4
  48.2 0.8 copy.116
  49.0 1.4 %reshape.273 = bf16[8,2,6144]{2,1,0:T(2,128)(2,1)} reshape(bf16[64,24,2,32]{3,2,1,0:T(2,128)(2,1)S(1)} %bitcast.153) | data formatting | bytes 393216
  50.4 3.6 %all-to-all-start.2 = ((bf16[8,2,6144]{2,1,0:T(2,128)(2,1)}), bf16[8,2,6144]{2,1,0:T(2,128)(2,1)S(1)}, u32[]{:S(2)}, u32[]{:S(2)}) async-start(bf16[8,2,6144]{2,1,0:T(2,128)(2,1)} %reshape.273), calls=%async_computation.2 | async-start | bytes 393216 | tf_op jit(solution)/shard_map/all_to_all | solution.py:178
  54.1 5.9 %all-to-all-done.2 = bf16[8,2,6144]{2,1,0:T(2,128)(2,1)S(1)} async-done(((bf16[8,2,6144]{2,1,0:T(2,128)(2,1)}), bf16[8,2,6144]{2,1,0:T(2,128)(2,1)S(1)}, u32[]{:S(2)}, u32[]{:S(2)}) %all-to-all-start.2) | async-done | bytes 196640 | tf_op jit(solution)/shard_map/all_to_all | solution.py:178
  60.0 0.4 reshape.274
  60.5 0.8 copy.142
  61.3 0.7 reshape.269
  62.3 0.3 fusion.31
  62.6 0.4 copy-done.4
  63.1 0.3 fusion.32
  63.4 0.3 fusion.34
  63.7 0.3 fusion.33
  64.2 1.4 %copy.125 = bf16[8,720,32]{2,0,1:T(8,128)(2,1)S(1)} copy(bf16[8,720,32]{1,2,0:T(8,128)(2,1)S(1)} %fusion.13) | data formatting | bytes 737280 | tf_op jit(solution)/shard_map/convert_element_type | solution.py:183
  65.6 1.8 %reshape.275 = bf16[4,2,23040]{2,1,0:T(2,128)(2,1)} reshape(bf16[720,8,32]{2,1,0:T(8,128)(2,1)S(1)} %bitcast.135) | data formatting | bytes 737280
  67.3 3.5 %all-to-all-start.3 = ((bf16[4,2,23040]{2,1,0:T(2,128)(2,1)}), bf16[4,2,23040]{2,1,0:T(2,128)(2,1)S(1)}, u32[]{:S(2)}, u32[]{:S(2)}) async-start(bf16[4,2,23040]{2,1,0:T(2,128)(2,1)} %reshape.275), calls=%async_computation.3 | async-start | bytes 737280 | tf_op jit(solution)/shard_map/all_to_all | solution.py:184
  70.8 0.7 pad_maximum_fusion.4
  71.5 2.0 %collective-permute-start.2 = (bf16[10,1,128]{2,1,0:T(2,128)(2,1)S(1)}, bf16[10,1,128]{2,1,0:T(2,128)(2,1)S(1)}, u32[]{:S(2)}, u32[]{:S(2)}) collective-permute-start(bf16[10,1,128]{2,1,0:T(2,128)(2,1)S(1)} %get-tuple-element.7), channel_id=1, source_target_pairs={{0,1},{1,2},{2,3},{3,0},{4,5},{5,6},{6,7},{7,4},{8,9},{9,10},{10,1... | collective-permute-start | bytes 7688 | tf_op jit(solution)/shard_map/ppermute | solution.py:134
  73.5 1.9 %collective-permute-start.3 = (bf16[10,1,128]{2,1,0:T(2,128)(2,1)S(1)}, bf16[10,1,128]{2,1,0:T(2,128)(2,1)S(1)}, u32[]{:S(2)}, u32[]{:S(2)}) collective-permute-start(bf16[10,1,128]{2,1,0:T(2,128)(2,1)S(1)} %get-tuple-element.8), channel_id=1, source_target_pairs={{1,0},{2,1},{3,2},{0,3},{5,4},{6,5},{7,6},{4,7},{9,8},{10,9},{11,1... | collective-permute-start | bytes 7688 | tf_op jit(solution)/shard_map/ppermute | solution.py:135
  75.5 0.7 select_n.101.coef_ref
  76.3 0.6 reshape.236.src_ref
  77.1 0.9 copy.101.w_ref
  78.1 3.0 %collective-permute-done.2 = bf16[10,1,128]{2,1,0:T(2,128)(2,1)S(1)} collective-permute-done((bf16[10,1,128]{2,1,0:T(2,128)(2,1)S(1)}, bf16[10,1,128]{2,1,0:T(2,128)(2,1)S(1)}, u32[]{:S(2)}, u32[]{:S(2)}) %collective-permute-start.2) | collective-permute-done | bytes 2592 | tf_op jit(solution)/shard_map/ppermute | solution.py:134
  81.1 1.8 %maximum_maximum_fusion.ext_ref = bf16[10,208,128]{2,1,0:T(8,128)(2,1)} fusion(bf16[10,1,128]{2,1,0:T(2,128)(2,1)S(1)} %collective-permute-done.3, bf16[1,180,128]{2,1,0:T(8,128)(2,1)} %collective-permute-done.1, bf16[8,180,128]{2,1,0:T(8,128)(2,1)S(1)} %copy_select_fusion, bf16[1,180,128]{2,1,0:T(8,128)(2,1)} %collective-permute-done, ...), kind=kLoop, calls=%fused_computation.31 | loop fusion | flops 3194880 | bytes 998816 | tf_op jit(solution)/shard_map/concatenate | solution.py:138
  83.0 13.9 %shard_map.109 = f32[8,192,128]{2,1,0:T(8,128)} custom-call(s32[24]{0:T(128)} %reshape.236.src_ref, f32[648]{0:T(1024)} %select_n.101.coef_ref, bf16[10,208,128]{2,1,0:T(8,128)(2,1)} %maximum_maximum_fusion.ext_ref, bf16[128,1152]{1,0:T(8,128)(2,1)} %copy.101.w_ref), custom_call_target="tpu_custom_call" | custom-call | tf_op jit(solution)/shard_map/pallas_call | solution.py:82
  96.8 0.8 reshape.276
  97.7 1.0 %copy.126 = f32[8,4,180,32]{2,3,1,0:T(8,128)S(1)} copy(bf16[8,4,180,32]{3,0,2,1:T(8,128)(2,1)S(1)} %bitcast.136) | data formatting | bytes 1105920 | tf_op jit(solution)/shard_map/convert_element_type | solution.py:190
  98.7 1.2 %copy.127 = f32[8,180,128]{2,1,0:T(8,128)} copy(f32[8,180,128]{1,2,0:T(8,128)S(1)} %bitcast.137) | data formatting | bytes 1474560 | tf_op jit(solution)/shard_map/convert_element_type | solution.py:190
  99.9 1.3 %fusion.10 = bf16[8,180,128]{2,1,0:T(8,128)(2,1)S(1)} fusion(f32[8,180,128]{2,1,0:T(8,128)} %copy.127, f32[8,192,128]{2,1,0:T(8,128)S(1)} %copy-done.7, pred[8]{0:T(512)(128)(4,1)S(1)} %iota_compare_fusion, bf16[8,180,128]{2,0,1:T(8,128)(2,1)S(1)} %copy-done.8), kind=kLoop, calls=%fused_computation.26 | loop fusion | flops 1105920 | bytes 2211848 | tf_op jit(solution)/shard_map/convert_element_type | solution.py:191
  101.3 0.8 copy.128
  (74 shorter events, 2.3 us)
Async XLA Ops:
  3.1 13.4 %copy-start.9 = (f32[2,360,128]{2,1,0:T(8,128)S(1)}, f32[2,360,128]{2,1,0:T(8,128)}, u32[]{:S(2)}) copy-start(f32[2,360,128]{2,1,0:T(8,128)} %param.15) | copy-start | bytes 1105924
  4.3 14.8 %copy-start.12 = (f32[64,9,9]{0,2,1:T(8,128)S(1)}, f32[64,9,9]{0,2,1:T(8,128)}, u32[]{:S(2)}) copy-start(f32[64,9,9]{0,2,1:T(8,128)} %param.16) | copy-start | bytes 62212
  4.3 20.9 %all-to-all-start = ((bf16[8,180,128]{1,0,2:T(8,128)(2,1)}), bf16[8,180,128]{1,0,2:T(8,128)(2,1)S(1)}, u32[]{:S(2)}, u32[]{:S(2)}) async-start(bf16[8,180,128]{1,0,2:T(8,128)(2,1)} %copy.103), calls=%async_computation | async-start | bytes 1048576 | tf_op jit(solution)/shard_map/all_to_all | solution.py:156
  12.7 58.1 %collective-permute-start = (bf16[1,180,128]{2,1,0:T(8,128)(2,1)}, bf16[1,180,128]{2,1,0:T(8,128)(2,1)}, u32[]{:S(2)}, u32[]{:S(2)}) collective-permute-start(bf16[1,180,128]{2,1,0:T(8,128)(2,1)} %get-tuple-element.9), channel_id=1, source_target_pairs={{0,4},{4,8},{8,12},{12,16},{16,20},{20,24},{24,28},{28,0},{1,5},{5... | collective-permute-start | bytes 138248 | tf_op jit(solution)/shard_map/ppermute | solution.py:131
  12.7 58.1 %collective-permute-start.1 = (bf16[1,180,128]{2,1,0:T(8,128)(2,1)}, bf16[1,180,128]{2,1,0:T(8,128)(2,1)}, u32[]{:S(2)}, u32[]{:S(2)}) collective-permute-start(bf16[1,180,128]{2,1,0:T(8,128)(2,1)} %get-tuple-element.10), channel_id=1, source_target_pairs={{4,0},{8,4},{12,8},{16,12},{20,16},{24,20},{28,24},{0,28},{5,1},{9... | collective-permute-start | bytes 138248 | tf_op jit(solution)/shard_map/ppermute | solution.py:132
  16.7 4.8 %copy-start.13 = (f32[45,192]{1,0:T(8,128)S(1)}, f32[45,192]{1,0:T(8,128)}, u32[]{:S(2)}) copy-start(f32[45,192]{1,0:T(8,128)} %constant.54.clone) | copy-start | bytes 103684
  16.7 4.7 %copy-start.14 = (f32[45,192]{1,0:T(8,128)S(1)}, f32[45,192]{1,0:T(8,128)}, u32[]{:S(2)}) copy-start(f32[45,192]{1,0:T(8,128)} %constant.55.clone) | copy-start | bytes 103684
  16.7 4.7 %copy-start.18 = (f32[16,192]{1,0:T(8,128)S(1)}, f32[16,192]{1,0:T(8,128)}, u32[]{:S(2)}) copy-start(f32[16,192]{1,0:T(8,128)} %constant.56.clone) | copy-start | bytes 36868
  16.7 4.7 %copy-start.19 = (f32[16,192]{1,0:T(8,128)S(1)}, f32[16,192]{1,0:T(8,128)}, u32[]{:S(2)}) copy-start(f32[16,192]{1,0:T(8,128)} %constant.57.clone) | copy-start | bytes 36868
  21.8 4.5 %copy-start.3 = (bf16[45,16,192]{2,1,0:T(8,128)(2,1)}, bf16[45,16,192]{2,1,0:T(8,128)(2,1)S(1)}, u32[]{:S(2)}) copy-start(bf16[45,16,192]{2,1,0:T(8,128)(2,1)S(1)} %get-tuple-element.18) | copy-start | bytes 829444
  21.8 4.8 %copy-start.1 = (bf16[45,16,192]{2,1,0:T(8,128)(2,1)}, bf16[45,16,192]{2,1,0:T(8,128)(2,1)S(1)}, u32[]{:S(2)}) copy-start(bf16[45,16,192]{2,1,0:T(8,128)(2,1)S(1)} %get-tuple-element.20) | copy-start | bytes 829444
  21.9 5.1 %copy-start.5 = (bf16[45,16,192]{2,1,0:T(8,128)(2,1)}, bf16[45,16,192]{2,1,0:T(8,128)(2,1)S(1)}, u32[]{:S(2)}) copy-start(bf16[45,16,192]{2,1,0:T(8,128)(2,1)S(1)} %get-tuple-element.21) | copy-start | bytes 829444
  29.4 10.0 %all-to-all-start.1 = ((bf16[8,2,6144]{2,1,0:T(2,128)(2,1)}), bf16[8,2,6144]{2,1,0:T(2,128)(2,1)S(1)}, u32[]{:S(2)}, u32[]{:S(2)}) async-start(bf16[8,2,6144]{2,1,0:T(2,128)(2,1)} %reshape.271), calls=%async_computation.1 | async-start | bytes 393216 | tf_op jit(solution)/shard_map/all_to_all | solution.py:161
  40.6 4.1 %copy-start = (f32[24,360,64]{1,2,0:T(8,128)S(1)}, f32[24,360,64]{1,2,0:T(8,128)}, u32[]{:S(2)}) copy-start(f32[24,360,64]{1,2,0:T(8,128)} %param.13) | copy-start | bytes 6635524
  45.2 0.8 copy-start.11
  46.9 0.7 copy-start.20
  48.2 5.8 %copy-start.15 = (f32[8,1,1,3,9]{4,1,0,3,2:T(1,128)S(1)}, f32[8,1,1,3,9]{4,1,0,3,2:T(1,128)}, u32[]{:S(2)}) copy-start(f32[8,1,1,3,9]{4,1,0,3,2:T(1,128)} %get-tuple-element.15) | copy-start | bytes 2596
  48.2 5.8 %copy-start.16 = (f32[8,1,1,3,9]{4,1,0,3,2:T(1,128)S(1)}, f32[8,1,1,3,9]{4,1,0,3,2:T(1,128)}, u32[]{:S(2)}) copy-start(f32[8,1,1,3,9]{4,1,0,3,2:T(1,128)} %get-tuple-element.16) | copy-start | bytes 2596
  48.2 5.8 %copy-start.17 = (f32[8,1,1,3,9]{4,1,0,3,2:T(1,128)S(1)}, f32[8,1,1,3,9]{4,1,0,3,2:T(1,128)}, u32[]{:S(2)}) copy-start(f32[8,1,1,3,9]{4,1,0,3,2:T(1,128)} %get-tuple-element.17) | copy-start | bytes 2596
  50.4 9.6 %all-to-all-start.2 = ((bf16[8,2,6144]{2,1,0:T(2,128)(2,1)}), bf16[8,2,6144]{2,1,0:T(2,128)(2,1)S(1)}, u32[]{:S(2)}, u32[]{:S(2)}) async-start(bf16[8,2,6144]{2,1,0:T(2,128)(2,1)} %reshape.273), calls=%async_computation.2 | async-start | bytes 393216 | tf_op jit(solution)/shard_map/all_to_all | solution.py:178
  61.3 1.0 copy-start.6
  62.0 1.0 copy-start.4
  62.3 1.0 %copy-start.2 = (bf16[45,16,192]{2,1,0:T(8,128)(2,1)S(1)}, bf16[45,16,192]{2,1,0:T(8,128)(2,1)}, u32[]{:S(2)}) copy-start(bf16[45,16,192]{2,1,0:T(8,128)(2,1)} %copy-done.1) | copy-start | bytes 829444
  65.5 9.9 %copy-start.21 = (s32[8,1]{0,1:T(1,128)S(1)}, s32[8,1]{0,1:T(1,128)}, u32[]{:S(2)}) copy-start(s32[8,1]{0,1:T(1,128)} %get-tuple-element.26) | copy-start | bytes 100
  65.5 9.9 %copy-start.22 = (s32[8,1]{0,1:T(1,128)S(1)}, s32[8,1]{0,1:T(1,128)}, u32[]{:S(2)}) copy-start(s32[8,1]{0,1:T(1,128)} %get-tuple-element.27) | copy-start | bytes 100
  65.6 11.3 %copy-start.10 = (bf16[128,9,128]{2,0,1:T(8,128)(2,1)S(1)}, bf16[128,9,128]{2,0,1:T(8,128)(2,1)}, u32[]{:S(2)}) copy-start(bf16[128,9,128]{2,0,1:T(8,128)(2,1)} %param.17) | copy-start | bytes 884740
  67.3 29.5 %all-to-all-start.3 = ((bf16[4,2,23040]{2,1,0:T(2,128)(2,1)}), bf16[4,2,23040]{2,1,0:T(2,128)(2,1)S(1)}, u32[]{:S(2)}, u32[]{:S(2)}) async-start(bf16[4,2,23040]{2,1,0:T(2,128)(2,1)} %reshape.275), calls=%async_computation.3 | async-start | bytes 737280 | tf_op jit(solution)/shard_map/all_to_all | solution.py:184
  71.5 9.6 %collective-permute-start.2 = (bf16[10,1,128]{2,1,0:T(2,128)(2,1)S(1)}, bf16[10,1,128]{2,1,0:T(2,128)(2,1)S(1)}, u32[]{:S(2)}, u32[]{:S(2)}) collective-permute-start(bf16[10,1,128]{2,1,0:T(2,128)(2,1)S(1)} %get-tuple-element.7), channel_id=1, source_target_pairs={{0,1},{1,2},{2,3},{3,0},{4,5},{5,6},{6,7},{7,4},{8,9},{9,10},{10,1... | collective-permute-start | bytes 7688 | tf_op jit(solution)/shard_map/ppermute | solution.py:134
  73.5 7.6 %collective-permute-start.3 = (bf16[10,1,128]{2,1,0:T(2,128)(2,1)S(1)}, bf16[10,1,128]{2,1,0:T(2,128)(2,1)S(1)}, u32[]{:S(2)}, u32[]{:S(2)}) collective-permute-start(bf16[10,1,128]{2,1,0:T(2,128)(2,1)S(1)} %get-tuple-element.8), channel_id=1, source_target_pairs={{1,0},{2,1},{3,2},{0,3},{5,4},{6,5},{7,6},{4,7},{9,8},{10,9},{11,1... | collective-permute-start | bytes 7688 | tf_op jit(solution)/shard_map/ppermute | solution.py:135
  98.7 1.2 %copy-start.7 = (f32[8,192,128]{2,1,0:T(8,128)S(1)}, f32[8,192,128]{2,1,0:T(8,128)}, u32[]{:S(2)}) copy-start(f32[8,192,128]{2,1,0:T(8,128)} %shard_map.109) | copy-start | bytes 2359300
  98.7 1.2 %copy-start.8 = (bf16[8,180,128]{2,0,1:T(8,128)(2,1)S(1)}, bf16[8,180,128]{2,0,1:T(8,128)(2,1)}, u32[]{:S(2)}) copy-start(bf16[8,180,128]{2,0,1:T(8,128)(2,1)} %param.11) | copy-start | bytes 1105924

commit v5 on v4

--- a/solution.py
+++ b/solution.py
@@ -116,7 +116,16 @@
     gathered = gathered.reshape(row_count, 3, 3, 3, disco_kernel.shape[2])
     coef = jnp.stack([gathered[:, 0, 2], gathered[:, 1, 1], gathered[:, 2, 0]], axis=1)
     coef = jnp.where(valid[:, :, None, None], coef, 0.0)
-    return src.reshape(-1).astype(jnp.int32), coef.reshape(-1).astype(jnp.float32)
+    return src.astype(jnp.int32), coef.reshape(row_count, -1).astype(jnp.float32)
+
+
+def disco_piece(src_rows, coef, ext, weight_flat, piece, pieces, lon_count):
+    share = src_rows.shape[0] // pieces
+    first = piece * share
+    rows = lax.slice_in_dim(ext, first, first + share + 2, axis=0)
+    local_src = (src_rows[first : first + share] - first).reshape(-1)
+    local_coef = coef[first : first + share].reshape(-1)
+    return disco_apply(local_src, local_coef, rows, weight_flat, share, lon_count)
 
 
 def halo_extend(masked, live_rows):
@@ -158,7 +167,15 @@
         [dot_split("rnc,nk->rkc", (portion,), parts).astype(jnp.bfloat16) for parts in trig_parts],
         axis=1,
     )
+    ext = halo_extend(masked, live_rows)
+    src_rows, coef = disco_tables(band_rows, disco_kernel, band_index, band_total, row_count)
+    weight_flat = disco_weight.reshape(channels, -1)
+    pieces = 2 if row_count % 2 == 0 else 1
+    disco_parts = []
+    spectra, ext_now = lax.optimization_barrier((spectra, ext))
     columns = lax.all_to_all(spectra, "lat", split_axis=2, concat_axis=0, tiled=True)
+    disco_parts.append(disco_piece(src_rows, coef, ext_now, weight_flat, 0, pieces, lon_count))
+    columns, disco_parts[0] = lax.optimization_barrier((columns, disco_parts[0]))
     legendre_parts = split_bf16(legendre)
     coefficients = dot_split("mls,spmc->lpmc", legendre_parts, (columns,))
     filter_slice = lax.dynamic_slice_in_dim(spectral_filter, lon_index * chan_share, chan_share, 2)
@@ -175,17 +192,20 @@
     )
     returned = dot_split("mls,lpmc->spmc", legendre_parts, split_bf16(filtered))
     returned = (returned * quad_weights[:, None, None, None]).astype(jnp.bfloat16)
+    returned, ext_now = lax.optimization_barrier((returned, ext))
     portion = lax.all_to_all(returned, "lat", split_axis=0, concat_axis=2, tiled=True)
+    for piece in range(1, pieces):
+        disco_parts.append(
+            disco_piece(src_rows, coef, ext_now, weight_flat, piece, pieces, lon_count)
+        )
+    portion, disco_parts = lax.optimization_barrier((portion, disco_parts))
     spectral_rows = None
     for p, parts in enumerate(trig_parts):
         term = dot_split("rkc,nk->rnc", (portion[:, p],), parts)
         spectral_rows = term if spectral_rows is None else spectral_rows + term
     spectral_rows = spectral_rows.astype(jnp.bfloat16)
     spectral = lax.all_to_all(spectral_rows, "lon", split_axis=1, concat_axis=2, tiled=True)
-    ext = halo_extend(masked, live_rows)
-    src_rows, coef = disco_tables(band_rows, disco_kernel, band_index, band_total, row_count)
-    weight_flat = disco_weight.reshape(channels, -1)
-    disco_full = disco_apply(src_rows, coef, ext, weight_flat, row_count, lon_count)
+    disco_full = jnp.concatenate(disco_parts, axis=0)
     disco_term = disco_full[:, :lon_count, :]
     summed = masked.astype(jnp.float32) + disco_term + spectral.astype(jnp.float32)
     return jnp.where(live_slot[:, None, None], summed, 0.0).astype(jnp.bfloat16)

time: 103 us -> 99.9 us (0.970)
  waiting for transfers between devices: 18.5 us -> 0.52 us
  blocking collectives: 0 us -> 15.2 us
  local copies, waits for them, and re-layouts: 29.2 us -> 32.5 us
  other arithmetic: 9.28 us -> 6.34 us
  starting transfers between devices: 23.7 us -> 21.2 us
  Pallas kernels: 13.9 us -> 15.9 us
    all_to_all x0 -> x1, blocking collectives: none -> 15.2 us  [on_device(): lax.all_to_all(spectral_rows, 'lon', split_axis=1, concat_axis=2, tiled=T...]
    all_to_all x1, waiting for transfers between devices: 6.16 us -> 0.01 us  [on_device(): lax.all_to_all(spectra, 'lat', split_axis=2, concat_axis=0, tiled=True)]
    all_to_all x1, waiting for transfers between devices: 5.88 us -> 0.01 us  [on_device(): lax.all_to_all(returned, 'lat', split_axis=0, concat_axis=2, tiled=True)]
    all_to_all x1 -> x0, starting transfers between devices: 3.46 us -> none  [on_device(): lax.all_to_all(spectral_rows, 'lon', split_axis=1, concat_axis=2, tiled=T...]
    optimization_barrier x0 -> x3, local copies, waits for them, and re-layouts: none -> 3.16 us  [the longest x1 1.73 us: on_device(): lax.optimization_barrier((columns, disco_parts[0]))]
    ppermute x1, waiting for transfers between devices: 3.01 us -> 0.01 us  [halo_extend(): from_left = lax.ppermute(rows[:, lon_count - 1:lon_count], 'lon', lon_up)]
    all_to_all x1, waiting for transfers between devices: 3.4 us -> 0.5 us  [on_device(): lax.all_to_all(masked, 'lon', split_axis=2, concat_axis=1, tiled=True)]
    slice x0 -> x5, local copies, waits for them, and re-layouts: none -> 2.13 us  [the longest x2 1.5 us: disco_piece(): rows = lax.slice_in_dim(ext, first, first + share + 2, axis=0)]
  transfers between devices with their start and end apart: 8 -> 7, of which waited for: 4 -> 1; matrix products, arithmetic and copies ran while one was open for 32% -> 13% of each run, Pallas kernels for 14% -> 16%
where the time goes in v5:
time: 99.9 us; the launch traced here: 99.1 us
  local copies, waits for them, and re-layouts  32.5 us (33%)
  starting transfers between devices  21.2 us (21%)
  Pallas kernels  15.9 us (16%)
  blocking collectives  15.2 us (15%)
  other arithmetic  6.34 us (6%)
  matrix products  5.02 us (5%)
  between operations  2.45 us (2%)
    pallas_call x2, Pallas kernels, disco_apply(): pl.pallas_call(disco_body, out_shape=jax.ShapeDtypeStruct((slot_total, ou...  15.9 us
    all_to_all x1, blocking collectives, on_device(): lax.all_to_all(spectral_rows, 'lon', split_axis=1, concat_axis=2, tiled=T...  15.2 us
    unnamed x54, local copies, waits for them, and re-layouts  9.55 us
    all_to_all x1, starting transfers between devices, on_device(): lax.all_to_all(masked, 'lon', split_axis=2, concat_axis=1, tiled=True)  5.71 us
    all_to_all x1, starting transfers between devices, on_device(): lax.all_to_all(returned, 'lat', split_axis=0, concat_axis=2, tiled=True)  3.93 us
    all_to_all x1, starting transfers between devices, on_device(): lax.all_to_all(spectra, 'lat', split_axis=2, concat_axis=0, tiled=True)  3.57 us
    ppermute x1, starting transfers between devices, halo_extend(): from_below = lax.ppermute(masked[0:1], 'lat', lat_down)  2.95 us
    dot_general x5, matrix products, dot_split(): term = jnp.einsum(spec, lp, rp, preferred_element_type=jnp.float32)  2.76 us
  transfers between devices with their start and end apart: 7, of which 1 were waited for; matrix products, arithmetic and copies ran while one was open for 13% of the time, Pallas kernels for 16%

profile of v5, /device:TPU:0, one launch (start us, length us, event | category | flops | bytes accessed | tf_op | source)
XLA Modules:
  0.0 99.1 jit_solution(4115378122860435072)
XLA Ops:
  0.0 1.4 %fusion.34 = (s32[1]{0:T(128)}, s32[1]{0:T(128)}) fusion(s32[8]{0:T(128)} %param.12, s32[]{:T(128)S(6)} %max.10, s32[]{:T(128)S(6)} %select_n.89), kind=kLoop, calls=%fused_computation.75 | loop fusion | bytes 24 | tf_op jit(solution)/shard_map/dynamic_slice | solution.py:107
  2.0 0.6 iota_compare_fusion.2
  3.3 1.1 %copy_select_fusion = bf16[8,180,128]{2,1,0:T(8,128)(2,1)S(1)} fusion(bf16[8,180,128]{2,0,1:T(8,128)(2,1)} %param.11, pred[8]{0:T(512)(128)(4,1)S(1)} %iota_compare_fusion.2), kind=kLoop, calls=%fused_computation.34 | loop fusion | flops 184320 | bytes 737288 | tf_op jit(solution)/shard_map/jit(_where)/select_n | solution.py:163
  4.4 0.5 collective-permute-start
  4.9 2.9 %collective-permute-start.1 = (bf16[1,180,128]{2,1,0:T(8,128)(2,1)S(1)}, bf16[1,180,128]{2,1,0:T(8,128)(2,1)S(1)}, u32[]{:S(2)}, u32[]{:S(2)}) collective-permute-start(bf16[1,180,128]{2,1,0:T(8,128)(2,1)S(1)} %get-tuple-element.28), channel_id=1, source_target_pairs={{4,0},{8,4},{12,8},{16,12},{20,16},{24,20},{28,24},{0,28},{5,1},{9... | collective-permute-start | bytes 138248 | tf_op jit(solution)/shard_map/ppermute | solution.py:141
  7.8 1.2 %copy.99 = bf16[8,180,128]{1,0,2:T(8,128)(2,1)} copy(bf16[8,180,128]{2,1,0:T(8,128)(2,1)S(1)} %copy_select_fusion) | data formatting | bytes 737280 | tf_op jit(solution)/shard_map/jit(_where)/select_n | solution.py:163
  9.0 5.7 %all-to-all-start = ((bf16[8,180,128]{1,0,2:T(8,128)(2,1)}), bf16[8,180,128]{1,0,2:T(8,128)(2,1)S(1)}, u32[]{:S(2)}, u32[]{:S(2)}) async-start(bf16[8,180,128]{1,0,2:T(8,128)(2,1)} %copy.99), calls=%async_computation | async-start | bytes 1048576 | tf_op jit(solution)/shard_map/all_to_all | solution.py:165
  15.5 0.6 fusion.23
  16.4 0.7 select_reduce_fusion
  17.4 0.3 copy.111
  17.7 0.6 gather_fusion
  18.5 0.7 maximum_select_fusion
  19.2 0.4 fusion.12
  19.7 2.1 %collective-permute-start.2 = (bf16[10,1,128]{2,1,0:T(2,128)(2,1)S(1)}, bf16[10,1,128]{2,1,0:T(2,128)(2,1)S(1)}, u32[]{:S(2)}, u32[]{:S(2)}) collective-permute-start(bf16[10,1,128]{2,1,0:T(2,128)(2,1)S(1)} %get-tuple-element.25), channel_id=1, source_target_pairs={{0,1},{1,2},{2,3},{3,0},{4,5},{5,6},{6,7},{7,4},{8,9},{9,10},{10,1... | collective-permute-start | bytes 7688 | tf_op jit(solution)/shard_map/ppermute | solution.py:143
  21.7 2.5 %collective-permute-start.3 = (bf16[10,1,128]{2,1,0:T(2,128)(2,1)S(1)}, bf16[10,1,128]{2,1,0:T(2,128)(2,1)S(1)}, u32[]{:S(2)}, u32[]{:S(2)}) collective-permute-start(bf16[10,1,128]{2,1,0:T(2,128)(2,1)S(1)} %get-tuple-element.26), channel_id=1, source_target_pairs={{1,0},{2,1},{3,2},{0,3},{5,4},{6,5},{7,6},{4,7},{9,8},{10,9},{11,1... | collective-permute-start | bytes 7688 | tf_op jit(solution)/shard_map/ppermute | solution.py:144
  24.4 0.6 reshape.245.src_ref
  25.2 0.9 copy.116.w_ref
  26.2 0.7 copy.119
  27.0 1.0 %maximum_maximum_fusion = bf16[10,208,128]{2,1,0:T(8,128)(2,1)S(1)} fusion(bf16[10,1,128]{2,1,0:T(2,128)(2,1)S(1)} %collective-permute-done.3, bf16[1,180,128]{2,1,0:T(8,128)(2,1)} %copy-done.14, bf16[8,180,128]{2,1,0:T(8,128)(2,1)S(1)} %copy_select_fusion, bf16[1,180,128]{2,1,0:T(8,128)(2,1)S(1)} %collective-permute-done, ...), kind=kLoop, calls=%fused_computation.32 | loop fusion | flops 3194880 | bytes 998816 | tf_op jit(solution)/shard_map/concatenate | solution.py:147
  28.0 0.5 all-to-all-done
  28.5 0.8 copy-done.7
  29.3 1.4 %copy.101 = bf16[8,4,180,32]{2,1,3,0:T(4,128)(2,1)S(1)} copy(bf16[8,4,180,32]{2,0,3,1:T(8,128)(2,1)} %bitcast.153) | data formatting | bytes 737280 | tf_op jit(solution)/shard_map/all_to_all | solution.py:165
  30.8 0.4 all_to_all.49
  31.4 0.3 fusion.40
  32.4 0.7 copy.106
  33.1 1.4 %reshape.285 = bf16[8,2,6144]{2,1,0:T(2,128)(2,1)} reshape(bf16[192,2,8,32]{3,2,1,0:T(8,128)(2,1)S(1)} %bitcast.152) | data formatting | bytes 393216
  34.5 3.6 %all-to-all-start.1 = ((bf16[8,2,6144]{2,1,0:T(2,128)(2,1)}), bf16[8,2,6144]{2,1,0:T(2,128)(2,1)S(1)}, u32[]{:S(2)}, u32[]{:S(2)}) async-start(bf16[8,2,6144]{2,1,0:T(2,128)(2,1)} %reshape.285), calls=%async_computation.1 | async-start | bytes 393216 | tf_op jit(solution)/shard_map/all_to_all | solution.py:176
  38.1 0.6 fusion.33
  38.7 0.7 reshape.247.coef_ref
  39.4 0.7 slice.68.ext_ref
  40.1 8.0 %shard_map.109 = f32[4,192,128]{2,1,0:T(8,128)} custom-call(s32[12]{0:T(128)} %reshape.245.src_ref, f32[324]{0:T(512)} %reshape.247.coef_ref, bf16[6,208,128]{2,1,0:T(8,128)(2,1)} %slice.68.ext_ref, bf16[128,1152]{1,0:T(8,128)(2,1)} %copy.116.w_ref), custom_call_target="tpu_custom_call" | custom-call | tf_op jit(solution)/shard_map/pallas_call | solution.py:82
  48.1 1.2 %reshape.286 = bf16[192,2,8,32]{3,2,1,0:T(8,128)(2,1)} reshape(bf16[8,2,6144]{2,1,0:T(2,128)(2,1)S(1)} %all-to-all-done.1) | data formatting | bytes 393216
  49.4 2.4 %copy.108 = bf16[8,8,2,24,32]{4,3,2,1,0:T(8,128)(2,1)} copy(bf16[8,8,2,24,32]{4,1,2,3,0:T(8,128)(2,1)} %bitcast.149) | data formatting | bytes 393216 | tf_op jit(solution)/shard_map/all_to_all | solution.py:176
  51.8 1.7 %copy.117 = bf16[64,2,24,32]{0,3,1,2:T(8,128)(2,1)S(1)} copy(bf16[64,2,24,32]{3,2,1,0:T(8,128)(2,1)} %bitcast.148) | data formatting | bytes 393216 | tf_op jit(solution)/shard_map/optimization_barrier | solution.py:178
  53.5 0.5 fusion.29
  54.0 0.5 add_bitcast_fusion
  54.5 0.3 copy-done.13
  54.8 0.3 multiply_add_fusion
  55.1 0.6 fusion.19
  55.7 0.6 convolution_add_fusion.1
  56.3 0.6 fusion.4
  57.0 0.8 copy.120
  57.7 1.4 %reshape.287 = bf16[8,2,6144]{2,1,0:T(2,128)(2,1)} reshape(bf16[64,24,2,32]{3,2,1,0:T(2,128)(2,1)S(1)} %bitcast.150) | data formatting | bytes 393216
  59.2 3.9 %all-to-all-start.2 = ((bf16[8,2,6144]{2,1,0:T(2,128)(2,1)}), bf16[8,2,6144]{2,1,0:T(2,128)(2,1)S(1)}, u32[]{:S(2)}, u32[]{:S(2)}) async-start(bf16[8,2,6144]{2,1,0:T(2,128)(2,1)} %reshape.287), calls=%async_computation.2 | async-start | bytes 393216 | tf_op jit(solution)/shard_map/all_to_all | solution.py:196
  63.1 0.7 reshape.249.src_ref
  63.8 0.7 reshape.250.coef_ref
  64.5 0.8 slice.74.ext_ref
  65.2 8.0 %shard_map.110 = f32[4,192,128]{2,1,0:T(8,128)} custom-call(s32[12]{0:T(128)} %reshape.249.src_ref, f32[324]{0:T(512)} %reshape.250.coef_ref, bf16[6,208,128]{2,1,0:T(8,128)(2,1)} %slice.74.ext_ref, bf16[128,1152]{1,0:T(8,128)(2,1)} %copy.116.w_ref), custom_call_target="tpu_custom_call" | custom-call | tf_op jit(solution)/shard_map/pallas_call | solution.py:82
  73.2 0.4 reshape.288
  73.7 0.8 copy.122
  74.5 0.7 all_to_all.57
  75.5 0.3 fusion.38
  75.8 0.4 copy-done.2
  76.2 0.3 fusion.37
  76.5 0.3 fusion.36
  76.8 0.3 fusion.35
  77.4 1.4 %copy.131 = bf16[8,720,32]{2,0,1:T(8,128)(2,1)S(1)} copy(bf16[8,720,32]{1,2,0:T(8,128)(2,1)S(1)} %fusion.14) | data formatting | bytes 737280 | tf_op jit(solution)/shard_map/convert_element_type | solution.py:206
  78.7 1.1 %reshape.289 = bf16[4,2,23040]{2,1,0:T(2,128)(2,1)S(1)} reshape(bf16[720,8,32]{2,1,0:T(8,128)(2,1)S(1)} %bitcast.132) | data formatting | bytes 737280
  79.8 15.2 %all_to_all.63 = bf16[4,2,23040]{2,1,0:T(2,128)(2,1)S(1)} all-to-all(bf16[4,2,23040]{2,1,0:T(2,128)(2,1)S(1)} %reshape.289), channel_id=1, replica_groups=mesh['lat'=8,'lon'=4] {'lon'}, dimensions={0} | all-to-all | bytes 737280 | tf_op jit(solution)/shard_map/all_to_all | solution.py:207
  95.0 0.8 reshape.290
  95.8 1.0 %copy.132 = f32[8,4,180,32]{2,3,1,0:T(8,128)S(1)} copy(bf16[8,4,180,32]{3,0,2,1:T(8,128)(2,1)S(1)} %bitcast.133) | data formatting | bytes 1105920 | tf_op jit(solution)/shard_map/convert_element_type | solution.py:210
  96.9 0.3 copy.133
  97.2 0.6 copy-done.8
  98.3 0.8 copy.134
  (80 shorter events, 3.5 us)
Async XLA Ops:
  4.4 13.0 %copy-start.16 = (f32[64,9,9]{0,2,1:T(8,128)S(1)}, f32[64,9,9]{0,2,1:T(8,128)}, u32[]{:S(2)}) copy-start(f32[64,9,9]{0,2,1:T(8,128)} %param.16) | copy-start | bytes 62212
  4.4 15.2 %collective-permute-start = (bf16[1,180,128]{2,1,0:T(8,128)(2,1)S(1)}, bf16[1,180,128]{2,1,0:T(8,128)(2,1)S(1)}, u32[]{:S(2)}, u32[]{:S(2)}) collective-permute-start(bf16[1,180,128]{2,1,0:T(8,128)(2,1)S(1)} %get-tuple-element.27), channel_id=1, source_target_pairs={{0,4},{4,8},{8,12},{12,16},{16,20},{20,24},{24,28},{28,0},{1,5},{5... | collective-permute-start | bytes 138248 | tf_op jit(solution)/shard_map/ppermute | solution.py:140
  4.9 14.7 %collective-permute-start.1 = (bf16[1,180,128]{2,1,0:T(8,128)(2,1)S(1)}, bf16[1,180,128]{2,1,0:T(8,128)(2,1)S(1)}, u32[]{:S(2)}, u32[]{:S(2)}) collective-permute-start(bf16[1,180,128]{2,1,0:T(8,128)(2,1)S(1)} %get-tuple-element.28), channel_id=1, source_target_pairs={{4,0},{8,4},{12,8},{16,12},{20,16},{24,20},{28,24},{0,28},{5,1},{9... | collective-permute-start | bytes 138248 | tf_op jit(solution)/shard_map/ppermute | solution.py:141
  9.0 10.2 %copy-start.18 = (f32[45,192]{1,0:T(8,128)S(1)}, f32[45,192]{1,0:T(8,128)}, u32[]{:S(2)}) copy-start(f32[45,192]{1,0:T(8,128)} %constant.58.clone) | copy-start | bytes 103684
  9.0 10.2 %copy-start.19 = (f32[45,192]{1,0:T(8,128)S(1)}, f32[45,192]{1,0:T(8,128)}, u32[]{:S(2)}) copy-start(f32[45,192]{1,0:T(8,128)} %constant.57.clone) | copy-start | bytes 103684
  9.0 10.2 %copy-start.20 = (f32[16,192]{1,0:T(8,128)S(1)}, f32[16,192]{1,0:T(8,128)}, u32[]{:S(2)}) copy-start(f32[16,192]{1,0:T(8,128)} %constant.60.clone) | copy-start | bytes 36868
  9.0 10.2 %copy-start.21 = (f32[16,192]{1,0:T(8,128)S(1)}, f32[16,192]{1,0:T(8,128)}, u32[]{:S(2)}) copy-start(f32[16,192]{1,0:T(8,128)} %constant.59.clone) | copy-start | bytes 36868
  9.0 19.5 %all-to-all-start = ((bf16[8,180,128]{1,0,2:T(8,128)(2,1)}), bf16[8,180,128]{1,0,2:T(8,128)(2,1)S(1)}, u32[]{:S(2)}, u32[]{:S(2)}) async-start(bf16[8,180,128]{1,0,2:T(8,128)(2,1)} %copy.99), calls=%async_computation | async-start | bytes 1048576 | tf_op jit(solution)/shard_map/all_to_all | solution.py:165
  18.4 5.8 %copy-start.11 = (f32[2,360,128]{2,1,0:T(8,128)S(1)}, f32[2,360,128]{2,1,0:T(8,128)}, u32[]{:S(2)}) copy-start(f32[2,360,128]{2,1,0:T(8,128)} %param.15) | copy-start | bytes 1105924
  19.2 5.8 %copy-start.12 = (bf16[128,9,128]{2,0,1:T(8,128)(2,1)S(1)}, bf16[128,9,128]{2,0,1:T(8,128)(2,1)}, u32[]{:S(2)}) copy-start(bf16[128,9,128]{2,0,1:T(8,128)(2,1)} %param.17) | copy-start | bytes 884740
  19.6 11.6 %copy-start.1 = (bf16[45,16,192]{2,1,0:T(8,128)(2,1)}, bf16[45,16,192]{2,1,0:T(8,128)(2,1)S(1)}, u32[]{:S(2)}) copy-start(bf16[45,16,192]{2,1,0:T(8,128)(2,1)S(1)} %get-tuple-element.37) | copy-start | bytes 829444
  19.6 12.1 %copy-start.3 = (bf16[45,16,192]{2,1,0:T(8,128)(2,1)}, bf16[45,16,192]{2,1,0:T(8,128)(2,1)S(1)}, u32[]{:S(2)}) copy-start(bf16[45,16,192]{2,1,0:T(8,128)(2,1)S(1)} %get-tuple-element.38) | copy-start | bytes 829444
  19.6 2.1 %copy-start.14 = (bf16[1,180,128]{2,1,0:T(8,128)(2,1)}, bf16[1,180,128]{2,1,0:T(8,128)(2,1)S(1)}, u32[]{:S(2)}) copy-start(bf16[1,180,128]{2,1,0:T(8,128)(2,1)S(1)} %collective-permute-done.1) | copy-start | bytes 138244
  19.7 7.3 %collective-permute-start.2 = (bf16[10,1,128]{2,1,0:T(2,128)(2,1)S(1)}, bf16[10,1,128]{2,1,0:T(2,128)(2,1)S(1)}, u32[]{:S(2)}, u32[]{:S(2)}) collective-permute-start(bf16[10,1,128]{2,1,0:T(2,128)(2,1)S(1)} %get-tuple-element.25), channel_id=1, source_target_pairs={{0,1},{1,2},{2,3},{3,0},{4,5},{5,6},{6,7},{7,4},{8,9},{9,10},{10,1... | collective-permute-start | bytes 7688 | tf_op jit(solution)/shard_map/ppermute | solution.py:143
  21.7 5.3 %collective-permute-start.3 = (bf16[10,1,128]{2,1,0:T(2,128)(2,1)S(1)}, bf16[10,1,128]{2,1,0:T(2,128)(2,1)S(1)}, u32[]{:S(2)}, u32[]{:S(2)}) collective-permute-start(bf16[10,1,128]{2,1,0:T(2,128)(2,1)S(1)} %get-tuple-element.26), channel_id=1, source_target_pairs={{1,0},{2,1},{3,2},{0,3},{5,4},{6,5},{7,6},{4,7},{9,8},{10,9},{11,1... | collective-permute-start | bytes 7688 | tf_op jit(solution)/shard_map/ppermute | solution.py:144
  28.0 11.4 %copy-start.5 = (bf16[10,208,128]{2,1,0:T(8,128)(2,1)}, bf16[10,208,128]{2,1,0:T(8,128)(2,1)S(1)}, u32[]{:S(2)}) copy-start(bf16[10,208,128]{2,1,0:T(8,128)(2,1)S(1)} %maximum_maximum_fusion) | copy-start | bytes 1597444
  28.5 0.8 copy-start.7
  32.4 5.7 %copy-start.15 = (f32[8,3,3,9]{3,0,2,1:T(8,128)S(1)}, f32[8,3,3,9]{3,0,2,1:T(8,128)}, u32[]{:S(2)}) copy-start(f32[8,3,3,9]{3,0,2,1:T(8,128)} %maximum_select_fusion) | copy-start | bytes 7780
  34.5 13.6 %all-to-all-start.1 = ((bf16[8,2,6144]{2,1,0:T(2,128)(2,1)}), bf16[8,2,6144]{2,1,0:T(2,128)(2,1)S(1)}, u32[]{:S(2)}, u32[]{:S(2)}) async-start(bf16[8,2,6144]{2,1,0:T(2,128)(2,1)} %reshape.285), calls=%async_computation.1 | async-start | bytes 393216 | tf_op jit(solution)/shard_map/all_to_all | solution.py:176
  49.4 4.1 %copy-start = (f32[24,360,64]{1,2,0:T(8,128)S(1)}, f32[24,360,64]{1,2,0:T(8,128)}, u32[]{:S(2)}) copy-start(f32[24,360,64]{1,2,0:T(8,128)} %param.13) | copy-start | bytes 6635524
  54.0 0.8 copy-start.13
  55.7 0.7 copy-start.22
  56.9 6.8 %copy-start.17 = (f32[4,3,3,9]{3,0,2,1:T(4,128)S(1)}, f32[4,3,3,9]{3,0,2,1:T(4,128)}, u32[]{:S(2)}) copy-start(f32[4,3,3,9]{3,0,2,1:T(4,128)} %get-tuple-element.40) | copy-start | bytes 3892
  56.9 7.5 %copy-start.6 = (bf16[10,208,128]{2,1,0:T(8,128)(2,1)S(1)}, bf16[10,208,128]{2,1,0:T(8,128)(2,1)}, u32[]{:S(2)}) copy-start(bf16[10,208,128]{2,1,0:T(8,128)(2,1)} %copy-done.5) | copy-start | bytes 1597444
  59.2 14.0 %all-to-all-start.2 = ((bf16[8,2,6144]{2,1,0:T(2,128)(2,1)}), bf16[8,2,6144]{2,1,0:T(2,128)(2,1)S(1)}, u32[]{:S(2)}, u32[]{:S(2)}) async-start(bf16[8,2,6144]{2,1,0:T(2,128)(2,1)} %reshape.287), calls=%async_computation.2 | async-start | bytes 393216 | tf_op jit(solution)/shard_map/all_to_all | solution.py:196
  74.5 1.0 copy-start.4
  75.2 1.0 %copy-start.2 = (bf16[45,16,192]{2,1,0:T(8,128)(2,1)S(1)}, bf16[45,16,192]{2,1,0:T(8,128)(2,1)}, u32[]{:S(2)}) copy-start(bf16[45,16,192]{2,1,0:T(8,128)(2,1)} %copy-done.1) | copy-start | bytes 829444
  96.8 1.0 %copy-start.8 = (f32[4,192,128]{2,1,0:T(8,128)S(1)}, f32[4,192,128]{2,1,0:T(8,128)}, u32[]{:S(2)}) copy-start(f32[4,192,128]{2,1,0:T(8,128)} %shard_map.109) | copy-start | bytes 1179652
  96.9 1.1 %copy-start.9 = (f32[4,192,128]{2,1,0:T(8,128)S(1)}, f32[4,192,128]{2,1,0:T(8,128)}, u32[]{:S(2)}) copy-start(f32[4,192,128]{2,1,0:T(8,128)} %shard_map.110) | copy-start | bytes 1179652
  96.9 1.2 %copy-start.10 = (bf16[8,180,128]{2,0,1:T(8,128)(2,1)S(1)}, bf16[8,180,128]{2,0,1:T(8,128)(2,1)}, u32[]{:S(2)}) copy-start(bf16[8,180,128]{2,0,1:T(8,128)(2,1)} %param.11) | copy-start | bytes 1105924

commit v6 on v5

--- a/solution.py
+++ b/solution.py
@@ -120,12 +120,13 @@
 
 
 def disco_piece(src_rows, coef, ext, weight_flat, piece, pieces, lon_count):
-    share = src_rows.shape[0] // pieces
-    first = piece * share
-    rows = lax.slice_in_dim(ext, first, first + share + 2, axis=0)
-    local_src = (src_rows[first : first + share] - first).reshape(-1)
-    local_coef = coef[first : first + share].reshape(-1)
-    return disco_apply(local_src, local_coef, rows, weight_flat, share, lon_count)
+    slot_total = src_rows.shape[0]
+    first = piece * slot_total // pieces
+    last = (piece + 1) * slot_total // pieces
+    rows = lax.slice_in_dim(ext, first, last + 2, axis=0)
+    local_src = (src_rows[first:last] - first).reshape(-1)
+    local_coef = coef[first:last].reshape(-1)
+    return disco_apply(local_src, local_coef, rows, weight_flat, last - first, lon_count)
 
 
 def halo_extend(masked, live_rows):
@@ -170,7 +171,7 @@
     ext = halo_extend(masked, live_rows)
     src_rows, coef = disco_tables(band_rows, disco_kernel, band_index, band_total, row_count)
     weight_flat = disco_weight.reshape(channels, -1)
-    pieces = 2 if row_count % 2 == 0 else 1
+    pieces = min(3, row_count)
     disco_parts = []
     spectra, ext_now = lax.optimization_barrier((spectra, ext))
     columns = lax.all_to_all(spectra, "lat", split_axis=2, concat_axis=0, tiled=True)
@@ -194,17 +195,20 @@
     returned = (returned * quad_weights[:, None, None, None]).astype(jnp.bfloat16)
     returned, ext_now = lax.optimization_barrier((returned, ext))
     portion = lax.all_to_all(returned, "lat", split_axis=0, concat_axis=2, tiled=True)
-    for piece in range(1, pieces):
-        disco_parts.append(
-            disco_piece(src_rows, coef, ext_now, weight_flat, piece, pieces, lon_count)
-        )
+    disco_parts.append(disco_piece(src_rows, coef, ext_now, weight_flat, 1, pieces, lon_count))
     portion, disco_parts = lax.optimization_barrier((portion, disco_parts))
     spectral_rows = None
     for p, parts in enumerate(trig_parts):
         term = dot_split("rkc,nk->rnc", (portion[:, p],), parts)
         spectral_rows = term if spectral_rows is None else spectral_rows + term
     spectral_rows = spectral_rows.astype(jnp.bfloat16)
+    spectral_rows, ext_now = lax.optimization_barrier((spectral_rows, ext))
     spectral = lax.all_to_all(spectral_rows, "lon", split_axis=1, concat_axis=2, tiled=True)
+    for piece in range(2, pieces):
+        disco_parts.append(
+            disco_piece(src_rows, coef, ext_now, weight_flat, piece, pieces, lon_count)
+        )
+    spectral, disco_parts = lax.optimization_barrier((spectral, disco_parts))
     disco_full = jnp.concatenate(disco_parts, axis=0)
     disco_term = disco_full[:, :lon_count, :]
     summed = masked.astype(jnp.float32) + disco_term + spectral.astype(jnp.float32)

time: 99.9 us -> 95.5 us (0.956)
  blocking collectives: 15.2 us -> 0 us
  waiting for transfers between devices: 0.52 us -> 3.51 us
  starting transfers between devices: 21.2 us -> 24 us
  Pallas kernels: 15.9 us -> 18 us
  local copies, waits for them, and re-layouts: 32.5 us -> 34.1 us
    all_to_all x1 -> x0, blocking collectives: 15.2 us -> none  [on_device(): lax.all_to_all(spectral_rows, 'lon', split_axis=1, concat_axis=2, tiled=T...]
    all_to_all x0 -> x1, waiting for transfers between devices: none -> 3.49 us  [on_device(): lax.all_to_all(spectral_rows, 'lon', split_axis=1, concat_axis=2, tiled=T...]
    all_to_all x0 -> x1, starting transfers between devices: none -> 3.46 us  [on_device(): lax.all_to_all(spectral_rows, 'lon', split_axis=1, concat_axis=2, tiled=T...]
    convert_element_type x3 -> x0, local copies, waits for them, and re-layouts: 2.72 us -> none  [the longest x1 1.37 us: on_device(): spectral_rows = spectral_rows.astype(jnp.bfloat16)]
    pallas_call x2 -> x3, Pallas kernels: 15.9 us -> 18 us  [disco_apply(): pl.pallas_call(disco_body, out_shape=jax.ShapeDtypeStruct((slot_total, ou...]
    optimization_barrier x0 -> x2, local copies, waits for them, and re-layouts: none -> 1.63 us  [the longest x1 1.37 us: on_device(): spectral_rows, ext_now = lax.optimization_barrier((spectral_rows, ext))]
    reshape x4 -> x6, local copies, waits for them, and re-layouts: 2.67 us -> 3.93 us  [the longest x3 1.98 us: disco_piece(): local_coef = coef[first:last].reshape(-1)]
    all_to_all x0 -> x1, local copies, waits for them, and re-layouts: none -> 1.01 us  [on_device(): lax.all_to_all(spectral_rows, 'lon', split_axis=1, concat_axis=2, tiled=T...]
  transfers between devices with their start and end apart: 7 -> 8, of which waited for: 1 -> 1; matrix products, arithmetic and copies ran while one was open for 13% -> 17% of each run, Pallas kernels for 16% -> 19%
where the time goes in v6:
time: 95.5 us; the launch traced here: 94.6 us
  local copies, waits for them, and re-layouts  34.1 us (36%)
  starting transfers between devices  24 us (25%)
  Pallas kernels  18 us (19%)
  other arithmetic  7.26 us (8%)
  matrix products  5 us (5%)
  waiting for transfers between devices  3.51 us (4%)
  between operations  2.72 us (3%)
    pallas_call x3, Pallas kernels, disco_apply(): pl.pallas_call(disco_body, out_shape=jax.ShapeDtypeStruct((slot_total, ou...  18 us
    unnamed x64, local copies, waits for them, and re-layouts  9.45 us
    all_to_all x1, starting transfers between devices, on_device(): lax.all_to_all(masked, 'lon', split_axis=2, concat_axis=1, tiled=True)  5.71 us
    all_to_all x1, starting transfers between devices, on_device(): lax.all_to_all(returned, 'lat', split_axis=0, concat_axis=2, tiled=True)  3.94 us
    all_to_all x1, starting transfers between devices, on_device(): lax.all_to_all(spectra, 'lat', split_axis=2, concat_axis=0, tiled=True)  3.57 us
    all_to_all x1, waiting for transfers between devices, on_device(): lax.all_to_all(spectral_rows, 'lon', split_axis=1, concat_axis=2, tiled=T...  3.49 us
    all_to_all x1, starting transfers between devices, on_device(): lax.all_to_all(spectral_rows, 'lon', split_axis=1, concat_axis=2, tiled=T...  3.46 us
    ppermute x1, starting transfers between devices, halo_extend(): from_below = lax.ppermute(masked[0:1], 'lat', lat_down)  2.95 us
  transfers between devices with their start and end apart: 8, of which 1 were waited for; matrix products, arithmetic and copies ran while one was open for 17% of the time, Pallas kernels for 19%

profile of v6, /device:TPU:0, one launch (start us, length us, event | category | flops | bytes accessed | tf_op | source)
XLA Modules:
  0.0 94.6 jit_solution(3686994006079159494)
XLA Ops:
  0.0 1.4 %fusion.34 = (s32[1]{0:T(128)}, s32[1]{0:T(128)}) fusion(s32[8]{0:T(128)} %param.12, s32[]{:T(128)S(6)} %max.10, s32[]{:T(128)S(6)} %select_n.89), kind=kLoop, calls=%fused_computation.77 | loop fusion | bytes 24 | tf_op jit(solution)/shard_map/dynamic_slice | solution.py:107
  2.1 0.7 iota_compare_fusion.2
  3.5 1.1 %copy_select_fusion = bf16[8,180,128]{2,1,0:T(8,128)(2,1)S(1)} fusion(bf16[8,180,128]{2,0,1:T(8,128)(2,1)} %param.11, pred[8]{0:T(512)(128)(4,1)S(1)} %iota_compare_fusion.2), kind=kLoop, calls=%fused_computation.35 | loop fusion | flops 184320 | bytes 737288 | tf_op jit(solution)/shard_map/jit(_where)/select_n | solution.py:164
  4.6 0.5 collective-permute-start
  5.1 2.9 %collective-permute-start.1 = (bf16[1,180,128]{2,1,0:T(8,128)(2,1)S(1)}, bf16[1,180,128]{2,1,0:T(8,128)(2,1)S(1)}, u32[]{:S(2)}, u32[]{:S(2)}) collective-permute-start(bf16[1,180,128]{2,1,0:T(8,128)(2,1)S(1)} %get-tuple-element.40), channel_id=1, source_target_pairs={{4,0},{8,4},{12,8},{16,12},{20,16},{24,20},{28,24},{0,28},{5,1},{9... | collective-permute-start | bytes 138248 | tf_op jit(solution)/shard_map/ppermute | solution.py:142
  8.1 1.2 %copy.103 = bf16[8,180,128]{1,0,2:T(8,128)(2,1)} copy(bf16[8,180,128]{2,1,0:T(8,128)(2,1)S(1)} %copy_select_fusion) | data formatting | bytes 737280 | tf_op jit(solution)/shard_map/jit(_where)/select_n | solution.py:164
  9.3 5.7 %all-to-all-start = ((bf16[8,180,128]{1,0,2:T(8,128)(2,1)}), bf16[8,180,128]{1,0,2:T(8,128)(2,1)S(1)}, u32[]{:S(2)}, u32[]{:S(2)}) async-start(bf16[8,180,128]{1,0,2:T(8,128)(2,1)} %copy.103), calls=%async_computation | async-start | bytes 1048576 | tf_op jit(solution)/shard_map/all_to_all | solution.py:166
  15.8 0.8 select_reduce_fusion
  16.9 0.3 copy.115
  17.2 0.6 gather_fusion
  18.0 0.7 fusion.23
  18.8 0.4 fusion.12
  19.2 0.7 pad_add_fusion.1
  19.9 0.6 pad_maximum_fusion.6
  20.6 2.0 %collective-permute-start.2 = (bf16[10,1,128]{2,1,0:T(2,128)(2,1)}, bf16[10,1,128]{2,1,0:T(2,128)(2,1)S(1)}, u32[]{:S(2)}, u32[]{:S(2)}) collective-permute-start(bf16[10,1,128]{2,1,0:T(2,128)(2,1)} %get-tuple-element.37), channel_id=1, source_target_pairs={{0,1},{1,2},{2,3},{3,0},{4,5},{5,6},{6,7},{7,4},{8,9},{9,10},{10,1... | collective-permute-start | bytes 7688 | tf_op jit(solution)/shard_map/ppermute | solution.py:144
  22.6 1.8 %collective-permute-start.3 = (bf16[10,1,128]{2,1,0:T(2,128)(2,1)}, bf16[10,1,128]{2,1,0:T(2,128)(2,1)}, u32[]{:S(2)}, u32[]{:S(2)}) collective-permute-start(bf16[10,1,128]{2,1,0:T(2,128)(2,1)} %get-tuple-element.38), channel_id=1, source_target_pairs={{1,0},{2,1},{3,2},{0,3},{5,4},{6,5},{7,6},{4,7},{9,8},{10,9},{11,1... | collective-permute-start | bytes 7688 | tf_op jit(solution)/shard_map/ppermute | solution.py:145
  24.6 0.7 copy.113
  25.2 0.7 reshape.249.src_ref
  25.9 0.6 reshape.253.src_ref
  26.7 0.9 copy.120.w_ref
  27.7 0.7 copy.123
  28.5 1.0 %maximum_maximum_fusion = bf16[10,208,128]{2,1,0:T(8,128)(2,1)S(1)} fusion(bf16[10,1,128]{2,1,0:T(2,128)(2,1)} %collective-permute-done.3, bf16[1,180,128]{2,1,0:T(8,128)(2,1)} %copy-done.15, bf16[8,180,128]{2,1,0:T(8,128)(2,1)S(1)} %copy_select_fusion, bf16[1,180,128]{2,1,0:T(8,128)(2,1)S(1)} %collective-permute-done, ...), kind=kLoop, calls=%fused_computation.33 | loop fusion | flops 3194880 | bytes 998816 | tf_op jit(solution)/shard_map/concatenate | solution.py:148
  29.6 0.8 copy-done.7
  30.4 1.4 %copy.105 = bf16[8,4,180,32]{2,1,3,0:T(4,128)(2,1)S(1)} copy(bf16[8,4,180,32]{2,0,3,1:T(8,128)(2,1)} %bitcast.151) | data formatting | bytes 737280 | tf_op jit(solution)/shard_map/all_to_all | solution.py:166
  31.9 0.4 all_to_all.55
  33.5 0.7 copy.110
  34.2 1.4 %reshape.289 = bf16[8,2,6144]{2,1,0:T(2,128)(2,1)} reshape(bf16[192,2,8,32]{3,2,1,0:T(8,128)(2,1)S(1)} %bitcast.150) | data formatting | bytes 393216
  35.6 3.6 %all-to-all-start.1 = ((bf16[8,2,6144]{2,1,0:T(2,128)(2,1)}), bf16[8,2,6144]{2,1,0:T(2,128)(2,1)S(1)}, u32[]{:S(2)}, u32[]{:S(2)}) async-start(bf16[8,2,6144]{2,1,0:T(2,128)(2,1)} %reshape.289), calls=%async_computation.1 | async-start | bytes 393216 | tf_op jit(solution)/shard_map/all_to_all | solution.py:177
  39.3 0.7 reshape.251.coef_ref
  40.0 0.7 slice.78.ext_ref
  40.7 5.0 %shard_map.109 = f32[2,192,128]{2,1,0:T(8,128)} custom-call(s32[6]{0:T(128)} %reshape.249.src_ref, f32[162]{0:T(256)} %reshape.251.coef_ref, bf16[4,208,128]{2,1,0:T(8,128)(2,1)} %slice.78.ext_ref, bf16[128,1152]{1,0:T(8,128)(2,1)} %copy.120.w_ref), custom_call_target="tpu_custom_call" | custom-call | tf_op jit(solution)/shard_map/pallas_call | solution.py:82
  45.7 1.3 %reshape.290 = bf16[192,2,8,32]{3,2,1,0:T(8,128)(2,1)} reshape(bf16[8,2,6144]{2,1,0:T(2,128)(2,1)S(1)} %all-to-all-done.1) | data formatting | bytes 393216
  47.0 2.4 %copy.112 = bf16[8,8,2,24,32]{4,3,2,1,0:T(8,128)(2,1)} copy(bf16[8,8,2,24,32]{4,1,2,3,0:T(8,128)(2,1)} %bitcast.147) | data formatting | bytes 393216 | tf_op jit(solution)/shard_map/all_to_all | solution.py:177
  49.3 1.7 %copy.121 = bf16[64,2,24,32]{0,3,1,2:T(8,128)(2,1)S(1)} copy(bf16[64,2,24,32]{3,2,1,0:T(8,128)(2,1)} %bitcast.146) | data formatting | bytes 393216 | tf_op jit(solution)/shard_map/optimization_barrier | solution.py:179
  51.1 0.5 fusion.29
  51.5 0.5 add_bitcast_fusion
  52.3 0.3 multiply_add_fusion
  52.7 0.6 fusion.19
  53.3 0.6 convolution_add_fusion.1
  53.9 0.6 fusion.4
  54.5 0.8 copy.124
  55.3 1.4 %reshape.291 = bf16[8,2,6144]{2,1,0:T(2,128)(2,1)} reshape(bf16[64,24,2,32]{3,2,1,0:T(2,128)(2,1)S(1)} %bitcast.148) | data formatting | bytes 393216
  56.7 3.9 %all-to-all-start.2 = ((bf16[8,2,6144]{2,1,0:T(2,128)(2,1)}), bf16[8,2,6144]{2,1,0:T(2,128)(2,1)S(1)}, u32[]{:S(2)}, u32[]{:S(2)}) async-start(bf16[8,2,6144]{2,1,0:T(2,128)(2,1)} %reshape.291), calls=%async_computation.2 | async-start | bytes 393216 | tf_op jit(solution)/shard_map/all_to_all | solution.py:197
  60.7 0.6 reshape.254.coef_ref
  61.3 0.7 slice.84.ext_ref
  62.1 6.5 %shard_map.110 = f32[3,192,128]{2,1,0:T(8,128)} custom-call(s32[9]{0:T(128)} %reshape.253.src_ref, f32[243]{0:T(256)} %reshape.254.coef_ref, bf16[5,208,128]{2,1,0:T(8,128)(2,1)} %slice.84.ext_ref, bf16[128,1152]{1,0:T(8,128)(2,1)} %copy.120.w_ref), custom_call_target="tpu_custom_call" | custom-call | tf_op jit(solution)/shard_map/pallas_call | solution.py:82
  68.5 0.4 reshape.292
  69.0 0.8 copy.126
  69.9 0.7 all_to_all.63
  70.9 0.3 fusion.38
  71.2 0.4 copy-done.2
  71.9 0.3 fusion.36
  72.2 0.3 fusion.35
  72.7 1.4 %copy.135 = bf16[8,720,32]{2,0,1:T(8,128)(2,1)S(1)} copy(bf16[8,720,32]{1,2,0:T(8,128)(2,1)S(1)} %fusion.14) | data formatting | bytes 737280 | tf_op jit(solution)/shard_map/optimization_barrier | solution.py:205
  74.1 1.8 %reshape.293 = bf16[4,2,23040]{2,1,0:T(2,128)(2,1)} reshape(bf16[720,8,32]{2,1,0:T(8,128)(2,1)S(1)} %bitcast.131) | data formatting | bytes 737280
  75.8 3.5 %all-to-all-start.3 = ((bf16[4,2,23040]{2,1,0:T(2,128)(2,1)}), bf16[4,2,23040]{2,1,0:T(2,128)(2,1)S(1)}, u32[]{:S(2)}, u32[]{:S(2)}) async-start(bf16[4,2,23040]{2,1,0:T(2,128)(2,1)} %reshape.293), calls=%async_computation.3 | async-start | bytes 737280 | tf_op jit(solution)/shard_map/all_to_all | solution.py:206
  79.3 0.7 reshape.255.src_ref
  80.0 0.7 reshape.256.coef_ref
  80.7 0.7 slice.89.ext_ref
  81.4 6.5 %shard_map.111 = f32[3,192,128]{2,1,0:T(8,128)} custom-call(s32[9]{0:T(128)} %reshape.255.src_ref, f32[243]{0:T(256)} %reshape.256.coef_ref, bf16[5,208,128]{2,1,0:T(8,128)(2,1)} %slice.89.ext_ref, bf16[128,1152]{1,0:T(8,128)(2,1)} %copy.120.w_ref), custom_call_target="tpu_custom_call" | custom-call | tf_op jit(solution)/shard_map/pallas_call | solution.py:82
  87.9 3.5 %all-to-all-done.3 = bf16[4,2,23040]{2,1,0:T(2,128)(2,1)S(1)} async-done(((bf16[4,2,23040]{2,1,0:T(2,128)(2,1)}), bf16[4,2,23040]{2,1,0:T(2,128)(2,1)S(1)}, u32[]{:S(2)}, u32[]{:S(2)}) %all-to-all-start.3) | async-done | bytes 368672 | tf_op jit(solution)/shard_map/all_to_all | solution.py:206
  91.4 0.8 reshape.294
  92.2 1.0 %copy.136 = bf16[8,4,180,32]{2,3,1,0:T(8,128)(2,1)S(1)} copy(bf16[8,4,180,32]{3,0,2,1:T(8,128)(2,1)S(1)} %bitcast.132) | data formatting | bytes 737280 | tf_op jit(solution)/shard_map/all_to_all | solution.py:206
  93.8 0.8 copy.140
  (98 shorter events, 4.3 us)
Async XLA Ops:
  2.8 6.5 %copy-start.23 = (pred[8]{0:T(512)(128)(4,1)}, pred[8]{0:T(512)(128)(4,1)S(1)}, u32[]{:S(2)}) copy-start(pred[8]{0:T(512)(128)(4,1)S(1)} %iota_compare_fusion.2) | copy-start | bytes 28
  4.6 12.3 %copy-start.18 = (f32[64,9,9]{0,2,1:T(8,128)S(1)}, f32[64,9,9]{0,2,1:T(8,128)}, u32[]{:S(2)}) copy-start(f32[64,9,9]{0,2,1:T(8,128)} %param.16) | copy-start | bytes 62212
  4.6 15.3 %collective-permute-start = (bf16[1,180,128]{2,1,0:T(8,128)(2,1)S(1)}, bf16[1,180,128]{2,1,0:T(8,128)(2,1)S(1)}, u32[]{:S(2)}, u32[]{:S(2)}) collective-permute-start(bf16[1,180,128]{2,1,0:T(8,128)(2,1)S(1)} %get-tuple-element.39), channel_id=1, source_target_pairs={{0,4},{4,8},{8,12},{12,16},{16,20},{20,24},{24,28},{28,0},{1,5},{5... | collective-permute-start | bytes 138248 | tf_op jit(solution)/shard_map/ppermute | solution.py:141
  5.1 14.8 %collective-permute-start.1 = (bf16[1,180,128]{2,1,0:T(8,128)(2,1)S(1)}, bf16[1,180,128]{2,1,0:T(8,128)(2,1)S(1)}, u32[]{:S(2)}, u32[]{:S(2)}) collective-permute-start(bf16[1,180,128]{2,1,0:T(8,128)(2,1)S(1)} %get-tuple-element.40), channel_id=1, source_target_pairs={{4,0},{8,4},{12,8},{16,12},{20,16},{24,20},{28,24},{0,28},{5,1},{9... | collective-permute-start | bytes 138248 | tf_op jit(solution)/shard_map/ppermute | solution.py:142
  9.3 9.5 %copy-start.19 = (f32[45,192]{1,0:T(8,128)S(1)}, f32[45,192]{1,0:T(8,128)}, u32[]{:S(2)}) copy-start(f32[45,192]{1,0:T(8,128)} %constant.61.clone) | copy-start | bytes 103684
  9.3 9.5 %copy-start.20 = (f32[45,192]{1,0:T(8,128)S(1)}, f32[45,192]{1,0:T(8,128)}, u32[]{:S(2)}) copy-start(f32[45,192]{1,0:T(8,128)} %constant.60.clone) | copy-start | bytes 103684
  9.3 9.5 %copy-start.21 = (f32[16,192]{1,0:T(8,128)S(1)}, f32[16,192]{1,0:T(8,128)}, u32[]{:S(2)}) copy-start(f32[16,192]{1,0:T(8,128)} %constant.63.clone) | copy-start | bytes 36868
  9.3 9.5 %copy-start.22 = (f32[16,192]{1,0:T(8,128)S(1)}, f32[16,192]{1,0:T(8,128)}, u32[]{:S(2)}) copy-start(f32[16,192]{1,0:T(8,128)} %constant.62.clone) | copy-start | bytes 36868
  9.3 20.3 %all-to-all-start = ((bf16[8,180,128]{1,0,2:T(8,128)(2,1)}), bf16[8,180,128]{1,0,2:T(8,128)(2,1)S(1)}, u32[]{:S(2)}, u32[]{:S(2)}) async-start(bf16[8,180,128]{1,0,2:T(8,128)(2,1)} %copy.103), calls=%async_computation | async-start | bytes 1048576 | tf_op jit(solution)/shard_map/all_to_all | solution.py:166
  17.9 6.5 %copy-start.12 = (f32[2,360,128]{2,1,0:T(8,128)S(1)}, f32[2,360,128]{2,1,0:T(8,128)}, u32[]{:S(2)}) copy-start(f32[2,360,128]{2,1,0:T(8,128)} %param.15) | copy-start | bytes 1105924
  18.8 7.7 %copy-start.13 = (bf16[128,9,128]{2,0,1:T(8,128)(2,1)S(1)}, bf16[128,9,128]{2,0,1:T(8,128)(2,1)}, u32[]{:S(2)}) copy-start(bf16[128,9,128]{2,0,1:T(8,128)(2,1)} %param.17) | copy-start | bytes 884740
  19.2 13.1 %copy-start.1 = (bf16[45,16,192]{2,1,0:T(8,128)(2,1)}, bf16[45,16,192]{2,1,0:T(8,128)(2,1)S(1)}, u32[]{:S(2)}) copy-start(bf16[45,16,192]{2,1,0:T(8,128)(2,1)S(1)} %get-tuple-element.49) | copy-start | bytes 829444
  19.2 13.6 %copy-start.3 = (bf16[45,16,192]{2,1,0:T(8,128)(2,1)}, bf16[45,16,192]{2,1,0:T(8,128)(2,1)S(1)}, u32[]{:S(2)}) copy-start(bf16[45,16,192]{2,1,0:T(8,128)(2,1)S(1)} %get-tuple-element.50) | copy-start | bytes 829444
  19.9 2.7 %copy-start.15 = (bf16[1,180,128]{2,1,0:T(8,128)(2,1)}, bf16[1,180,128]{2,1,0:T(8,128)(2,1)S(1)}, u32[]{:S(2)}) copy-start(bf16[1,180,128]{2,1,0:T(8,128)(2,1)S(1)} %collective-permute-done.1) | copy-start | bytes 138244
  19.9 4.6 %copy-start.25 = (pred[8,3]{1,0:T(8,128)(4,1)S(1)}, pred[8,3]{1,0:T(8,128)(4,1)}, u32[]{:S(2)}) copy-start(pred[8,3]{1,0:T(8,128)(4,1)} %pad_add_fusion.1) | copy-start | bytes 76
  20.6 8.0 %collective-permute-start.2 = (bf16[10,1,128]{2,1,0:T(2,128)(2,1)}, bf16[10,1,128]{2,1,0:T(2,128)(2,1)S(1)}, u32[]{:S(2)}, u32[]{:S(2)}) collective-permute-start(bf16[10,1,128]{2,1,0:T(2,128)(2,1)} %get-tuple-element.37), channel_id=1, source_target_pairs={{0,1},{1,2},{2,3},{3,0},{4,5},{5,6},{6,7},{7,4},{8,9},{9,10},{10,1... | collective-permute-start | bytes 7688 | tf_op jit(solution)/shard_map/ppermute | solution.py:144
  22.6 6.0 %collective-permute-start.3 = (bf16[10,1,128]{2,1,0:T(2,128)(2,1)}, bf16[10,1,128]{2,1,0:T(2,128)(2,1)}, u32[]{:S(2)}, u32[]{:S(2)}) collective-permute-start(bf16[10,1,128]{2,1,0:T(2,128)(2,1)} %get-tuple-element.38), channel_id=1, source_target_pairs={{1,0},{2,1},{3,2},{0,3},{5,4},{6,5},{7,6},{4,7},{9,8},{10,9},{11,1... | collective-permute-start | bytes 7688 | tf_op jit(solution)/shard_map/ppermute | solution.py:145
  29.6 10.4 %copy-start.5 = (bf16[10,208,128]{2,1,0:T(8,128)(2,1)}, bf16[10,208,128]{2,1,0:T(8,128)(2,1)S(1)}, u32[]{:S(2)}) copy-start(bf16[10,208,128]{2,1,0:T(8,128)(2,1)S(1)} %maximum_maximum_fusion) | copy-start | bytes 1597444
  29.6 0.8 copy-start.7
  33.5 5.7 %copy-start.27 = (pred[8,3]{0,1:T(4,128)(4,1)S(1)}, pred[8,3]{0,1:T(4,128)(4,1)}, u32[]{:S(2)}) copy-start(pred[8,3]{0,1:T(4,128)(4,1)} %copy.113) | copy-start | bytes 76
  35.6 10.1 %all-to-all-start.1 = ((bf16[8,2,6144]{2,1,0:T(2,128)(2,1)}), bf16[8,2,6144]{2,1,0:T(2,128)(2,1)S(1)}, u32[]{:S(2)}, u32[]{:S(2)}) async-start(bf16[8,2,6144]{2,1,0:T(2,128)(2,1)} %reshape.289), calls=%async_computation.1 | async-start | bytes 393216 | tf_op jit(solution)/shard_map/all_to_all | solution.py:177
  39.3 7.7 %copy-start.16 = (f32[8,3,3,9]{3,0,2,1:T(8,128)}, f32[8,3,3,9]{3,0,2,1:T(8,128)S(1)}, u32[]{:S(2)}) copy-start(f32[8,3,3,9]{3,0,2,1:T(8,128)S(1)} %maximum_select_fusion) | copy-start | bytes 7780
  47.0 4.1 %copy-start = (f32[24,360,64]{1,2,0:T(8,128)S(1)}, f32[24,360,64]{1,2,0:T(8,128)}, u32[]{:S(2)}) copy-start(f32[24,360,64]{1,2,0:T(8,128)} %param.13) | copy-start | bytes 6635524
  51.5 0.8 copy-start.14
  53.3 0.7 copy-start.26
  54.5 6.2 %copy-start.17 = (f32[8,3,3,9]{3,0,2,1:T(8,128)S(1)}, f32[8,3,3,9]{3,0,2,1:T(8,128)}, u32[]{:S(2)}) copy-start(f32[8,3,3,9]{3,0,2,1:T(8,128)} %copy-done.16) | copy-start | bytes 7780
  54.5 6.8 %copy-start.6 = (bf16[10,208,128]{2,1,0:T(8,128)(2,1)S(1)}, bf16[10,208,128]{2,1,0:T(8,128)(2,1)}, u32[]{:S(2)}) copy-start(bf16[10,208,128]{2,1,0:T(8,128)(2,1)} %copy-done.5) | copy-start | bytes 1597444
  56.7 11.8 %all-to-all-start.2 = ((bf16[8,2,6144]{2,1,0:T(2,128)(2,1)}), bf16[8,2,6144]{2,1,0:T(2,128)(2,1)S(1)}, u32[]{:S(2)}, u32[]{:S(2)}) async-start(bf16[8,2,6144]{2,1,0:T(2,128)(2,1)} %reshape.291), calls=%async_computation.2 | async-start | bytes 393216 | tf_op jit(solution)/shard_map/all_to_all | solution.py:197
  69.9 1.0 %copy-start.4 = (bf16[45,16,192]{2,1,0:T(8,128)(2,1)S(1)}, bf16[45,16,192]{2,1,0:T(8,128)(2,1)}, u32[]{:S(2)}) copy-start(bf16[45,16,192]{2,1,0:T(8,128)(2,1)} %copy-done.3) | copy-start | bytes 829444
  70.6 1.0 %copy-start.2 = (bf16[45,16,192]{2,1,0:T(8,128)(2,1)S(1)}, bf16[45,16,192]{2,1,0:T(8,128)(2,1)}, u32[]{:S(2)}) copy-start(bf16[45,16,192]{2,1,0:T(8,128)(2,1)} %copy-done.1) | copy-start | bytes 829444
  75.8 15.5 %all-to-all-start.3 = ((bf16[4,2,23040]{2,1,0:T(2,128)(2,1)}), bf16[4,2,23040]{2,1,0:T(2,128)(2,1)S(1)}, u32[]{:S(2)}, u32[]{:S(2)}) async-start(bf16[4,2,23040]{2,1,0:T(2,128)(2,1)} %reshape.293), calls=%async_computation.3 | async-start | bytes 737280 | tf_op jit(solution)/shard_map/all_to_all | solution.py:206
  92.2 1.3 %copy-start.8 = (bf16[8,180,128]{2,0,1:T(8,128)(2,1)S(1)}, bf16[8,180,128]{2,0,1:T(8,128)(2,1)}, u32[]{:S(2)}) copy-start(bf16[8,180,128]{2,0,1:T(8,128)(2,1)} %param.11) | copy-start | bytes 1105924
  92.2 1.3 %copy-start.9 = (f32[3,192,128]{2,1,0:T(8,128)S(1)}, f32[3,192,128]{2,1,0:T(8,128)}, u32[]{:S(2)}) copy-start(f32[3,192,128]{2,1,0:T(8,128)} %shard_map.110) | copy-start | bytes 884740
  92.2 1.3 %copy-start.10 = (f32[3,192,128]{2,1,0:T(8,128)S(1)}, f32[3,192,128]{2,1,0:T(8,128)}, u32[]{:S(2)}) copy-start(f32[3,192,128]{2,1,0:T(8,128)} %shard_map.111) | copy-start | bytes 884740
  92.2 1.3 %copy-start.11 = (f32[2,192,128]{2,1,0:T(8,128)S(1)}, f32[2,192,128]{2,1,0:T(8,128)}, u32[]{:S(2)}) copy-start(f32[2,192,128]{2,1,0:T(8,128)} %shard_map.109) | copy-start | bytes 589828
  92.2 1.3 %copy-start.24 = (pred[8]{0:T(512)(128)(4,1)S(1)}, pred[8]{0:T(512)(128)(4,1)}, u32[]{:S(2)}) copy-start(pred[8]{0:T(512)(128)(4,1)} %copy-done.23) | copy-start | bytes 28

commit v7 on v6

--- a/solution.py
+++ b/solution.py
@@ -148,34 +148,21 @@
     return jnp.concatenate([from_left, rows, from_right, pad], axis=1)
 
 
-def on_device(
-    grad_output, band_rows, legendre, quad_weights, spectral_filter, disco_kernel, disco_weight
+def spectral_by_channels(
+    masked, legendre, quad_weights, spectral_filter, trig_parts, ext, disco_work
 ):
-    row_count, lon_count, channels = grad_output.shape
-    band_index = lax.axis_index("lat")
-    band_total = lax.axis_size("lat")
+    channels = masked.shape[2]
     lon_index = lax.axis_index("lon")
-    point_count = lon_count * lax.axis_size("lon")
-    mode_count = legendre.shape[0] * band_total
     chan_share = channels // lax.axis_size("lon")
-    slot_ids = jnp.arange(row_count, dtype=jnp.int32)
-    live_rows = band_rows[band_index]
-    live_slot = slot_ids < live_rows
-    masked = jnp.where(live_slot[:, None, None], grad_output, jnp.zeros_like(grad_output))
-    trig_parts = make_trig(mode_count, point_count)
+    disco_parts = []
     portion = lax.all_to_all(masked, "lon", split_axis=2, concat_axis=1, tiled=True)
     spectra = jnp.stack(
         [dot_split("rnc,nk->rkc", (portion,), parts).astype(jnp.bfloat16) for parts in trig_parts],
         axis=1,
     )
-    ext = halo_extend(masked, live_rows)
-    src_rows, coef = disco_tables(band_rows, disco_kernel, band_index, band_total, row_count)
-    weight_flat = disco_weight.reshape(channels, -1)
-    pieces = min(3, row_count)
-    disco_parts = []
     spectra, ext_now = lax.optimization_barrier((spectra, ext))
     columns = lax.all_to_all(spectra, "lat", split_axis=2, concat_axis=0, tiled=True)
-    disco_parts.append(disco_piece(src_rows, coef, ext_now, weight_flat, 0, pieces, lon_count))
+    disco_parts.append(disco_work(ext_now, 0))
     columns, disco_parts[0] = lax.optimization_barrier((columns, disco_parts[0]))
     legendre_parts = split_bf16(legendre)
     coefficients = dot_split("mls,spmc->lpmc", legendre_parts, (columns,))
@@ -195,7 +182,7 @@
     returned = (returned * quad_weights[:, None, None, None]).astype(jnp.bfloat16)
     returned, ext_now = lax.optimization_barrier((returned, ext))
     portion = lax.all_to_all(returned, "lat", split_axis=0, concat_axis=2, tiled=True)
-    disco_parts.append(disco_piece(src_rows, coef, ext_now, weight_flat, 1, pieces, lon_count))
+    disco_parts.append(disco_work(ext_now, 1))
     portion, disco_parts = lax.optimization_barrier((portion, disco_parts))
     spectral_rows = None
     for p, parts in enumerate(trig_parts):
@@ -204,11 +191,90 @@
     spectral_rows = spectral_rows.astype(jnp.bfloat16)
     spectral_rows, ext_now = lax.optimization_barrier((spectral_rows, ext))
     spectral = lax.all_to_all(spectral_rows, "lon", split_axis=1, concat_axis=2, tiled=True)
-    for piece in range(2, pieces):
-        disco_parts.append(
-            disco_piece(src_rows, coef, ext_now, weight_flat, piece, pieces, lon_count)
-        )
+    disco_parts.append(disco_work(ext_now, 2))
     spectral, disco_parts = lax.optimization_barrier((spectral, disco_parts))
+    return spectral, disco_parts
+
+
+def filter_modes(coefficients, spectral_filter):
+    filter_real = spectral_filter[0][:, None, :]
+    filter_imag = spectral_filter[1][:, None, :]
+    real_part = coefficients[:, 0]
+    imag_part = coefficients[:, 1]
+    return jnp.stack(
+        [
+            filter_real * real_part + filter_imag * imag_part,
+            filter_real * imag_part - filter_imag * real_part,
+        ],
+        axis=1,
+    )
+
+
+def spectral_by_modes(masked, legendre, quad_weights, spectral_filter, trig_parts, ext, disco_work):
+    both = ("lat", "lon")
+    lon_total = lax.axis_size("lon")
+    mode_share = legendre.shape[0] // lon_total
+    disco_parts = []
+    portion = lax.all_to_all(masked, "lon", split_axis=0, concat_axis=1, tiled=True)
+    spectra = jnp.stack(
+        [dot_split("rnc,nk->rkc", (portion,), parts).astype(jnp.bfloat16) for parts in trig_parts],
+        axis=1,
+    )
+    spectra, ext_now = lax.optimization_barrier((spectra, ext))
+    columns = lax.all_to_all(spectra, both, split_axis=2, concat_axis=0, tiled=True)
+    disco_parts.append(disco_work(ext_now, 0))
+    columns, disco_parts[0] = lax.optimization_barrier((columns, disco_parts[0]))
+    own_legendre = lax.dynamic_slice_in_dim(
+        legendre, lax.axis_index("lon") * mode_share, mode_share, 0
+    )
+    legendre_parts = split_bf16(own_legendre)
+    coefficients = dot_split("mls,spmc->lpmc", legendre_parts, (columns,))
+    filtered = filter_modes(coefficients, spectral_filter)
+    returned = dot_split("mls,lpmc->spmc", legendre_parts, split_bf16(filtered))
+    returned = (returned * quad_weights[:, None, None, None]).astype(jnp.bfloat16)
+    returned, ext_now = lax.optimization_barrier((returned, ext))
+    portion = lax.all_to_all(returned, both, split_axis=0, concat_axis=2, tiled=True)
+    disco_parts.append(disco_work(ext_now, 1))
+    portion, disco_parts = lax.optimization_barrier((portion, disco_parts))
+    spectral_rows = None
+    for p, parts in enumerate(trig_parts):
+        term = dot_split("rkc,nk->rnc", (portion[:, p],), parts)
+        spectral_rows = term if spectral_rows is None else spectral_rows + term
+    spectral_rows = spectral_rows.astype(jnp.bfloat16)
+    spectral_rows, ext_now = lax.optimization_barrier((spectral_rows, ext))
+    spectral = lax.all_to_all(spectral_rows, "lon", split_axis=1, concat_axis=0, tiled=True)
+    disco_parts.append(disco_work(ext_now, 2))
+    spectral, disco_parts = lax.optimization_barrier((spectral, disco_parts))
+    return spectral, disco_parts
+
+
+def on_device(
+    grad_output, band_rows, legendre, quad_weights, spectral_filter, disco_kernel, disco_weight
+):
+    row_count, lon_count, channels = grad_output.shape
+    band_index = lax.axis_index("lat")
+    band_total = lax.axis_size("lat")
+    lon_total = lax.axis_size("lon")
+    point_count = lon_count * lon_total
+    mode_count = legendre.shape[0] * band_total
+    slot_ids = jnp.arange(row_count, dtype=jnp.int32)
+    live_rows = band_rows[band_index]
+    live_slot = slot_ids < live_rows
+    masked = jnp.where(live_slot[:, None, None], grad_output, jnp.zeros_like(grad_output))
+    trig_parts = make_trig(mode_count, point_count)
+    ext = halo_extend(masked, live_rows)
+    src_rows, coef = disco_tables(band_rows, disco_kernel, band_index, band_total, row_count)
+    weight_flat = disco_weight.reshape(channels, -1)
+    pieces = min(3, row_count)
+
+    def disco_work(ext_now, piece):
+        return disco_piece(src_rows, coef, ext_now, weight_flat, piece, pieces, lon_count)
+
+    by_modes = legendre.shape[0] % lon_total == 0 and row_count % lon_total == 0
+    path = spectral_by_modes if by_modes else spectral_by_channels
+    spectral, disco_parts = path(
+        masked, legendre, quad_weights, spectral_filter, trig_parts, ext, disco_work
+    )
     disco_full = jnp.concatenate(disco_parts, axis=0)
     disco_term = disco_full[:, :lon_count, :]
     summed = masked.astype(jnp.float32) + disco_term + spectral.astype(jnp.float32)

time: 95.5 us -> 84.3 us (0.88)
  local copies, waits for them, and re-layouts: 34.1 us -> 16.4 us
  starting transfers between devices: 24 us -> 27.8 us
  other arithmetic: 7.26 us -> 9.13 us
  waiting for transfers between devices: 3.51 us -> 5.36 us
    unnamed x64 -> x26, local copies, waits for them, and re-layouts: 9.45 us -> 1.97 us
    all_to_all x7 -> x5, local copies, waits for them, and re-layouts: 6.81 us -> 0.45 us  [the longest x1 0.16 us: spectral_by_modes(): lax.all_to_all(spectra, both, split_axis=2, concat_axis=0, tiled=True)]
    all_to_all x4, starting transfers between devices: 16.7 us -> 21.2 us  [the longest x1 6.32 us: spectral_by_modes(): lax.all_to_all(masked, 'lon', split_axis=0, concat_axis=1, tiled=True)]
    unnamed x8 -> x0, matrix products: 2.24 us -> none
    optimization_barrier x5 -> x4, local copies, waits for them, and re-layouts: 4.79 us -> 2.82 us  [the longest x1 1.02 us: spectral_by_modes(): spectral_rows, ext_now = lax.optimization_barrier((spectral_rows, ext))]
    dot_general x5 -> x13, matrix products: 2.76 us -> 4.32 us  [dot_split(): term = jnp.einsum(spec, lp, rp, preferred_element_type=jnp.float32)]
    ppermute x1, waiting for transfers between devices: 0.01 us -> 1.46 us  [halo_extend(): from_left = lax.ppermute(rows[:, lon_count - 1:lon_count], 'lon', lon_up)]
    select_n x1 -> x0, local copies, waits for them, and re-layouts: 1.2 us -> none  [on_device(): jnp.where(live_slot[:, None, None], grad_output, jnp.zeros_like(grad_outp...]
  transfers between devices with their start and end apart: 8 -> 8, of which waited for: 1 -> 4; matrix products, arithmetic and copies ran while one was open for 17% -> 18% of each run, Pallas kernels for 19% -> 22%
where the time goes in v7:
time: 84.3 us; the launch traced here: 83.4 us
  starting transfers between devices  27.8 us (33%)
  Pallas kernels  18 us (21%)
  local copies, waits for them, and re-layouts  16.4 us (19%)
  other arithmetic  9.13 us (11%)
  waiting for transfers between devices  5.36 us (6%)
  matrix products  4.32 us (5%)
  between operations  2.37 us (3%)
    pallas_call x3, Pallas kernels, disco_apply(): pl.pallas_call(disco_body, out_shape=jax.ShapeDtypeStruct((slot_total, ou...  18 us
    all_to_all x1, starting transfers between devices, spectral_by_modes(): lax.all_to_all(masked, 'lon', split_axis=0, concat_axis=1, tiled=True)  6.32 us
    all_to_all x1, starting transfers between devices, spectral_by_modes(): lax.all_to_all(returned, both, split_axis=0, concat_axis=2, tiled=True)  5.83 us
    all_to_all x1, starting transfers between devices, spectral_by_modes(): lax.all_to_all(spectra, both, split_axis=2, concat_axis=0, tiled=True)  5.01 us
    dot_general x13, matrix products, dot_split(): term = jnp.einsum(spec, lp, rp, preferred_element_type=jnp.float32)  4.32 us
    all_to_all x1, starting transfers between devices, spectral_by_modes(): lax.all_to_all(spectral_rows, 'lon', split_axis=1, concat_axis=0, tiled=T...  4.07 us
    all_to_all x1, waiting for transfers between devices, spectral_by_modes(): lax.all_to_all(spectral_rows, 'lon', split_axis=1, concat_axis=0, tiled=T...  2.88 us
    ppermute x1, starting transfers between devices, halo_extend(): from_below = lax.ppermute(masked[0:1], 'lat', lat_down)  2.63 us
  transfers between devices with their start and end apart: 8, of which 4 were waited for; matrix products, arithmetic and copies ran while one was open for 18% of the time, Pallas kernels for 22%

profile of v7, /device:TPU:0, one launch (start us, length us, event | category | flops | bytes accessed | tf_op | source)
XLA Modules:
  0.0 83.4 jit_solution(16975508562288680130)
XLA Ops:
  0.0 1.3 %fusion.40 = (s32[1]{0:T(128)}, s32[1]{0:T(128)}) fusion(s32[8]{0:T(128)} %param.12, s32[]{:T(128)S(6)} %max.10, s32[]{:T(128)S(6)} %select_n.89), kind=kLoop, calls=%fused_computation.90 | loop fusion | bytes 24 | tf_op jit(solution)/shard_map/dynamic_slice | solution.py:107
  1.3 0.6 iota_compare_fusion.2
  2.0 1.8 %copy_select_fusion = bf16[8,180,128]{2,1,0:T(8,128)(2,1)} fusion(bf16[8,180,128]{2,0,1:T(8,128)(2,1)} %param.11, pred[8]{0:T(512)(128)(4,1)S(1)} %iota_compare_fusion.2), kind=kLoop, calls=%fused_computation.43 | loop fusion | flops 184320 | bytes 737288 | tf_op jit(solution)/shard_map/jit(_where)/select_n | solution.py:263
  3.8 6.3 %all-to-all-start = ((bf16[8,180,128]{2,1,0:T(8,128)(2,1)}), bf16[8,180,128]{2,1,0:T(8,128)(2,1)S(1)}, u32[]{:S(2)}, u32[]{:S(2)}) async-start(bf16[8,180,128]{2,1,0:T(8,128)(2,1)} %copy_select_fusion), calls=%async_computation | async-start | bytes 753664 | tf_op jit(solution)/shard_map/all_to_all | solution.py:218
  11.5 0.8 constant_dynamic-slice_fusion
  12.3 2.6 %collective-permute-start.1 = (bf16[1,180,128]{2,1,0:T(8,128)(2,1)S(1)}, bf16[1,180,128]{2,1,0:T(8,128)(2,1)S(1)}, u32[]{:S(2)}, u32[]{:S(2)}) collective-permute-start(bf16[1,180,128]{2,1,0:T(8,128)(2,1)S(1)} %get-tuple-element.40), channel_id=1, source_target_pairs={{4,0},{8,4},{12,8},{16,12},{20,16},{24,20},{28,24},{0,28},{5,1},{9... | collective-permute-start | bytes 138248 | tf_op jit(solution)/shard_map/ppermute | solution.py:142
  15.7 0.6 fusion.32
  16.4 0.1 copy.126
  16.5 0.1 fusion.30
  16.7 0.8 select_reduce_fusion
  17.4 0.1 copy.127
  17.5 0.1 reshape.259
  17.6 0.3 copy.128
  17.9 0.6 gather_fusion
  18.7 0.3 fusion.16
  19.1 0.8 pad_maximum_fusion.6
  19.9 2.1 %collective-permute-start.2 = (bf16[10,1,128]{2,1,0:T(2,128)(2,1)S(1)}, bf16[10,1,128]{2,1,0:T(2,128)(2,1)S(1)}, u32[]{:S(2)}, u32[]{:S(2)}) collective-permute-start(bf16[10,1,128]{2,1,0:T(2,128)(2,1)S(1)} %get-tuple-element.37), channel_id=1, source_target_pairs={{0,1},{1,2},{2,3},{3,0},{4,5},{5,6},{6,7},{7,4},{8,9},{9,10},{10,1... | collective-permute-start | bytes 7688 | tf_op jit(solution)/shard_map/ppermute | solution.py:144
  22.0 1.9 %collective-permute-start.3 = (bf16[10,1,128]{2,1,0:T(2,128)(2,1)S(1)}, bf16[10,1,128]{2,1,0:T(2,128)(2,1)S(1)}, u32[]{:S(2)}, u32[]{:S(2)}) collective-permute-start(bf16[10,1,128]{2,1,0:T(2,128)(2,1)S(1)} %get-tuple-element.38), channel_id=1, source_target_pairs={{1,0},{2,1},{3,2},{0,3},{5,4},{6,5},{7,6},{4,7},{9,8},{10,9},{11,1... | collective-permute-start | bytes 7688 | tf_op jit(solution)/shard_map/ppermute | solution.py:145
  23.9 1.5 %collective-permute-done.2 = bf16[10,1,128]{2,1,0:T(2,128)(2,1)S(1)} collective-permute-done((bf16[10,1,128]{2,1,0:T(2,128)(2,1)S(1)}, bf16[10,1,128]{2,1,0:T(2,128)(2,1)S(1)}, u32[]{:S(2)}, u32[]{:S(2)}) %collective-permute-start.2) | collective-permute-done | bytes 2592 | tf_op jit(solution)/shard_map/ppermute | solution.py:144
  25.4 0.2 collective-permute-done.3
  25.6 1.2 %maximum_maximum_fusion = bf16[10,208,128]{2,1,0:T(8,128)(2,1)S(1)} fusion(bf16[10,1,128]{2,1,0:T(2,128)(2,1)S(1)} %collective-permute-done.3, bf16[1,180,128]{2,1,0:T(8,128)(2,1)S(1)} %collective-permute-done.1, bf16[8,180,128]{2,1,0:T(8,128)(2,1)} %copy_select_fusion, bf16[1,180,128]{2,1,0:T(8,128)(2,1)S(1)} %collective-permute-done, ...), kind=kLoop, calls=%fused_computation.41 | loop fusion | flops 3194880 | bytes 998816 | tf_op jit(solution)/shard_map/concatenate | solution.py:148
  26.9 0.3 fusion.42
  27.2 0.3 fusion.41
  27.5 0.3 fusion.9
  27.8 0.3 fusion.10
  28.2 0.9 %copy.123 = bf16[2,2,192,128]{3,0,1,2:T(2,128)(2,1)} copy(bf16[2,2,192,128]{3,2,0,1:T(8,128)(2,1)S(1)} %pad_maximum_fusion.3) | data formatting | bytes 393216 | tf_op jit(solution)/shard_map/optimization_barrier | solution.py:223
  29.0 5.0 %all-to-all-start.1 = ((bf16[2,2,192,128]{3,0,1,2:T(2,128)(2,1)}), bf16[2,2,192,128]{3,0,1,2:T(2,128)(2,1)S(1)}, u32[]{:S(2)}, u32[]{:S(2)}) async-start(bf16[2,2,192,128]{3,0,1,2:T(2,128)(2,1)} %copy.123), calls=%async_computation.1 | async-start | bytes 393216 | tf_op jit(solution)/shard_map/all_to_all | solution.py:224
  34.1 0.7 reshape.249.src_ref
  34.8 0.2 copy.132
  35.0 0.9 %copy.133.w_ref = bf16[128,1152]{1,0:T(8,128)(2,1)} copy(bf16[128,1152]{0,1:T(8,128)(2,1)S(1)} %bitcast.114) | data formatting | bytes 589824 | tf_op jit(solution)/shard_map/reshape | solution.py:267
  36.0 0.6 reshape.251.coef_ref
  36.6 1.1 %fusion.20 = bf16[6,360,64,1]{1,2,3,0:T(8,128)(2,1)S(1)} fusion(f32[24,360,64]{1,2,0:T(8,128)} %param.13, s32[]{:T(128)S(6)} %select_n.98), kind=kLoop, calls=%fused_computation.45 | loop fusion | flops 276480 | bytes 829444 | tf_op jit(solution)/shard_map/convert_element_type | solution.py:32
  37.7 0.7 slice.78.ext_ref
  38.4 5.0 %shard_map.109 = f32[2,192,128]{2,1,0:T(8,128)} custom-call(s32[6]{0:T(128)} %reshape.249.src_ref, f32[162]{0:T(256)} %reshape.251.coef_ref, bf16[4,208,128]{2,1,0:T(8,128)(2,1)} %slice.78.ext_ref, bf16[128,1152]{1,0:T(8,128)(2,1)} %copy.133.w_ref), custom_call_target="tpu_custom_call" | custom-call | tf_op jit(solution)/shard_map/pallas_call | solution.py:82
  43.5 0.2 copy.125
  43.7 0.5 fusion.22
  44.2 1.1 %copy-done.1 = f32[24,360,64]{1,2,0:T(8,128)S(1)} copy-done((f32[24,360,64]{1,2,0:T(8,128)S(1)}, f32[24,360,64]{1,2,0:T(8,128)}, u32[]{:S(2)}) %copy-start.1) | copy-done | bytes 2211864
  45.3 0.5 add_bitcast_fusion
  45.8 0.2 multiply_add_fusion
  46.1 0.4 fusion.28
  46.5 0.4 convolution_add_fusion.3
  46.9 0.2 copy-done.11
  47.1 0.4 fusion.6
  47.5 0.9 %copy.136 = bf16[64,2,6,128]{3,1,2,0:T(2,128)(2,1)} copy(bf16[64,2,6,128]{3,0,1,2:T(8,128)(2,1)S(1)} %fusion.6) | data formatting | bytes 393216 | tf_op jit(solution)/shard_map/optimization_barrier | solution.py:235
  48.4 5.8 %all-to-all-start.2 = ((bf16[64,2,6,128]{3,1,2,0:T(2,128)(2,1)}), bf16[64,2,6,128]{3,1,2,0:T(2,128)(2,1)S(1)}, u32[]{:S(2)}, u32[]{:S(2)}) async-start(bf16[64,2,6,128]{3,1,2,0:T(2,128)(2,1)} %copy.136), calls=%async_computation.2 | async-start | bytes 393216 | tf_op jit(solution)/shard_map/all_to_all | solution.py:236
  54.2 0.6 reshape.253.src_ref
  54.8 0.7 reshape.254.coef_ref
  55.5 0.7 slice.84.ext_ref
  56.3 6.5 %shard_map.110 = f32[3,192,128]{2,1,0:T(8,128)} custom-call(s32[9]{0:T(128)} %reshape.253.src_ref, f32[243]{0:T(256)} %reshape.254.coef_ref, bf16[5,208,128]{2,1,0:T(8,128)(2,1)} %slice.84.ext_ref, bf16[128,1152]{1,0:T(8,128)(2,1)} %copy.133.w_ref), custom_call_target="tpu_custom_call" | custom-call | tf_op jit(solution)/shard_map/pallas_call | solution.py:82
  62.7 0.8 all-to-all-done.2
  63.6 0.1 copy.137
  63.7 0.2 fusion.25
  64.0 0.2 fusion.24
  64.2 0.2 convolution_add_fusion.1
  64.5 0.3 fusion.4
  64.8 1.0 %copy.146 = bf16[2,720,128]{2,0,1:T(2,128)(2,1)} copy(bf16[2,720,128]{2,1,0:T(8,128)(2,1)S(1)} %fusion.4) | data formatting | bytes 737280 | tf_op jit(solution)/shard_map/optimization_barrier | solution.py:244
  65.8 4.1 %all-to-all-start.3 = ((bf16[2,720,128]{2,0,1:T(2,128)(2,1)}), bf16[2,720,128]{2,0,1:T(2,128)(2,1)S(1)}, u32[]{:S(2)}, u32[]{:S(2)}) async-start(bf16[2,720,128]{2,0,1:T(2,128)(2,1)} %copy.146), calls=%async_computation.3 | async-start | bytes 737280 | tf_op jit(solution)/shard_map/all_to_all | solution.py:245
  69.9 0.7 reshape.255.src_ref
  70.5 0.7 reshape.256.coef_ref
  71.2 0.7 slice.89.ext_ref
  72.0 6.5 %shard_map.111 = f32[3,192,128]{2,1,0:T(8,128)} custom-call(s32[9]{0:T(128)} %reshape.255.src_ref, f32[243]{0:T(256)} %reshape.256.coef_ref, bf16[5,208,128]{2,1,0:T(8,128)(2,1)} %slice.89.ext_ref, bf16[128,1152]{1,0:T(8,128)(2,1)} %copy.133.w_ref), custom_call_target="tpu_custom_call" | custom-call | tf_op jit(solution)/shard_map/pallas_call | solution.py:82
  78.4 2.9 %all-to-all-done.3 = bf16[2,720,128]{2,0,1:T(2,128)(2,1)S(1)} async-done(((bf16[2,720,128]{2,0,1:T(2,128)(2,1)}), bf16[2,720,128]{2,0,1:T(2,128)(2,1)S(1)}, u32[]{:S(2)}, u32[]{:S(2)}) %all-to-all-start.3) | async-done | bytes 368672 | tf_op jit(solution)/shard_map/all_to_all | solution.py:245
  81.4 1.2 %fusion.15 = bf16[8,180,128]{2,1,0:T(8,128)(2,1)S(1)} fusion(f32[3,192,128]{2,1,0:T(8,128)} %shard_map.111, f32[3,192,128]{2,1,0:T(8,128)S(1)} %copy-done.2, f32[2,192,128]{2,1,0:T(8,128)S(1)} %copy-done.3, bf16[8,180,128]{2,1,0:T(8,128)(2,1)S(1)} %bitcast.111, pred[8]{0:T(512)(128)(4,1)S(1)} %iota_compare_fusion.2, bf16[8,180,128]{2,0,1:T(8,128)(2,1)S(1)} %copy-done), kind=kLoop, calls=%fused_computation.34 | loop fusion | flops 1658880 | bytes 1892360 | tf_op jit(solution)/shard_map/convert_element_type | solution.py:281
  82.6 0.8 copy.151
  (52 shorter events, 0.9 us)
Async XLA Ops:
  0.0 17.6 %copy-start.6 = (f32[64,9,9]{0,2,1:T(8,128)S(1)}, f32[64,9,9]{0,2,1:T(8,128)}, u32[]{:S(2)}) copy-start(f32[64,9,9]{0,2,1:T(8,128)} %param.16) | copy-start | bytes 62212
  3.8 23.0 %all-to-all-start = ((bf16[8,180,128]{2,1,0:T(8,128)(2,1)}), bf16[8,180,128]{2,1,0:T(8,128)(2,1)S(1)}, u32[]{:S(2)}, u32[]{:S(2)}) async-start(bf16[8,180,128]{2,1,0:T(8,128)(2,1)} %copy_select_fusion), calls=%async_computation | async-start | bytes 753664 | tf_op jit(solution)/shard_map/all_to_all | solution.py:218
  10.1 8.5 %copy-start.7 = (f32[45,192]{1,0:T(8,128)S(1)}, f32[45,192]{1,0:T(8,128)}, u32[]{:S(2)}) copy-start(f32[45,192]{1,0:T(8,128)} %constant.61.clone) | copy-start | bytes 103684
  10.1 8.5 %copy-start.8 = (f32[45,192]{1,0:T(8,128)S(1)}, f32[45,192]{1,0:T(8,128)}, u32[]{:S(2)}) copy-start(f32[45,192]{1,0:T(8,128)} %constant.60.clone) | copy-start | bytes 103684
  10.1 8.5 %copy-start.9 = (f32[16,192]{1,0:T(8,128)S(1)}, f32[16,192]{1,0:T(8,128)}, u32[]{:S(2)}) copy-start(f32[16,192]{1,0:T(8,128)} %constant.63.clone) | copy-start | bytes 36868
  10.2 8.6 %copy-start.10 = (f32[16,192]{1,0:T(8,128)S(1)}, f32[16,192]{1,0:T(8,128)}, u32[]{:S(2)}) copy-start(f32[16,192]{1,0:T(8,128)} %constant.62.clone) | copy-start | bytes 36868
  12.3 6.8 %collective-permute-start = (bf16[1,180,128]{2,1,0:T(8,128)(2,1)S(1)}, bf16[1,180,128]{2,1,0:T(8,128)(2,1)S(1)}, u32[]{:S(2)}, u32[]{:S(2)}) collective-permute-start(bf16[1,180,128]{2,1,0:T(8,128)(2,1)S(1)} %get-tuple-element.39), channel_id=1, source_target_pairs={{0,4},{4,8},{8,12},{12,16},{16,20},{20,24},{24,28},{28,0},{1,5},{5... | collective-permute-start | bytes 138248 | tf_op jit(solution)/shard_map/ppermute | solution.py:141
  12.3 6.8 %collective-permute-start.1 = (bf16[1,180,128]{2,1,0:T(8,128)(2,1)S(1)}, bf16[1,180,128]{2,1,0:T(8,128)(2,1)S(1)}, u32[]{:S(2)}, u32[]{:S(2)}) collective-permute-start(bf16[1,180,128]{2,1,0:T(8,128)(2,1)S(1)} %get-tuple-element.40), channel_id=1, source_target_pairs={{4,0},{8,4},{12,8},{16,12},{20,16},{24,20},{28,24},{0,28},{5,1},{9... | collective-permute-start | bytes 138248 | tf_op jit(solution)/shard_map/ppermute | solution.py:142
  19.9 5.5 %collective-permute-start.2 = (bf16[10,1,128]{2,1,0:T(2,128)(2,1)S(1)}, bf16[10,1,128]{2,1,0:T(2,128)(2,1)S(1)}, u32[]{:S(2)}, u32[]{:S(2)}) collective-permute-start(bf16[10,1,128]{2,1,0:T(2,128)(2,1)S(1)} %get-tuple-element.37), channel_id=1, source_target_pairs={{0,1},{1,2},{2,3},{3,0},{4,5},{5,6},{6,7},{7,4},{8,9},{9,10},{10,1... | collective-permute-start | bytes 7688 | tf_op jit(solution)/shard_map/ppermute | solution.py:144
  22.0 3.6 %collective-permute-start.3 = (bf16[10,1,128]{2,1,0:T(2,128)(2,1)S(1)}, bf16[10,1,128]{2,1,0:T(2,128)(2,1)S(1)}, u32[]{:S(2)}, u32[]{:S(2)}) collective-permute-start(bf16[10,1,128]{2,1,0:T(2,128)(2,1)S(1)} %get-tuple-element.38), channel_id=1, source_target_pairs={{1,0},{2,1},{3,2},{0,3},{5,4},{6,5},{7,6},{4,7},{9,8},{10,9},{11,1... | collective-permute-start | bytes 7688 | tf_op jit(solution)/shard_map/ppermute | solution.py:145
  27.8 7.0 %copy-start.5 = (bf16[128,9,128]{2,0,1:T(8,128)(2,1)S(1)}, bf16[128,9,128]{2,0,1:T(8,128)(2,1)}, u32[]{:S(2)}) copy-start(bf16[128,9,128]{2,0,1:T(8,128)(2,1)} %param.17) | copy-start | bytes 884740
  29.0 14.5 %all-to-all-start.1 = ((bf16[2,2,192,128]{3,0,1,2:T(2,128)(2,1)}), bf16[2,2,192,128]{3,0,1,2:T(2,128)(2,1)S(1)}, u32[]{:S(2)}, u32[]{:S(2)}) async-start(bf16[2,2,192,128]{3,0,1,2:T(2,128)(2,1)} %copy.123), calls=%async_computation.1 | async-start | bytes 393216 | tf_op jit(solution)/shard_map/all_to_all | solution.py:224
  34.1 3.6 %copy-start.4 = (f32[2,360,128]{2,1,0:T(8,128)S(1)}, f32[2,360,128]{2,1,0:T(8,128)}, u32[]{:S(2)}) copy-start(f32[2,360,128]{2,1,0:T(8,128)} %param.15) | copy-start | bytes 1105924
  43.7 1.7 %copy-start.1 = (f32[24,360,64]{1,2,0:T(8,128)S(1)}, f32[24,360,64]{1,2,0:T(8,128)}, u32[]{:S(2)}) copy-start(f32[24,360,64]{1,2,0:T(8,128)} %param.13) | copy-start | bytes 6635524
  46.5 0.7 copy-start.11
  48.4 15.2 %all-to-all-start.2 = ((bf16[64,2,6,128]{3,1,2,0:T(2,128)(2,1)}), bf16[64,2,6,128]{3,1,2,0:T(2,128)(2,1)S(1)}, u32[]{:S(2)}, u32[]{:S(2)}) async-start(bf16[64,2,6,128]{3,1,2,0:T(2,128)(2,1)} %copy.136), calls=%async_computation.2 | async-start | bytes 393216 | tf_op jit(solution)/shard_map/all_to_all | solution.py:236
  65.8 15.6 %all-to-all-start.3 = ((bf16[2,720,128]{2,0,1:T(2,128)(2,1)}), bf16[2,720,128]{2,0,1:T(2,128)(2,1)S(1)}, u32[]{:S(2)}, u32[]{:S(2)}) async-start(bf16[2,720,128]{2,0,1:T(2,128)(2,1)} %copy.146), calls=%async_computation.3 | async-start | bytes 737280 | tf_op jit(solution)/shard_map/all_to_all | solution.py:245
  69.8 11.5 %copy-start = (bf16[8,180,128]{2,0,1:T(8,128)(2,1)S(1)}, bf16[8,180,128]{2,0,1:T(8,128)(2,1)}, u32[]{:S(2)}) copy-start(bf16[8,180,128]{2,0,1:T(8,128)(2,1)} %param.11) | copy-start | bytes 1105924
  69.9 11.5 %copy-start.2 = (f32[3,192,128]{2,1,0:T(8,128)S(1)}, f32[3,192,128]{2,1,0:T(8,128)}, u32[]{:S(2)}) copy-start(f32[3,192,128]{2,1,0:T(8,128)} %shard_map.110) | copy-start | bytes 884740
  69.9 11.5 %copy-start.3 = (f32[2,192,128]{2,1,0:T(8,128)S(1)}, f32[2,192,128]{2,1,0:T(8,128)}, u32[]{:S(2)}) copy-start(f32[2,192,128]{2,1,0:T(8,128)} %shard_map.109) | copy-start | bytes 589828

commit v8 on v7

--- a/solution.py
+++ b/solution.py
@@ -1,3 +1,5 @@
+import functools
+
 import ml_dtypes
 import numpy as np
 import jax
@@ -50,38 +52,39 @@
     return -(-value // step) * step
 
 
-def disco_body(src_ref, coef_ref, ext_ref, w_ref, out_ref, mix_ref):
-    row_total = ext_ref.shape[0]
-    slot_total = out_ref.shape[0]
+def disco_body(first, last, src_ref, coef_ref, ext_ref, w_ref, out_ref, mix_ref):
     kinds = w_ref.shape[1] // w_ref.shape[0]
     channels = w_ref.shape[0]
-    for r in range(row_total):
-        mix_ref[r] = jnp.dot(ext_ref[r], w_ref[...], preferred_element_type=jnp.float32)
+    for r in range(last - first + 2):
+        mix_ref[r] = jnp.dot(ext_ref[first + r], w_ref[...], preferred_element_type=jnp.float32)
 
     def slot_step(s, carry):
         for c0 in range(0, out_ref.shape[1], CHUNK):
             acc = jnp.zeros((CHUNK, channels), jnp.float32)
             for a_i in range(3):
-                row = src_ref[s * 3 + a_i]
+                row = src_ref[(first + s) * 3 + a_i] - first
                 for b_i in range(3):
                     for k in range(kinds):
-                        coef = coef_ref[((s * 3 + a_i) * 3 + b_i) * kinds + k]
+                        coef = coef_ref[(((first + s) * 3 + a_i) * 3 + b_i) * kinds + k]
                         acc = acc + coef * mix_ref[
                             row, pl.ds(c0 + 2 - b_i, CHUNK), pl.ds(k * channels, channels)
                         ]
             out_ref[s, pl.ds(c0, CHUNK), :] = acc
         return carry
 
-    lax.fori_loop(0, slot_total, slot_step, 0)
-
-
-def disco_apply(src, coef, ext, weight_flat, slot_total, lon_count):
-    row_total, lon_pad, channels = ext.shape
+    lax.fori_loop(0, last - first, slot_step, 0)
+
+
+def disco_piece(src_rows, coef, ext, weight_flat, piece, pieces, lon_count):
+    slot_total = ext.shape[0] - 2
+    first = piece * slot_total // pieces
+    last = (piece + 1) * slot_total // pieces
+    lon_pad, channels = ext.shape[1:]
     out_rows = round_up(lon_count, CHUNK)
     smem = pltpu.MemorySpace.SMEM if hasattr(pltpu, "MemorySpace") else pltpu.SMEM
     return pl.pallas_call(
-        disco_body,
-        out_shape=jax.ShapeDtypeStruct((slot_total, out_rows, channels), jnp.float32),
+        functools.partial(disco_body, first, last),
+        out_shape=jax.ShapeDtypeStruct((last - first, out_rows, channels), jnp.float32),
         in_specs=[
             pl.BlockSpec(memory_space=smem),
             pl.BlockSpec(memory_space=smem),
@@ -89,8 +92,8 @@
             pl.BlockSpec(memory_space=pltpu.VMEM),
         ],
         out_specs=pl.BlockSpec(memory_space=pltpu.VMEM),
-        scratch_shapes=[pltpu.VMEM((row_total, lon_pad, weight_flat.shape[1]), jnp.float32)],
-    )(src, coef, ext, weight_flat)
+        scratch_shapes=[pltpu.VMEM((last - first + 2, lon_pad, weight_flat.shape[1]), jnp.float32)],
+    )(src_rows, coef, ext, weight_flat)
 
 
 def disco_tables(band_rows, disco_kernel, band_index, band_total, row_count):
@@ -116,17 +119,7 @@
     gathered = gathered.reshape(row_count, 3, 3, 3, disco_kernel.shape[2])
     coef = jnp.stack([gathered[:, 0, 2], gathered[:, 1, 1], gathered[:, 2, 0]], axis=1)
     coef = jnp.where(valid[:, :, None, None], coef, 0.0)
-    return src.astype(jnp.int32), coef.reshape(row_count, -1).astype(jnp.float32)
-
-
-def disco_piece(src_rows, coef, ext, weight_flat, piece, pieces, lon_count):
-    slot_total = src_rows.shape[0]
-    first = piece * slot_total // pieces
-    last = (piece + 1) * slot_total // pieces
-    rows = lax.slice_in_dim(ext, first, last + 2, axis=0)
-    local_src = (src_rows[first:last] - first).reshape(-1)
-    local_coef = coef[first:last].reshape(-1)
-    return disco_apply(local_src, local_coef, rows, weight_flat, last - first, lon_count)
+    return src.reshape(-1).astype(jnp.int32), coef.reshape(-1).astype(jnp.float32)
 
 
 def halo_extend(masked, live_rows):

time: 84.3 us -> 83.6 us (level)
  local copies, waits for them, and re-layouts: 16.4 us -> 11.6 us
  waiting for transfers between devices: 5.36 us -> 8.95 us
  other arithmetic: 9.13 us -> 10.2 us
  starting transfers between devices: 27.8 us -> 26.9 us
    reshape x6 -> x1, local copies, waits for them, and re-layouts: 3.94 us -> 0.59 us  [disco_tables(): src.reshape(-1).astype(jnp.int32)]
    slice x9 -> x0, local copies, waits for them, and re-layouts: 2.18 us -> none  [the longest x3 2.14 us: disco_piece(): rows = lax.slice_in_dim(ext, first, last + 2, axis=0)]
    all_to_all x1, waiting for transfers between devices: 0.81 us -> 2.77 us  [spectral_by_modes(): lax.all_to_all(returned, both, split_axis=0, concat_axis=2, tiled=True)]
    all_to_all x1, waiting for transfers between devices: 2.88 us -> 4.63 us  [spectral_by_modes(): lax.all_to_all(spectral_rows, 'lon', split_axis=1, concat_axis=0, tiled=T...]
  transfers between devices with their start and end apart: 8 -> 8, of which waited for: 4 -> 5; matrix products, arithmetic and copies ran while one was open for 18% -> 13% of each run, Pallas kernels for 22% -> 22%
where the time goes in v8:
time: 83.6 us; the launch traced here: 82.7 us
  starting transfers between devices  26.9 us (32%)
  Pallas kernels  18.3 us (22%)
  local copies, waits for them, and re-layouts  11.6 us (14%)
  other arithmetic  10.2 us (12%)
  waiting for transfers between devices  8.95 us (11%)
  matrix products  4.31 us (5%)
  between operations  2.4 us (3%)
    pallas_call x3, Pallas kernels, disco_piece(): pl.pallas_call(functools.partial(disco_body, first, last), out_shape=jax....  18.3 us
    all_to_all x1, starting transfers between devices, spectral_by_modes(): lax.all_to_all(masked, 'lon', split_axis=0, concat_axis=1, tiled=True)  6.32 us
    all_to_all x1, starting transfers between devices, spectral_by_modes(): lax.all_to_all(returned, both, split_axis=0, concat_axis=2, tiled=True)  5.31 us
    all_to_all x1, starting transfers between devices, spectral_by_modes(): lax.all_to_all(spectra, both, split_axis=2, concat_axis=0, tiled=True)  5.01 us
    all_to_all x1, waiting for transfers between devices, spectral_by_modes(): lax.all_to_all(spectral_rows, 'lon', split_axis=1, concat_axis=0, tiled=T...  4.63 us
    dot_general x13, matrix products, dot_split(): term = jnp.einsum(spec, lp, rp, preferred_element_type=jnp.float32)  4.31 us
    all_to_all x1, starting transfers between devices, spectral_by_modes(): lax.all_to_all(spectral_rows, 'lon', split_axis=1, concat_axis=0, tiled=T...  3.64 us
    all_to_all x1, waiting for transfers between devices, spectral_by_modes(): lax.all_to_all(returned, both, split_axis=0, concat_axis=2, tiled=True)  2.77 us
  transfers between devices with their start and end apart: 8, of which 5 were waited for; matrix products, arithmetic and copies ran while one was open for 13% of the time, Pallas kernels for 22%

profile of v8, /device:TPU:0, one launch (start us, length us, event | category | flops | bytes accessed | tf_op | source)
XLA Modules:
  0.0 82.7 jit_solution(16781330758953025286)
XLA Ops:
  0.0 1.4 %fusion.37 = (s32[1]{0:T(128)}, s32[1]{0:T(128)}) fusion(s32[8]{0:T(128)} %param.12, s32[]{:T(128)S(6)} %max.10, s32[]{:T(128)S(6)} %select_n.93), kind=kLoop, calls=%fused_computation.85 | loop fusion | bytes 24 | tf_op jit(solution)/shard_map/dynamic_slice | solution.py:110
  1.4 0.6 iota_compare_fusion
  2.0 1.8 %copy_select_fusion = bf16[8,180,128]{2,1,0:T(8,128)(2,1)} fusion(bf16[8,180,128]{2,0,1:T(8,128)(2,1)} %param.11, pred[8]{0:T(512)(128)(4,1)S(1)} %iota_compare_fusion), kind=kLoop, calls=%fused_computation.43 | loop fusion | flops 184320 | bytes 737288 | tf_op jit(solution)/shard_map/jit(_where)/select_n | solution.py:256
  3.9 6.3 %all-to-all-start = ((bf16[8,180,128]{2,1,0:T(8,128)(2,1)}), bf16[8,180,128]{2,1,0:T(8,128)(2,1)S(1)}, u32[]{:S(2)}, u32[]{:S(2)}) async-start(bf16[8,180,128]{2,1,0:T(8,128)(2,1)} %copy_select_fusion), calls=%async_computation | async-start | bytes 753664 | tf_op jit(solution)/shard_map/all_to_all | solution.py:211
  11.5 0.8 %constant_dynamic-slice_fusion = (bf16[1,180,128]{2,1,0:T(8,128)(2,1)S(1)}, bf16[1,180,128]{2,1,0:T(8,128)(2,1)S(1)}) fusion(bf16[8,180,128]{2,1,0:T(8,128)(2,1)} %copy_select_fusion, s32[]{:T(128)S(6)} %select_n.95), kind=kLoop, calls=%fused_computation.78 | loop fusion | bytes 184324 | tf_op jit(solution)/shard_map/dynamic_slice | solution.py:133
  12.4 2.6 %collective-permute-start.1 = (bf16[1,180,128]{2,1,0:T(8,128)(2,1)S(1)}, bf16[1,180,128]{2,1,0:T(8,128)(2,1)S(1)}, u32[]{:S(2)}, u32[]{:S(2)}) collective-permute-start(bf16[1,180,128]{2,1,0:T(8,128)(2,1)S(1)} %get-tuple-element.40), channel_id=1, source_target_pairs={{4,0},{8,4},{12,8},{16,12},{20,16},{24,20},{28,24},{0,28},{5,1},{9... | collective-permute-start | bytes 138248 | tf_op jit(solution)/shard_map/ppermute | solution.py:135
  15.7 0.6 select_bitcast_fusion
  16.3 0.1 copy.121
  16.4 0.1 reshape.237
  16.5 0.3 copy.122
  16.8 0.6 gather_fusion
  17.6 0.6 compare_or_fusion
  18.2 0.1 pad.12.clone
  18.3 0.1 pad_add_fusion.1
  18.4 0.1 maximum_select_fusion
  18.5 0.3 fusion.16
  18.9 0.8 pad_maximum_fusion.6
  19.6 2.1 %collective-permute-start.2 = (bf16[10,1,128]{2,1,0:T(2,128)(2,1)S(1)}, bf16[10,1,128]{2,1,0:T(2,128)(2,1)S(1)}, u32[]{:S(2)}, u32[]{:S(2)}) collective-permute-start(bf16[10,1,128]{2,1,0:T(2,128)(2,1)S(1)} %get-tuple-element.37), channel_id=1, source_target_pairs={{0,1},{1,2},{2,3},{3,0},{4,5},{5,6},{6,7},{7,4},{8,9},{9,10},{10,1... | collective-permute-start | bytes 7688 | tf_op jit(solution)/shard_map/ppermute | solution.py:137
  21.7 1.9 %collective-permute-start.3 = (bf16[10,1,128]{2,1,0:T(2,128)(2,1)S(1)}, bf16[10,1,128]{2,1,0:T(2,128)(2,1)S(1)}, u32[]{:S(2)}, u32[]{:S(2)}) collective-permute-start(bf16[10,1,128]{2,1,0:T(2,128)(2,1)S(1)} %get-tuple-element.38), channel_id=1, source_target_pairs={{1,0},{2,1},{3,2},{0,3},{5,4},{6,5},{7,6},{4,7},{9,8},{10,9},{11,1... | collective-permute-start | bytes 7688 | tf_op jit(solution)/shard_map/ppermute | solution.py:138
  23.5 0.6 add_select_fusion
  24.2 0.1 pad.22.clone
  24.3 0.8 collective-permute-done.2
  25.1 0.2 collective-permute-done.3
  25.3 2.0 %maximum_maximum_fusion.ext_ref = bf16[10,208,128]{2,1,0:T(8,128)(2,1)} fusion(bf16[10,1,128]{2,1,0:T(2,128)(2,1)S(1)} %collective-permute-done.3, bf16[1,180,128]{2,1,0:T(8,128)(2,1)S(1)} %collective-permute-done.1, bf16[8,180,128]{2,1,0:T(8,128)(2,1)} %copy_select_fusion, bf16[1,180,128]{2,1,0:T(8,128)(2,1)S(1)} %collective-permute-done, ...), kind=kLoop, calls=%fused_computation.41 | loop fusion | flops 3194880 | bytes 998816 | tf_op jit(solution)/shard_map/concatenate | solution.py:141
  27.3 0.1 all_to_all.55
  27.4 0.3 fusion.39
  27.7 0.3 fusion.38
  28.0 0.3 fusion.9
  28.3 0.3 fusion.10
  28.6 0.9 %copy.117 = bf16[2,2,192,128]{3,0,1,2:T(2,128)(2,1)} copy(bf16[2,2,192,128]{3,2,0,1:T(8,128)(2,1)S(1)} %pad_maximum_fusion.3) | data formatting | bytes 393216 | tf_op jit(solution)/shard_map/optimization_barrier | solution.py:216
  29.5 5.0 %all-to-all-start.1 = ((bf16[2,2,192,128]{3,0,1,2:T(2,128)(2,1)}), bf16[2,2,192,128]{3,0,1,2:T(2,128)(2,1)S(1)}, u32[]{:S(2)}, u32[]{:S(2)}) async-start(bf16[2,2,192,128]{3,0,1,2:T(2,128)(2,1)} %copy.117), calls=%async_computation.1 | async-start | bytes 393216 | tf_op jit(solution)/shard_map/all_to_all | solution.py:217
  34.6 0.1 copy.120
  34.7 0.6 reshape.232.src_ref
  35.2 0.2 copy.126
  35.5 0.9 %copy.127.w_ref = bf16[128,1152]{1,0:T(8,128)(2,1)} copy(bf16[128,1152]{0,1:T(8,128)(2,1)S(1)} %bitcast.117) | data formatting | bytes 589824 | tf_op jit(solution)/shard_map/reshape | solution.py:260
  36.4 0.7 select_n.102.coef_ref
  37.1 1.1 %fusion.20 = bf16[6,360,64,1]{1,2,3,0:T(8,128)(2,1)S(1)} fusion(f32[24,360,64]{1,2,0:T(8,128)} %param.13, s32[]{:T(128)S(6)} %select_n.103), kind=kLoop, calls=%fused_computation.45 | loop fusion | flops 276480 | bytes 829444 | tf_op jit(solution)/shard_map/convert_element_type | solution.py:34
  38.3 5.1 %shard_map.109 = f32[2,192,128]{2,1,0:T(8,128)} custom-call(s32[24]{0:T(128)} %reshape.232.src_ref, f32[648]{0:T(1024)} %select_n.102.coef_ref, bf16[10,208,128]{2,1,0:T(8,128)(2,1)} %maximum_maximum_fusion.ext_ref, bf16[128,1152]{1,0:T(8,128)(2,1)} %copy.127.w_ref), custom_call_target="tpu_custom_call" | custom-call | tf_op jit(solution)/shard_map/pallas_call | solution.py:85
  43.3 0.5 all-to-all-done.1
  43.9 0.2 copy.119
  44.1 0.5 fusion.22
  44.6 1.1 %copy-done.1 = f32[24,360,64]{1,2,0:T(8,128)S(1)} copy-done((f32[24,360,64]{1,2,0:T(8,128)S(1)}, f32[24,360,64]{1,2,0:T(8,128)}, u32[]{:S(2)}) %copy-start.1) | copy-done | bytes 2211864
  45.7 0.5 add_bitcast_fusion
  46.2 0.2 multiply_add_fusion
  46.5 0.4 fusion.28
  46.9 0.4 convolution_add_fusion.3
  47.3 0.2 copy-done.11
  47.5 0.4 fusion.6
  47.9 0.9 %copy.130 = bf16[64,2,6,128]{3,1,2,0:T(2,128)(2,1)} copy(bf16[64,2,6,128]{3,0,1,2:T(8,128)(2,1)S(1)} %fusion.6) | data formatting | bytes 393216 | tf_op jit(solution)/shard_map/optimization_barrier | solution.py:228
  48.8 5.3 %all-to-all-start.2 = ((bf16[64,2,6,128]{3,1,2,0:T(2,128)(2,1)}), bf16[64,2,6,128]{3,1,2,0:T(2,128)(2,1)S(1)}, u32[]{:S(2)}, u32[]{:S(2)}) async-start(bf16[64,2,6,128]{3,1,2,0:T(2,128)(2,1)} %copy.130), calls=%async_computation.2 | async-start | bytes 393216 | tf_op jit(solution)/shard_map/all_to_all | solution.py:229
  54.1 6.6 %shard_map.110 = f32[3,192,128]{2,1,0:T(8,128)} custom-call(s32[24]{0:T(128)} %reshape.232.src_ref, f32[648]{0:T(1024)} %select_n.102.coef_ref, bf16[10,208,128]{2,1,0:T(8,128)(2,1)} %maximum_maximum_fusion.ext_ref, bf16[128,1152]{1,0:T(8,128)(2,1)} %copy.127.w_ref), custom_call_target="tpu_custom_call" | custom-call | tf_op jit(solution)/shard_map/pallas_call | solution.py:85
  60.6 2.8 %all-to-all-done.2 = bf16[64,2,6,128]{3,1,2,0:T(2,128)(2,1)S(1)} async-done(((bf16[64,2,6,128]{3,1,2,0:T(2,128)(2,1)}), bf16[64,2,6,128]{3,1,2,0:T(2,128)(2,1)S(1)}, u32[]{:S(2)}, u32[]{:S(2)}) %all-to-all-start.2) | async-done | bytes 196640 | tf_op jit(solution)/shard_map/all_to_all | solution.py:229
  63.4 0.1 copy.131
  63.6 0.2 fusion.25
  63.8 0.2 fusion.24
  64.1 0.2 convolution_add_fusion.1
  64.3 0.3 fusion.4
  64.6 1.0 %copy.139 = bf16[2,720,128]{2,0,1:T(2,128)(2,1)} copy(bf16[2,720,128]{2,1,0:T(8,128)(2,1)S(1)} %fusion.4) | data formatting | bytes 737280 | tf_op jit(solution)/shard_map/optimization_barrier | solution.py:237
  65.6 3.6 %all-to-all-start.3 = ((bf16[2,720,128]{2,0,1:T(2,128)(2,1)}), bf16[2,720,128]{2,0,1:T(2,128)(2,1)S(1)}, u32[]{:S(2)}, u32[]{:S(2)}) async-start(bf16[2,720,128]{2,0,1:T(2,128)(2,1)} %copy.139), calls=%async_computation.3 | async-start | bytes 737280 | tf_op jit(solution)/shard_map/all_to_all | solution.py:238
  69.3 6.7 %shard_map.111 = f32[3,192,128]{2,1,0:T(8,128)} custom-call(s32[24]{0:T(128)} %reshape.232.src_ref, f32[648]{0:T(1024)} %select_n.102.coef_ref, bf16[10,208,128]{2,1,0:T(8,128)(2,1)} %maximum_maximum_fusion.ext_ref, bf16[128,1152]{1,0:T(8,128)(2,1)} %copy.127.w_ref), custom_call_target="tpu_custom_call" | custom-call | tf_op jit(solution)/shard_map/pallas_call | solution.py:85
  76.0 4.6 %all-to-all-done.3 = bf16[2,720,128]{2,0,1:T(2,128)(2,1)S(1)} async-done(((bf16[2,720,128]{2,0,1:T(2,128)(2,1)}), bf16[2,720,128]{2,0,1:T(2,128)(2,1)S(1)}, u32[]{:S(2)}, u32[]{:S(2)}) %all-to-all-start.3) | async-done | bytes 368672 | tf_op jit(solution)/shard_map/all_to_all | solution.py:238
  80.6 0.1 copy.164
  80.7 1.2 %fusion.15 = bf16[8,180,128]{2,1,0:T(8,128)(2,1)S(1)} fusion(f32[3,192,128]{2,1,0:T(8,128)} %shard_map.111, f32[3,192,128]{2,1,0:T(8,128)S(1)} %copy-done.2, f32[2,192,128]{2,1,0:T(8,128)S(1)} %copy-done.3, bf16[8,180,128]{2,1,0:T(8,128)(2,1)S(1)} %bitcast.114, pred[8]{0:T(512)(128)(4,1)S(1)} %iota_compare_fusion, bf16[8,180,128]{2,0,1:T(8,128)(2,1)S(1)} %copy-done), kind=kLoop, calls=%fused_computation.34 | loop fusion | flops 1658880 | bytes 1892360 | tf_op jit(solution)/shard_map/convert_element_type | solution.py:274
  81.9 0.8 copy.143
  (40 shorter events, 0.4 us)
Async XLA Ops:
  0.0 16.5 %copy-start.6 = (f32[64,9,9]{0,2,1:T(8,128)S(1)}, f32[64,9,9]{0,2,1:T(8,128)}, u32[]{:S(2)}) copy-start(f32[64,9,9]{0,2,1:T(8,128)} %param.16) | copy-start | bytes 62212
  3.9 23.4 %all-to-all-start = ((bf16[8,180,128]{2,1,0:T(8,128)(2,1)}), bf16[8,180,128]{2,1,0:T(8,128)(2,1)S(1)}, u32[]{:S(2)}, u32[]{:S(2)}) async-start(bf16[8,180,128]{2,1,0:T(8,128)(2,1)} %copy_select_fusion), calls=%async_computation | async-start | bytes 753664 | tf_op jit(solution)/shard_map/all_to_all | solution.py:211
  10.2 8.3 %copy-start.7 = (f32[45,192]{1,0:T(8,128)S(1)}, f32[45,192]{1,0:T(8,128)}, u32[]{:S(2)}) copy-start(f32[45,192]{1,0:T(8,128)} %constant.55.clone) | copy-start | bytes 103684
  10.2 8.3 %copy-start.8 = (f32[45,192]{1,0:T(8,128)S(1)}, f32[45,192]{1,0:T(8,128)}, u32[]{:S(2)}) copy-start(f32[45,192]{1,0:T(8,128)} %constant.54.clone) | copy-start | bytes 103684
  10.2 8.3 %copy-start.9 = (f32[16,192]{1,0:T(8,128)S(1)}, f32[16,192]{1,0:T(8,128)}, u32[]{:S(2)}) copy-start(f32[16,192]{1,0:T(8,128)} %constant.57.clone) | copy-start | bytes 36868
  10.2 8.3 %copy-start.10 = (f32[16,192]{1,0:T(8,128)S(1)}, f32[16,192]{1,0:T(8,128)}, u32[]{:S(2)}) copy-start(f32[16,192]{1,0:T(8,128)} %constant.56.clone) | copy-start | bytes 36868
  12.3 6.5 %collective-permute-start = (bf16[1,180,128]{2,1,0:T(8,128)(2,1)S(1)}, bf16[1,180,128]{2,1,0:T(8,128)(2,1)S(1)}, u32[]{:S(2)}, u32[]{:S(2)}) collective-permute-start(bf16[1,180,128]{2,1,0:T(8,128)(2,1)S(1)} %get-tuple-element.39), channel_id=1, source_target_pairs={{0,4},{4,8},{8,12},{12,16},{16,20},{20,24},{24,28},{28,0},{1,5},{5... | collective-permute-start | bytes 138248 | tf_op jit(solution)/shard_map/ppermute | solution.py:134
  12.4 6.5 %collective-permute-start.1 = (bf16[1,180,128]{2,1,0:T(8,128)(2,1)S(1)}, bf16[1,180,128]{2,1,0:T(8,128)(2,1)S(1)}, u32[]{:S(2)}, u32[]{:S(2)}) collective-permute-start(bf16[1,180,128]{2,1,0:T(8,128)(2,1)S(1)} %get-tuple-element.40), channel_id=1, source_target_pairs={{4,0},{8,4},{12,8},{16,12},{20,16},{24,20},{28,24},{0,28},{5,1},{9... | collective-permute-start | bytes 138248 | tf_op jit(solution)/shard_map/ppermute | solution.py:135
  19.6 5.5 %collective-permute-start.2 = (bf16[10,1,128]{2,1,0:T(2,128)(2,1)S(1)}, bf16[10,1,128]{2,1,0:T(2,128)(2,1)S(1)}, u32[]{:S(2)}, u32[]{:S(2)}) collective-permute-start(bf16[10,1,128]{2,1,0:T(2,128)(2,1)S(1)} %get-tuple-element.37), channel_id=1, source_target_pairs={{0,1},{1,2},{2,3},{3,0},{4,5},{5,6},{6,7},{7,4},{8,9},{9,10},{10,1... | collective-permute-start | bytes 7688 | tf_op jit(solution)/shard_map/ppermute | solution.py:137
  21.7 3.6 %collective-permute-start.3 = (bf16[10,1,128]{2,1,0:T(2,128)(2,1)S(1)}, bf16[10,1,128]{2,1,0:T(2,128)(2,1)S(1)}, u32[]{:S(2)}, u32[]{:S(2)}) collective-permute-start(bf16[10,1,128]{2,1,0:T(2,128)(2,1)S(1)} %get-tuple-element.38), channel_id=1, source_target_pairs={{1,0},{2,1},{3,2},{0,3},{5,4},{6,5},{7,6},{4,7},{9,8},{10,9},{11,1... | collective-permute-start | bytes 7688 | tf_op jit(solution)/shard_map/ppermute | solution.py:138
  28.3 6.9 %copy-start.5 = (bf16[128,9,128]{2,0,1:T(8,128)(2,1)S(1)}, bf16[128,9,128]{2,0,1:T(8,128)(2,1)}, u32[]{:S(2)}) copy-start(bf16[128,9,128]{2,0,1:T(8,128)(2,1)} %param.17) | copy-start | bytes 884740
  29.5 14.3 %all-to-all-start.1 = ((bf16[2,2,192,128]{3,0,1,2:T(2,128)(2,1)}), bf16[2,2,192,128]{3,0,1,2:T(2,128)(2,1)S(1)}, u32[]{:S(2)}, u32[]{:S(2)}) async-start(bf16[2,2,192,128]{3,0,1,2:T(2,128)(2,1)} %copy.117), calls=%async_computation.1 | async-start | bytes 393216 | tf_op jit(solution)/shard_map/all_to_all | solution.py:217
  34.7 3.6 %copy-start.4 = (f32[2,360,128]{2,1,0:T(8,128)S(1)}, f32[2,360,128]{2,1,0:T(8,128)}, u32[]{:S(2)}) copy-start(f32[2,360,128]{2,1,0:T(8,128)} %param.15) | copy-start | bytes 1105924
  44.1 1.7 %copy-start.1 = (f32[24,360,64]{1,2,0:T(8,128)S(1)}, f32[24,360,64]{1,2,0:T(8,128)}, u32[]{:S(2)}) copy-start(f32[24,360,64]{1,2,0:T(8,128)} %param.13) | copy-start | bytes 6635524
  46.8 0.7 copy-start.11
  48.8 14.7 %all-to-all-start.2 = ((bf16[64,2,6,128]{3,1,2,0:T(2,128)(2,1)}), bf16[64,2,6,128]{3,1,2,0:T(2,128)(2,1)S(1)}, u32[]{:S(2)}, u32[]{:S(2)}) async-start(bf16[64,2,6,128]{3,1,2,0:T(2,128)(2,1)} %copy.130), calls=%async_computation.2 | async-start | bytes 393216 | tf_op jit(solution)/shard_map/all_to_all | solution.py:229
  65.6 15.0 %all-to-all-start.3 = ((bf16[2,720,128]{2,0,1:T(2,128)(2,1)}), bf16[2,720,128]{2,0,1:T(2,128)(2,1)S(1)}, u32[]{:S(2)}, u32[]{:S(2)}) async-start(bf16[2,720,128]{2,0,1:T(2,128)(2,1)} %copy.139), calls=%async_computation.3 | async-start | bytes 737280 | tf_op jit(solution)/shard_map/all_to_all | solution.py:238
  69.3 11.4 %copy-start = (bf16[8,180,128]{2,0,1:T(8,128)(2,1)S(1)}, bf16[8,180,128]{2,0,1:T(8,128)(2,1)}, u32[]{:S(2)}) copy-start(bf16[8,180,128]{2,0,1:T(8,128)(2,1)} %param.11) | copy-start | bytes 1105924
  69.3 11.4 %copy-start.2 = (f32[3,192,128]{2,1,0:T(8,128)S(1)}, f32[3,192,128]{2,1,0:T(8,128)}, u32[]{:S(2)}) copy-start(f32[3,192,128]{2,1,0:T(8,128)} %shard_map.110) | copy-start | bytes 884740
  69.3 11.4 %copy-start.3 = (f32[2,192,128]{2,1,0:T(8,128)S(1)}, f32[2,192,128]{2,1,0:T(8,128)}, u32[]{:S(2)}) copy-start(f32[2,192,128]{2,1,0:T(8,128)} %shard_map.109) | copy-start | bytes 589828

commit v9 on v8

--- a/solution.py
+++ b/solution.py
@@ -229,15 +229,20 @@
     portion = lax.all_to_all(returned, both, split_axis=0, concat_axis=2, tiled=True)
     disco_parts.append(disco_work(ext_now, 1))
     portion, disco_parts = lax.optimization_barrier((portion, disco_parts))
-    spectral_rows = None
+    portion, ext_now = lax.optimization_barrier((portion, ext))
+    gathered = lax.all_gather(portion, "lon", axis=0, tiled=True)
+    disco_parts.append(disco_work(ext_now, 2))
+    gathered, disco_parts = lax.optimization_barrier((gathered, disco_parts))
+    lon_count = masked.shape[1]
+    lon_index = lax.axis_index("lon")
+    spectral = None
     for p, parts in enumerate(trig_parts):
-        term = dot_split("rkc,nk->rnc", (portion[:, p],), parts)
-        spectral_rows = term if spectral_rows is None else spectral_rows + term
-    spectral_rows = spectral_rows.astype(jnp.bfloat16)
-    spectral_rows, ext_now = lax.optimization_barrier((spectral_rows, ext))
-    spectral = lax.all_to_all(spectral_rows, "lon", split_axis=1, concat_axis=0, tiled=True)
-    disco_parts.append(disco_work(ext_now, 2))
-    spectral, disco_parts = lax.optimization_barrier((spectral, disco_parts))
+        own = tuple(
+            lax.dynamic_slice_in_dim(part, lon_index * lon_count, lon_count, 0) for part in parts
+        )
+        term = dot_split("rkc,nk->rnc", (gathered[:, p],), own)
+        spectral = term if spectral is None else spectral + term
+    spectral = spectral.astype(jnp.bfloat16)
     return spectral, disco_parts
 
 

time: 83.6 us -> 92.5 us (1.11)
  blocking collectives: 0 us -> 17.7 us
  waiting for transfers between devices: 8.95 us -> 4.06 us
  starting transfers between devices: 26.9 us -> 23.4 us
    all_gather x0 -> x1, blocking collectives: none -> 17.7 us  [spectral_by_modes(): gathered = lax.all_gather(portion, 'lon', axis=0, tiled=True)]
    all_to_all x1 -> x0, waiting for transfers between devices: 4.63 us -> none  [spectral_by_modes(): lax.all_to_all(spectral_rows, 'lon', split_axis=1, concat_axis=0, tiled=T...]
    all_to_all x1 -> x0, starting transfers between devices: 3.64 us -> none  [spectral_by_modes(): lax.all_to_all(spectral_rows, 'lon', split_axis=1, concat_axis=0, tiled=T...]
    convert_element_type x2 -> x0, other arithmetic: 1.54 us -> none  [the longest x1 1.21 us: on_device(): return jnp.where(live_slot[:, None, None], summed, 0.0).astype(jnp.bfloat16)]
    unnamed x26 -> x32, local copies, waits for them, and re-layouts: 1.97 us -> 3.29 us
    neg x0 -> x1, other arithmetic: none -> 1.27 us  [make_trig(): minus_sine = -(coarse_sin * fine_cos + coarse_cos * fine_sin)]
    optimization_barrier x2 -> x1, local copies, waits for them, and re-layouts: 1.05 us -> 0.03 us  [spectral_by_modes(): portion, ext_now = lax.optimization_barrier((portion, ext))]
  transfers between devices with their start and end apart: 8 -> 7, of which waited for: 5 -> 4; matrix products, arithmetic and copies ran while one was open for 13% -> 13% of each run, Pallas kernels for 22% -> 13%
where the time goes in v9:
time: 92.5 us; the launch traced here: 91.7 us
  starting transfers between devices  23.4 us (25%)
  Pallas kernels  18.2 us (20%)
  blocking collectives  17.7 us (19%)
  local copies, waits for them, and re-layouts  11.8 us (13%)
  other arithmetic  9.77 us (11%)
  matrix products  4.44 us (5%)
  waiting for transfers between devices  4.06 us (4%)
  between operations  2.22 us (2%)
    pallas_call x3, Pallas kernels, disco_piece(): pl.pallas_call(functools.partial(disco_body, first, last), out_shape=jax....  18.2 us
    all_gather x1, blocking collectives, spectral_by_modes(): gathered = lax.all_gather(portion, 'lon', axis=0, tiled=True)  17.7 us
    all_to_all x1, starting transfers between devices, spectral_by_modes(): lax.all_to_all(masked, 'lon', split_axis=0, concat_axis=1, tiled=True)  6.32 us
    all_to_all x1, starting transfers between devices, spectral_by_modes(): lax.all_to_all(returned, both, split_axis=0, concat_axis=2, tiled=True)  5.51 us
    all_to_all x1, starting transfers between devices, spectral_by_modes(): lax.all_to_all(spectra, both, split_axis=2, concat_axis=0, tiled=True)  5.01 us
    dot_general x13, matrix products, dot_split(): term = jnp.einsum(spec, lp, rp, preferred_element_type=jnp.float32)  4.44 us
    unnamed x32, local copies, waits for them, and re-layouts  3.29 us
    ppermute x1, starting transfers between devices, halo_extend(): from_below = lax.ppermute(masked[0:1], 'lat', lat_down)  2.63 us
  transfers between devices with their start and end apart: 7, of which 4 were waited for; matrix products, arithmetic and copies ran while one was open for 13% of the time, Pallas kernels for 13%

profile of v9, /device:TPU:0, one launch (start us, length us, event | category | flops | bytes accessed | tf_op | source)
XLA Modules:
  0.0 91.7 jit_solution(9800610958433009273)
XLA Ops:
  0.0 1.3 %fusion.60 = (s32[1]{0:T(128)}, s32[1]{0:T(128)}) fusion(s32[8]{0:T(128)} %param.12, s32[]{:T(128)S(6)} %max.10, s32[]{:T(128)S(6)} %select_n.99), kind=kLoop, calls=%fused_computation.108 | loop fusion | bytes 24 | tf_op jit(solution)/shard_map/dynamic_slice | solution.py:110
  1.3 0.6 iota_compare_fusion
  1.9 1.8 %copy_select_fusion = bf16[8,180,128]{2,1,0:T(8,128)(2,1)} fusion(bf16[8,180,128]{2,0,1:T(8,128)(2,1)} %param.11, pred[8]{0:T(512)(128)(4,1)S(1)} %iota_compare_fusion), kind=kLoop, calls=%fused_computation.50 | loop fusion | flops 184320 | bytes 737288 | tf_op jit(solution)/shard_map/jit(_where)/select_n | solution.py:261
  3.7 6.3 %all-to-all-start = ((bf16[8,180,128]{2,1,0:T(8,128)(2,1)}), bf16[8,180,128]{2,1,0:T(8,128)(2,1)S(1)}, u32[]{:S(2)}, u32[]{:S(2)}) async-start(bf16[8,180,128]{2,1,0:T(8,128)(2,1)} %copy_select_fusion), calls=%async_computation | async-start | bytes 753664 | tf_op jit(solution)/shard_map/all_to_all | solution.py:211
  11.2 0.8 constant_dynamic-slice_fusion
  12.1 2.6 %collective-permute-start.1 = (bf16[1,180,128]{2,1,0:T(8,128)(2,1)S(1)}, bf16[1,180,128]{2,1,0:T(8,128)(2,1)S(1)}, u32[]{:S(2)}, u32[]{:S(2)}) collective-permute-start(bf16[1,180,128]{2,1,0:T(8,128)(2,1)S(1)} %get-tuple-element.40), channel_id=1, source_target_pairs={{4,0},{8,4},{12,8},{16,12},{20,16},{24,20},{28,24},{0,28},{5,1},{9... | collective-permute-start | bytes 138248 | tf_op jit(solution)/shard_map/ppermute | solution.py:135
  15.4 0.6 select_bitcast_fusion
  16.0 0.1 copy.104
  16.1 0.1 reshape.228
  16.2 0.3 copy.105
  16.5 0.6 gather_fusion
  17.2 0.6 compare_or_fusion
  17.8 0.1 pad.12.clone
  17.8 0.1 pad_add_fusion.1
  17.9 1.3 %add_negate_fusion = (f32[45,16,192]{2,1,0:T(8,128)S(1)}, bf16[45,16,192]{2,1,0:T(8,128)(2,1)}, bf16[45,16,192]{2,1,0:T(8,128)(2,1)S(1)}, bf16[45,16,192]{2,1,0:...) fusion(f32[16,192]{1,0:T(8,128)S(1)} %copy-done.13, f32[45,192]{1,0:T(8,128)S(1)} %copy-done.11, ...), kind=kLoop, calls=%fused_computation.39 | loop fusion | flops 2073600 | bytes 2305536 | tf_op jit(solution)/shard_map/neg | solution.py:26
  19.2 0.1 maximum_select_fusion
  19.3 0.8 pad_maximum_fusion.6
  20.1 2.1 %collective-permute-start.2 = (bf16[10,1,128]{2,1,0:T(2,128)(2,1)S(1)}, bf16[10,1,128]{2,1,0:T(2,128)(2,1)S(1)}, u32[]{:S(2)}, u32[]{:S(2)}) collective-permute-start(bf16[10,1,128]{2,1,0:T(2,128)(2,1)S(1)} %get-tuple-element.37), channel_id=1, source_target_pairs={{0,1},{1,2},{2,3},{3,0},{4,5},{5,6},{6,7},{7,4},{8,9},{9,10},{10,1... | collective-permute-start | bytes 7688 | tf_op jit(solution)/shard_map/ppermute | solution.py:137
  22.1 1.9 %collective-permute-start.3 = (bf16[10,1,128]{2,1,0:T(2,128)(2,1)S(1)}, bf16[10,1,128]{2,1,0:T(2,128)(2,1)S(1)}, u32[]{:S(2)}, u32[]{:S(2)}) collective-permute-start(bf16[10,1,128]{2,1,0:T(2,128)(2,1)S(1)} %get-tuple-element.38), channel_id=1, source_target_pairs={{1,0},{2,1},{3,2},{0,3},{5,4},{6,5},{7,6},{4,7},{9,8},{10,9},{11,1... | collective-permute-start | bytes 7688 | tf_op jit(solution)/shard_map/ppermute | solution.py:138
  24.0 0.6 add_select_fusion
  24.6 0.1 pad.22.clone
  24.7 0.9 collective-permute-done.2
  25.6 0.2 collective-permute-done.3
  25.8 2.0 %maximum_maximum_fusion.ext_ref = bf16[10,208,128]{2,1,0:T(8,128)(2,1)} fusion(bf16[10,1,128]{2,1,0:T(2,128)(2,1)S(1)} %collective-permute-done.3, bf16[1,180,128]{2,1,0:T(8,128)(2,1)S(1)} %collective-permute-done.1, bf16[8,180,128]{2,1,0:T(8,128)(2,1)} %copy_select_fusion, bf16[1,180,128]{2,1,0:T(8,128)(2,1)S(1)} %collective-permute-done, ...), kind=kLoop, calls=%fused_computation.42 | loop fusion | flops 3194880 | bytes 998816 | tf_op jit(solution)/shard_map/concatenate | solution.py:141
  27.9 0.3 fusion.61
  28.2 0.3 fusion.62
  28.5 0.4 copy-done.2
  28.9 0.3 fusion.14
  29.2 0.3 fusion.13
  29.5 0.9 copy.100
  30.4 5.0 %all-to-all-start.1 = ((bf16[2,2,192,128]{3,0,1,2:T(2,128)(2,1)}), bf16[2,2,192,128]{3,0,1,2:T(2,128)(2,1)S(1)}, u32[]{:S(2)}, u32[]{:S(2)}) async-start(bf16[2,2,192,128]{3,0,1,2:T(2,128)(2,1)} %copy.100), calls=%async_computation.1 | async-start | bytes 393216 | tf_op jit(solution)/shard_map/all_to_all | solution.py:217
  35.5 0.7 select_n.108.coef_ref
  36.2 0.1 copy.103
  36.3 0.6 reshape.223.src_ref
  36.9 0.2 copy.109
  37.1 0.9 copy.110.w_ref
  38.0 1.1 %fusion.31 = bf16[6,360,64,1]{1,2,3,0:T(8,128)(2,1)S(1)} fusion(f32[24,360,64]{1,2,0:T(8,128)} %param.13, s32[]{:T(128)S(6)} %select_n.109), kind=kLoop, calls=%fused_computation.56 | loop fusion | flops 276480 | bytes 829444 | tf_op jit(solution)/shard_map/convert_element_type | solution.py:34
  39.2 5.1 %shard_map.109 = f32[2,192,128]{2,1,0:T(8,128)} custom-call(s32[24]{0:T(128)} %reshape.223.src_ref, f32[648]{0:T(1024)} %select_n.108.coef_ref, bf16[10,208,128]{2,1,0:T(8,128)(2,1)} %maximum_maximum_fusion.ext_ref, bf16[128,1152]{1,0:T(8,128)(2,1)} %copy.110.w_ref), custom_call_target="tpu_custom_call" | custom-call | tf_op jit(solution)/shard_map/pallas_call | solution.py:85
  44.3 0.5 all-to-all-done.1
  44.8 0.2 copy.102
  45.0 0.5 fusion.35
  45.5 1.2 %copy-done.3 = f32[24,360,64]{1,2,0:T(8,128)S(1)} copy-done((f32[24,360,64]{1,2,0:T(8,128)S(1)}, f32[24,360,64]{1,2,0:T(8,128)}, u32[]{:S(2)}) %copy-start.3) | copy-done | bytes 2211864
  46.6 0.5 add_bitcast_fusion
  47.1 0.2 multiply_add_fusion
  47.4 0.4 fusion.47
  47.8 0.4 convolution_add_fusion.3
  48.2 0.2 copy-done.14
  48.4 0.4 fusion.10
  48.8 0.9 copy.113
  49.7 5.5 %all-to-all-start.2 = ((bf16[64,2,6,128]{3,1,2,0:T(2,128)(2,1)}), bf16[64,2,6,128]{3,1,2,0:T(2,128)(2,1)S(1)}, u32[]{:S(2)}, u32[]{:S(2)}) async-start(bf16[64,2,6,128]{3,1,2,0:T(2,128)(2,1)} %copy.113), calls=%async_computation.2 | async-start | bytes 393216 | tf_op jit(solution)/shard_map/all_to_all | solution.py:229
  55.2 0.1 bitcast_reduce-precision_fusion
  55.3 6.6 %shard_map.110 = f32[3,192,128]{2,1,0:T(8,128)} custom-call(s32[24]{0:T(128)} %reshape.223.src_ref, f32[648]{0:T(1024)} %select_n.108.coef_ref, bf16[10,208,128]{2,1,0:T(8,128)(2,1)} %maximum_maximum_fusion.ext_ref, bf16[128,1152]{1,0:T(8,128)(2,1)} %copy.110.w_ref), custom_call_target="tpu_custom_call" | custom-call | tf_op jit(solution)/shard_map/pallas_call | solution.py:85
  61.9 2.5 %all-to-all-done.2 = bf16[64,2,6,128]{3,1,2,0:T(2,128)(2,1)S(1)} async-done(((bf16[64,2,6,128]{3,1,2,0:T(2,128)(2,1)}), bf16[64,2,6,128]{3,1,2,0:T(2,128)(2,1)S(1)}, u32[]{:S(2)}, u32[]{:S(2)}) %all-to-all-start.2) | async-done | bytes 196640 | tf_op jit(solution)/shard_map/all_to_all | solution.py:229
  64.3 0.1 copy.114
  64.5 6.6 %shard_map.111 = f32[3,192,128]{2,1,0:T(8,128)} custom-call(s32[24]{0:T(128)} %reshape.223.src_ref, f32[648]{0:T(1024)} %select_n.108.coef_ref, bf16[10,208,128]{2,1,0:T(8,128)(2,1)} %maximum_maximum_fusion.ext_ref, bf16[128,1152]{1,0:T(8,128)(2,1)} %copy.110.w_ref), custom_call_target="tpu_custom_call" | custom-call | tf_op jit(solution)/shard_map/pallas_call | solution.py:85
  71.1 17.7 %all_gather.3 = bf16[8,2,192,128]{3,2,0,1:T(8,128)(2,1)S(1)} all-gather(bf16[2,2,192,128]{3,2,0,1:T(8,128)(2,1)S(1)} %copy.116), channel_id=1, replica_groups=mesh['lat'=8,'lon'=4] {'lon'}, dimensions={0}, use_global_device_ids=true | all-gather | bytes 983040 | tf_op jit(solution)/shard_map/all_gather | solution.py:233
  88.8 0.2 fusion.21
  89.1 0.2 fusion.24
  89.4 0.3 convolution_add_fusion.1
  89.6 0.7 copy-done
  90.3 0.1 copy-done.4
  90.4 0.1 copy-done.5
  90.6 0.4 fusion.7
  90.9 0.8 copy.118
  (43 shorter events, 0.6 us)
Async XLA Ops:
  0.0 16.1 %copy-start.9 = (f32[64,9,9]{0,2,1:T(8,128)S(1)}, f32[64,9,9]{0,2,1:T(8,128)}, u32[]{:S(2)}) copy-start(f32[64,9,9]{0,2,1:T(8,128)} %param.16) | copy-start | bytes 62212
  3.7 24.0 %all-to-all-start = ((bf16[8,180,128]{2,1,0:T(8,128)(2,1)}), bf16[8,180,128]{2,1,0:T(8,128)(2,1)S(1)}, u32[]{:S(2)}, u32[]{:S(2)}) async-start(bf16[8,180,128]{2,1,0:T(8,128)(2,1)} %copy_select_fusion), calls=%async_computation | async-start | bytes 753664 | tf_op jit(solution)/shard_map/all_to_all | solution.py:211
  10.0 7.9 %copy-start.10 = (f32[45,192]{1,0:T(8,128)S(1)}, f32[45,192]{1,0:T(8,128)}, u32[]{:S(2)}) copy-start(f32[45,192]{1,0:T(8,128)} %constant.58.clone) | copy-start | bytes 103684
  10.0 7.9 %copy-start.11 = (f32[45,192]{1,0:T(8,128)S(1)}, f32[45,192]{1,0:T(8,128)}, u32[]{:S(2)}) copy-start(f32[45,192]{1,0:T(8,128)} %constant.59.clone) | copy-start | bytes 103684
  10.0 7.9 %copy-start.12 = (f32[16,192]{1,0:T(8,128)S(1)}, f32[16,192]{1,0:T(8,128)}, u32[]{:S(2)}) copy-start(f32[16,192]{1,0:T(8,128)} %constant.60.clone) | copy-start | bytes 36868
  10.1 7.9 %copy-start.13 = (f32[16,192]{1,0:T(8,128)S(1)}, f32[16,192]{1,0:T(8,128)}, u32[]{:S(2)}) copy-start(f32[16,192]{1,0:T(8,128)} %constant.61.clone) | copy-start | bytes 36868
  12.0 7.3 %collective-permute-start = (bf16[1,180,128]{2,1,0:T(8,128)(2,1)S(1)}, bf16[1,180,128]{2,1,0:T(8,128)(2,1)S(1)}, u32[]{:S(2)}, u32[]{:S(2)}) collective-permute-start(bf16[1,180,128]{2,1,0:T(8,128)(2,1)S(1)} %get-tuple-element.39), channel_id=1, source_target_pairs={{0,4},{4,8},{8,12},{12,16},{16,20},{20,24},{24,28},{28,0},{1,5},{5... | collective-permute-start | bytes 138248 | tf_op jit(solution)/shard_map/ppermute | solution.py:134
  12.1 7.2 %collective-permute-start.1 = (bf16[1,180,128]{2,1,0:T(8,128)(2,1)S(1)}, bf16[1,180,128]{2,1,0:T(8,128)(2,1)S(1)}, u32[]{:S(2)}, u32[]{:S(2)}) collective-permute-start(bf16[1,180,128]{2,1,0:T(8,128)(2,1)S(1)} %get-tuple-element.40), channel_id=1, source_target_pairs={{4,0},{8,4},{12,8},{16,12},{20,16},{24,20},{28,24},{0,28},{5,1},{9... | collective-permute-start | bytes 138248 | tf_op jit(solution)/shard_map/ppermute | solution.py:135
  20.1 5.5 %collective-permute-start.2 = (bf16[10,1,128]{2,1,0:T(2,128)(2,1)S(1)}, bf16[10,1,128]{2,1,0:T(2,128)(2,1)S(1)}, u32[]{:S(2)}, u32[]{:S(2)}) collective-permute-start(bf16[10,1,128]{2,1,0:T(2,128)(2,1)S(1)} %get-tuple-element.37), channel_id=1, source_target_pairs={{0,1},{1,2},{2,3},{3,0},{4,5},{5,6},{6,7},{7,4},{8,9},{9,10},{10,1... | collective-permute-start | bytes 7688 | tf_op jit(solution)/shard_map/ppermute | solution.py:137
  22.1 3.6 %collective-permute-start.3 = (bf16[10,1,128]{2,1,0:T(2,128)(2,1)S(1)}, bf16[10,1,128]{2,1,0:T(2,128)(2,1)S(1)}, u32[]{:S(2)}, u32[]{:S(2)}) collective-permute-start(bf16[10,1,128]{2,1,0:T(2,128)(2,1)S(1)} %get-tuple-element.38), channel_id=1, source_target_pairs={{1,0},{2,1},{3,2},{0,3},{5,4},{6,5},{7,6},{4,7},{9,8},{10,9},{11,1... | collective-permute-start | bytes 7688 | tf_op jit(solution)/shard_map/ppermute | solution.py:138
  27.9 1.0 %copy-start.2 = (bf16[45,16,192]{2,1,0:T(8,128)(2,1)S(1)}, bf16[45,16,192]{2,1,0:T(8,128)(2,1)}, u32[]{:S(2)}) copy-start(bf16[45,16,192]{2,1,0:T(8,128)(2,1)} %get-tuple-element.47) | copy-start | bytes 829444
  28.2 1.0 %copy-start.1 = (bf16[45,16,192]{2,1,0:T(8,128)(2,1)S(1)}, bf16[45,16,192]{2,1,0:T(8,128)(2,1)}, u32[]{:S(2)}) copy-start(bf16[45,16,192]{2,1,0:T(8,128)(2,1)} %get-tuple-element.49) | copy-start | bytes 829444
  29.2 7.7 %copy-start.8 = (bf16[128,9,128]{2,0,1:T(8,128)(2,1)S(1)}, bf16[128,9,128]{2,0,1:T(8,128)(2,1)}, u32[]{:S(2)}) copy-start(bf16[128,9,128]{2,0,1:T(8,128)(2,1)} %param.17) | copy-start | bytes 884740
  30.4 14.4 %all-to-all-start.1 = ((bf16[2,2,192,128]{3,0,1,2:T(2,128)(2,1)}), bf16[2,2,192,128]{3,0,1,2:T(2,128)(2,1)S(1)}, u32[]{:S(2)}, u32[]{:S(2)}) async-start(bf16[2,2,192,128]{3,0,1,2:T(2,128)(2,1)} %copy.100), calls=%async_computation.1 | async-start | bytes 393216 | tf_op jit(solution)/shard_map/all_to_all | solution.py:217
  35.5 3.7 %copy-start.7 = (f32[2,360,128]{2,1,0:T(8,128)S(1)}, f32[2,360,128]{2,1,0:T(8,128)}, u32[]{:S(2)}) copy-start(f32[2,360,128]{2,1,0:T(8,128)} %param.15) | copy-start | bytes 1105924
  44.9 1.7 %copy-start.3 = (f32[24,360,64]{1,2,0:T(8,128)S(1)}, f32[24,360,64]{1,2,0:T(8,128)}, u32[]{:S(2)}) copy-start(f32[24,360,64]{1,2,0:T(8,128)} %param.13) | copy-start | bytes 6635524
  47.8 0.7 copy-start.14
  49.7 14.7 %all-to-all-start.2 = ((bf16[64,2,6,128]{3,1,2,0:T(2,128)(2,1)}), bf16[64,2,6,128]{3,1,2,0:T(2,128)(2,1)S(1)}, u32[]{:S(2)}, u32[]{:S(2)}) async-start(bf16[64,2,6,128]{3,1,2,0:T(2,128)(2,1)} %copy.113), calls=%async_computation.2 | async-start | bytes 393216 | tf_op jit(solution)/shard_map/all_to_all | solution.py:229
  89.3 1.0 %copy-start = (bf16[8,180,128]{2,0,1:T(8,128)(2,1)S(1)}, bf16[8,180,128]{2,0,1:T(8,128)(2,1)}, u32[]{:S(2)}) copy-start(bf16[8,180,128]{2,0,1:T(8,128)(2,1)} %param.11) | copy-start | bytes 1105924
  89.3 1.1 %copy-start.4 = (f32[3,192,128]{2,1,0:T(8,128)S(1)}, f32[3,192,128]{2,1,0:T(8,128)}, u32[]{:S(2)}) copy-start(f32[3,192,128]{2,1,0:T(8,128)} %shard_map.110) | copy-start | bytes 884740
  89.4 1.1 %copy-start.5 = (f32[3,192,128]{2,1,0:T(8,128)S(1)}, f32[3,192,128]{2,1,0:T(8,128)}, u32[]{:S(2)}) copy-start(f32[3,192,128]{2,1,0:T(8,128)} %shard_map.111) | copy-start | bytes 884740
  89.4 1.2 %copy-start.6 = (f32[2,192,128]{2,1,0:T(8,128)S(1)}, f32[2,192,128]{2,1,0:T(8,128)}, u32[]{:S(2)}) copy-start(f32[2,192,128]{2,1,0:T(8,128)} %shard_map.109) | copy-start | bytes 589828

commit v10 on v8

--- a/solution.py
+++ b/solution.py
@@ -122,6 +122,22 @@
     return src.reshape(-1).astype(jnp.int32), coef.reshape(-1).astype(jnp.float32)
 
 
+def lat_extend(block, live_rows):
+    lat_total = lax.axis_size("lat")
+    lat_up = [(i, (i + 1) % lat_total) for i in range(lat_total)]
+    lat_down = [(j, i) for i, j in lat_up]
+    last_row = lax.dynamic_slice_in_dim(block, live_rows - 1, 1, 0)
+    from_above = lax.ppermute(last_row, "lat", lat_up)
+    from_below = lax.ppermute(block[0:1], "lat", lat_down)
+    return jnp.concatenate([from_above, block, from_below], axis=0)
+
+
+def pad_lon(rows, lon_count):
+    lon_pad = round_up(round_up(lon_count, CHUNK) + 2, 16)
+    pad = jnp.zeros((rows.shape[0], lon_pad - rows.shape[1], rows.shape[2]), rows.dtype)
+    return jnp.concatenate([rows, pad], axis=1)
+
+
 def halo_extend(masked, live_rows):
     row_count, lon_count, channels = masked.shape
     lat_total = lax.axis_size("lat")
@@ -142,8 +158,9 @@
 
 
 def spectral_by_channels(
-    masked, legendre, quad_weights, spectral_filter, trig_parts, ext, disco_work
+    masked, legendre, quad_weights, spectral_filter, trig_parts, live_rows, disco_work
 ):
+    ext = halo_extend(masked, live_rows)
     channels = masked.shape[2]
     lon_index = lax.axis_index("lon")
     chan_share = channels // lax.axis_size("lon")
@@ -203,12 +220,29 @@
     )
 
 
-def spectral_by_modes(masked, legendre, quad_weights, spectral_filter, trig_parts, ext, disco_work):
+def spectral_by_modes(
+    masked, legendre, quad_weights, spectral_filter, trig_parts, live_rows, disco_work
+):
     both = ("lat", "lon")
     lon_total = lax.axis_size("lon")
     mode_share = legendre.shape[0] // lon_total
+    row_count, lon_count, channels = masked.shape
+    share = row_count // lon_total
+    body = masked.reshape(lon_total, share * lon_count, channels)
+    edges = jnp.concatenate([masked[:, 0], masked[:, lon_count - 1]], axis=0)
+    edges = jnp.broadcast_to(edges[None], (lon_total, 2 * row_count, channels))
+    received = lax.all_to_all(
+        jnp.concatenate([body, edges], axis=1), "lon", split_axis=0, concat_axis=0, tiled=True
+    )
+    portion = received[:, : share * lon_count].reshape(lon_total, share, lon_count, channels)
+    portion = portion.transpose(1, 0, 2, 3).reshape(share, lon_total * lon_count, channels)
+    edge_block = received[:, share * lon_count :]
+    lon_index = lax.axis_index("lon")
+    left = lax.dynamic_index_in_dim(edge_block, (lon_index - 1) % lon_total, 0, keepdims=False)
+    right = lax.dynamic_index_in_dim(edge_block, (lon_index + 1) % lon_total, 0, keepdims=False)
+    own = jnp.concatenate([left[row_count:, None], masked, right[:row_count, None]], axis=1)
+    ext = pad_lon(lat_extend(own, live_rows), lon_count)
     disco_parts = []
-    portion = lax.all_to_all(masked, "lon", split_axis=0, concat_axis=1, tiled=True)
     spectra = jnp.stack(
         [dot_split("rnc,nk->rkc", (portion,), parts).astype(jnp.bfloat16) for parts in trig_parts],
         axis=1,
@@ -255,7 +289,6 @@
     live_slot = slot_ids < live_rows
     masked = jnp.where(live_slot[:, None, None], grad_output, jnp.zeros_like(grad_output))
     trig_parts = make_trig(mode_count, point_count)
-    ext = halo_extend(masked, live_rows)
     src_rows, coef = disco_tables(band_rows, disco_kernel, band_index, band_total, row_count)
     weight_flat = disco_weight.reshape(channels, -1)
     pieces = min(3, row_count)
@@ -266,7 +299,7 @@
     by_modes = legendre.shape[0] % lon_total == 0 and row_count % lon_total == 0
     path = spectral_by_modes if by_modes else spectral_by_channels
     spectral, disco_parts = path(
-        masked, legendre, quad_weights, spectral_filter, trig_parts, ext, disco_work
+        masked, legendre, quad_weights, spectral_filter, trig_parts, live_rows, disco_work
     )
     disco_full = jnp.concatenate(disco_parts, axis=0)
     disco_term = disco_full[:, :lon_count, :]

time: 83.6 us -> 81.3 us (0.972)
  waiting for transfers between devices: 8.95 us -> 14.1 us
  starting transfers between devices: 26.9 us -> 21.9 us
  other arithmetic: 10.2 us -> 8.51 us
    all_to_all x1, waiting for transfers between devices: 0.01 us -> 5.73 us  [spectral_by_modes(): lax.all_to_all(jnp.concatenate([body, edges], axis=1), 'lon', split_axis=...]
    ppermute x4 -> x2, starting transfers between devices: 6.6 us -> 2.69 us  [the longest x1 2.63 us: lat_extend(): from_below = lax.ppermute(block[0:1], 'lat', lat_down)]
    all_to_all x1, starting transfers between devices: 5.01 us -> 3.96 us  [spectral_by_modes(): lax.all_to_all(spectra, both, split_axis=2, concat_axis=0, tiled=True)]
    concatenate x1 -> x4, other arithmetic: 1.99 us -> 1.81 us  [the longest x1 0.93 us: lat_extend(): return jnp.concatenate([from_above, block, from_below], axis=0)]
    unnamed x26 -> x27, local copies, waits for them, and re-layouts: 1.97 us -> 1.99 us
  transfers between devices with their start and end apart: 8 -> 6, of which waited for: 5 -> 5; matrix products, arithmetic and copies ran while one was open for 13% -> 11% of each run, Pallas kernels for 22% -> 23%
where the time goes in v10:
time: 81.3 us; the launch traced here: 80.6 us
  starting transfers between devices  21.9 us (27%)
  Pallas kernels  18.3 us (23%)
  waiting for transfers between devices  14.1 us (17%)
  local copies, waits for them, and re-layouts  10.9 us (13%)
  other arithmetic  8.51 us (10%)
  matrix products  4.31 us (5%)
  between operations  2.49 us (3%)
    pallas_call x3, Pallas kernels, disco_piece(): pl.pallas_call(functools.partial(disco_body, first, last), out_shape=jax....  18.3 us
    all_to_all x1, starting transfers between devices, spectral_by_modes(): lax.all_to_all(jnp.concatenate([body, edges], axis=1), 'lon', split_axis=...  6.32 us
    all_to_all x1, waiting for transfers between devices, spectral_by_modes(): lax.all_to_all(jnp.concatenate([body, edges], axis=1), 'lon', split_axis=...  5.73 us
    all_to_all x1, starting transfers between devices, spectral_by_modes(): lax.all_to_all(returned, both, split_axis=0, concat_axis=2, tiled=True)  5.3 us
    all_to_all x1, waiting for transfers between devices, spectral_by_modes(): lax.all_to_all(spectral_rows, 'lon', split_axis=1, concat_axis=0, tiled=T...  4.63 us
    dot_general x13, matrix products, dot_split(): term = jnp.einsum(spec, lp, rp, preferred_element_type=jnp.float32)  4.31 us
    all_to_all x1, starting transfers between devices, spectral_by_modes(): lax.all_to_all(spectra, both, split_axis=2, concat_axis=0, tiled=True)  3.96 us
    all_to_all x1, starting transfers between devices, spectral_by_modes(): lax.all_to_all(spectral_rows, 'lon', split_axis=1, concat_axis=0, tiled=T...  3.64 us
  transfers between devices with their start and end apart: 6, of which 5 were waited for; matrix products, arithmetic and copies ran while one was open for 11% of the time, Pallas kernels for 23%

profile of v10, /device:TPU:0, one launch (start us, length us, event | category | flops | bytes accessed | tf_op | source)
XLA Modules:
  0.0 80.6 jit_solution(10363827229250287446)
XLA Ops:
  0.0 1.4 %fusion.47 = (s32[1]{0:T(128)}, s32[1]{0:T(128)}) fusion(s32[8]{0:T(128)} %param.12, s32[]{:T(128)S(6)} %max.10, s32[]{:T(128)S(6)} %select_n.111), kind=kLoop, calls=%fused_computation.98 | loop fusion | bytes 24 | tf_op jit(solution)/shard_map/dynamic_slice | solution.py:110
  1.4 0.6 iota_compare_fusion.1
  2.0 1.1 %copy_select_fusion = bf16[8,180,128]{2,1,0:T(8,128)(2,1)S(1)} fusion(bf16[8,180,128]{2,0,1:T(8,128)(2,1)} %param.11, pred[8]{0:T(512)(128)(4,1)S(1)} %iota_compare_fusion.1), kind=kLoop, calls=%fused_computation.53 | loop fusion | flops 184320 | bytes 737288 | tf_op jit(solution)/shard_map/jit(_where)/select_n | solution.py:290
  3.1 0.1 reshape.246
  3.2 0.8 pad_maximum_fusion.3
  4.0 6.3 %all-to-all-start = ((bf16[4,376,128]{2,1,0:T(8,128)(2,1)}), bf16[4,376,128]{2,1,0:T(8,128)(2,1)S(1)}, u32[]{:S(2)}, u32[]{:S(2)}) async-start(bf16[4,376,128]{2,1,0:T(8,128)(2,1)} %pad_maximum_fusion.3), calls=%async_computation | async-start | bytes 770048 | tf_op jit(solution)/shard_map/all_to_all | solution.py:234
  11.7 0.6 compare_select_fusion.2
  13.0 0.6 fusion.40
  13.6 0.1 copy.130
  13.7 0.1 reshape.254
  13.8 0.3 copy.131
  14.1 0.6 gather_fusion
  14.9 0.6 compare_or_fusion
  15.5 0.1 pad.13.clone
  15.6 0.1 pad_add_fusion.1
  15.6 0.1 maximum_select_fusion
  15.7 0.4 fusion.21
  16.1 5.7 %all-to-all-done = bf16[4,376,128]{2,1,0:T(8,128)(2,1)S(1)} async-done(((bf16[4,376,128]{2,1,0:T(8,128)(2,1)}), bf16[4,376,128]{2,1,0:T(8,128)(2,1)S(1)}, u32[]{:S(2)}, u32[]{:S(2)}) %all-to-all-start) | async-done | bytes 385056 | tf_op jit(solution)/shard_map/all_to_all | solution.py:234
  21.9 0.1 reshape.247
  22.0 0.1 reshape.248
  22.1 0.1 pad_maximum_fusion.4
  22.2 0.1 collective-permute-start
  22.3 2.6 %collective-permute-start.1 = (bf16[1,182,128]{2,1,0:T(8,128)(2,1)S(1)}, bf16[1,182,128]{2,1,0:T(8,128)(2,1)S(1)}, u32[]{:S(2)}, u32[]{:S(2)}) collective-permute-start(bf16[1,182,128]{2,1,0:T(8,128)(2,1)S(1)} %get-tuple-element.38), channel_id=1, source_target_pairs={{4,0},{8,4},{12,8},{16,12},{20,16},{24,20},{28,24},{0,28},{5,1},{9... | collective-permute-start | bytes 139784 | tf_op jit(solution)/shard_map/ppermute | solution.py:131
  24.9 0.3 fusion.49
  25.2 0.3 fusion.48
  25.5 0.3 fusion.9
  25.8 0.3 fusion.10
  26.2 0.5 collective-permute-done
  26.7 0.9 %fusion.25.ext_ref = bf16[10,208,128]{2,1,0:T(8,128)(2,1)} fusion(bf16[1,182,128]{2,1,0:T(8,128)(2,1)S(1)} %collective-permute-done.1, bf16[1,182,128]{2,1,0:T(8,128)(2,1)S(1)} %collective-permute-done, bf16[8,1,128]{2,1,0:T(2,128)(2,1)S(1)} %copy.125, bf16[8,180,128]{2,1,0:T(8,128)(2,1)S(1)} %copy_select_fusion, bf16[8,1,128]{2,1,0:T(2,128)(2,1)S(1)} %copy.124), kind=kLoop, calls=%fused_computation.48 | loop fusion | flops 4259840 | bytes 998400 | tf_op jit(solution)/shard_map/concatenate | solution.py:132
  27.6 0.9 %copy.126 = bf16[2,2,192,128]{3,0,1,2:T(2,128)(2,1)} copy(bf16[2,2,192,128]{3,2,0,1:T(8,128)(2,1)S(1)} %pad_maximum_fusion.5) | data formatting | bytes 393216 | tf_op jit(solution)/shard_map/optimization_barrier | solution.py:250
  28.5 4.0 %all-to-all-start.1 = ((bf16[2,2,192,128]{3,0,1,2:T(2,128)(2,1)}), bf16[2,2,192,128]{3,0,1,2:T(2,128)(2,1)S(1)}, u32[]{:S(2)}, u32[]{:S(2)}) async-start(bf16[2,2,192,128]{3,0,1,2:T(2,128)(2,1)} %copy.126), calls=%async_computation.1 | async-start | bytes 393216 | tf_op jit(solution)/shard_map/all_to_all | solution.py:251
  32.5 0.1 copy.129
  32.6 0.6 reshape.249.src_ref
  33.1 0.2 copy.135
  33.4 0.9 %copy.136.w_ref = bf16[128,1152]{1,0:T(8,128)(2,1)} copy(bf16[128,1152]{0,1:T(8,128)(2,1)S(1)} %bitcast.121) | data formatting | bytes 589824 | tf_op jit(solution)/shard_map/reshape | solution.py:293
  34.3 0.7 select_n.124.coef_ref
  35.0 1.1 %fusion.29 = bf16[6,360,64,1]{1,2,3,0:T(8,128)(2,1)S(1)} fusion(f32[24,360,64]{1,2,0:T(8,128)} %param.13, s32[]{:T(128)S(6)} %select_n.125), kind=kLoop, calls=%fused_computation.55 | loop fusion | flops 276480 | bytes 829444 | tf_op jit(solution)/shard_map/convert_element_type | solution.py:34
  36.2 5.1 %shard_map.109 = f32[2,192,128]{2,1,0:T(8,128)} custom-call(s32[24]{0:T(128)} %reshape.249.src_ref, f32[648]{0:T(1024)} %select_n.124.coef_ref, bf16[10,208,128]{2,1,0:T(8,128)(2,1)} %fusion.25.ext_ref, bf16[128,1152]{1,0:T(8,128)(2,1)} %copy.136.w_ref), custom_call_target="tpu_custom_call" | custom-call | tf_op jit(solution)/shard_map/pallas_call | solution.py:85
  41.3 0.5 all-to-all-done.1
  41.8 0.2 copy.128
  42.0 0.5 fusion.31
  42.5 1.2 %copy-done.1 = f32[24,360,64]{1,2,0:T(8,128)S(1)} copy-done((f32[24,360,64]{1,2,0:T(8,128)S(1)}, f32[24,360,64]{1,2,0:T(8,128)}, u32[]{:S(2)}) %copy-start.1) | copy-done | bytes 2211864
  43.6 0.5 add_bitcast_fusion
  44.1 0.2 multiply_add_fusion
  44.4 0.4 fusion.37
  44.8 0.4 convolution_add_fusion.3
  45.2 0.2 copy-done.11
  45.4 0.4 fusion.6
  45.8 0.9 %copy.139 = bf16[64,2,6,128]{3,1,2,0:T(2,128)(2,1)} copy(bf16[64,2,6,128]{3,0,1,2:T(8,128)(2,1)S(1)} %fusion.6) | data formatting | bytes 393216 | tf_op jit(solution)/shard_map/optimization_barrier | solution.py:262
  46.7 5.3 %all-to-all-start.2 = ((bf16[64,2,6,128]{3,1,2,0:T(2,128)(2,1)}), bf16[64,2,6,128]{3,1,2,0:T(2,128)(2,1)S(1)}, u32[]{:S(2)}, u32[]{:S(2)}) async-start(bf16[64,2,6,128]{3,1,2,0:T(2,128)(2,1)} %copy.139), calls=%async_computation.2 | async-start | bytes 393216 | tf_op jit(solution)/shard_map/all_to_all | solution.py:263
  52.0 6.6 %shard_map.110 = f32[3,192,128]{2,1,0:T(8,128)} custom-call(s32[24]{0:T(128)} %reshape.249.src_ref, f32[648]{0:T(1024)} %select_n.124.coef_ref, bf16[10,208,128]{2,1,0:T(8,128)(2,1)} %fusion.25.ext_ref, bf16[128,1152]{1,0:T(8,128)(2,1)} %copy.136.w_ref), custom_call_target="tpu_custom_call" | custom-call | tf_op jit(solution)/shard_map/pallas_call | solution.py:85
  58.5 2.8 %all-to-all-done.2 = bf16[64,2,6,128]{3,1,2,0:T(2,128)(2,1)S(1)} async-done(((bf16[64,2,6,128]{3,1,2,0:T(2,128)(2,1)}), bf16[64,2,6,128]{3,1,2,0:T(2,128)(2,1)S(1)}, u32[]{:S(2)}, u32[]{:S(2)}) %all-to-all-start.2) | async-done | bytes 196640 | tf_op jit(solution)/shard_map/all_to_all | solution.py:263
  61.3 0.1 copy.140
  61.5 0.2 fusion.34
  61.7 0.3 fusion.33
  62.0 0.2 convolution_add_fusion.1
  62.2 0.3 fusion.4
  62.5 1.0 %copy.148 = bf16[2,720,128]{2,0,1:T(2,128)(2,1)} copy(bf16[2,720,128]{2,1,0:T(8,128)(2,1)S(1)} %fusion.4) | data formatting | bytes 737280 | tf_op jit(solution)/shard_map/optimization_barrier | solution.py:271
  63.5 3.6 %all-to-all-start.3 = ((bf16[2,720,128]{2,0,1:T(2,128)(2,1)}), bf16[2,720,128]{2,0,1:T(2,128)(2,1)S(1)}, u32[]{:S(2)}, u32[]{:S(2)}) async-start(bf16[2,720,128]{2,0,1:T(2,128)(2,1)} %copy.148), calls=%async_computation.3 | async-start | bytes 737280 | tf_op jit(solution)/shard_map/all_to_all | solution.py:272
  67.2 6.7 %shard_map.111 = f32[3,192,128]{2,1,0:T(8,128)} custom-call(s32[24]{0:T(128)} %reshape.249.src_ref, f32[648]{0:T(1024)} %select_n.124.coef_ref, bf16[10,208,128]{2,1,0:T(8,128)(2,1)} %fusion.25.ext_ref, bf16[128,1152]{1,0:T(8,128)(2,1)} %copy.136.w_ref), custom_call_target="tpu_custom_call" | custom-call | tf_op jit(solution)/shard_map/pallas_call | solution.py:85
  73.9 4.6 %all-to-all-done.3 = bf16[2,720,128]{2,0,1:T(2,128)(2,1)S(1)} async-done(((bf16[2,720,128]{2,0,1:T(2,128)(2,1)}), bf16[2,720,128]{2,0,1:T(2,128)(2,1)S(1)}, u32[]{:S(2)}, u32[]{:S(2)}) %all-to-all-start.3) | async-done | bytes 368672 | tf_op jit(solution)/shard_map/all_to_all | solution.py:272
  78.5 0.1 copy.173
  78.6 1.2 %fusion.20 = bf16[8,180,128]{2,1,0:T(8,128)(2,1)S(1)} fusion(f32[3,192,128]{2,1,0:T(8,128)} %shard_map.111, f32[3,192,128]{2,1,0:T(8,128)S(1)} %copy-done.2, f32[2,192,128]{2,1,0:T(8,128)S(1)} %copy-done.3, bf16[8,180,128]{2,1,0:T(8,128)(2,1)S(1)} %bitcast.118, pred[8]{0:T(512)(128)(4,1)S(1)} %iota_compare_fusion.1, bf16[8,180,128]{2,0,1:T(8,128)(2,1)S(1)} %copy-done), kind=kLoop, calls=%fused_computation.40 | loop fusion | flops 1658880 | bytes 1892360 | tf_op jit(solution)/shard_map/convert_element_type | solution.py:307
  79.8 0.8 copy.152
  (46 shorter events, 0.4 us)
Async XLA Ops:
  3.1 10.7 %copy-start.6 = (f32[64,9,9]{0,2,1:T(8,128)S(1)}, f32[64,9,9]{0,2,1:T(8,128)}, u32[]{:S(2)}) copy-start(f32[64,9,9]{0,2,1:T(8,128)} %param.16) | copy-start | bytes 62212
  4.0 17.8 %all-to-all-start = ((bf16[4,376,128]{2,1,0:T(8,128)(2,1)}), bf16[4,376,128]{2,1,0:T(8,128)(2,1)S(1)}, u32[]{:S(2)}, u32[]{:S(2)}) async-start(bf16[4,376,128]{2,1,0:T(8,128)(2,1)} %pad_maximum_fusion.3), calls=%async_computation | async-start | bytes 770048 | tf_op jit(solution)/shard_map/all_to_all | solution.py:234
  10.3 5.4 %copy-start.7 = (f32[45,192]{1,0:T(8,128)S(1)}, f32[45,192]{1,0:T(8,128)}, u32[]{:S(2)}) copy-start(f32[45,192]{1,0:T(8,128)} %constant.78.clone) | copy-start | bytes 103684
  10.3 5.4 %copy-start.8 = (f32[45,192]{1,0:T(8,128)S(1)}, f32[45,192]{1,0:T(8,128)}, u32[]{:S(2)}) copy-start(f32[45,192]{1,0:T(8,128)} %constant.77.clone) | copy-start | bytes 103684
  10.3 5.4 %copy-start.9 = (f32[16,192]{1,0:T(8,128)S(1)}, f32[16,192]{1,0:T(8,128)}, u32[]{:S(2)}) copy-start(f32[16,192]{1,0:T(8,128)} %constant.80.clone) | copy-start | bytes 36868
  10.3 5.4 %copy-start.10 = (f32[16,192]{1,0:T(8,128)S(1)}, f32[16,192]{1,0:T(8,128)}, u32[]{:S(2)}) copy-start(f32[16,192]{1,0:T(8,128)} %constant.79.clone) | copy-start | bytes 36868
  22.2 4.4 %collective-permute-start = (bf16[1,182,128]{2,1,0:T(8,128)(2,1)S(1)}, bf16[1,182,128]{2,1,0:T(8,128)(2,1)S(1)}, u32[]{:S(2)}, u32[]{:S(2)}) collective-permute-start(bf16[1,182,128]{2,1,0:T(8,128)(2,1)S(1)} %get-tuple-element.37), channel_id=1, source_target_pairs={{0,4},{4,8},{8,12},{12,16},{16,20},{20,24},{24,28},{28,0},{1,5},{5... | collective-permute-start | bytes 139784 | tf_op jit(solution)/shard_map/ppermute | solution.py:130
  22.3 4.4 %collective-permute-start.1 = (bf16[1,182,128]{2,1,0:T(8,128)(2,1)S(1)}, bf16[1,182,128]{2,1,0:T(8,128)(2,1)S(1)}, u32[]{:S(2)}, u32[]{:S(2)}) collective-permute-start(bf16[1,182,128]{2,1,0:T(8,128)(2,1)S(1)} %get-tuple-element.38), channel_id=1, source_target_pairs={{4,0},{8,4},{12,8},{16,12},{20,16},{24,20},{28,24},{0,28},{5,1},{9... | collective-permute-start | bytes 139784 | tf_op jit(solution)/shard_map/ppermute | solution.py:131
  26.1 7.0 %copy-start.5 = (bf16[128,9,128]{2,0,1:T(8,128)(2,1)S(1)}, bf16[128,9,128]{2,0,1:T(8,128)(2,1)}, u32[]{:S(2)}) copy-start(bf16[128,9,128]{2,0,1:T(8,128)(2,1)} %param.17) | copy-start | bytes 884740
  28.5 13.3 %all-to-all-start.1 = ((bf16[2,2,192,128]{3,0,1,2:T(2,128)(2,1)}), bf16[2,2,192,128]{3,0,1,2:T(2,128)(2,1)S(1)}, u32[]{:S(2)}, u32[]{:S(2)}) async-start(bf16[2,2,192,128]{3,0,1,2:T(2,128)(2,1)} %copy.126), calls=%async_computation.1 | async-start | bytes 393216 | tf_op jit(solution)/shard_map/all_to_all | solution.py:251
  32.6 3.6 %copy-start.4 = (f32[2,360,128]{2,1,0:T(8,128)S(1)}, f32[2,360,128]{2,1,0:T(8,128)}, u32[]{:S(2)}) copy-start(f32[2,360,128]{2,1,0:T(8,128)} %param.15) | copy-start | bytes 1105924
  42.0 1.7 %copy-start.1 = (f32[24,360,64]{1,2,0:T(8,128)S(1)}, f32[24,360,64]{1,2,0:T(8,128)}, u32[]{:S(2)}) copy-start(f32[24,360,64]{1,2,0:T(8,128)} %param.13) | copy-start | bytes 6635524
  44.8 0.7 copy-start.11
  46.7 14.6 %all-to-all-start.2 = ((bf16[64,2,6,128]{3,1,2,0:T(2,128)(2,1)}), bf16[64,2,6,128]{3,1,2,0:T(2,128)(2,1)S(1)}, u32[]{:S(2)}, u32[]{:S(2)}) async-start(bf16[64,2,6,128]{3,1,2,0:T(2,128)(2,1)} %copy.139), calls=%async_computation.2 | async-start | bytes 393216 | tf_op jit(solution)/shard_map/all_to_all | solution.py:263
  63.5 15.0 %all-to-all-start.3 = ((bf16[2,720,128]{2,0,1:T(2,128)(2,1)}), bf16[2,720,128]{2,0,1:T(2,128)(2,1)S(1)}, u32[]{:S(2)}, u32[]{:S(2)}) async-start(bf16[2,720,128]{2,0,1:T(2,128)(2,1)} %copy.148), calls=%async_computation.3 | async-start | bytes 737280 | tf_op jit(solution)/shard_map/all_to_all | solution.py:272
  67.2 11.4 %copy-start = (bf16[8,180,128]{2,0,1:T(8,128)(2,1)S(1)}, bf16[8,180,128]{2,0,1:T(8,128)(2,1)}, u32[]{:S(2)}) copy-start(bf16[8,180,128]{2,0,1:T(8,128)(2,1)} %param.11) | copy-start | bytes 1105924
  67.2 11.4 %copy-start.2 = (f32[3,192,128]{2,1,0:T(8,128)S(1)}, f32[3,192,128]{2,1,0:T(8,128)}, u32[]{:S(2)}) copy-start(f32[3,192,128]{2,1,0:T(8,128)} %shard_map.110) | copy-start | bytes 884740
  67.2 11.4 %copy-start.3 = (f32[2,192,128]{2,1,0:T(8,128)S(1)}, f32[2,192,128]{2,1,0:T(8,128)}, u32[]{:S(2)}) copy-start(f32[2,192,128]{2,1,0:T(8,128)} %shard_map.109) | copy-start | bytes 589828

commit v11 on v10

--- a/solution.py
+++ b/solution.py
@@ -158,7 +158,7 @@
 
 
 def spectral_by_channels(
-    masked, legendre, quad_weights, spectral_filter, trig_parts, live_rows, disco_work
+    masked, legendre, quad_weights, spectral_filter, trig_parts, live_rows, disco_work, prep
 ):
     ext = halo_extend(masked, live_rows)
     channels = masked.shape[2]
@@ -172,7 +172,7 @@
     )
     spectra, ext_now = lax.optimization_barrier((spectra, ext))
     columns = lax.all_to_all(spectra, "lat", split_axis=2, concat_axis=0, tiled=True)
-    disco_parts.append(disco_work(ext_now, 0))
+    disco_parts.append(disco_work(ext_now, 0, prep))
     columns, disco_parts[0] = lax.optimization_barrier((columns, disco_parts[0]))
     legendre_parts = split_bf16(legendre)
     coefficients = dot_split("mls,spmc->lpmc", legendre_parts, (columns,))
@@ -192,7 +192,7 @@
     returned = (returned * quad_weights[:, None, None, None]).astype(jnp.bfloat16)
     returned, ext_now = lax.optimization_barrier((returned, ext))
     portion = lax.all_to_all(returned, "lat", split_axis=0, concat_axis=2, tiled=True)
-    disco_parts.append(disco_work(ext_now, 1))
+    disco_parts.append(disco_work(ext_now, 1, prep))
     portion, disco_parts = lax.optimization_barrier((portion, disco_parts))
     spectral_rows = None
     for p, parts in enumerate(trig_parts):
@@ -201,7 +201,7 @@
     spectral_rows = spectral_rows.astype(jnp.bfloat16)
     spectral_rows, ext_now = lax.optimization_barrier((spectral_rows, ext))
     spectral = lax.all_to_all(spectral_rows, "lon", split_axis=1, concat_axis=2, tiled=True)
-    disco_parts.append(disco_work(ext_now, 2))
+    disco_parts.append(disco_work(ext_now, 2, prep))
     spectral, disco_parts = lax.optimization_barrier((spectral, disco_parts))
     return spectral, disco_parts
 
@@ -221,7 +221,7 @@
 
 
 def spectral_by_modes(
-    masked, legendre, quad_weights, spectral_filter, trig_parts, live_rows, disco_work
+    masked, legendre, quad_weights, spectral_filter, trig_parts, live_rows, disco_work, prep
 ):
     both = ("lat", "lon")
     lon_total = lax.axis_size("lon")
@@ -234,6 +234,11 @@
     received = lax.all_to_all(
         jnp.concatenate([body, edges], axis=1), "lon", split_axis=0, concat_axis=0, tiled=True
     )
+    own_legendre = lax.dynamic_slice_in_dim(
+        legendre, lax.axis_index("lon") * mode_share, mode_share, 0
+    )
+    legendre_parts = split_bf16(own_legendre)
+    received, legendre_parts, prep = lax.optimization_barrier((received, legendre_parts, prep))
     portion = received[:, : share * lon_count].reshape(lon_total, share, lon_count, channels)
     portion = portion.transpose(1, 0, 2, 3).reshape(share, lon_total * lon_count, channels)
     edge_block = received[:, share * lon_count :]
@@ -249,19 +254,15 @@
     )
     spectra, ext_now = lax.optimization_barrier((spectra, ext))
     columns = lax.all_to_all(spectra, both, split_axis=2, concat_axis=0, tiled=True)
-    disco_parts.append(disco_work(ext_now, 0))
+    disco_parts.append(disco_work(ext_now, 0, prep))
     columns, disco_parts[0] = lax.optimization_barrier((columns, disco_parts[0]))
-    own_legendre = lax.dynamic_slice_in_dim(
-        legendre, lax.axis_index("lon") * mode_share, mode_share, 0
-    )
-    legendre_parts = split_bf16(own_legendre)
     coefficients = dot_split("mls,spmc->lpmc", legendre_parts, (columns,))
     filtered = filter_modes(coefficients, spectral_filter)
     returned = dot_split("mls,lpmc->spmc", legendre_parts, split_bf16(filtered))
     returned = (returned * quad_weights[:, None, None, None]).astype(jnp.bfloat16)
     returned, ext_now = lax.optimization_barrier((returned, ext))
     portion = lax.all_to_all(returned, both, split_axis=0, concat_axis=2, tiled=True)
-    disco_parts.append(disco_work(ext_now, 1))
+    disco_parts.append(disco_work(ext_now, 1, prep))
     portion, disco_parts = lax.optimization_barrier((portion, disco_parts))
     spectral_rows = None
     for p, parts in enumerate(trig_parts):
@@ -270,7 +271,7 @@
     spectral_rows = spectral_rows.astype(jnp.bfloat16)
     spectral_rows, ext_now = lax.optimization_barrier((spectral_rows, ext))
     spectral = lax.all_to_all(spectral_rows, "lon", split_axis=1, concat_axis=0, tiled=True)
-    disco_parts.append(disco_work(ext_now, 2))
+    disco_parts.append(disco_work(ext_now, 2, prep))
     spectral, disco_parts = lax.optimization_barrier((spectral, disco_parts))
     return spectral, disco_parts
 
@@ -293,13 +294,20 @@
     weight_flat = disco_weight.reshape(channels, -1)
     pieces = min(3, row_count)
 
-    def disco_work(ext_now, piece):
-        return disco_piece(src_rows, coef, ext_now, weight_flat, piece, pieces, lon_count)
+    def disco_work(ext_now, piece, prep):
+        return disco_piece(prep[0], prep[1], ext_now, prep[2], piece, pieces, lon_count)
 
     by_modes = legendre.shape[0] % lon_total == 0 and row_count % lon_total == 0
     path = spectral_by_modes if by_modes else spectral_by_channels
     spectral, disco_parts = path(
-        masked, legendre, quad_weights, spectral_filter, trig_parts, live_rows, disco_work
+        masked,
+        legendre,
+        quad_weights,
+        spectral_filter,
+        trig_parts,
+        live_rows,
+        disco_work,
+        (src_rows, coef, weight_flat),
     )
     disco_full = jnp.concatenate(disco_parts, axis=0)
     disco_term = disco_full[:, :lon_count, :]

time: 81.3 us -> 79.1 us (0.973)
  waiting for transfers between devices: 14.1 us -> 12.4 us
  starting transfers between devices: 21.9 us -> 20.3 us
  other arithmetic: 8.51 us -> 9.49 us
    all_to_all x1, waiting for transfers between devices: 5.73 us -> 1.24 us  [spectral_by_modes(): lax.all_to_all(jnp.concatenate([body, edges], axis=1), 'lon', split_axis=...]
    all_to_all x1, waiting for transfers between devices: 0.53 us -> 3.28 us  [spectral_by_modes(): lax.all_to_all(spectra, both, split_axis=2, concat_axis=0, tiled=True)]
    all_to_all x1, starting transfers between devices: 5.3 us -> 2.58 us  [spectral_by_modes(): lax.all_to_all(returned, both, split_axis=0, concat_axis=2, tiled=True)]
    convert_element_type x1 -> x2, other arithmetic: 0.35 us -> 2.22 us  [split_bf16(): (values - rounded).astype(jnp.bfloat16)]
    all_to_all x1, starting transfers between devices: 3.96 us -> 5.11 us  [spectral_by_modes(): lax.all_to_all(spectra, both, split_axis=2, concat_axis=0, tiled=True)]
    convert_element_type x1 -> x0, other arithmetic: 1.1 us -> none  [split_bf16(): rounded.astype(jnp.bfloat16)]
    optimization_barrier x0 -> x1, local copies, waits for them, and re-layouts: none -> 0.9 us  [spectral_by_modes(): lax.optimization_barrier((received, legendre_parts, prep))]
    reshape x1 -> x0, local copies, waits for them, and re-layouts: 0.9 us -> none  [on_device(): weight_flat = disco_weight.reshape(channels, -1)]
  transfers between devices with their start and end apart: 6 -> 6, of which waited for: 5 -> 5; matrix products, arithmetic and copies ran while one was open for 11% -> 13% of each run, Pallas kernels for 23% -> 23%
where the time goes in v11:
time: 79.1 us; the launch traced here: 78.4 us
  starting transfers between devices  20.3 us (26%)
  Pallas kernels  18.3 us (23%)
  waiting for transfers between devices  12.4 us (16%)
  local copies, waits for them, and re-layouts  11 us (14%)
  other arithmetic  9.49 us (12%)
  matrix products  4.27 us (5%)
  between operations  2.57 us (3%)
    pallas_call x3, Pallas kernels, disco_piece(): pl.pallas_call(functools.partial(disco_body, first, last), out_shape=jax....  18.3 us
    all_to_all x1, starting transfers between devices, spectral_by_modes(): lax.all_to_all(jnp.concatenate([body, edges], axis=1), 'lon', split_axis=...  6.32 us
    all_to_all x1, starting transfers between devices, spectral_by_modes(): lax.all_to_all(spectra, both, split_axis=2, concat_axis=0, tiled=True)  5.11 us
    all_to_all x1, waiting for transfers between devices, spectral_by_modes(): lax.all_to_all(spectral_rows, 'lon', split_axis=1, concat_axis=0, tiled=T...  4.64 us
    dot_general x13, matrix products, dot_split(): term = jnp.einsum(spec, lp, rp, preferred_element_type=jnp.float32)  4.27 us
    all_to_all x1, starting transfers between devices, spectral_by_modes(): lax.all_to_all(spectral_rows, 'lon', split_axis=1, concat_axis=0, tiled=T...  3.64 us
    all_to_all x1, waiting for transfers between devices, spectral_by_modes(): lax.all_to_all(spectra, both, split_axis=2, concat_axis=0, tiled=True)  3.28 us
    all_to_all x1, waiting for transfers between devices, spectral_by_modes(): lax.all_to_all(returned, both, split_axis=0, concat_axis=2, tiled=True)  2.75 us
  transfers between devices with their start and end apart: 6, of which 5 were waited for; matrix products, arithmetic and copies ran while one was open for 13% of the time, Pallas kernels for 23%

profile of v11, /device:TPU:0, one launch (start us, length us, event | category | flops | bytes accessed | tf_op | source)
XLA Modules:
  0.0 78.4 jit_solution(11347410777368222158)
XLA Ops:
  0.0 1.4 %fusion.46 = (s32[1]{0:T(128)}, s32[1]{0:T(128)}) fusion(s32[8]{0:T(128)} %param.12, s32[]{:T(128)S(6)} %max.10, s32[]{:T(128)S(6)} %select_n.111), kind=kLoop, calls=%fused_computation.99 | loop fusion | bytes 24 | tf_op jit(solution)/shard_map/dynamic_slice | solution.py:110
  1.4 0.7 iota_compare_fusion.1
  2.1 1.1 %copy_select_fusion = bf16[8,180,128]{2,1,0:T(8,128)(2,1)S(1)} fusion(bf16[8,180,128]{2,0,1:T(8,128)(2,1)} %param.11, pred[8]{0:T(512)(128)(4,1)S(1)} %iota_compare_fusion.1), kind=kLoop, calls=%fused_computation.53 | loop fusion | flops 184320 | bytes 737288 | tf_op jit(solution)/shard_map/jit(_where)/select_n | solution.py:291
  3.2 0.1 reshape.246
  3.3 0.8 pad_maximum_fusion.3
  4.1 6.3 %all-to-all-start = ((bf16[4,376,128]{2,1,0:T(8,128)(2,1)}), bf16[4,376,128]{2,1,0:T(8,128)(2,1)S(1)}, u32[]{:S(2)}, u32[]{:S(2)}) async-start(bf16[4,376,128]{2,1,0:T(8,128)(2,1)} %pad_maximum_fusion.3), calls=%async_computation | async-start | bytes 770048 | tf_op jit(solution)/shard_map/all_to_all | solution.py:234
  11.8 0.7 compare_select_fusion.2
  13.1 0.1 copy.119
  13.2 0.7 reshape.247.src_ref
  13.9 0.7 fusion.39
  14.6 0.1 copy.120
  14.7 0.1 reshape.254
  14.8 0.9 %copy.125 = bf16[128,9,128]{0,2,1:T(8,128)(2,1)} copy(bf16[128,9,128]{2,0,1:T(8,128)(2,1)S(1)} %copy-done.6) | data formatting | bytes 589824 | tf_op args[6]
  15.7 0.3 copy.121
  16.0 0.6 gather_fusion
  16.7 0.7 compare_or_fusion
  17.4 0.1 pad.23.clone
  17.5 0.1 pad_add_fusion.1
  17.6 0.1 maximum_select_fusion
  17.7 0.7 select_n.120.coef_ref
  18.4 1.9 %fusion.23 = (bf16[6,360,64]{1,2,0:T(8,128)(2,1)}, bf16[6,360,64]{1,2,0:T(8,128)(2,1)S(1)}) fusion(f32[24,360,64]{1,2,0:T(8,128)} %param.13, s32[]{:T(128)S(6)} %select_n.113), kind=kLoop, calls=%fused_computation.46 | loop fusion | flops 552960 | bytes 1105924 | tf_op jit(solution)/shard_map/convert_element_type | solution.py:34
  20.3 0.4 fusion.21
  20.7 1.2 %all-to-all-done = bf16[4,376,128]{2,1,0:T(8,128)(2,1)S(1)} async-done(((bf16[4,376,128]{2,1,0:T(8,128)(2,1)}), bf16[4,376,128]{2,1,0:T(8,128)(2,1)S(1)}, u32[]{:S(2)}, u32[]{:S(2)}) %all-to-all-start) | async-done | bytes 385056 | tf_op jit(solution)/shard_map/all_to_all | solution.py:234
  22.0 0.1 reshape.250
  22.1 0.1 reshape.251
  22.2 0.1 pad_maximum_fusion.4
  22.3 0.1 collective-permute-start
  22.4 2.6 %collective-permute-start.1 = (bf16[1,182,128]{2,1,0:T(8,128)(2,1)S(1)}, bf16[1,182,128]{2,1,0:T(8,128)(2,1)S(1)}, u32[]{:S(2)}, u32[]{:S(2)}) collective-permute-start(bf16[1,182,128]{2,1,0:T(8,128)(2,1)S(1)} %get-tuple-element.52), channel_id=1, source_target_pairs={{4,0},{8,4},{12,8},{16,12},{20,16},{24,20},{28,24},{0,28},{5,1},{9... | collective-permute-start | bytes 139784 | tf_op jit(solution)/shard_map/ppermute | solution.py:131
  25.0 0.3 fusion.48
  25.3 0.3 fusion.47
  25.6 0.3 fusion.9
  25.9 0.3 fusion.10
  26.3 0.5 collective-permute-done
  26.8 0.9 %fusion.25.ext_ref = bf16[10,208,128]{2,1,0:T(8,128)(2,1)} fusion(bf16[1,182,128]{2,1,0:T(8,128)(2,1)S(1)} %collective-permute-done.1, bf16[1,182,128]{2,1,0:T(8,128)(2,1)S(1)} %collective-permute-done, bf16[8,1,128]{2,1,0:T(2,128)(2,1)S(1)} %copy.132, bf16[8,180,128]{2,1,0:T(8,128)(2,1)S(1)} %copy_select_fusion, bf16[8,1,128]{2,1,0:T(2,128)(2,1)S(1)} %copy.131), kind=kLoop, calls=%fused_computation.48 | loop fusion | flops 4259840 | bytes 998400 | tf_op jit(solution)/shard_map/concatenate | solution.py:132
  27.7 0.9 %copy.133 = bf16[2,2,192,128]{3,0,1,2:T(2,128)(2,1)} copy(bf16[2,2,192,128]{3,2,0,1:T(8,128)(2,1)S(1)} %pad_maximum_fusion.5) | data formatting | bytes 393216 | tf_op jit(solution)/shard_map/optimization_barrier | solution.py:255
  28.6 5.1 %all-to-all-start.1 = ((bf16[2,2,192,128]{3,0,1,2:T(2,128)(2,1)}), bf16[2,2,192,128]{3,0,1,2:T(2,128)(2,1)S(1)}, u32[]{:S(2)}, u32[]{:S(2)}) async-start(bf16[2,2,192,128]{3,0,1,2:T(2,128)(2,1)} %copy.133), calls=%async_computation.1 | async-start | bytes 393216 | tf_op jit(solution)/shard_map/all_to_all | solution.py:256
  33.7 0.9 %copy.136.w_ref = bf16[128,1152]{1,0:T(8,128)(2,1)} copy(bf16[128,1152]{0,1:T(8,128)(2,1)S(1)} %bitcast.124) | data formatting | bytes 589824 | tf_op jit(solution)/shard_map/optimization_barrier | solution.py:241
  34.6 5.1 %shard_map.109 = f32[2,192,128]{2,1,0:T(8,128)} custom-call(s32[24]{0:T(128)} %reshape.247.src_ref, f32[648]{0:T(1024)} %select_n.120.coef_ref, bf16[10,208,128]{2,1,0:T(8,128)(2,1)} %fusion.25.ext_ref, bf16[128,1152]{1,0:T(8,128)(2,1)} %copy.136.w_ref), custom_call_target="tpu_custom_call" | custom-call | tf_op jit(solution)/shard_map/pallas_call | solution.py:85
  39.7 3.3 %all-to-all-done.1 = bf16[2,2,192,128]{3,0,1,2:T(2,128)(2,1)S(1)} async-done(((bf16[2,2,192,128]{3,0,1,2:T(2,128)(2,1)}), bf16[2,2,192,128]{3,0,1,2:T(2,128)(2,1)S(1)}, u32[]{:S(2)}, u32[]{:S(2)}) %all-to-all-start.1) | async-done | bytes 196640 | tf_op jit(solution)/shard_map/all_to_all | solution.py:256
  43.0 0.2 copy.135
  43.2 0.5 fusion.33
  43.7 0.5 copy-done.1
  44.2 0.5 add_bitcast_fusion
  44.7 0.2 multiply_add_fusion
  44.9 0.4 fusion.31
  45.3 0.4 convolution_add_fusion.3
  45.7 0.2 copy-done.12
  45.9 0.4 fusion.6
  46.3 0.9 %copy.139 = bf16[64,2,6,128]{3,1,2,0:T(2,128)(2,1)} copy(bf16[64,2,6,128]{3,0,1,2:T(8,128)(2,1)S(1)} %fusion.6) | data formatting | bytes 393216 | tf_op jit(solution)/shard_map/optimization_barrier | solution.py:263
  47.2 2.6 %all-to-all-start.2 = ((bf16[64,2,6,128]{3,1,2,0:T(2,128)(2,1)}), bf16[64,2,6,128]{3,1,2,0:T(2,128)(2,1)S(1)}, u32[]{:S(2)}, u32[]{:S(2)}) async-start(bf16[64,2,6,128]{3,1,2,0:T(2,128)(2,1)} %copy.139), calls=%async_computation.2 | async-start | bytes 393216 | tf_op jit(solution)/shard_map/all_to_all | solution.py:264
  49.8 6.6 %shard_map.110 = f32[3,192,128]{2,1,0:T(8,128)} custom-call(s32[24]{0:T(128)} %reshape.247.src_ref, f32[648]{0:T(1024)} %select_n.120.coef_ref, bf16[10,208,128]{2,1,0:T(8,128)(2,1)} %fusion.25.ext_ref, bf16[128,1152]{1,0:T(8,128)(2,1)} %copy.136.w_ref), custom_call_target="tpu_custom_call" | custom-call | tf_op jit(solution)/shard_map/pallas_call | solution.py:85
  56.4 2.8 %all-to-all-done.2 = bf16[64,2,6,128]{3,1,2,0:T(2,128)(2,1)S(1)} async-done(((bf16[64,2,6,128]{3,1,2,0:T(2,128)(2,1)}), bf16[64,2,6,128]{3,1,2,0:T(2,128)(2,1)S(1)}, u32[]{:S(2)}, u32[]{:S(2)}) %all-to-all-start.2) | async-done | bytes 196640 | tf_op jit(solution)/shard_map/all_to_all | solution.py:264
  59.1 0.1 copy.140
  59.3 0.2 fusion.38
  59.5 0.2 fusion.37
  59.8 0.2 convolution_add_fusion.1
  60.0 0.2 fusion.4
  60.3 1.0 %copy.148 = bf16[2,720,128]{2,0,1:T(2,128)(2,1)} copy(bf16[2,720,128]{2,1,0:T(8,128)(2,1)S(1)} %fusion.4) | data formatting | bytes 737280 | tf_op jit(solution)/shard_map/optimization_barrier | solution.py:272
  61.3 3.6 %all-to-all-start.3 = ((bf16[2,720,128]{2,0,1:T(2,128)(2,1)}), bf16[2,720,128]{2,0,1:T(2,128)(2,1)S(1)}, u32[]{:S(2)}, u32[]{:S(2)}) async-start(bf16[2,720,128]{2,0,1:T(2,128)(2,1)} %copy.148), calls=%async_computation.3 | async-start | bytes 737280 | tf_op jit(solution)/shard_map/all_to_all | solution.py:273
  65.0 6.6 %shard_map.111 = f32[3,192,128]{2,1,0:T(8,128)} custom-call(s32[24]{0:T(128)} %reshape.247.src_ref, f32[648]{0:T(1024)} %select_n.120.coef_ref, bf16[10,208,128]{2,1,0:T(8,128)(2,1)} %fusion.25.ext_ref, bf16[128,1152]{1,0:T(8,128)(2,1)} %copy.136.w_ref), custom_call_target="tpu_custom_call" | custom-call | tf_op jit(solution)/shard_map/pallas_call | solution.py:85
  71.6 4.6 %all-to-all-done.3 = bf16[2,720,128]{2,0,1:T(2,128)(2,1)S(1)} async-done(((bf16[2,720,128]{2,0,1:T(2,128)(2,1)}), bf16[2,720,128]{2,0,1:T(2,128)(2,1)S(1)}, u32[]{:S(2)}, u32[]{:S(2)}) %all-to-all-start.3) | async-done | bytes 368672 | tf_op jit(solution)/shard_map/all_to_all | solution.py:273
  76.3 0.1 copy.173
  76.4 1.2 %fusion.20 = bf16[8,180,128]{2,1,0:T(8,128)(2,1)S(1)} fusion(f32[3,192,128]{2,1,0:T(8,128)} %shard_map.111, f32[3,192,128]{2,1,0:T(8,128)S(1)} %copy-done.3, f32[2,192,128]{2,1,0:T(8,128)S(1)} %copy-done.4, bf16[8,180,128]{2,1,0:T(8,128)(2,1)S(1)} %bitcast.121, pred[8]{0:T(512)(128)(4,1)S(1)} %iota_compare_fusion.1, bf16[8,180,128]{2,0,1:T(8,128)(2,1)S(1)} %copy-done), kind=kLoop, calls=%fused_computation.40 | loop fusion | flops 1658880 | bytes 1892360 | tf_op jit(solution)/shard_map/convert_element_type | solution.py:315
  77.6 0.8 %copy.152 = bf16[8,180,128]{2,0,1:T(8,128)(2,1)} copy(bf16[8,180,128]{2,1,0:T(8,128)(2,1)S(1)} %fusion.20) | data formatting | bytes 737280 | tf_op jit(solution)/shard_map/convert_element_type | solution.py:315
  (48 shorter events, 0.4 us)
Async XLA Ops:
  3.2 11.6 %copy-start.6 = (bf16[128,9,128]{2,0,1:T(8,128)(2,1)S(1)}, bf16[128,9,128]{2,0,1:T(8,128)(2,1)}, u32[]{:S(2)}) copy-start(bf16[128,9,128]{2,0,1:T(8,128)(2,1)} %param.17) | copy-start | bytes 884740
  3.3 12.4 %copy-start.7 = (f32[64,9,9]{0,2,1:T(8,128)S(1)}, f32[64,9,9]{0,2,1:T(8,128)}, u32[]{:S(2)}) copy-start(f32[64,9,9]{0,2,1:T(8,128)} %param.16) | copy-start | bytes 62212
  4.1 17.8 %all-to-all-start = ((bf16[4,376,128]{2,1,0:T(8,128)(2,1)}), bf16[4,376,128]{2,1,0:T(8,128)(2,1)S(1)}, u32[]{:S(2)}, u32[]{:S(2)}) async-start(bf16[4,376,128]{2,1,0:T(8,128)(2,1)} %pad_maximum_fusion.3), calls=%async_computation | async-start | bytes 770048 | tf_op jit(solution)/shard_map/all_to_all | solution.py:234
  16.6 3.7 %copy-start.8 = (f32[45,192]{1,0:T(8,128)S(1)}, f32[45,192]{1,0:T(8,128)}, u32[]{:S(2)}) copy-start(f32[45,192]{1,0:T(8,128)} %constant.78.clone) | copy-start | bytes 103684
  16.6 3.7 %copy-start.9 = (f32[45,192]{1,0:T(8,128)S(1)}, f32[45,192]{1,0:T(8,128)}, u32[]{:S(2)}) copy-start(f32[45,192]{1,0:T(8,128)} %constant.77.clone) | copy-start | bytes 103684
  16.6 3.7 %copy-start.10 = (f32[16,192]{1,0:T(8,128)S(1)}, f32[16,192]{1,0:T(8,128)}, u32[]{:S(2)}) copy-start(f32[16,192]{1,0:T(8,128)} %constant.80.clone) | copy-start | bytes 36868
  16.6 3.7 %copy-start.11 = (f32[16,192]{1,0:T(8,128)S(1)}, f32[16,192]{1,0:T(8,128)}, u32[]{:S(2)}) copy-start(f32[16,192]{1,0:T(8,128)} %constant.79.clone) | copy-start | bytes 36868
  22.3 4.4 %collective-permute-start = (bf16[1,182,128]{2,1,0:T(8,128)(2,1)S(1)}, bf16[1,182,128]{2,1,0:T(8,128)(2,1)S(1)}, u32[]{:S(2)}, u32[]{:S(2)}) collective-permute-start(bf16[1,182,128]{2,1,0:T(8,128)(2,1)S(1)} %get-tuple-element.51), channel_id=1, source_target_pairs={{0,4},{4,8},{8,12},{12,16},{16,20},{20,24},{24,28},{28,0},{1,5},{5... | collective-permute-start | bytes 139784 | tf_op jit(solution)/shard_map/ppermute | solution.py:130
  22.4 4.4 %collective-permute-start.1 = (bf16[1,182,128]{2,1,0:T(8,128)(2,1)S(1)}, bf16[1,182,128]{2,1,0:T(8,128)(2,1)S(1)}, u32[]{:S(2)}, u32[]{:S(2)}) collective-permute-start(bf16[1,182,128]{2,1,0:T(8,128)(2,1)S(1)} %get-tuple-element.52), channel_id=1, source_target_pairs={{4,0},{8,4},{12,8},{16,12},{20,16},{24,20},{28,24},{0,28},{5,1},{9... | collective-permute-start | bytes 139784 | tf_op jit(solution)/shard_map/ppermute | solution.py:131
  26.2 7.5 %copy-start.5 = (f32[2,360,128]{2,1,0:T(8,128)S(1)}, f32[2,360,128]{2,1,0:T(8,128)}, u32[]{:S(2)}) copy-start(f32[2,360,128]{2,1,0:T(8,128)} %param.15) | copy-start | bytes 1105924
  26.3 7.5 %copy-start.2 = (bf16[128,9,128]{0,2,1:T(8,128)(2,1)S(1)}, bf16[128,9,128]{0,2,1:T(8,128)(2,1)}, u32[]{:S(2)}) copy-start(bf16[128,9,128]{0,2,1:T(8,128)(2,1)} %copy.125) | copy-start | bytes 884740
  28.6 14.4 %all-to-all-start.1 = ((bf16[2,2,192,128]{3,0,1,2:T(2,128)(2,1)}), bf16[2,2,192,128]{3,0,1,2:T(2,128)(2,1)S(1)}, u32[]{:S(2)}, u32[]{:S(2)}) async-start(bf16[2,2,192,128]{3,0,1,2:T(2,128)(2,1)} %copy.133), calls=%async_computation.1 | async-start | bytes 393216 | tf_op jit(solution)/shard_map/all_to_all | solution.py:256
  43.2 1.0 %copy-start.1 = (bf16[6,360,64]{1,2,0:T(8,128)(2,1)S(1)}, bf16[6,360,64]{1,2,0:T(8,128)(2,1)}, u32[]{:S(2)}) copy-start(bf16[6,360,64]{1,2,0:T(8,128)(2,1)} %get-tuple-element.34) | copy-start | bytes 829444
  45.3 0.7 copy-start.12
  47.2 11.9 %all-to-all-start.2 = ((bf16[64,2,6,128]{3,1,2,0:T(2,128)(2,1)}), bf16[64,2,6,128]{3,1,2,0:T(2,128)(2,1)S(1)}, u32[]{:S(2)}, u32[]{:S(2)}) async-start(bf16[64,2,6,128]{3,1,2,0:T(2,128)(2,1)} %copy.139), calls=%async_computation.2 | async-start | bytes 393216 | tf_op jit(solution)/shard_map/all_to_all | solution.py:264
  61.3 15.0 %all-to-all-start.3 = ((bf16[2,720,128]{2,0,1:T(2,128)(2,1)}), bf16[2,720,128]{2,0,1:T(2,128)(2,1)S(1)}, u32[]{:S(2)}, u32[]{:S(2)}) async-start(bf16[2,720,128]{2,0,1:T(2,128)(2,1)} %copy.148), calls=%async_computation.3 | async-start | bytes 737280 | tf_op jit(solution)/shard_map/all_to_all | solution.py:273
  65.0 11.4 %copy-start = (bf16[8,180,128]{2,0,1:T(8,128)(2,1)S(1)}, bf16[8,180,128]{2,0,1:T(8,128)(2,1)}, u32[]{:S(2)}) copy-start(bf16[8,180,128]{2,0,1:T(8,128)(2,1)} %param.11) | copy-start | bytes 1105924
  65.0 11.4 %copy-start.3 = (f32[3,192,128]{2,1,0:T(8,128)S(1)}, f32[3,192,128]{2,1,0:T(8,128)}, u32[]{:S(2)}) copy-start(f32[3,192,128]{2,1,0:T(8,128)} %shard_map.110) | copy-start | bytes 884740
  65.0 11.4 %copy-start.4 = (f32[2,192,128]{2,1,0:T(8,128)S(1)}, f32[2,192,128]{2,1,0:T(8,128)}, u32[]{:S(2)}) copy-start(f32[2,192,128]{2,1,0:T(8,128)} %shard_map.109) | copy-start | bytes 589828

commit v12 on v11

--- a/solution.py
+++ b/solution.py
@@ -246,13 +246,14 @@
     left = lax.dynamic_index_in_dim(edge_block, (lon_index - 1) % lon_total, 0, keepdims=False)
     right = lax.dynamic_index_in_dim(edge_block, (lon_index + 1) % lon_total, 0, keepdims=False)
     own = jnp.concatenate([left[row_count:, None], masked, right[:row_count, None]], axis=1)
-    ext = pad_lon(lat_extend(own, live_rows), lon_count)
     disco_parts = []
     spectra = jnp.stack(
         [dot_split("rnc,nk->rkc", (portion,), parts).astype(jnp.bfloat16) for parts in trig_parts],
         axis=1,
     )
-    spectra, ext_now = lax.optimization_barrier((spectra, ext))
+    spectra, own = lax.optimization_barrier((spectra, own))
+    ext = pad_lon(lat_extend(own, live_rows), lon_count)
+    ext_now = ext
     columns = lax.all_to_all(spectra, both, split_axis=2, concat_axis=0, tiled=True)
     disco_parts.append(disco_work(ext_now, 0, prep))
     columns, disco_parts[0] = lax.optimization_barrier((columns, disco_parts[0]))

time: 79.1 us -> 80 us (1.011)
  starting transfers between devices: 20.3 us -> 22.8 us
  waiting for transfers between devices: 12.4 us -> 10.3 us
    all_to_all x1, waiting for transfers between devices: 3.28 us -> 0.01 us  [spectral_by_modes(): lax.all_to_all(spectra, both, split_axis=2, concat_axis=0, tiled=True)]
    all_to_all x1, starting transfers between devices: 2.58 us -> 5.38 us  [spectral_by_modes(): lax.all_to_all(returned, both, split_axis=0, concat_axis=2, tiled=True)]
    ppermute x1, waiting for transfers between devices: 0.48 us -> 1.68 us  [lat_extend(): from_above = lax.ppermute(last_row, 'lat', lat_up)]
  transfers between devices with their start and end apart: 6 -> 6, of which waited for: 5 -> 4; matrix products, arithmetic and copies ran while one was open for 13% -> 13% of each run, Pallas kernels for 23% -> 23%
where the time goes in v12:
time: 80 us; the launch traced here: 79.3 us
  starting transfers between devices  22.8 us (28%)
  Pallas kernels  18.3 us (23%)
  local copies, waits for them, and re-layouts  11.6 us (14%)
  waiting for transfers between devices  10.3 us (13%)
  other arithmetic  9.4 us (12%)
  matrix products  4.3 us (5%)
  between operations  2.54 us (3%)
    pallas_call x3, Pallas kernels, disco_piece(): pl.pallas_call(functools.partial(disco_body, first, last), out_shape=jax....  18.3 us
    all_to_all x1, starting transfers between devices, spectral_by_modes(): lax.all_to_all(jnp.concatenate([body, edges], axis=1), 'lon', split_axis=...  6.32 us
    all_to_all x1, starting transfers between devices, spectral_by_modes(): lax.all_to_all(returned, both, split_axis=0, concat_axis=2, tiled=True)  5.38 us
    all_to_all x1, starting transfers between devices, spectral_by_modes(): lax.all_to_all(spectra, both, split_axis=2, concat_axis=0, tiled=True)  4.85 us
    all_to_all x1, waiting for transfers between devices, spectral_by_modes(): lax.all_to_all(spectral_rows, 'lon', split_axis=1, concat_axis=0, tiled=T...  4.64 us
    dot_general x13, matrix products, dot_split(): term = jnp.einsum(spec, lp, rp, preferred_element_type=jnp.float32)  4.3 us
    all_to_all x1, starting transfers between devices, spectral_by_modes(): lax.all_to_all(spectral_rows, 'lon', split_axis=1, concat_axis=0, tiled=T...  3.64 us
    all_to_all x1, waiting for transfers between devices, spectral_by_modes(): lax.all_to_all(returned, both, split_axis=0, concat_axis=2, tiled=True)  2.75 us
  transfers between devices with their start and end apart: 6, of which 4 were waited for; matrix products, arithmetic and copies ran while one was open for 13% of the time, Pallas kernels for 23%

profile of v12, /device:TPU:0, one launch (start us, length us, event | category | flops | bytes accessed | tf_op | source)
XLA Modules:
  0.0 79.3 jit_solution(10813733652695027590)
XLA Ops:
  0.0 1.4 %fusion.42 = (s32[1]{0:T(128)}, s32[1]{0:T(128)}) fusion(s32[8]{0:T(128)} %param.12, s32[]{:T(128)S(6)} %max.10, s32[]{:T(128)S(6)} %select_n.111), kind=kLoop, calls=%fused_computation.95 | loop fusion | bytes 24 | tf_op jit(solution)/shard_map/dynamic_slice | solution.py:110
  1.4 0.7 iota_compare_fusion.1
  2.1 1.1 %copy_select_fusion = bf16[8,180,128]{2,1,0:T(8,128)(2,1)S(1)} fusion(bf16[8,180,128]{2,0,1:T(8,128)(2,1)} %param.11, pred[8]{0:T(512)(128)(4,1)S(1)} %iota_compare_fusion.1), kind=kLoop, calls=%fused_computation.49 | loop fusion | flops 184320 | bytes 737288 | tf_op jit(solution)/shard_map/jit(_where)/select_n | solution.py:292
  3.2 0.1 reshape.246
  3.3 0.8 pad_maximum_fusion.3
  4.1 6.3 %all-to-all-start = ((bf16[4,376,128]{2,1,0:T(8,128)(2,1)}), bf16[4,376,128]{2,1,0:T(8,128)(2,1)S(1)}, u32[]{:S(2)}, u32[]{:S(2)}) async-start(bf16[4,376,128]{2,1,0:T(8,128)(2,1)} %pad_maximum_fusion.3), calls=%async_computation | async-start | bytes 770048 | tf_op jit(solution)/shard_map/all_to_all | solution.py:234
  11.8 0.7 compare_select_fusion.2
  13.1 0.1 copy.119
  13.2 0.7 reshape.247.src_ref
  13.9 0.7 fusion.35
  14.6 0.1 copy.120
  14.7 0.1 reshape.254
  14.8 0.9 %copy.125 = bf16[128,9,128]{0,2,1:T(8,128)(2,1)} copy(bf16[128,9,128]{2,0,1:T(8,128)(2,1)S(1)} %copy-done.6) | data formatting | bytes 589824 | tf_op args[6]
  15.7 0.3 copy.121
  16.0 0.6 gather_fusion
  16.7 0.7 compare_or_fusion
  17.4 0.1 pad.21.clone
  17.5 0.1 pad_add_fusion.1
  17.6 0.1 maximum_select_fusion
  17.7 0.7 select_n.120.coef_ref
  18.4 1.9 %fusion.21 = (bf16[6,360,64]{1,2,0:T(8,128)(2,1)}, bf16[6,360,64]{1,2,0:T(8,128)(2,1)S(1)}) fusion(f32[24,360,64]{1,2,0:T(8,128)} %param.13, s32[]{:T(128)S(6)} %select_n.113), kind=kLoop, calls=%fused_computation.44 | loop fusion | flops 552960 | bytes 1105924 | tf_op jit(solution)/shard_map/convert_element_type | solution.py:34
  20.3 0.3 fusion.19
  20.7 1.2 %all-to-all-done = bf16[4,376,128]{2,1,0:T(8,128)(2,1)S(1)} async-done(((bf16[4,376,128]{2,1,0:T(8,128)(2,1)}), bf16[4,376,128]{2,1,0:T(8,128)(2,1)S(1)}, u32[]{:S(2)}, u32[]{:S(2)}) %all-to-all-start) | async-done | bytes 385056 | tf_op jit(solution)/shard_map/all_to_all | solution.py:234
  22.0 0.1 reshape.250
  22.1 0.1 reshape.251
  22.2 0.3 fusion.44
  22.5 0.3 fusion.43
  22.8 0.1 pad_maximum_fusion.4
  22.9 0.3 fusion.9
  23.2 0.3 fusion.10
  23.6 0.9 %copy.133 = bf16[2,2,192,128]{3,0,1,2:T(2,128)(2,1)} copy(bf16[2,2,192,128]{3,2,0,1:T(8,128)(2,1)S(1)} %pad_maximum_fusion.5) | data formatting | bytes 393216 | tf_op jit(solution)/shard_map/optimization_barrier | solution.py:254
  24.4 4.8 %all-to-all-start.1 = ((bf16[2,2,192,128]{3,0,1,2:T(2,128)(2,1)}), bf16[2,2,192,128]{3,0,1,2:T(2,128)(2,1)S(1)}, u32[]{:S(2)}, u32[]{:S(2)}) async-start(bf16[2,2,192,128]{3,0,1,2:T(2,128)(2,1)} %copy.133), calls=%async_computation.1 | async-start | bytes 393216 | tf_op jit(solution)/shard_map/all_to_all | solution.py:257
  29.3 0.6 constant_dynamic-slice_fusion
  29.9 0.3 collective-permute-start
  30.2 2.4 %collective-permute-start.1 = (bf16[1,182,128]{2,1,0:T(8,128)(2,1)S(1)}, bf16[1,182,128]{2,1,0:T(8,128)(2,1)S(1)}, u32[]{:S(2)}, u32[]{:S(2)}) collective-permute-start(bf16[1,182,128]{2,1,0:T(8,128)(2,1)S(1)} %get-tuple-element.52), channel_id=1, source_target_pairs={{4,0},{8,4},{12,8},{16,12},{20,16},{24,20},{28,24},{0,28},{5,1},{9... | collective-permute-start | bytes 139784 | tf_op jit(solution)/shard_map/ppermute | solution.py:131
  32.6 0.9 %copy.136.w_ref = bf16[128,1152]{1,0:T(8,128)(2,1)} copy(bf16[128,1152]{0,1:T(8,128)(2,1)S(1)} %bitcast.124) | data formatting | bytes 589824 | tf_op jit(solution)/shard_map/optimization_barrier | solution.py:241
  33.5 1.7 %collective-permute-done = bf16[1,182,128]{2,1,0:T(8,128)(2,1)S(1)} collective-permute-done((bf16[1,182,128]{2,1,0:T(8,128)(2,1)}, bf16[1,182,128]{2,1,0:T(8,128)(2,1)S(1)}, u32[]{:S(2)}, u32[]{:S(2)}) %collective-permute-start) | collective-permute-done | bytes 46624 | tf_op jit(solution)/shard_map/ppermute | solution.py:130
  35.2 0.8 %fusion.23.ext_ref = bf16[10,208,128]{2,1,0:T(8,128)(2,1)} fusion(bf16[1,182,128]{2,1,0:T(8,128)(2,1)S(1)} %collective-permute-done.1, bf16[8,182,128]{2,1,0:T(8,128)(2,1)S(1)} %pad_maximum_fusion.4, bf16[1,182,128]{2,1,0:T(8,128)(2,1)S(1)} %collective-permute-done), kind=kLoop, calls=%fused_computation.46 | loop fusion | flops 2662400 | bytes 998400 | tf_op jit(solution)/shard_map/concatenate | solution.py:132
  36.0 5.1 %shard_map.109 = f32[2,192,128]{2,1,0:T(8,128)} custom-call(s32[24]{0:T(128)} %reshape.247.src_ref, f32[648]{0:T(1024)} %select_n.120.coef_ref, bf16[10,208,128]{2,1,0:T(8,128)(2,1)} %fusion.23.ext_ref, bf16[128,1152]{1,0:T(8,128)(2,1)} %copy.136.w_ref), custom_call_target="tpu_custom_call" | custom-call | tf_op jit(solution)/shard_map/pallas_call | solution.py:85
  41.1 0.2 copy.135
  41.3 0.5 fusion.29
  41.8 0.4 copy-done.1
  42.3 0.5 add_bitcast_fusion
  42.8 0.2 multiply_add_fusion
  43.0 0.4 fusion.27
  43.4 0.4 convolution_add_fusion.3
  43.8 0.2 copy-done.12
  44.1 0.4 fusion.6
  44.4 0.9 %copy.139 = bf16[64,2,6,128]{3,1,2,0:T(2,128)(2,1)} copy(bf16[64,2,6,128]{3,0,1,2:T(8,128)(2,1)S(1)} %fusion.6) | data formatting | bytes 393216 | tf_op jit(solution)/shard_map/optimization_barrier | solution.py:264
  45.3 5.4 %all-to-all-start.2 = ((bf16[64,2,6,128]{3,1,2,0:T(2,128)(2,1)}), bf16[64,2,6,128]{3,1,2,0:T(2,128)(2,1)S(1)}, u32[]{:S(2)}, u32[]{:S(2)}) async-start(bf16[64,2,6,128]{3,1,2,0:T(2,128)(2,1)} %copy.139), calls=%async_computation.2 | async-start | bytes 393216 | tf_op jit(solution)/shard_map/all_to_all | solution.py:265
  50.7 6.6 %shard_map.110 = f32[3,192,128]{2,1,0:T(8,128)} custom-call(s32[24]{0:T(128)} %reshape.247.src_ref, f32[648]{0:T(1024)} %select_n.120.coef_ref, bf16[10,208,128]{2,1,0:T(8,128)(2,1)} %fusion.23.ext_ref, bf16[128,1152]{1,0:T(8,128)(2,1)} %copy.136.w_ref), custom_call_target="tpu_custom_call" | custom-call | tf_op jit(solution)/shard_map/pallas_call | solution.py:85
  57.3 2.8 %all-to-all-done.2 = bf16[64,2,6,128]{3,1,2,0:T(2,128)(2,1)S(1)} async-done(((bf16[64,2,6,128]{3,1,2,0:T(2,128)(2,1)}), bf16[64,2,6,128]{3,1,2,0:T(2,128)(2,1)S(1)}, u32[]{:S(2)}, u32[]{:S(2)}) %all-to-all-start.2) | async-done | bytes 196640 | tf_op jit(solution)/shard_map/all_to_all | solution.py:265
  60.0 0.1 copy.140
  60.2 0.2 fusion.34
  60.5 0.2 fusion.33
  60.7 0.2 convolution_add_fusion.1
  61.0 0.2 fusion.4
  61.2 1.0 %copy.148 = bf16[2,720,128]{2,0,1:T(2,128)(2,1)} copy(bf16[2,720,128]{2,1,0:T(8,128)(2,1)S(1)} %fusion.4) | data formatting | bytes 737280 | tf_op jit(solution)/shard_map/optimization_barrier | solution.py:273
  62.3 3.6 %all-to-all-start.3 = ((bf16[2,720,128]{2,0,1:T(2,128)(2,1)}), bf16[2,720,128]{2,0,1:T(2,128)(2,1)S(1)}, u32[]{:S(2)}, u32[]{:S(2)}) async-start(bf16[2,720,128]{2,0,1:T(2,128)(2,1)} %copy.148), calls=%async_computation.3 | async-start | bytes 737280 | tf_op jit(solution)/shard_map/all_to_all | solution.py:274
  65.9 6.6 %shard_map.111 = f32[3,192,128]{2,1,0:T(8,128)} custom-call(s32[24]{0:T(128)} %reshape.247.src_ref, f32[648]{0:T(1024)} %select_n.120.coef_ref, bf16[10,208,128]{2,1,0:T(8,128)(2,1)} %fusion.23.ext_ref, bf16[128,1152]{1,0:T(8,128)(2,1)} %copy.136.w_ref), custom_call_target="tpu_custom_call" | custom-call | tf_op jit(solution)/shard_map/pallas_call | solution.py:85
  72.6 4.6 %all-to-all-done.3 = bf16[2,720,128]{2,0,1:T(2,128)(2,1)S(1)} async-done(((bf16[2,720,128]{2,0,1:T(2,128)(2,1)}), bf16[2,720,128]{2,0,1:T(2,128)(2,1)S(1)}, u32[]{:S(2)}, u32[]{:S(2)}) %all-to-all-start.3) | async-done | bytes 368672 | tf_op jit(solution)/shard_map/all_to_all | solution.py:274
  77.2 0.1 copy.173
  77.3 1.2 %fusion.18 = bf16[8,180,128]{2,1,0:T(8,128)(2,1)S(1)} fusion(f32[3,192,128]{2,1,0:T(8,128)} %shard_map.111, f32[3,192,128]{2,1,0:T(8,128)S(1)} %copy-done.3, f32[2,192,128]{2,1,0:T(8,128)S(1)} %copy-done.4, bf16[8,180,128]{2,1,0:T(8,128)(2,1)S(1)} %bitcast.121, pred[8]{0:T(512)(128)(4,1)S(1)} %iota_compare_fusion.1, bf16[8,180,128]{2,0,1:T(8,128)(2,1)S(1)} %copy-done), kind=kLoop, calls=%fused_computation.38 | loop fusion | flops 1658880 | bytes 1892360 | tf_op jit(solution)/shard_map/convert_element_type | solution.py:316
  78.5 0.8 copy.152
  (48 shorter events, 0.4 us)
Async XLA Ops:
  3.2 11.6 %copy-start.6 = (bf16[128,9,128]{2,0,1:T(8,128)(2,1)S(1)}, bf16[128,9,128]{2,0,1:T(8,128)(2,1)}, u32[]{:S(2)}) copy-start(bf16[128,9,128]{2,0,1:T(8,128)(2,1)} %param.17) | copy-start | bytes 884740
  3.3 12.4 %copy-start.7 = (f32[64,9,9]{0,2,1:T(8,128)S(1)}, f32[64,9,9]{0,2,1:T(8,128)}, u32[]{:S(2)}) copy-start(f32[64,9,9]{0,2,1:T(8,128)} %param.16) | copy-start | bytes 62212
  4.1 17.8 %all-to-all-start = ((bf16[4,376,128]{2,1,0:T(8,128)(2,1)}), bf16[4,376,128]{2,1,0:T(8,128)(2,1)S(1)}, u32[]{:S(2)}, u32[]{:S(2)}) async-start(bf16[4,376,128]{2,1,0:T(8,128)(2,1)} %pad_maximum_fusion.3), calls=%async_computation | async-start | bytes 770048 | tf_op jit(solution)/shard_map/all_to_all | solution.py:234
  16.6 3.7 %copy-start.8 = (f32[45,192]{1,0:T(8,128)S(1)}, f32[45,192]{1,0:T(8,128)}, u32[]{:S(2)}) copy-start(f32[45,192]{1,0:T(8,128)} %constant.78.clone) | copy-start | bytes 103684
  16.6 3.7 %copy-start.9 = (f32[45,192]{1,0:T(8,128)S(1)}, f32[45,192]{1,0:T(8,128)}, u32[]{:S(2)}) copy-start(f32[45,192]{1,0:T(8,128)} %constant.77.clone) | copy-start | bytes 103684
  16.6 3.7 %copy-start.10 = (f32[16,192]{1,0:T(8,128)S(1)}, f32[16,192]{1,0:T(8,128)}, u32[]{:S(2)}) copy-start(f32[16,192]{1,0:T(8,128)} %constant.80.clone) | copy-start | bytes 36868
  16.6 3.7 %copy-start.11 = (f32[16,192]{1,0:T(8,128)S(1)}, f32[16,192]{1,0:T(8,128)}, u32[]{:S(2)}) copy-start(f32[16,192]{1,0:T(8,128)} %constant.79.clone) | copy-start | bytes 36868
  23.2 9.4 %copy-start.5 = (f32[2,360,128]{2,1,0:T(8,128)S(1)}, f32[2,360,128]{2,1,0:T(8,128)}, u32[]{:S(2)}) copy-start(f32[2,360,128]{2,1,0:T(8,128)} %param.15) | copy-start | bytes 1105924
  23.5 9.1 %copy-start.2 = (bf16[128,9,128]{0,2,1:T(8,128)(2,1)S(1)}, bf16[128,9,128]{0,2,1:T(8,128)(2,1)}, u32[]{:S(2)}) copy-start(bf16[128,9,128]{0,2,1:T(8,128)(2,1)} %copy.125) | copy-start | bytes 884740
  24.4 16.7 %all-to-all-start.1 = ((bf16[2,2,192,128]{3,0,1,2:T(2,128)(2,1)}), bf16[2,2,192,128]{3,0,1,2:T(2,128)(2,1)S(1)}, u32[]{:S(2)}, u32[]{:S(2)}) async-start(bf16[2,2,192,128]{3,0,1,2:T(2,128)(2,1)} %copy.133), calls=%async_computation.1 | async-start | bytes 393216 | tf_op jit(solution)/shard_map/all_to_all | solution.py:257
  29.9 5.3 %collective-permute-start = (bf16[1,182,128]{2,1,0:T(8,128)(2,1)}, bf16[1,182,128]{2,1,0:T(8,128)(2,1)S(1)}, u32[]{:S(2)}, u32[]{:S(2)}) collective-permute-start(bf16[1,182,128]{2,1,0:T(8,128)(2,1)} %get-tuple-element.51), channel_id=1, source_target_pairs={{0,4},{4,8},{8,12},{12,16},{16,20},{20,24},{24,28},{28,0},{1,5},{5... | collective-permute-start | bytes 139784 | tf_op jit(solution)/shard_map/ppermute | solution.py:130
  30.2 5.0 %collective-permute-start.1 = (bf16[1,182,128]{2,1,0:T(8,128)(2,1)S(1)}, bf16[1,182,128]{2,1,0:T(8,128)(2,1)S(1)}, u32[]{:S(2)}, u32[]{:S(2)}) collective-permute-start(bf16[1,182,128]{2,1,0:T(8,128)(2,1)S(1)} %get-tuple-element.52), channel_id=1, source_target_pairs={{4,0},{8,4},{12,8},{16,12},{20,16},{24,20},{28,24},{0,28},{5,1},{9... | collective-permute-start | bytes 139784 | tf_op jit(solution)/shard_map/ppermute | solution.py:131
  41.3 1.0 %copy-start.1 = (bf16[6,360,64]{1,2,0:T(8,128)(2,1)S(1)}, bf16[6,360,64]{1,2,0:T(8,128)(2,1)}, u32[]{:S(2)}) copy-start(bf16[6,360,64]{1,2,0:T(8,128)(2,1)} %get-tuple-element.34) | copy-start | bytes 829444
  43.4 0.7 copy-start.12
  45.3 14.7 %all-to-all-start.2 = ((bf16[64,2,6,128]{3,1,2,0:T(2,128)(2,1)}), bf16[64,2,6,128]{3,1,2,0:T(2,128)(2,1)S(1)}, u32[]{:S(2)}, u32[]{:S(2)}) async-start(bf16[64,2,6,128]{3,1,2,0:T(2,128)(2,1)} %copy.139), calls=%async_computation.2 | async-start | bytes 393216 | tf_op jit(solution)/shard_map/all_to_all | solution.py:265
  62.3 15.0 %all-to-all-start.3 = ((bf16[2,720,128]{2,0,1:T(2,128)(2,1)}), bf16[2,720,128]{2,0,1:T(2,128)(2,1)S(1)}, u32[]{:S(2)}, u32[]{:S(2)}) async-start(bf16[2,720,128]{2,0,1:T(2,128)(2,1)} %copy.148), calls=%async_computation.3 | async-start | bytes 737280 | tf_op jit(solution)/shard_map/all_to_all | solution.py:274
  65.9 11.4 %copy-start = (bf16[8,180,128]{2,0,1:T(8,128)(2,1)S(1)}, bf16[8,180,128]{2,0,1:T(8,128)(2,1)}, u32[]{:S(2)}) copy-start(bf16[8,180,128]{2,0,1:T(8,128)(2,1)} %param.11) | copy-start | bytes 1105924
  65.9 11.4 %copy-start.3 = (f32[3,192,128]{2,1,0:T(8,128)S(1)}, f32[3,192,128]{2,1,0:T(8,128)}, u32[]{:S(2)}) copy-start(f32[3,192,128]{2,1,0:T(8,128)} %shard_map.110) | copy-start | bytes 884740
  65.9 11.4 %copy-start.4 = (f32[2,192,128]{2,1,0:T(8,128)S(1)}, f32[2,192,128]{2,1,0:T(8,128)}, u32[]{:S(2)}) copy-start(f32[2,192,128]{2,1,0:T(8,128)} %shard_map.109) | copy-start | bytes 589828

commit v13 on v12

--- a/solution.py
+++ b/solution.py
@@ -77,8 +77,10 @@
 
 def disco_piece(src_rows, coef, ext, weight_flat, piece, pieces, lon_count):
     slot_total = ext.shape[0] - 2
-    first = piece * slot_total // pieces
-    last = (piece + 1) * slot_total // pieces
+    bounds = [i * slot_total // pieces for i in range(pieces + 1)]
+    if pieces == 3 and slot_total >= 8:
+        bounds = [0, slot_total // 8, slot_total // 2, slot_total]
+    first, last = bounds[piece], bounds[piece + 1]
     lon_pad, channels = ext.shape[1:]
     out_rows = round_up(lon_count, CHUNK)
     smem = pltpu.MemorySpace.SMEM if hasattr(pltpu, "MemorySpace") else pltpu.SMEM

time: 80 us -> 78.2 us (0.978)
  waiting for transfers between devices: 10.3 us -> 8.85 us
    all_to_all x1, waiting for transfers between devices: 4.64 us -> 3.17 us  [spectral_by_modes(): lax.all_to_all(spectral_rows, 'lon', split_axis=1, concat_axis=0, tiled=T...]
where the time goes in v13:
time: 78.2 us; the launch traced here: 77.5 us
  starting transfers between devices  22.9 us (29%)
  Pallas kernels  18 us (23%)
  local copies, waits for them, and re-layouts  11.6 us (15%)
  other arithmetic  9.43 us (12%)
  waiting for transfers between devices  8.85 us (11%)
  matrix products  4.29 us (5%)
  between operations  2.54 us (3%)
    pallas_call x3, Pallas kernels, disco_piece(): pl.pallas_call(functools.partial(disco_body, first, last), out_shape=jax....  18 us
    all_to_all x1, starting transfers between devices, spectral_by_modes(): lax.all_to_all(jnp.concatenate([body, edges], axis=1), 'lon', split_axis=...  6.32 us
    all_to_all x1, starting transfers between devices, spectral_by_modes(): lax.all_to_all(returned, both, split_axis=0, concat_axis=2, tiled=True)  5.41 us
    all_to_all x1, starting transfers between devices, spectral_by_modes(): lax.all_to_all(spectra, both, split_axis=2, concat_axis=0, tiled=True)  4.85 us
    dot_general x13, matrix products, dot_split(): term = jnp.einsum(spec, lp, rp, preferred_element_type=jnp.float32)  4.29 us
    all_to_all x1, starting transfers between devices, spectral_by_modes(): lax.all_to_all(spectral_rows, 'lon', split_axis=1, concat_axis=0, tiled=T...  3.64 us
    all_to_all x1, waiting for transfers between devices, spectral_by_modes(): lax.all_to_all(spectral_rows, 'lon', split_axis=1, concat_axis=0, tiled=T...  3.17 us
    all_to_all x1, waiting for transfers between devices, spectral_by_modes(): lax.all_to_all(returned, both, split_axis=0, concat_axis=2, tiled=True)  2.75 us
  transfers between devices with their start and end apart: 6, of which 4 were waited for; matrix products, arithmetic and copies ran while one was open for 13% of the time, Pallas kernels for 23%

profile of v13, /device:TPU:0, one launch (start us, length us, event | category | flops | bytes accessed | tf_op | source)
XLA Modules:
  0.0 77.5 jit_solution(15036674502263940563)
XLA Ops:
  0.0 1.4 %fusion.42 = (s32[1]{0:T(128)}, s32[1]{0:T(128)}) fusion(s32[8]{0:T(128)} %param.12, s32[]{:T(128)S(6)} %max.10, s32[]{:T(128)S(6)} %select_n.111), kind=kLoop, calls=%fused_computation.95 | loop fusion | bytes 24 | tf_op jit(solution)/shard_map/dynamic_slice | solution.py:112
  1.4 0.7 iota_compare_fusion.1
  2.1 1.1 %copy_select_fusion = bf16[8,180,128]{2,1,0:T(8,128)(2,1)S(1)} fusion(bf16[8,180,128]{2,0,1:T(8,128)(2,1)} %param.11, pred[8]{0:T(512)(128)(4,1)S(1)} %iota_compare_fusion.1), kind=kLoop, calls=%fused_computation.49 | loop fusion | flops 184320 | bytes 737288 | tf_op jit(solution)/shard_map/jit(_where)/select_n | solution.py:294
  3.2 0.1 reshape.246
  3.3 0.8 pad_maximum_fusion.3
  4.1 6.3 %all-to-all-start = ((bf16[4,376,128]{2,1,0:T(8,128)(2,1)}), bf16[4,376,128]{2,1,0:T(8,128)(2,1)S(1)}, u32[]{:S(2)}, u32[]{:S(2)}) async-start(bf16[4,376,128]{2,1,0:T(8,128)(2,1)} %pad_maximum_fusion.3), calls=%async_computation | async-start | bytes 770048 | tf_op jit(solution)/shard_map/all_to_all | solution.py:236
  11.8 0.7 compare_select_fusion.2
  13.1 0.1 copy.119
  13.2 0.7 reshape.247.src_ref
  13.9 0.7 fusion.35
  14.6 0.1 copy.120
  14.7 0.1 reshape.254
  14.8 0.9 %copy.125 = bf16[128,9,128]{0,2,1:T(8,128)(2,1)} copy(bf16[128,9,128]{2,0,1:T(8,128)(2,1)S(1)} %copy-done.6) | data formatting | bytes 589824 | tf_op args[6]
  15.7 0.3 copy.121
  16.0 0.6 gather_fusion
  16.7 0.7 compare_or_fusion
  17.4 0.1 pad.21.clone
  17.5 0.1 pad_add_fusion.1
  17.6 0.1 maximum_select_fusion
  17.7 0.7 select_n.120.coef_ref
  18.4 1.9 %fusion.21 = (bf16[6,360,64]{1,2,0:T(8,128)(2,1)}, bf16[6,360,64]{1,2,0:T(8,128)(2,1)S(1)}) fusion(f32[24,360,64]{1,2,0:T(8,128)} %param.13, s32[]{:T(128)S(6)} %select_n.113), kind=kLoop, calls=%fused_computation.44 | loop fusion | flops 552960 | bytes 1105924 | tf_op jit(solution)/shard_map/convert_element_type | solution.py:34
  20.3 0.3 fusion.19
  20.7 1.2 %all-to-all-done = bf16[4,376,128]{2,1,0:T(8,128)(2,1)S(1)} async-done(((bf16[4,376,128]{2,1,0:T(8,128)(2,1)}), bf16[4,376,128]{2,1,0:T(8,128)(2,1)S(1)}, u32[]{:S(2)}, u32[]{:S(2)}) %all-to-all-start) | async-done | bytes 385056 | tf_op jit(solution)/shard_map/all_to_all | solution.py:236
  22.0 0.1 reshape.250
  22.1 0.1 reshape.251
  22.2 0.3 fusion.44
  22.5 0.3 fusion.43
  22.8 0.1 pad_maximum_fusion.4
  22.9 0.3 fusion.9
  23.2 0.3 fusion.10
  23.6 0.9 %copy.133 = bf16[2,2,192,128]{3,0,1,2:T(2,128)(2,1)} copy(bf16[2,2,192,128]{3,2,0,1:T(8,128)(2,1)S(1)} %pad_maximum_fusion.5) | data formatting | bytes 393216 | tf_op jit(solution)/shard_map/optimization_barrier | solution.py:256
  24.4 4.8 %all-to-all-start.1 = ((bf16[2,2,192,128]{3,0,1,2:T(2,128)(2,1)}), bf16[2,2,192,128]{3,0,1,2:T(2,128)(2,1)S(1)}, u32[]{:S(2)}, u32[]{:S(2)}) async-start(bf16[2,2,192,128]{3,0,1,2:T(2,128)(2,1)} %copy.133), calls=%async_computation.1 | async-start | bytes 393216 | tf_op jit(solution)/shard_map/all_to_all | solution.py:259
  29.3 0.6 constant_dynamic-slice_fusion
  29.9 0.3 collective-permute-start
  30.2 2.4 %collective-permute-start.1 = (bf16[1,182,128]{2,1,0:T(8,128)(2,1)S(1)}, bf16[1,182,128]{2,1,0:T(8,128)(2,1)S(1)}, u32[]{:S(2)}, u32[]{:S(2)}) collective-permute-start(bf16[1,182,128]{2,1,0:T(8,128)(2,1)S(1)} %get-tuple-element.52), channel_id=1, source_target_pairs={{4,0},{8,4},{12,8},{16,12},{20,16},{24,20},{28,24},{0,28},{5,1},{9... | collective-permute-start | bytes 139784 | tf_op jit(solution)/shard_map/ppermute | solution.py:133
  32.6 0.9 %copy.136.w_ref = bf16[128,1152]{1,0:T(8,128)(2,1)} copy(bf16[128,1152]{0,1:T(8,128)(2,1)S(1)} %bitcast.124) | data formatting | bytes 589824 | tf_op jit(solution)/shard_map/optimization_barrier | solution.py:243
  33.5 1.7 %collective-permute-done = bf16[1,182,128]{2,1,0:T(8,128)(2,1)S(1)} collective-permute-done((bf16[1,182,128]{2,1,0:T(8,128)(2,1)}, bf16[1,182,128]{2,1,0:T(8,128)(2,1)S(1)}, u32[]{:S(2)}, u32[]{:S(2)}) %collective-permute-start) | collective-permute-done | bytes 46624 | tf_op jit(solution)/shard_map/ppermute | solution.py:132
  35.2 0.8 %fusion.23.ext_ref = bf16[10,208,128]{2,1,0:T(8,128)(2,1)} fusion(bf16[1,182,128]{2,1,0:T(8,128)(2,1)S(1)} %collective-permute-done.1, bf16[8,182,128]{2,1,0:T(8,128)(2,1)S(1)} %pad_maximum_fusion.4, bf16[1,182,128]{2,1,0:T(8,128)(2,1)S(1)} %collective-permute-done), kind=kLoop, calls=%fused_computation.46 | loop fusion | flops 2662400 | bytes 998400 | tf_op jit(solution)/shard_map/concatenate | solution.py:134
  36.0 3.3 %shard_map.109 = f32[1,192,128]{2,1,0:T(8,128)} custom-call(s32[24]{0:T(128)} %reshape.247.src_ref, f32[648]{0:T(1024)} %select_n.120.coef_ref, bf16[10,208,128]{2,1,0:T(8,128)(2,1)} %fusion.23.ext_ref, bf16[128,1152]{1,0:T(8,128)(2,1)} %copy.136.w_ref), custom_call_target="tpu_custom_call" | custom-call | tf_op jit(solution)/shard_map/pallas_call | solution.py:87
  39.3 0.2 copy.135
  39.5 0.5 fusion.29
  40.0 0.4 copy-done.1
  40.5 0.5 add_bitcast_fusion
  41.0 0.2 multiply_add_fusion
  41.2 0.4 fusion.27
  41.6 0.4 convolution_add_fusion.3
  42.0 0.2 copy-done.12
  42.2 0.4 fusion.6
  42.6 0.9 %copy.139 = bf16[64,2,6,128]{3,1,2,0:T(2,128)(2,1)} copy(bf16[64,2,6,128]{3,0,1,2:T(8,128)(2,1)S(1)} %fusion.6) | data formatting | bytes 393216 | tf_op jit(solution)/shard_map/optimization_barrier | solution.py:266
  43.5 5.4 %all-to-all-start.2 = ((bf16[64,2,6,128]{3,1,2,0:T(2,128)(2,1)}), bf16[64,2,6,128]{3,1,2,0:T(2,128)(2,1)S(1)}, u32[]{:S(2)}, u32[]{:S(2)}) async-start(bf16[64,2,6,128]{3,1,2,0:T(2,128)(2,1)} %copy.139), calls=%async_computation.2 | async-start | bytes 393216 | tf_op jit(solution)/shard_map/all_to_all | solution.py:267
  48.9 6.6 %shard_map.110 = f32[3,192,128]{2,1,0:T(8,128)} custom-call(s32[24]{0:T(128)} %reshape.247.src_ref, f32[648]{0:T(1024)} %select_n.120.coef_ref, bf16[10,208,128]{2,1,0:T(8,128)(2,1)} %fusion.23.ext_ref, bf16[128,1152]{1,0:T(8,128)(2,1)} %copy.136.w_ref), custom_call_target="tpu_custom_call" | custom-call | tf_op jit(solution)/shard_map/pallas_call | solution.py:87
  55.5 2.8 %all-to-all-done.2 = bf16[64,2,6,128]{3,1,2,0:T(2,128)(2,1)S(1)} async-done(((bf16[64,2,6,128]{3,1,2,0:T(2,128)(2,1)}), bf16[64,2,6,128]{3,1,2,0:T(2,128)(2,1)S(1)}, u32[]{:S(2)}, u32[]{:S(2)}) %all-to-all-start.2) | async-done | bytes 196640 | tf_op jit(solution)/shard_map/all_to_all | solution.py:267
  58.2 0.1 copy.140
  58.4 0.2 fusion.34
  58.7 0.2 fusion.33
  58.9 0.2 convolution_add_fusion.1
  59.2 0.3 fusion.4
  59.4 1.0 %copy.148 = bf16[2,720,128]{2,0,1:T(2,128)(2,1)} copy(bf16[2,720,128]{2,1,0:T(8,128)(2,1)S(1)} %fusion.4) | data formatting | bytes 737280 | tf_op jit(solution)/shard_map/optimization_barrier | solution.py:275
  60.4 3.6 %all-to-all-start.3 = ((bf16[2,720,128]{2,0,1:T(2,128)(2,1)}), bf16[2,720,128]{2,0,1:T(2,128)(2,1)S(1)}, u32[]{:S(2)}, u32[]{:S(2)}) async-start(bf16[2,720,128]{2,0,1:T(2,128)(2,1)} %copy.148), calls=%async_computation.3 | async-start | bytes 737280 | tf_op jit(solution)/shard_map/all_to_all | solution.py:276
  64.1 8.1 %shard_map.111 = f32[4,192,128]{2,1,0:T(8,128)} custom-call(s32[24]{0:T(128)} %reshape.247.src_ref, f32[648]{0:T(1024)} %select_n.120.coef_ref, bf16[10,208,128]{2,1,0:T(8,128)(2,1)} %fusion.23.ext_ref, bf16[128,1152]{1,0:T(8,128)(2,1)} %copy.136.w_ref), custom_call_target="tpu_custom_call" | custom-call | tf_op jit(solution)/shard_map/pallas_call | solution.py:87
  72.3 3.2 %all-to-all-done.3 = bf16[2,720,128]{2,0,1:T(2,128)(2,1)S(1)} async-done(((bf16[2,720,128]{2,0,1:T(2,128)(2,1)}), bf16[2,720,128]{2,0,1:T(2,128)(2,1)S(1)}, u32[]{:S(2)}, u32[]{:S(2)}) %all-to-all-start.3) | async-done | bytes 368672 | tf_op jit(solution)/shard_map/all_to_all | solution.py:276
  75.4 0.1 copy.173
  75.5 1.2 %fusion.18 = bf16[8,180,128]{2,1,0:T(8,128)(2,1)S(1)} fusion(f32[4,192,128]{2,1,0:T(8,128)} %shard_map.111, f32[3,192,128]{2,1,0:T(8,128)S(1)} %copy-done.3, f32[1,192,128]{2,1,0:T(8,128)S(1)} %copy-done.4, bf16[8,180,128]{2,1,0:T(8,128)(2,1)S(1)} %bitcast.121, pred[8]{0:T(512)(128)(4,1)S(1)} %iota_compare_fusion.1, bf16[8,180,128]{2,0,1:T(8,128)(2,1)S(1)} %copy-done), kind=kLoop, calls=%fused_computation.38 | loop fusion | flops 1658880 | bytes 1892360 | tf_op jit(solution)/shard_map/convert_element_type | solution.py:318
  76.8 0.8 %copy.152 = bf16[8,180,128]{2,0,1:T(8,128)(2,1)} copy(bf16[8,180,128]{2,1,0:T(8,128)(2,1)S(1)} %fusion.18) | data formatting | bytes 737280 | tf_op jit(solution)/shard_map/convert_element_type | solution.py:318
  (48 shorter events, 0.4 us)
Async XLA Ops:
  3.2 11.6 %copy-start.6 = (bf16[128,9,128]{2,0,1:T(8,128)(2,1)S(1)}, bf16[128,9,128]{2,0,1:T(8,128)(2,1)}, u32[]{:S(2)}) copy-start(bf16[128,9,128]{2,0,1:T(8,128)(2,1)} %param.17) | copy-start | bytes 884740
  3.3 12.4 %copy-start.7 = (f32[64,9,9]{0,2,1:T(8,128)S(1)}, f32[64,9,9]{0,2,1:T(8,128)}, u32[]{:S(2)}) copy-start(f32[64,9,9]{0,2,1:T(8,128)} %param.16) | copy-start | bytes 62212
  4.1 17.8 %all-to-all-start = ((bf16[4,376,128]{2,1,0:T(8,128)(2,1)}), bf16[4,376,128]{2,1,0:T(8,128)(2,1)S(1)}, u32[]{:S(2)}, u32[]{:S(2)}) async-start(bf16[4,376,128]{2,1,0:T(8,128)(2,1)} %pad_maximum_fusion.3), calls=%async_computation | async-start | bytes 770048 | tf_op jit(solution)/shard_map/all_to_all | solution.py:236
  16.6 3.7 %copy-start.8 = (f32[45,192]{1,0:T(8,128)S(1)}, f32[45,192]{1,0:T(8,128)}, u32[]{:S(2)}) copy-start(f32[45,192]{1,0:T(8,128)} %constant.78.clone) | copy-start | bytes 103684
  16.6 3.7 %copy-start.9 = (f32[45,192]{1,0:T(8,128)S(1)}, f32[45,192]{1,0:T(8,128)}, u32[]{:S(2)}) copy-start(f32[45,192]{1,0:T(8,128)} %constant.77.clone) | copy-start | bytes 103684
  16.6 3.7 %copy-start.10 = (f32[16,192]{1,0:T(8,128)S(1)}, f32[16,192]{1,0:T(8,128)}, u32[]{:S(2)}) copy-start(f32[16,192]{1,0:T(8,128)} %constant.80.clone) | copy-start | bytes 36868
  16.6 3.7 %copy-start.11 = (f32[16,192]{1,0:T(8,128)S(1)}, f32[16,192]{1,0:T(8,128)}, u32[]{:S(2)}) copy-start(f32[16,192]{1,0:T(8,128)} %constant.79.clone) | copy-start | bytes 36868
  23.2 9.4 %copy-start.5 = (f32[2,360,128]{2,1,0:T(8,128)S(1)}, f32[2,360,128]{2,1,0:T(8,128)}, u32[]{:S(2)}) copy-start(f32[2,360,128]{2,1,0:T(8,128)} %param.15) | copy-start | bytes 1105924
  23.5 9.1 %copy-start.2 = (bf16[128,9,128]{0,2,1:T(8,128)(2,1)S(1)}, bf16[128,9,128]{0,2,1:T(8,128)(2,1)}, u32[]{:S(2)}) copy-start(bf16[128,9,128]{0,2,1:T(8,128)(2,1)} %copy.125) | copy-start | bytes 884740
  24.4 14.9 %all-to-all-start.1 = ((bf16[2,2,192,128]{3,0,1,2:T(2,128)(2,1)}), bf16[2,2,192,128]{3,0,1,2:T(2,128)(2,1)S(1)}, u32[]{:S(2)}, u32[]{:S(2)}) async-start(bf16[2,2,192,128]{3,0,1,2:T(2,128)(2,1)} %copy.133), calls=%async_computation.1 | async-start | bytes 393216 | tf_op jit(solution)/shard_map/all_to_all | solution.py:259
  29.9 5.3 %collective-permute-start = (bf16[1,182,128]{2,1,0:T(8,128)(2,1)}, bf16[1,182,128]{2,1,0:T(8,128)(2,1)S(1)}, u32[]{:S(2)}, u32[]{:S(2)}) collective-permute-start(bf16[1,182,128]{2,1,0:T(8,128)(2,1)} %get-tuple-element.51), channel_id=1, source_target_pairs={{0,4},{4,8},{8,12},{12,16},{16,20},{20,24},{24,28},{28,0},{1,5},{5... | collective-permute-start | bytes 139784 | tf_op jit(solution)/shard_map/ppermute | solution.py:132
  30.2 5.0 %collective-permute-start.1 = (bf16[1,182,128]{2,1,0:T(8,128)(2,1)S(1)}, bf16[1,182,128]{2,1,0:T(8,128)(2,1)S(1)}, u32[]{:S(2)}, u32[]{:S(2)}) collective-permute-start(bf16[1,182,128]{2,1,0:T(8,128)(2,1)S(1)} %get-tuple-element.52), channel_id=1, source_target_pairs={{4,0},{8,4},{12,8},{16,12},{20,16},{24,20},{28,24},{0,28},{5,1},{9... | collective-permute-start | bytes 139784 | tf_op jit(solution)/shard_map/ppermute | solution.py:133
  39.5 1.0 %copy-start.1 = (bf16[6,360,64]{1,2,0:T(8,128)(2,1)S(1)}, bf16[6,360,64]{1,2,0:T(8,128)(2,1)}, u32[]{:S(2)}) copy-start(bf16[6,360,64]{1,2,0:T(8,128)(2,1)} %get-tuple-element.34) | copy-start | bytes 829444
  41.6 0.7 copy-start.12
  43.5 14.7 %all-to-all-start.2 = ((bf16[64,2,6,128]{3,1,2,0:T(2,128)(2,1)}), bf16[64,2,6,128]{3,1,2,0:T(2,128)(2,1)S(1)}, u32[]{:S(2)}, u32[]{:S(2)}) async-start(bf16[64,2,6,128]{3,1,2,0:T(2,128)(2,1)} %copy.139), calls=%async_computation.2 | async-start | bytes 393216 | tf_op jit(solution)/shard_map/all_to_all | solution.py:267
  60.4 15.0 %all-to-all-start.3 = ((bf16[2,720,128]{2,0,1:T(2,128)(2,1)}), bf16[2,720,128]{2,0,1:T(2,128)(2,1)S(1)}, u32[]{:S(2)}, u32[]{:S(2)}) async-start(bf16[2,720,128]{2,0,1:T(2,128)(2,1)} %copy.148), calls=%async_computation.3 | async-start | bytes 737280 | tf_op jit(solution)/shard_map/all_to_all | solution.py:276
  64.1 11.4 %copy-start = (bf16[8,180,128]{2,0,1:T(8,128)(2,1)S(1)}, bf16[8,180,128]{2,0,1:T(8,128)(2,1)}, u32[]{:S(2)}) copy-start(bf16[8,180,128]{2,0,1:T(8,128)(2,1)} %param.11) | copy-start | bytes 1105924
  64.1 11.4 %copy-start.3 = (f32[3,192,128]{2,1,0:T(8,128)S(1)}, f32[3,192,128]{2,1,0:T(8,128)}, u32[]{:S(2)}) copy-start(f32[3,192,128]{2,1,0:T(8,128)} %shard_map.110) | copy-start | bytes 884740
  64.1 11.4 %copy-start.4 = (f32[1,192,128]{2,1,0:T(8,128)S(1)}, f32[1,192,128]{2,1,0:T(8,128)}, u32[]{:S(2)}) copy-start(f32[1,192,128]{2,1,0:T(8,128)} %shard_map.109) | copy-start | bytes 294916

commit v14 on v13

--- a/solution.py
+++ b/solution.py
@@ -160,7 +160,7 @@
 
 
 def spectral_by_channels(
-    masked, legendre, quad_weights, spectral_filter, trig_parts, live_rows, disco_work, prep
+    masked, legendre, quad_weights, spectral_filter, trig_parts, live_rows, disco_work, prep, raw
 ):
     ext = halo_extend(masked, live_rows)
     channels = masked.shape[2]
@@ -223,15 +223,15 @@
 
 
 def spectral_by_modes(
-    masked, legendre, quad_weights, spectral_filter, trig_parts, live_rows, disco_work, prep
+    masked, legendre, quad_weights, spectral_filter, trig_parts, live_rows, disco_work, prep, raw
 ):
     both = ("lat", "lon")
     lon_total = lax.axis_size("lon")
     mode_share = legendre.shape[0] // lon_total
     row_count, lon_count, channels = masked.shape
     share = row_count // lon_total
-    body = masked.reshape(lon_total, share * lon_count, channels)
-    edges = jnp.concatenate([masked[:, 0], masked[:, lon_count - 1]], axis=0)
+    body = raw.reshape(lon_total, share * lon_count, channels)
+    edges = jnp.concatenate([raw[:, 0], raw[:, lon_count - 1]], axis=0)
     edges = jnp.broadcast_to(edges[None], (lon_total, 2 * row_count, channels))
     received = lax.all_to_all(
         jnp.concatenate([body, edges], axis=1), "lon", split_axis=0, concat_axis=0, tiled=True
@@ -243,6 +243,8 @@
     received, legendre_parts, prep = lax.optimization_barrier((received, legendre_parts, prep))
     portion = received[:, : share * lon_count].reshape(lon_total, share, lon_count, channels)
     portion = portion.transpose(1, 0, 2, 3).reshape(share, lon_total * lon_count, channels)
+    portion_live = lax.axis_index("lon") * share + jnp.arange(share) < live_rows
+    portion = jnp.where(portion_live[:, None, None], portion, jnp.zeros_like(portion))
     edge_block = received[:, share * lon_count :]
     lon_index = lax.axis_index("lon")
     left = lax.dynamic_index_in_dim(edge_block, (lon_index - 1) % lon_total, 0, keepdims=False)
@@ -311,6 +313,7 @@
         live_rows,
         disco_work,
         (src_rows, coef, weight_flat),
+        grad_output,
     )
     disco_full = jnp.concatenate(disco_parts, axis=0)
     disco_term = disco_full[:, :lon_count, :]

time: 78.2 us -> 77.7 us (level)
    ppermute x1, waiting for transfers between devices: 1.67 us -> 0.21 us  [lat_extend(): from_above = lax.ppermute(last_row, 'lat', lat_up)]
    unnamed x29 -> x22, local copies, waits for them, and re-layouts: 1.97 us -> 0.82 us
    mul x1, local copies, waits for them, and re-layouts: 0.02 us -> 1.04 us  [filter_modes(): filter_real * real_part + filter_imag * imag_part]
  transfers between devices with their start and end apart: 6 -> 6, of which waited for: 4 -> 5; matrix products, arithmetic and copies ran while one was open for 13% -> 13% of each run, Pallas kernels for 23% -> 23%
where the time goes in v14:
time: 77.7 us; the launch traced here: 77 us
  starting transfers between devices  22.7 us (29%)
  Pallas kernels  18 us (23%)
  local copies, waits for them, and re-layouts  11.5 us (15%)
  other arithmetic  9.53 us (12%)
  waiting for transfers between devices  8.38 us (11%)
  matrix products  4.32 us (6%)
  between operations  2.57 us (3%)
    pallas_call x3, Pallas kernels, disco_piece(): pl.pallas_call(functools.partial(disco_body, first, last), out_shape=jax....  18 us
    all_to_all x1, starting transfers between devices, spectral_by_modes(): lax.all_to_all(jnp.concatenate([body, edges], axis=1), 'lon', split_axis=...  6.32 us
    all_to_all x1, starting transfers between devices, spectral_by_modes(): lax.all_to_all(returned, both, split_axis=0, concat_axis=2, tiled=True)  5.88 us
    dot_general x13, matrix products, dot_split(): term = jnp.einsum(spec, lp, rp, preferred_element_type=jnp.float32)  4.32 us
    all_to_all x1, starting transfers between devices, spectral_by_modes(): lax.all_to_all(spectra, both, split_axis=2, concat_axis=0, tiled=True)  4.19 us
    all_to_all x1, starting transfers between devices, spectral_by_modes(): lax.all_to_all(spectral_rows, 'lon', split_axis=1, concat_axis=0, tiled=T...  3.64 us
    all_to_all x1, waiting for transfers between devices, spectral_by_modes(): lax.all_to_all(spectral_rows, 'lon', split_axis=1, concat_axis=0, tiled=T...  3.16 us
    all_to_all x1, waiting for transfers between devices, spectral_by_modes(): lax.all_to_all(returned, both, split_axis=0, concat_axis=2, tiled=True)  2.75 us
  transfers between devices with their start and end apart: 6, of which 5 were waited for; matrix products, arithmetic and copies ran while one was open for 13% of the time, Pallas kernels for 23%

profile of v14, /device:TPU:0, one launch (start us, length us, event | category | flops | bytes accessed | tf_op | source)
XLA Modules:
  0.0 77.0 jit_solution(5440305017766608242)
XLA Ops:
  0.0 1.4 %fusion.41 = (s32[1]{0:T(128)}, s32[1]{0:T(128)}) fusion(s32[8]{0:T(128)} %param.12, s32[]{:T(128)S(6)} %max.10, s32[]{:T(128)S(6)} %select_n.124), kind=kLoop, calls=%fused_computation.96 | loop fusion | bytes 24 | tf_op jit(solution)/shard_map/dynamic_slice | solution.py:112
  1.4 0.7 iota_compare_fusion.1
  2.1 0.7 slice_bitcast_fusion.9
  2.8 1.1 %broadcast_select_fusion = (bf16[8,180,128]{2,1,0:T(8,128)(2,1)S(1)}, bf16[8,180,128]{2,1,0:T(8,128)(2,1)S(1)}) fusion(pred[8]{0:T(512)(128)(4,1)S(1)} %iota_compare_fusion.1, bf16[8,180,128]{2,0,1:T(8,128)(2,1)} %param.11), kind=kLoop, calls=%fused_computation.50 | loop fusion | flops 184320 | bytes 1105928 | tf_op jit(solution)/shard_map/jit(_where)/select_n | solution.py:296
  3.9 0.1 reshape.253
  4.0 0.8 %pad_maximum_fusion.3 = bf16[4,376,128]{2,1,0:T(8,128)(2,1)} fusion(bf16[4,16,128]{2,1,0:T(8,128)(2,1)S(1)} %broadcast_in_dim.84, bf16[4,360,128]{2,1,0:T(8,128)(2,1)S(1)} %reshape.253), kind=kLoop, calls=%fused_computation.47 | loop fusion | flops 770048 | bytes 770048 | tf_op jit(solution)/shard_map/concatenate | solution.py:237
  4.7 6.3 %all-to-all-start = ((bf16[4,376,128]{2,1,0:T(8,128)(2,1)}), bf16[4,376,128]{2,1,0:T(8,128)(2,1)S(1)}, u32[]{:S(2)}, u32[]{:S(2)}) async-start(bf16[4,376,128]{2,1,0:T(8,128)(2,1)} %pad_maximum_fusion.3), calls=%async_computation | async-start | bytes 770048 | tf_op jit(solution)/shard_map/all_to_all | solution.py:236
  12.5 0.7 compare_select_fusion.2
  13.8 0.7 fusion.35
  14.5 0.1 copy.124
  14.6 0.1 reshape.260
  14.7 0.3 copy.125
  15.0 0.6 gather_fusion
  15.8 0.7 compare_or_fusion
  16.5 0.1 pad.21.clone
  16.6 0.1 pad_add_fusion.1
  16.6 0.1 maximum_select_fusion
  16.7 0.1 copy.123
  16.8 0.6 reshape.254.src_ref
  17.4 0.2 copy.129
  17.7 0.7 select_n.133.coef_ref
  18.4 0.7 add_compare_fusion
  19.1 1.2 %fusion.21 = (bf16[6,360,64]{1,2,0:T(8,128)(2,1)S(1)}, bf16[6,360,64]{1,2,0:T(8,128)(2,1)S(1)}) fusion(f32[24,360,64]{1,2,0:T(8,128)} %param.13, s32[]{:T(128)S(6)} %select_n.126), kind=kLoop, calls=%fused_computation.44 | loop fusion | flops 552960 | bytes 1105924 | tf_op jit(solution)/shard_map/convert_element_type | solution.py:34
  20.3 0.4 fusion.19
  20.7 1.9 %all-to-all-done = bf16[4,376,128]{2,1,0:T(8,128)(2,1)S(1)} async-done(((bf16[4,376,128]{2,1,0:T(8,128)(2,1)}), bf16[4,376,128]{2,1,0:T(8,128)(2,1)S(1)}, u32[]{:S(2)}, u32[]{:S(2)}) %all-to-all-start) | async-done | bytes 385056 | tf_op jit(solution)/shard_map/all_to_all | solution.py:236
  22.7 0.1 select_bitcast_fusion
  22.9 0.3 fusion.43
  23.2 0.3 fusion.42
  23.5 0.3 fusion.9
  23.9 0.3 fusion.10
  24.2 0.1 pad_maximum_fusion.4
  24.3 0.9 %copy.137 = bf16[2,2,192,128]{3,0,1,2:T(2,128)(2,1)} copy(bf16[2,2,192,128]{3,2,0,1:T(8,128)(2,1)S(1)} %pad_maximum_fusion.5) | data formatting | bytes 393216 | tf_op jit(solution)/shard_map/optimization_barrier | solution.py:258
  25.2 4.2 %all-to-all-start.1 = ((bf16[2,2,192,128]{3,0,1,2:T(2,128)(2,1)}), bf16[2,2,192,128]{3,0,1,2:T(2,128)(2,1)S(1)}, u32[]{:S(2)}, u32[]{:S(2)}) async-start(bf16[2,2,192,128]{3,0,1,2:T(2,128)(2,1)} %copy.137), calls=%async_computation.1 | async-start | bytes 393216 | tf_op jit(solution)/shard_map/all_to_all | solution.py:261
  29.4 0.3 collective-permute-start
  29.7 2.4 %collective-permute-start.1 = (bf16[1,182,128]{2,1,0:T(8,128)(2,1)S(1)}, bf16[1,182,128]{2,1,0:T(8,128)(2,1)S(1)}, u32[]{:S(2)}, u32[]{:S(2)}) collective-permute-start(bf16[1,182,128]{2,1,0:T(8,128)(2,1)S(1)} %get-tuple-element.52), channel_id=1, source_target_pairs={{4,0},{8,4},{12,8},{16,12},{20,16},{24,20},{28,24},{0,28},{5,1},{9... | collective-permute-start | bytes 139784 | tf_op jit(solution)/shard_map/ppermute | solution.py:133
  32.1 1.0 %slice_bitcast_fusion.1 = (f32[360,128]{1,0:T(8,128)S(1)}, f32[360,128]{1,0:T(8,128)S(1)}) fusion(f32[2,360,128]{2,1,0:T(8,128)} %param.15), kind=kLoop, calls=%fused_computation.60 | loop fusion | bytes 737280 | tf_op jit(solution)/shard_map/mul | solution.py:218
  33.1 0.9 %copy.140.w_ref = bf16[128,1152]{1,0:T(8,128)(2,1)} copy(bf16[128,1152]{0,1:T(8,128)(2,1)S(1)} %bitcast.124) | data formatting | bytes 589824 | tf_op jit(solution)/shard_map/optimization_barrier | solution.py:243
  34.0 0.2 collective-permute-done
  34.2 0.9 %fusion.23.ext_ref = bf16[10,208,128]{2,1,0:T(8,128)(2,1)} fusion(bf16[1,182,128]{2,1,0:T(8,128)(2,1)S(1)} %collective-permute-done.1, bf16[8,182,128]{2,1,0:T(8,128)(2,1)S(1)} %pad_maximum_fusion.4, bf16[1,182,128]{2,1,0:T(8,128)(2,1)S(1)} %collective-permute-done), kind=kLoop, calls=%fused_computation.46 | loop fusion | flops 2662400 | bytes 998400 | tf_op jit(solution)/shard_map/concatenate | solution.py:134
  35.1 3.3 %shard_map.109 = f32[1,192,128]{2,1,0:T(8,128)} custom-call(s32[24]{0:T(128)} %reshape.254.src_ref, f32[648]{0:T(1024)} %select_n.133.coef_ref, bf16[10,208,128]{2,1,0:T(8,128)(2,1)} %fusion.23.ext_ref, bf16[128,1152]{1,0:T(8,128)(2,1)} %copy.140.w_ref), custom_call_target="tpu_custom_call" | custom-call | tf_op jit(solution)/shard_map/pallas_call | solution.py:87
  38.4 0.3 all-to-all-done.1
  38.7 0.2 copy.139
  38.9 0.5 fusion.29
  39.4 0.5 add_bitcast_fusion
  39.9 0.2 multiply_add_fusion
  40.2 0.4 fusion.27
  40.5 0.4 convolution_add_fusion.3
  40.9 0.2 copy-done.9
  41.2 0.4 fusion.6
  41.6 0.9 %copy.143 = bf16[64,2,6,128]{3,1,2,0:T(2,128)(2,1)} copy(bf16[64,2,6,128]{3,0,1,2:T(8,128)(2,1)S(1)} %fusion.6) | data formatting | bytes 393216 | tf_op jit(solution)/shard_map/optimization_barrier | solution.py:268
  42.4 5.9 %all-to-all-start.2 = ((bf16[64,2,6,128]{3,1,2,0:T(2,128)(2,1)}), bf16[64,2,6,128]{3,1,2,0:T(2,128)(2,1)S(1)}, u32[]{:S(2)}, u32[]{:S(2)}) async-start(bf16[64,2,6,128]{3,1,2,0:T(2,128)(2,1)} %copy.143), calls=%async_computation.2 | async-start | bytes 393216 | tf_op jit(solution)/shard_map/all_to_all | solution.py:269
  48.3 6.6 %shard_map.110 = f32[3,192,128]{2,1,0:T(8,128)} custom-call(s32[24]{0:T(128)} %reshape.254.src_ref, f32[648]{0:T(1024)} %select_n.133.coef_ref, bf16[10,208,128]{2,1,0:T(8,128)(2,1)} %fusion.23.ext_ref, bf16[128,1152]{1,0:T(8,128)(2,1)} %copy.140.w_ref), custom_call_target="tpu_custom_call" | custom-call | tf_op jit(solution)/shard_map/pallas_call | solution.py:87
  54.9 2.7 %all-to-all-done.2 = bf16[64,2,6,128]{3,1,2,0:T(2,128)(2,1)S(1)} async-done(((bf16[64,2,6,128]{3,1,2,0:T(2,128)(2,1)}), bf16[64,2,6,128]{3,1,2,0:T(2,128)(2,1)S(1)}, u32[]{:S(2)}, u32[]{:S(2)}) %all-to-all-start.2) | async-done | bytes 196640 | tf_op jit(solution)/shard_map/all_to_all | solution.py:269
  57.7 0.1 copy.144
  57.8 0.2 fusion.34
  58.1 0.2 fusion.33
  58.3 0.2 convolution_add_fusion.1
  58.6 0.3 fusion.4
  58.9 1.0 %copy.152 = bf16[2,720,128]{2,0,1:T(2,128)(2,1)} copy(bf16[2,720,128]{2,1,0:T(8,128)(2,1)S(1)} %fusion.4) | data formatting | bytes 737280 | tf_op jit(solution)/shard_map/optimization_barrier | solution.py:277
  59.9 3.6 %all-to-all-start.3 = ((bf16[2,720,128]{2,0,1:T(2,128)(2,1)}), bf16[2,720,128]{2,0,1:T(2,128)(2,1)S(1)}, u32[]{:S(2)}, u32[]{:S(2)}) async-start(bf16[2,720,128]{2,0,1:T(2,128)(2,1)} %copy.152), calls=%async_computation.3 | async-start | bytes 737280 | tf_op jit(solution)/shard_map/all_to_all | solution.py:278
  63.6 8.1 %shard_map.111 = f32[4,192,128]{2,1,0:T(8,128)} custom-call(s32[24]{0:T(128)} %reshape.254.src_ref, f32[648]{0:T(1024)} %select_n.133.coef_ref, bf16[10,208,128]{2,1,0:T(8,128)(2,1)} %fusion.23.ext_ref, bf16[128,1152]{1,0:T(8,128)(2,1)} %copy.140.w_ref), custom_call_target="tpu_custom_call" | custom-call | tf_op jit(solution)/shard_map/pallas_call | solution.py:87
  71.7 3.2 %all-to-all-done.3 = bf16[2,720,128]{2,0,1:T(2,128)(2,1)S(1)} async-done(((bf16[2,720,128]{2,0,1:T(2,128)(2,1)}), bf16[2,720,128]{2,0,1:T(2,128)(2,1)S(1)}, u32[]{:S(2)}, u32[]{:S(2)}) %all-to-all-start.3) | async-done | bytes 368672 | tf_op jit(solution)/shard_map/all_to_all | solution.py:278
  74.9 1.2 %fusion.18 = bf16[8,180,128]{2,1,0:T(8,128)(2,1)S(1)} fusion(f32[4,192,128]{2,1,0:T(8,128)} %shard_map.111, f32[3,192,128]{2,1,0:T(8,128)S(1)} %copy-done.1, f32[1,192,128]{2,1,0:T(8,128)S(1)} %copy-done.2, bf16[8,180,128]{2,1,0:T(8,128)(2,1)S(1)} %bitcast.122, pred[8]{0:T(512)(128)(4,1)S(1)} %iota_compare_fusion.1, bf16[8,180,128]{2,0,1:T(8,128)(2,1)S(1)} %copy-done), kind=kLoop, calls=%fused_computation.38 | loop fusion | flops 1658880 | bytes 1892360 | tf_op jit(solution)/shard_map/convert_element_type | solution.py:321
  76.2 0.8 %copy.156 = bf16[8,180,128]{2,0,1:T(8,128)(2,1)} copy(bf16[8,180,128]{2,1,0:T(8,128)(2,1)S(1)} %fusion.18) | data formatting | bytes 737280 | tf_op jit(solution)/shard_map/convert_element_type | solution.py:321
  (43 shorter events, 0.6 us)
Async XLA Ops:
  3.9 10.9 %copy-start.4 = (f32[64,9,9]{0,2,1:T(8,128)S(1)}, f32[64,9,9]{0,2,1:T(8,128)}, u32[]{:S(2)}) copy-start(f32[64,9,9]{0,2,1:T(8,128)} %param.16) | copy-start | bytes 62212
  4.7 17.8 %all-to-all-start = ((bf16[4,376,128]{2,1,0:T(8,128)(2,1)}), bf16[4,376,128]{2,1,0:T(8,128)(2,1)S(1)}, u32[]{:S(2)}, u32[]{:S(2)}) async-start(bf16[4,376,128]{2,1,0:T(8,128)(2,1)} %pad_maximum_fusion.3), calls=%async_computation | async-start | bytes 770048 | tf_op jit(solution)/shard_map/all_to_all | solution.py:236
  11.1 6.4 %copy-start.3 = (bf16[128,9,128]{2,0,1:T(8,128)(2,1)S(1)}, bf16[128,9,128]{2,0,1:T(8,128)(2,1)}, u32[]{:S(2)}) copy-start(bf16[128,9,128]{2,0,1:T(8,128)(2,1)} %param.17) | copy-start | bytes 884740
  15.7 4.6 %copy-start.5 = (f32[45,192]{1,0:T(8,128)S(1)}, f32[45,192]{1,0:T(8,128)}, u32[]{:S(2)}) copy-start(f32[45,192]{1,0:T(8,128)} %constant.80.clone) | copy-start | bytes 103684
  15.7 4.6 %copy-start.6 = (f32[45,192]{1,0:T(8,128)S(1)}, f32[45,192]{1,0:T(8,128)}, u32[]{:S(2)}) copy-start(f32[45,192]{1,0:T(8,128)} %constant.79.clone) | copy-start | bytes 103684
  15.7 4.6 %copy-start.7 = (f32[16,192]{1,0:T(8,128)S(1)}, f32[16,192]{1,0:T(8,128)}, u32[]{:S(2)}) copy-start(f32[16,192]{1,0:T(8,128)} %constant.82.clone) | copy-start | bytes 36868
  15.7 4.6 %copy-start.8 = (f32[16,192]{1,0:T(8,128)S(1)}, f32[16,192]{1,0:T(8,128)}, u32[]{:S(2)}) copy-start(f32[16,192]{1,0:T(8,128)} %constant.81.clone) | copy-start | bytes 36868
  25.2 13.5 %all-to-all-start.1 = ((bf16[2,2,192,128]{3,0,1,2:T(2,128)(2,1)}), bf16[2,2,192,128]{3,0,1,2:T(2,128)(2,1)S(1)}, u32[]{:S(2)}, u32[]{:S(2)}) async-start(bf16[2,2,192,128]{3,0,1,2:T(2,128)(2,1)} %copy.137), calls=%async_computation.1 | async-start | bytes 393216 | tf_op jit(solution)/shard_map/all_to_all | solution.py:261
  29.4 4.8 %collective-permute-start = (bf16[1,182,128]{2,1,0:T(8,128)(2,1)S(1)}, bf16[1,182,128]{2,1,0:T(8,128)(2,1)S(1)}, u32[]{:S(2)}, u32[]{:S(2)}) collective-permute-start(bf16[1,182,128]{2,1,0:T(8,128)(2,1)S(1)} %get-tuple-element.51), channel_id=1, source_target_pairs={{0,4},{4,8},{8,12},{12,16},{16,20},{20,24},{24,28},{28,0},{1,5},{5... | collective-permute-start | bytes 139784 | tf_op jit(solution)/shard_map/ppermute | solution.py:132
  29.7 4.5 %collective-permute-start.1 = (bf16[1,182,128]{2,1,0:T(8,128)(2,1)S(1)}, bf16[1,182,128]{2,1,0:T(8,128)(2,1)S(1)}, u32[]{:S(2)}, u32[]{:S(2)}) collective-permute-start(bf16[1,182,128]{2,1,0:T(8,128)(2,1)S(1)} %get-tuple-element.52), channel_id=1, source_target_pairs={{4,0},{8,4},{12,8},{16,12},{20,16},{24,20},{28,24},{0,28},{5,1},{9... | collective-permute-start | bytes 139784 | tf_op jit(solution)/shard_map/ppermute | solution.py:133
  40.5 0.7 copy-start.9
  42.4 15.2 %all-to-all-start.2 = ((bf16[64,2,6,128]{3,1,2,0:T(2,128)(2,1)}), bf16[64,2,6,128]{3,1,2,0:T(2,128)(2,1)S(1)}, u32[]{:S(2)}, u32[]{:S(2)}) async-start(bf16[64,2,6,128]{3,1,2,0:T(2,128)(2,1)} %copy.143), calls=%async_computation.2 | async-start | bytes 393216 | tf_op jit(solution)/shard_map/all_to_all | solution.py:269
  59.9 15.0 %all-to-all-start.3 = ((bf16[2,720,128]{2,0,1:T(2,128)(2,1)}), bf16[2,720,128]{2,0,1:T(2,128)(2,1)S(1)}, u32[]{:S(2)}, u32[]{:S(2)}) async-start(bf16[2,720,128]{2,0,1:T(2,128)(2,1)} %copy.152), calls=%async_computation.3 | async-start | bytes 737280 | tf_op jit(solution)/shard_map/all_to_all | solution.py:278
  63.5 11.4 %copy-start = (bf16[8,180,128]{2,0,1:T(8,128)(2,1)S(1)}, bf16[8,180,128]{2,0,1:T(8,128)(2,1)}, u32[]{:S(2)}) copy-start(bf16[8,180,128]{2,0,1:T(8,128)(2,1)} %param.11) | copy-start | bytes 1105924
  63.5 11.4 %copy-start.1 = (f32[3,192,128]{2,1,0:T(8,128)S(1)}, f32[3,192,128]{2,1,0:T(8,128)}, u32[]{:S(2)}) copy-start(f32[3,192,128]{2,1,0:T(8,128)} %shard_map.110) | copy-start | bytes 884740
  63.6 11.4 %copy-start.2 = (f32[1,192,128]{2,1,0:T(8,128)S(1)}, f32[1,192,128]{2,1,0:T(8,128)}, u32[]{:S(2)}) copy-start(f32[1,192,128]{2,1,0:T(8,128)} %shard_map.109) | copy-start | bytes 294916

commit v15 on v14

--- a/solution.py
+++ b/solution.py
@@ -55,14 +55,18 @@
 def disco_body(first, last, src_ref, coef_ref, ext_ref, w_ref, out_ref, mix_ref):
     kinds = w_ref.shape[1] // w_ref.shape[0]
     channels = w_ref.shape[0]
-    for r in range(last - first + 2):
+    span = last - first + 2
+    below = ext_ref.shape[0] - 1
+    for r in range(span):
         mix_ref[r] = jnp.dot(ext_ref[first + r], w_ref[...], preferred_element_type=jnp.float32)
+    mix_ref[span] = jnp.dot(ext_ref[below], w_ref[...], preferred_element_type=jnp.float32)
 
     def slot_step(s, carry):
         for c0 in range(0, out_ref.shape[1], CHUNK):
             acc = jnp.zeros((CHUNK, channels), jnp.float32)
             for a_i in range(3):
-                row = src_ref[(first + s) * 3 + a_i] - first
+                source = src_ref[(first + s) * 3 + a_i]
+                row = jnp.where(source == below, span, source - first)
                 for b_i in range(3):
                     for k in range(kinds):
                         coef = coef_ref[(((first + s) * 3 + a_i) * 3 + b_i) * kinds + k]
@@ -94,7 +98,7 @@
             pl.BlockSpec(memory_space=pltpu.VMEM),
         ],
         out_specs=pl.BlockSpec(memory_space=pltpu.VMEM),
-        scratch_shapes=[pltpu.VMEM((last - first + 2, lon_pad, weight_flat.shape[1]), jnp.float32)],
+        scratch_shapes=[pltpu.VMEM((last - first + 3, lon_pad, weight_flat.shape[1]), jnp.float32)],
     )(src_rows, coef, ext, weight_flat)
 
 

time: 77.7 us -> 77.8 us (level)
  transfers between devices with their start and end apart: 6 -> 6, of which waited for: 5 -> 5; matrix products, arithmetic and copies ran while one was open for 13% -> 13% of each run, Pallas kernels for 23% -> 24%
where the time goes in v15:
time: 77.8 us; the launch traced here: 77.1 us
  starting transfers between devices  22.9 us (29%)
  Pallas kernels  18.3 us (24%)
  local copies, waits for them, and re-layouts  11.5 us (15%)
  other arithmetic  9.53 us (12%)
  waiting for transfers between devices  7.99 us (10%)
  matrix products  4.33 us (6%)
  between operations  2.57 us (3%)
    pallas_call x3, Pallas kernels, disco_piece(): pl.pallas_call(functools.partial(disco_body, first, last), out_shape=jax....  18.3 us
    all_to_all x1, starting transfers between devices, spectral_by_modes(): lax.all_to_all(jnp.concatenate([body, edges], axis=1), 'lon', split_axis=...  6.32 us
    all_to_all x1, starting transfers between devices, spectral_by_modes(): lax.all_to_all(returned, both, split_axis=0, concat_axis=2, tiled=True)  6.02 us
    dot_general x13, matrix products, dot_split(): term = jnp.einsum(spec, lp, rp, preferred_element_type=jnp.float32)  4.33 us
    all_to_all x1, starting transfers between devices, spectral_by_modes(): lax.all_to_all(spectra, both, split_axis=2, concat_axis=0, tiled=True)  4.19 us
    all_to_all x1, starting transfers between devices, spectral_by_modes(): lax.all_to_all(spectral_rows, 'lon', split_axis=1, concat_axis=0, tiled=T...  3.64 us
    all_to_all x1, waiting for transfers between devices, spectral_by_modes(): lax.all_to_all(spectral_rows, 'lon', split_axis=1, concat_axis=0, tiled=T...  3.06 us
    all_to_all x1, waiting for transfers between devices, spectral_by_modes(): lax.all_to_all(returned, both, split_axis=0, concat_axis=2, tiled=True)  2.61 us
  transfers between devices with their start and end apart: 6, of which 5 were waited for; matrix products, arithmetic and copies ran while one was open for 13% of the time, Pallas kernels for 24%

profile of v15, /device:TPU:0, one launch (start us, length us, event | category | flops | bytes accessed | tf_op | source)
XLA Modules:
  0.0 77.1 jit_solution(2629013620814373600)
XLA Ops:
  0.0 1.4 %fusion.41 = (s32[1]{0:T(128)}, s32[1]{0:T(128)}) fusion(s32[8]{0:T(128)} %param.12, s32[]{:T(128)S(6)} %max.10, s32[]{:T(128)S(6)} %select_n.124), kind=kLoop, calls=%fused_computation.96 | loop fusion | bytes 24 | tf_op jit(solution)/shard_map/dynamic_slice | solution.py:116
  1.4 0.7 iota_compare_fusion.1
  2.1 0.7 slice_bitcast_fusion.9
  2.8 1.1 %broadcast_select_fusion = (bf16[8,180,128]{2,1,0:T(8,128)(2,1)S(1)}, bf16[8,180,128]{2,1,0:T(8,128)(2,1)S(1)}) fusion(pred[8]{0:T(512)(128)(4,1)S(1)} %iota_compare_fusion.1, bf16[8,180,128]{2,0,1:T(8,128)(2,1)} %param.11), kind=kLoop, calls=%fused_computation.50 | loop fusion | flops 184320 | bytes 1105928 | tf_op jit(solution)/shard_map/jit(_where)/select_n | solution.py:300
  3.9 0.1 reshape.253
  4.0 0.8 %pad_maximum_fusion.3 = bf16[4,376,128]{2,1,0:T(8,128)(2,1)} fusion(bf16[4,16,128]{2,1,0:T(8,128)(2,1)S(1)} %broadcast_in_dim.84, bf16[4,360,128]{2,1,0:T(8,128)(2,1)S(1)} %reshape.253), kind=kLoop, calls=%fused_computation.47 | loop fusion | flops 770048 | bytes 770048 | tf_op jit(solution)/shard_map/concatenate | solution.py:241
  4.7 6.3 %all-to-all-start = ((bf16[4,376,128]{2,1,0:T(8,128)(2,1)}), bf16[4,376,128]{2,1,0:T(8,128)(2,1)S(1)}, u32[]{:S(2)}, u32[]{:S(2)}) async-start(bf16[4,376,128]{2,1,0:T(8,128)(2,1)} %pad_maximum_fusion.3), calls=%async_computation | async-start | bytes 770048 | tf_op jit(solution)/shard_map/all_to_all | solution.py:240
  12.5 0.7 compare_select_fusion.2
  13.8 0.7 fusion.35
  14.5 0.1 copy.124
  14.6 0.1 reshape.260
  14.7 0.3 copy.125
  15.0 0.6 gather_fusion
  15.8 0.7 compare_or_fusion
  16.5 0.1 pad.21.clone
  16.6 0.1 pad_add_fusion.1
  16.6 0.1 maximum_select_fusion
  16.7 0.1 copy.123
  16.8 0.6 reshape.254.src_ref
  17.4 0.2 copy.129
  17.7 0.7 select_n.133.coef_ref
  18.4 0.7 add_compare_fusion
  19.1 1.2 %fusion.21 = (bf16[6,360,64]{1,2,0:T(8,128)(2,1)S(1)}, bf16[6,360,64]{1,2,0:T(8,128)(2,1)S(1)}) fusion(f32[24,360,64]{1,2,0:T(8,128)} %param.13, s32[]{:T(128)S(6)} %select_n.126), kind=kLoop, calls=%fused_computation.44 | loop fusion | flops 552960 | bytes 1105924 | tf_op jit(solution)/shard_map/convert_element_type | solution.py:34
  20.3 0.4 fusion.19
  20.7 1.9 %all-to-all-done = bf16[4,376,128]{2,1,0:T(8,128)(2,1)S(1)} async-done(((bf16[4,376,128]{2,1,0:T(8,128)(2,1)}), bf16[4,376,128]{2,1,0:T(8,128)(2,1)S(1)}, u32[]{:S(2)}, u32[]{:S(2)}) %all-to-all-start) | async-done | bytes 385056 | tf_op jit(solution)/shard_map/all_to_all | solution.py:240
  22.7 0.1 select_bitcast_fusion
  22.9 0.3 fusion.43
  23.2 0.3 fusion.42
  23.5 0.3 fusion.9
  23.9 0.3 fusion.10
  24.2 0.1 pad_maximum_fusion.4
  24.3 0.9 %copy.137 = bf16[2,2,192,128]{3,0,1,2:T(2,128)(2,1)} copy(bf16[2,2,192,128]{3,2,0,1:T(8,128)(2,1)S(1)} %pad_maximum_fusion.5) | data formatting | bytes 393216 | tf_op jit(solution)/shard_map/optimization_barrier | solution.py:262
  25.2 4.2 %all-to-all-start.1 = ((bf16[2,2,192,128]{3,0,1,2:T(2,128)(2,1)}), bf16[2,2,192,128]{3,0,1,2:T(2,128)(2,1)S(1)}, u32[]{:S(2)}, u32[]{:S(2)}) async-start(bf16[2,2,192,128]{3,0,1,2:T(2,128)(2,1)} %copy.137), calls=%async_computation.1 | async-start | bytes 393216 | tf_op jit(solution)/shard_map/all_to_all | solution.py:265
  29.4 0.3 collective-permute-start
  29.7 2.4 %collective-permute-start.1 = (bf16[1,182,128]{2,1,0:T(8,128)(2,1)S(1)}, bf16[1,182,128]{2,1,0:T(8,128)(2,1)S(1)}, u32[]{:S(2)}, u32[]{:S(2)}) collective-permute-start(bf16[1,182,128]{2,1,0:T(8,128)(2,1)S(1)} %get-tuple-element.52), channel_id=1, source_target_pairs={{4,0},{8,4},{12,8},{16,12},{20,16},{24,20},{28,24},{0,28},{5,1},{9... | collective-permute-start | bytes 139784 | tf_op jit(solution)/shard_map/ppermute | solution.py:137
  32.1 1.0 %slice_bitcast_fusion.1 = (f32[360,128]{1,0:T(8,128)S(1)}, f32[360,128]{1,0:T(8,128)S(1)}) fusion(f32[2,360,128]{2,1,0:T(8,128)} %param.15), kind=kLoop, calls=%fused_computation.60 | loop fusion | bytes 737280 | tf_op jit(solution)/shard_map/mul | solution.py:222
  33.1 0.9 %copy.140.w_ref = bf16[128,1152]{1,0:T(8,128)(2,1)} copy(bf16[128,1152]{0,1:T(8,128)(2,1)S(1)} %bitcast.124) | data formatting | bytes 589824 | tf_op jit(solution)/shard_map/optimization_barrier | solution.py:247
  34.0 0.2 collective-permute-done
  34.2 0.9 %fusion.23.ext_ref = bf16[10,208,128]{2,1,0:T(8,128)(2,1)} fusion(bf16[1,182,128]{2,1,0:T(8,128)(2,1)S(1)} %collective-permute-done.1, bf16[8,182,128]{2,1,0:T(8,128)(2,1)S(1)} %pad_maximum_fusion.4, bf16[1,182,128]{2,1,0:T(8,128)(2,1)S(1)} %collective-permute-done), kind=kLoop, calls=%fused_computation.46 | loop fusion | flops 2662400 | bytes 998400 | tf_op jit(solution)/shard_map/concatenate | solution.py:138
  35.1 3.4 %shard_map.109 = f32[1,192,128]{2,1,0:T(8,128)} custom-call(s32[24]{0:T(128)} %reshape.254.src_ref, f32[648]{0:T(1024)} %select_n.133.coef_ref, bf16[10,208,128]{2,1,0:T(8,128)(2,1)} %fusion.23.ext_ref, bf16[128,1152]{1,0:T(8,128)(2,1)} %copy.140.w_ref), custom_call_target="tpu_custom_call" | custom-call | tf_op jit(solution)/shard_map/pallas_call | solution.py:91
  38.5 0.2 all-to-all-done.1
  38.7 0.2 copy.139
  38.9 0.5 fusion.29
  39.4 0.5 add_bitcast_fusion
  39.9 0.2 multiply_add_fusion
  40.2 0.4 fusion.27
  40.5 0.4 convolution_add_fusion.3
  40.9 0.2 copy-done.9
  41.2 0.4 fusion.6
  41.6 0.9 %copy.143 = bf16[64,2,6,128]{3,1,2,0:T(2,128)(2,1)} copy(bf16[64,2,6,128]{3,0,1,2:T(8,128)(2,1)S(1)} %fusion.6) | data formatting | bytes 393216 | tf_op jit(solution)/shard_map/optimization_barrier | solution.py:272
  42.4 6.0 %all-to-all-start.2 = ((bf16[64,2,6,128]{3,1,2,0:T(2,128)(2,1)}), bf16[64,2,6,128]{3,1,2,0:T(2,128)(2,1)S(1)}, u32[]{:S(2)}, u32[]{:S(2)}) async-start(bf16[64,2,6,128]{3,1,2,0:T(2,128)(2,1)} %copy.143), calls=%async_computation.2 | async-start | bytes 393216 | tf_op jit(solution)/shard_map/all_to_all | solution.py:273
  48.5 6.7 %shard_map.110 = f32[3,192,128]{2,1,0:T(8,128)} custom-call(s32[24]{0:T(128)} %reshape.254.src_ref, f32[648]{0:T(1024)} %select_n.133.coef_ref, bf16[10,208,128]{2,1,0:T(8,128)(2,1)} %fusion.23.ext_ref, bf16[128,1152]{1,0:T(8,128)(2,1)} %copy.140.w_ref), custom_call_target="tpu_custom_call" | custom-call | tf_op jit(solution)/shard_map/pallas_call | solution.py:91
  55.2 2.6 %all-to-all-done.2 = bf16[64,2,6,128]{3,1,2,0:T(2,128)(2,1)S(1)} async-done(((bf16[64,2,6,128]{3,1,2,0:T(2,128)(2,1)}), bf16[64,2,6,128]{3,1,2,0:T(2,128)(2,1)S(1)}, u32[]{:S(2)}, u32[]{:S(2)}) %all-to-all-start.2) | async-done | bytes 196640 | tf_op jit(solution)/shard_map/all_to_all | solution.py:273
  57.8 0.1 copy.144
  58.0 0.2 fusion.34
  58.2 0.2 fusion.33
  58.5 0.3 convolution_add_fusion.1
  58.7 0.3 fusion.4
  59.0 1.0 %copy.152 = bf16[2,720,128]{2,0,1:T(2,128)(2,1)} copy(bf16[2,720,128]{2,1,0:T(8,128)(2,1)S(1)} %fusion.4) | data formatting | bytes 737280 | tf_op jit(solution)/shard_map/optimization_barrier | solution.py:281
  60.0 3.6 %all-to-all-start.3 = ((bf16[2,720,128]{2,0,1:T(2,128)(2,1)}), bf16[2,720,128]{2,0,1:T(2,128)(2,1)S(1)}, u32[]{:S(2)}, u32[]{:S(2)}) async-start(bf16[2,720,128]{2,0,1:T(2,128)(2,1)} %copy.152), calls=%async_computation.3 | async-start | bytes 737280 | tf_op jit(solution)/shard_map/all_to_all | solution.py:282
  63.7 8.2 %shard_map.111 = f32[4,192,128]{2,1,0:T(8,128)} custom-call(s32[24]{0:T(128)} %reshape.254.src_ref, f32[648]{0:T(1024)} %select_n.133.coef_ref, bf16[10,208,128]{2,1,0:T(8,128)(2,1)} %fusion.23.ext_ref, bf16[128,1152]{1,0:T(8,128)(2,1)} %copy.140.w_ref), custom_call_target="tpu_custom_call" | custom-call | tf_op jit(solution)/shard_map/pallas_call | solution.py:91
  71.9 3.1 %all-to-all-done.3 = bf16[2,720,128]{2,0,1:T(2,128)(2,1)S(1)} async-done(((bf16[2,720,128]{2,0,1:T(2,128)(2,1)}), bf16[2,720,128]{2,0,1:T(2,128)(2,1)S(1)}, u32[]{:S(2)}, u32[]{:S(2)}) %all-to-all-start.3) | async-done | bytes 368672 | tf_op jit(solution)/shard_map/all_to_all | solution.py:282
  75.1 1.2 %fusion.18 = bf16[8,180,128]{2,1,0:T(8,128)(2,1)S(1)} fusion(f32[4,192,128]{2,1,0:T(8,128)} %shard_map.111, f32[3,192,128]{2,1,0:T(8,128)S(1)} %copy-done.1, f32[1,192,128]{2,1,0:T(8,128)S(1)} %copy-done.2, bf16[8,180,128]{2,1,0:T(8,128)(2,1)S(1)} %bitcast.122, pred[8]{0:T(512)(128)(4,1)S(1)} %iota_compare_fusion.1, bf16[8,180,128]{2,0,1:T(8,128)(2,1)S(1)} %copy-done), kind=kLoop, calls=%fused_computation.38 | loop fusion | flops 1658880 | bytes 1892360 | tf_op jit(solution)/shard_map/convert_element_type | solution.py:325
  76.3 0.8 %copy.156 = bf16[8,180,128]{2,0,1:T(8,128)(2,1)} copy(bf16[8,180,128]{2,1,0:T(8,128)(2,1)S(1)} %fusion.18) | data formatting | bytes 737280 | tf_op jit(solution)/shard_map/convert_element_type | solution.py:325
  (43 shorter events, 0.6 us)
Async XLA Ops:
  3.9 10.9 %copy-start.4 = (f32[64,9,9]{0,2,1:T(8,128)S(1)}, f32[64,9,9]{0,2,1:T(8,128)}, u32[]{:S(2)}) copy-start(f32[64,9,9]{0,2,1:T(8,128)} %param.16) | copy-start | bytes 62212
  4.7 17.8 %all-to-all-start = ((bf16[4,376,128]{2,1,0:T(8,128)(2,1)}), bf16[4,376,128]{2,1,0:T(8,128)(2,1)S(1)}, u32[]{:S(2)}, u32[]{:S(2)}) async-start(bf16[4,376,128]{2,1,0:T(8,128)(2,1)} %pad_maximum_fusion.3), calls=%async_computation | async-start | bytes 770048 | tf_op jit(solution)/shard_map/all_to_all | solution.py:240
  11.1 6.4 %copy-start.3 = (bf16[128,9,128]{2,0,1:T(8,128)(2,1)S(1)}, bf16[128,9,128]{2,0,1:T(8,128)(2,1)}, u32[]{:S(2)}) copy-start(bf16[128,9,128]{2,0,1:T(8,128)(2,1)} %param.17) | copy-start | bytes 884740
  15.7 4.6 %copy-start.5 = (f32[45,192]{1,0:T(8,128)S(1)}, f32[45,192]{1,0:T(8,128)}, u32[]{:S(2)}) copy-start(f32[45,192]{1,0:T(8,128)} %constant.80.clone) | copy-start | bytes 103684
  15.7 4.6 %copy-start.6 = (f32[45,192]{1,0:T(8,128)S(1)}, f32[45,192]{1,0:T(8,128)}, u32[]{:S(2)}) copy-start(f32[45,192]{1,0:T(8,128)} %constant.79.clone) | copy-start | bytes 103684
  15.7 4.6 %copy-start.7 = (f32[16,192]{1,0:T(8,128)S(1)}, f32[16,192]{1,0:T(8,128)}, u32[]{:S(2)}) copy-start(f32[16,192]{1,0:T(8,128)} %constant.82.clone) | copy-start | bytes 36868
  15.7 4.6 %copy-start.8 = (f32[16,192]{1,0:T(8,128)S(1)}, f32[16,192]{1,0:T(8,128)}, u32[]{:S(2)}) copy-start(f32[16,192]{1,0:T(8,128)} %constant.81.clone) | copy-start | bytes 36868
  25.2 13.5 %all-to-all-start.1 = ((bf16[2,2,192,128]{3,0,1,2:T(2,128)(2,1)}), bf16[2,2,192,128]{3,0,1,2:T(2,128)(2,1)S(1)}, u32[]{:S(2)}, u32[]{:S(2)}) async-start(bf16[2,2,192,128]{3,0,1,2:T(2,128)(2,1)} %copy.137), calls=%async_computation.1 | async-start | bytes 393216 | tf_op jit(solution)/shard_map/all_to_all | solution.py:265
  29.4 4.8 %collective-permute-start = (bf16[1,182,128]{2,1,0:T(8,128)(2,1)S(1)}, bf16[1,182,128]{2,1,0:T(8,128)(2,1)S(1)}, u32[]{:S(2)}, u32[]{:S(2)}) collective-permute-start(bf16[1,182,128]{2,1,0:T(8,128)(2,1)S(1)} %get-tuple-element.51), channel_id=1, source_target_pairs={{0,4},{4,8},{8,12},{12,16},{16,20},{20,24},{24,28},{28,0},{1,5},{5... | collective-permute-start | bytes 139784 | tf_op jit(solution)/shard_map/ppermute | solution.py:136
  29.7 4.5 %collective-permute-start.1 = (bf16[1,182,128]{2,1,0:T(8,128)(2,1)S(1)}, bf16[1,182,128]{2,1,0:T(8,128)(2,1)S(1)}, u32[]{:S(2)}, u32[]{:S(2)}) collective-permute-start(bf16[1,182,128]{2,1,0:T(8,128)(2,1)S(1)} %get-tuple-element.52), channel_id=1, source_target_pairs={{4,0},{8,4},{12,8},{16,12},{20,16},{24,20},{28,24},{0,28},{5,1},{9... | collective-permute-start | bytes 139784 | tf_op jit(solution)/shard_map/ppermute | solution.py:137
  40.5 0.7 copy-start.9
  42.4 15.4 %all-to-all-start.2 = ((bf16[64,2,6,128]{3,1,2,0:T(2,128)(2,1)}), bf16[64,2,6,128]{3,1,2,0:T(2,128)(2,1)S(1)}, u32[]{:S(2)}, u32[]{:S(2)}) async-start(bf16[64,2,6,128]{3,1,2,0:T(2,128)(2,1)} %copy.143), calls=%async_computation.2 | async-start | bytes 393216 | tf_op jit(solution)/shard_map/all_to_all | solution.py:273
  60.0 14.9 %all-to-all-start.3 = ((bf16[2,720,128]{2,0,1:T(2,128)(2,1)}), bf16[2,720,128]{2,0,1:T(2,128)(2,1)S(1)}, u32[]{:S(2)}, u32[]{:S(2)}) async-start(bf16[2,720,128]{2,0,1:T(2,128)(2,1)} %copy.152), calls=%async_computation.3 | async-start | bytes 737280 | tf_op jit(solution)/shard_map/all_to_all | solution.py:282
  63.7 11.3 %copy-start = (bf16[8,180,128]{2,0,1:T(8,128)(2,1)S(1)}, bf16[8,180,128]{2,0,1:T(8,128)(2,1)}, u32[]{:S(2)}) copy-start(bf16[8,180,128]{2,0,1:T(8,128)(2,1)} %param.11) | copy-start | bytes 1105924
  63.7 11.3 %copy-start.1 = (f32[3,192,128]{2,1,0:T(8,128)S(1)}, f32[3,192,128]{2,1,0:T(8,128)}, u32[]{:S(2)}) copy-start(f32[3,192,128]{2,1,0:T(8,128)} %shard_map.110) | copy-start | bytes 884740
  63.7 11.3 %copy-start.2 = (f32[1,192,128]{2,1,0:T(8,128)S(1)}, f32[1,192,128]{2,1,0:T(8,128)}, u32[]{:S(2)}) copy-start(f32[1,192,128]{2,1,0:T(8,128)} %shard_map.109) | copy-start | bytes 294916

commit v16 on v15

--- a/solution.py
+++ b/solution.py
@@ -209,7 +209,7 @@
     spectral = lax.all_to_all(spectral_rows, "lon", split_axis=1, concat_axis=2, tiled=True)
     disco_parts.append(disco_work(ext_now, 2, prep))
     spectral, disco_parts = lax.optimization_barrier((spectral, disco_parts))
-    return spectral, disco_parts
+    return spectral, disco_parts, masked
 
 
 def filter_modes(coefficients, spectral_filter):
@@ -237,9 +237,10 @@
     body = raw.reshape(lon_total, share * lon_count, channels)
     edges = jnp.concatenate([raw[:, 0], raw[:, lon_count - 1]], axis=0)
     edges = jnp.broadcast_to(edges[None], (lon_total, 2 * row_count, channels))
-    received = lax.all_to_all(
-        jnp.concatenate([body, edges], axis=1), "lon", split_axis=0, concat_axis=0, tiled=True
-    )
+    send, raw = lax.optimization_barrier((jnp.concatenate([body, edges], axis=1), raw))
+    received = lax.all_to_all(send, "lon", split_axis=0, concat_axis=0, tiled=True)
+    slot_live = jnp.arange(row_count) < live_rows
+    masked = jnp.where(slot_live[:, None, None], raw, jnp.zeros_like(raw))
     own_legendre = lax.dynamic_slice_in_dim(
         legendre, lax.axis_index("lon") * mode_share, mode_share, 0
     )
@@ -282,7 +283,7 @@
     spectral = lax.all_to_all(spectral_rows, "lon", split_axis=1, concat_axis=0, tiled=True)
     disco_parts.append(disco_work(ext_now, 2, prep))
     spectral, disco_parts = lax.optimization_barrier((spectral, disco_parts))
-    return spectral, disco_parts
+    return spectral, disco_parts, masked
 
 
 def on_device(
@@ -308,7 +309,7 @@
 
     by_modes = legendre.shape[0] % lon_total == 0 and row_count % lon_total == 0
     path = spectral_by_modes if by_modes else spectral_by_channels
-    spectral, disco_parts = path(
+    spectral, disco_parts, masked = path(
         masked,
         legendre,
         quad_weights,

time: 77.8 us -> 78.9 us (1.014)
  local copies, waits for them, and re-layouts: 11.5 us -> 13.5 us
  waiting for transfers between devices: 7.99 us -> 6.4 us
  starting transfers between devices: 22.9 us -> 24.1 us
    unnamed x22 -> x29, local copies, waits for them, and re-layouts: 0.82 us -> 3.01 us
    all_to_all x1, waiting for transfers between devices: 1.91 us -> 0.01 us  [spectral_by_modes(): lax.all_to_all(send, 'lon', split_axis=0, concat_axis=0, tiled=True)]
    all_to_all x1, starting transfers between devices: 4.19 us -> 6.07 us  [spectral_by_modes(): lax.all_to_all(spectra, both, split_axis=2, concat_axis=0, tiled=True)]
    select_n x1, other arithmetic: 1.08 us -> 0.1 us  [spectral_by_modes(): masked = jnp.where(slot_live[:, None, None], raw, jnp.zeros_like(raw))]
  transfers between devices with their start and end apart: 6 -> 6, of which waited for: 5 -> 3; matrix products, arithmetic and copies ran while one was open for 13% -> 17% of each run, Pallas kernels for 24% -> 23%
where the time goes in v16:
time: 78.9 us; the launch traced here: 78.2 us
  starting transfers between devices  24.1 us (31%)
  Pallas kernels  18.3 us (23%)
  local copies, waits for them, and re-layouts  13.5 us (17%)
  other arithmetic  9.03 us (11%)
  waiting for transfers between devices  6.4 us (8%)
  matrix products  4.31 us (5%)
  between operations  2.51 us (3%)
    pallas_call x3, Pallas kernels, disco_piece(): pl.pallas_call(functools.partial(disco_body, first, last), out_shape=jax....  18.3 us
    all_to_all x1, starting transfers between devices, spectral_by_modes(): lax.all_to_all(send, 'lon', split_axis=0, concat_axis=0, tiled=True)  6.32 us
    all_to_all x1, starting transfers between devices, spectral_by_modes(): lax.all_to_all(spectra, both, split_axis=2, concat_axis=0, tiled=True)  6.07 us
    all_to_all x1, starting transfers between devices, spectral_by_modes(): lax.all_to_all(returned, both, split_axis=0, concat_axis=2, tiled=True)  5.4 us
    dot_general x13, matrix products, dot_split(): term = jnp.einsum(spec, lp, rp, preferred_element_type=jnp.float32)  4.31 us
    all_to_all x1, starting transfers between devices, spectral_by_modes(): lax.all_to_all(spectral_rows, 'lon', split_axis=1, concat_axis=0, tiled=T...  3.64 us
    all_to_all x1, waiting for transfers between devices, spectral_by_modes(): lax.all_to_all(spectral_rows, 'lon', split_axis=1, concat_axis=0, tiled=T...  3.11 us
    unnamed x29, local copies, waits for them, and re-layouts  3.01 us
  transfers between devices with their start and end apart: 6, of which 3 were waited for; matrix products, arithmetic and copies ran while one was open for 17% of the time, Pallas kernels for 23%

profile of v16, /device:TPU:0, one launch (start us, length us, event | category | flops | bytes accessed | tf_op | source)
XLA Modules:
  0.0 78.2 jit_solution(2662233103434514994)
XLA Ops:
  0.0 0.7 slice_bitcast_fusion.9
  0.7 1.0 %copy.121 = bf16[8,180,128]{2,1,0:T(8,128)(2,1)S(1)} copy(bf16[8,180,128]{2,0,1:T(8,128)(2,1)} %param.11) | data formatting | bytes 737280 | tf_op args[0]
  1.9 0.8 pad_maximum_fusion.3
  2.6 6.3 %all-to-all-start = ((bf16[4,376,128]{2,1,0:T(8,128)(2,1)}), bf16[4,376,128]{2,1,0:T(8,128)(2,1)S(1)}, u32[]{:S(2)}, u32[]{:S(2)}) async-start(bf16[4,376,128]{2,1,0:T(8,128)(2,1)} %pad_maximum_fusion.3), calls=%async_computation | async-start | bytes 770048 | tf_op jit(solution)/shard_map/all_to_all | solution.py:241
  9.0 0.6 fusion.41
  10.9 0.6 iota_compare_fusion.1
  11.5 0.6 compare_select_fusion.2
  12.9 0.1 copy.123
  12.9 0.7 reshape.254.src_ref
  13.6 0.6 fusion.35
  14.3 0.1 copy.124
  14.4 0.1 reshape.260
  14.4 0.9 %copy.129 = bf16[128,9,128]{0,2,1:T(8,128)(2,1)} copy(bf16[128,9,128]{2,0,1:T(8,128)(2,1)S(1)} %copy-done.5) | data formatting | bytes 589824 | tf_op args[6]
  15.3 0.3 copy.125
  15.7 0.6 gather_fusion
  16.5 0.6 compare_or_fusion
  17.1 0.1 pad.21.clone
  17.2 0.1 pad_add_fusion.1
  17.3 0.1 maximum_select_fusion
  17.4 0.7 select_n.133.coef_ref
  18.1 1.9 %fusion.21 = (bf16[6,360,64]{1,2,0:T(8,128)(2,1)}, bf16[6,360,64]{1,2,0:T(8,128)(2,1)S(1)}) fusion(f32[24,360,64]{1,2,0:T(8,128)} %param.13, s32[]{:T(128)S(6)} %select_n.126), kind=kLoop, calls=%fused_computation.44 | loop fusion | flops 552960 | bytes 1105924 | tf_op jit(solution)/shard_map/convert_element_type | solution.py:34
  20.0 0.6 add_compare_fusion
  20.6 0.1 copy_select_fusion
  20.8 0.3 fusion.19
  21.3 0.1 select_bitcast_fusion
  21.5 0.3 fusion.43
  21.8 0.3 fusion.42
  22.1 0.3 fusion.9
  22.4 0.3 fusion.10
  22.8 0.1 pad_maximum_fusion.4
  22.9 0.9 %copy.137 = bf16[2,2,192,128]{3,0,1,2:T(2,128)(2,1)} copy(bf16[2,2,192,128]{3,2,0,1:T(8,128)(2,1)S(1)} %pad_maximum_fusion.5) | data formatting | bytes 393216 | tf_op jit(solution)/shard_map/optimization_barrier | solution.py:263
  23.8 6.1 %all-to-all-start.1 = ((bf16[2,2,192,128]{3,0,1,2:T(2,128)(2,1)}), bf16[2,2,192,128]{3,0,1,2:T(2,128)(2,1)S(1)}, u32[]{:S(2)}, u32[]{:S(2)}) async-start(bf16[2,2,192,128]{3,0,1,2:T(2,128)(2,1)} %copy.137), calls=%async_computation.1 | async-start | bytes 393216 | tf_op jit(solution)/shard_map/all_to_all | solution.py:266
  29.8 0.6 constant_dynamic-slice_fusion
  30.5 0.3 collective-permute-start
  30.7 2.4 %collective-permute-start.1 = (bf16[1,182,128]{2,1,0:T(8,128)(2,1)S(1)}, bf16[1,182,128]{2,1,0:T(8,128)(2,1)S(1)}, u32[]{:S(2)}, u32[]{:S(2)}) collective-permute-start(bf16[1,182,128]{2,1,0:T(8,128)(2,1)S(1)} %get-tuple-element.56), channel_id=1, source_target_pairs={{4,0},{8,4},{12,8},{16,12},{20,16},{24,20},{28,24},{0,28},{5,1},{9... | collective-permute-start | bytes 139784 | tf_op jit(solution)/shard_map/ppermute | solution.py:137
  33.1 1.0 %slice_bitcast_fusion.1 = (f32[360,128]{1,0:T(8,128)S(1)}, f32[360,128]{1,0:T(8,128)S(1)}) fusion(f32[2,360,128]{2,1,0:T(8,128)} %param.15), kind=kLoop, calls=%fused_computation.60 | loop fusion | bytes 737280 | tf_op jit(solution)/shard_map/mul | solution.py:222
  34.2 0.9 %copy.140.w_ref = bf16[128,1152]{1,0:T(8,128)(2,1)} copy(bf16[128,1152]{0,1:T(8,128)(2,1)S(1)} %bitcast.124) | data formatting | bytes 589824 | tf_op jit(solution)/shard_map/optimization_barrier | solution.py:248
  35.0 0.7 collective-permute-done
  35.7 0.8 %fusion.23.ext_ref = bf16[10,208,128]{2,1,0:T(8,128)(2,1)} fusion(bf16[1,182,128]{2,1,0:T(8,128)(2,1)S(1)} %collective-permute-done.1, bf16[8,182,128]{2,1,0:T(8,128)(2,1)S(1)} %pad_maximum_fusion.4, bf16[1,182,128]{2,1,0:T(8,128)(2,1)S(1)} %collective-permute-done), kind=kLoop, calls=%fused_computation.46 | loop fusion | flops 2662400 | bytes 998400 | tf_op jit(solution)/shard_map/concatenate | solution.py:138
  36.6 3.4 %shard_map.109 = f32[1,192,128]{2,1,0:T(8,128)} custom-call(s32[24]{0:T(128)} %reshape.254.src_ref, f32[648]{0:T(1024)} %select_n.133.coef_ref, bf16[10,208,128]{2,1,0:T(8,128)(2,1)} %fusion.23.ext_ref, bf16[128,1152]{1,0:T(8,128)(2,1)} %copy.140.w_ref), custom_call_target="tpu_custom_call" | custom-call | tf_op jit(solution)/shard_map/pallas_call | solution.py:91
  40.0 0.2 copy.139
  40.2 0.5 fusion.29
  40.7 0.4 copy-done.1
  41.1 0.5 add_bitcast_fusion
  41.6 0.2 multiply_add_fusion
  41.9 0.4 fusion.27
  42.2 0.4 convolution_add_fusion.3
  42.6 0.2 copy-done.12
  42.9 0.4 fusion.6
  43.3 0.9 %copy.143 = bf16[64,2,6,128]{3,1,2,0:T(2,128)(2,1)} copy(bf16[64,2,6,128]{3,0,1,2:T(8,128)(2,1)S(1)} %fusion.6) | data formatting | bytes 393216 | tf_op jit(solution)/shard_map/optimization_barrier | solution.py:273
  44.1 5.4 %all-to-all-start.2 = ((bf16[64,2,6,128]{3,1,2,0:T(2,128)(2,1)}), bf16[64,2,6,128]{3,1,2,0:T(2,128)(2,1)S(1)}, u32[]{:S(2)}, u32[]{:S(2)}) async-start(bf16[64,2,6,128]{3,1,2,0:T(2,128)(2,1)} %copy.143), calls=%async_computation.2 | async-start | bytes 393216 | tf_op jit(solution)/shard_map/all_to_all | solution.py:274
  49.6 6.7 %shard_map.110 = f32[3,192,128]{2,1,0:T(8,128)} custom-call(s32[24]{0:T(128)} %reshape.254.src_ref, f32[648]{0:T(1024)} %select_n.133.coef_ref, bf16[10,208,128]{2,1,0:T(8,128)(2,1)} %fusion.23.ext_ref, bf16[128,1152]{1,0:T(8,128)(2,1)} %copy.140.w_ref), custom_call_target="tpu_custom_call" | custom-call | tf_op jit(solution)/shard_map/pallas_call | solution.py:91
  56.3 2.6 %all-to-all-done.2 = bf16[64,2,6,128]{3,1,2,0:T(2,128)(2,1)S(1)} async-done(((bf16[64,2,6,128]{3,1,2,0:T(2,128)(2,1)}), bf16[64,2,6,128]{3,1,2,0:T(2,128)(2,1)S(1)}, u32[]{:S(2)}, u32[]{:S(2)}) %all-to-all-start.2) | async-done | bytes 196640 | tf_op jit(solution)/shard_map/all_to_all | solution.py:274
  58.9 0.1 copy.144
  59.1 0.2 fusion.34
  59.3 0.2 fusion.33
  59.6 0.2 convolution_add_fusion.1
  59.8 0.3 fusion.4
  60.1 1.0 %copy.152 = bf16[2,720,128]{2,0,1:T(2,128)(2,1)} copy(bf16[2,720,128]{2,1,0:T(8,128)(2,1)S(1)} %fusion.4) | data formatting | bytes 737280 | tf_op jit(solution)/shard_map/optimization_barrier | solution.py:282
  61.1 3.6 %all-to-all-start.3 = ((bf16[2,720,128]{2,0,1:T(2,128)(2,1)}), bf16[2,720,128]{2,0,1:T(2,128)(2,1)S(1)}, u32[]{:S(2)}, u32[]{:S(2)}) async-start(bf16[2,720,128]{2,0,1:T(2,128)(2,1)} %copy.152), calls=%async_computation.3 | async-start | bytes 737280 | tf_op jit(solution)/shard_map/all_to_all | solution.py:283
  64.8 8.2 %shard_map.111 = f32[4,192,128]{2,1,0:T(8,128)} custom-call(s32[24]{0:T(128)} %reshape.254.src_ref, f32[648]{0:T(1024)} %select_n.133.coef_ref, bf16[10,208,128]{2,1,0:T(8,128)(2,1)} %fusion.23.ext_ref, bf16[128,1152]{1,0:T(8,128)(2,1)} %copy.140.w_ref), custom_call_target="tpu_custom_call" | custom-call | tf_op jit(solution)/shard_map/pallas_call | solution.py:91
  73.0 3.1 %all-to-all-done.3 = bf16[2,720,128]{2,0,1:T(2,128)(2,1)S(1)} async-done(((bf16[2,720,128]{2,0,1:T(2,128)(2,1)}), bf16[2,720,128]{2,0,1:T(2,128)(2,1)S(1)}, u32[]{:S(2)}, u32[]{:S(2)}) %all-to-all-start.3) | async-done | bytes 368672 | tf_op jit(solution)/shard_map/all_to_all | solution.py:283
  76.1 1.2 %fusion.18 = bf16[8,180,128]{2,1,0:T(8,128)(2,1)S(1)} fusion(f32[4,192,128]{2,1,0:T(8,128)} %shard_map.111, f32[3,192,128]{2,1,0:T(8,128)S(1)} %copy-done.3, f32[1,192,128]{2,1,0:T(8,128)S(1)} %copy-done.4, bf16[8,180,128]{2,1,0:T(8,128)(2,1)S(1)} %bitcast.122, pred[8]{0:T(512)(128)(4,1)S(1)} %iota_compare_fusion.1, bf16[8,180,128]{2,0,1:T(8,128)(2,1)S(1)} %copy-done), kind=kLoop, calls=%fused_computation.38 | loop fusion | flops 1658880 | bytes 1892360 | tf_op jit(solution)/shard_map/convert_element_type | solution.py:326
  77.4 0.8 %copy.156 = bf16[8,180,128]{2,0,1:T(8,128)(2,1)} copy(bf16[8,180,128]{2,1,0:T(8,128)(2,1)S(1)} %fusion.18) | data formatting | bytes 737280 | tf_op jit(solution)/shard_map/convert_element_type | solution.py:326
  (50 shorter events, 0.7 us)
Async XLA Ops:
  1.7 7.2 %copy-start.11 = (s32[8]{0:T(128)S(1)}, s32[8]{0:T(128)}, u32[]{:S(2)}) copy-start(s32[8]{0:T(128)} %param.12) | copy-start | bytes 100
  1.8 12.7 %copy-start.5 = (bf16[128,9,128]{2,0,1:T(8,128)(2,1)S(1)}, bf16[128,9,128]{2,0,1:T(8,128)(2,1)}, u32[]{:S(2)}) copy-start(bf16[128,9,128]{2,0,1:T(8,128)(2,1)} %param.17) | copy-start | bytes 884740
  1.9 13.5 %copy-start.6 = (f32[64,9,9]{0,2,1:T(8,128)S(1)}, f32[64,9,9]{0,2,1:T(8,128)}, u32[]{:S(2)}) copy-start(f32[64,9,9]{0,2,1:T(8,128)} %param.16) | copy-start | bytes 62212
  2.6 18.5 %all-to-all-start = ((bf16[4,376,128]{2,1,0:T(8,128)(2,1)}), bf16[4,376,128]{2,1,0:T(8,128)(2,1)S(1)}, u32[]{:S(2)}, u32[]{:S(2)}) async-start(bf16[4,376,128]{2,1,0:T(8,128)(2,1)} %pad_maximum_fusion.3), calls=%async_computation | async-start | bytes 770048 | tf_op jit(solution)/shard_map/all_to_all | solution.py:241
  16.2 4.4 %copy-start = (bf16[8,180,128]{2,0,1:T(8,128)(2,1)S(1)}, bf16[8,180,128]{2,0,1:T(8,128)(2,1)}, u32[]{:S(2)}) copy-start(bf16[8,180,128]{2,0,1:T(8,128)(2,1)} %param.11) | copy-start | bytes 1105924
  16.4 4.4 %copy-start.7 = (f32[45,192]{1,0:T(8,128)S(1)}, f32[45,192]{1,0:T(8,128)}, u32[]{:S(2)}) copy-start(f32[45,192]{1,0:T(8,128)} %constant.80.clone) | copy-start | bytes 103684
  16.4 4.4 %copy-start.8 = (f32[45,192]{1,0:T(8,128)S(1)}, f32[45,192]{1,0:T(8,128)}, u32[]{:S(2)}) copy-start(f32[45,192]{1,0:T(8,128)} %constant.79.clone) | copy-start | bytes 103684
  16.4 4.4 %copy-start.9 = (f32[16,192]{1,0:T(8,128)S(1)}, f32[16,192]{1,0:T(8,128)}, u32[]{:S(2)}) copy-start(f32[16,192]{1,0:T(8,128)} %constant.82.clone) | copy-start | bytes 36868
  16.4 4.4 %copy-start.10 = (f32[16,192]{1,0:T(8,128)S(1)}, f32[16,192]{1,0:T(8,128)}, u32[]{:S(2)}) copy-start(f32[16,192]{1,0:T(8,128)} %constant.81.clone) | copy-start | bytes 36868
  22.8 11.4 %copy-start.2 = (bf16[128,9,128]{0,2,1:T(8,128)(2,1)S(1)}, bf16[128,9,128]{0,2,1:T(8,128)(2,1)}, u32[]{:S(2)}) copy-start(bf16[128,9,128]{0,2,1:T(8,128)(2,1)} %copy.129) | copy-start | bytes 884740
  23.8 16.2 %all-to-all-start.1 = ((bf16[2,2,192,128]{3,0,1,2:T(2,128)(2,1)}), bf16[2,2,192,128]{3,0,1,2:T(2,128)(2,1)S(1)}, u32[]{:S(2)}, u32[]{:S(2)}) async-start(bf16[2,2,192,128]{3,0,1,2:T(2,128)(2,1)} %copy.137), calls=%async_computation.1 | async-start | bytes 393216 | tf_op jit(solution)/shard_map/all_to_all | solution.py:266
  30.5 5.3 %collective-permute-start = (bf16[1,182,128]{2,1,0:T(8,128)(2,1)}, bf16[1,182,128]{2,1,0:T(8,128)(2,1)S(1)}, u32[]{:S(2)}, u32[]{:S(2)}) collective-permute-start(bf16[1,182,128]{2,1,0:T(8,128)(2,1)} %get-tuple-element.55), channel_id=1, source_target_pairs={{0,4},{4,8},{8,12},{12,16},{16,20},{20,24},{24,28},{28,0},{1,5},{5... | collective-permute-start | bytes 139784 | tf_op jit(solution)/shard_map/ppermute | solution.py:136
  30.7 5.0 %collective-permute-start.1 = (bf16[1,182,128]{2,1,0:T(8,128)(2,1)S(1)}, bf16[1,182,128]{2,1,0:T(8,128)(2,1)S(1)}, u32[]{:S(2)}, u32[]{:S(2)}) collective-permute-start(bf16[1,182,128]{2,1,0:T(8,128)(2,1)S(1)} %get-tuple-element.56), channel_id=1, source_target_pairs={{4,0},{8,4},{12,8},{16,12},{20,16},{24,20},{28,24},{0,28},{5,1},{9... | collective-permute-start | bytes 139784 | tf_op jit(solution)/shard_map/ppermute | solution.py:137
  40.1 1.0 %copy-start.1 = (bf16[6,360,64]{1,2,0:T(8,128)(2,1)S(1)}, bf16[6,360,64]{1,2,0:T(8,128)(2,1)}, u32[]{:S(2)}) copy-start(bf16[6,360,64]{1,2,0:T(8,128)(2,1)} %get-tuple-element.38) | copy-start | bytes 829444
  42.2 0.7 copy-start.12
  44.1 14.7 %all-to-all-start.2 = ((bf16[64,2,6,128]{3,1,2,0:T(2,128)(2,1)}), bf16[64,2,6,128]{3,1,2,0:T(2,128)(2,1)S(1)}, u32[]{:S(2)}, u32[]{:S(2)}) async-start(bf16[64,2,6,128]{3,1,2,0:T(2,128)(2,1)} %copy.143), calls=%async_computation.2 | async-start | bytes 393216 | tf_op jit(solution)/shard_map/all_to_all | solution.py:274
  61.1 15.0 %all-to-all-start.3 = ((bf16[2,720,128]{2,0,1:T(2,128)(2,1)}), bf16[2,720,128]{2,0,1:T(2,128)(2,1)S(1)}, u32[]{:S(2)}, u32[]{:S(2)}) async-start(bf16[2,720,128]{2,0,1:T(2,128)(2,1)} %copy.152), calls=%async_computation.3 | async-start | bytes 737280 | tf_op jit(solution)/shard_map/all_to_all | solution.py:283
  64.8 11.4 %copy-start.3 = (f32[3,192,128]{2,1,0:T(8,128)S(1)}, f32[3,192,128]{2,1,0:T(8,128)}, u32[]{:S(2)}) copy-start(f32[3,192,128]{2,1,0:T(8,128)} %shard_map.110) | copy-start | bytes 884740
  64.8 11.4 %copy-start.4 = (f32[1,192,128]{2,1,0:T(8,128)S(1)}, f32[1,192,128]{2,1,0:T(8,128)}, u32[]{:S(2)}) copy-start(f32[1,192,128]{2,1,0:T(8,128)} %shard_map.109) | copy-start | bytes 294916

commit v17 on v15

--- a/solution.py
+++ b/solution.py
@@ -263,15 +263,13 @@
     ext = pad_lon(lat_extend(own, live_rows), lon_count)
     ext_now = ext
     columns = lax.all_to_all(spectra, both, split_axis=2, concat_axis=0, tiled=True)
-    disco_parts.append(disco_work(ext_now, 0, prep))
-    columns, disco_parts[0] = lax.optimization_barrier((columns, disco_parts[0]))
     coefficients = dot_split("mls,spmc->lpmc", legendre_parts, (columns,))
     filtered = filter_modes(coefficients, spectral_filter)
     returned = dot_split("mls,lpmc->spmc", legendre_parts, split_bf16(filtered))
     returned = (returned * quad_weights[:, None, None, None]).astype(jnp.bfloat16)
     returned, ext_now = lax.optimization_barrier((returned, ext))
     portion = lax.all_to_all(returned, both, split_axis=0, concat_axis=2, tiled=True)
-    disco_parts.append(disco_work(ext_now, 1, prep))
+    disco_parts.append(disco_work(ext_now, 0, prep))
     portion, disco_parts = lax.optimization_barrier((portion, disco_parts))
     spectral_rows = None
     for p, parts in enumerate(trig_parts):
@@ -280,7 +278,7 @@
     spectral_rows = spectral_rows.astype(jnp.bfloat16)
     spectral_rows, ext_now = lax.optimization_barrier((spectral_rows, ext))
     spectral = lax.all_to_all(spectral_rows, "lon", split_axis=1, concat_axis=0, tiled=True)
-    disco_parts.append(disco_work(ext_now, 2, prep))
+    disco_parts.append(disco_work(ext_now, 1, prep))
     spectral, disco_parts = lax.optimization_barrier((spectral, disco_parts))
     return spectral, disco_parts
 
@@ -301,12 +299,12 @@
     trig_parts = make_trig(mode_count, point_count)
     src_rows, coef = disco_tables(band_rows, disco_kernel, band_index, band_total, row_count)
     weight_flat = disco_weight.reshape(channels, -1)
-    pieces = min(3, row_count)
+    by_modes = legendre.shape[0] % lon_total == 0 and row_count % lon_total == 0
+    pieces = min(2 if by_modes else 3, row_count)
 
     def disco_work(ext_now, piece, prep):
         return disco_piece(prep[0], prep[1], ext_now, prep[2], piece, pieces, lon_count)
 
-    by_modes = legendre.shape[0] % lon_total == 0 and row_count % lon_total == 0
     path = spectral_by_modes if by_modes else spectral_by_channels
     spectral, disco_parts = path(
         masked,

time: 77.8 us -> 77.1 us (level)
  starting transfers between devices: 22.9 us -> 20.8 us
  Pallas kernels: 18.3 us -> 16.3 us
  waiting for transfers between devices: 7.99 us -> 9.75 us
  local copies, waits for them, and re-layouts: 11.5 us -> 13.2 us
    all_to_all x1, starting transfers between devices: 6.02 us -> 2.58 us  [spectral_by_modes(): lax.all_to_all(returned, both, split_axis=0, concat_axis=2, tiled=True)]
    ppermute x1, waiting for transfers between devices: 0.21 us -> 2.67 us  [lat_extend(): from_above = lax.ppermute(last_row, 'lat', lat_up)]
    all_to_all x1, waiting for transfers between devices: 2.61 us -> 0.29 us  [spectral_by_modes(): lax.all_to_all(returned, both, split_axis=0, concat_axis=2, tiled=True)]
    pallas_call x3 -> x2, Pallas kernels: 18.3 us -> 16.3 us  [disco_piece(): pl.pallas_call(functools.partial(disco_body, first, last), out_shape=jax....]
    unnamed x22 -> x26, local copies, waits for them, and re-layouts: 0.82 us -> 2.49 us
    all_to_all x1, waiting for transfers between devices: 0.21 us -> 1.58 us  [spectral_by_modes(): lax.all_to_all(spectra, both, split_axis=2, concat_axis=0, tiled=True)]
    all_to_all x1, starting transfers between devices: 3.64 us -> 4.59 us  [spectral_by_modes(): lax.all_to_all(spectral_rows, 'lon', split_axis=1, concat_axis=0, tiled=T...]
  transfers between devices with their start and end apart: 6 -> 6, of which waited for: 5 -> 6; matrix products, arithmetic and copies ran while one was open for 13% -> 15% of each run, Pallas kernels for 24% -> 21%
where the time goes in v17:
time: 77.1 us; the launch traced here: 76.3 us
  starting transfers between devices  20.8 us (27%)
  Pallas kernels  16.3 us (21%)
  local copies, waits for them, and re-layouts  13.2 us (17%)
  waiting for transfers between devices  9.75 us (13%)
  other arithmetic  9.64 us (13%)
  matrix products  4.29 us (6%)
  between operations  2.25 us (3%)
    pallas_call x2, Pallas kernels, disco_piece(): pl.pallas_call(functools.partial(disco_body, first, last), out_shape=jax....  16.3 us
    all_to_all x1, starting transfers between devices, spectral_by_modes(): lax.all_to_all(jnp.concatenate([body, edges], axis=1), 'lon', split_axis=...  6.32 us
    all_to_all x1, starting transfers between devices, spectral_by_modes(): lax.all_to_all(spectra, both, split_axis=2, concat_axis=0, tiled=True)  4.87 us
    all_to_all x1, starting transfers between devices, spectral_by_modes(): lax.all_to_all(spectral_rows, 'lon', split_axis=1, concat_axis=0, tiled=T...  4.59 us
    dot_general x13, matrix products, dot_split(): term = jnp.einsum(spec, lp, rp, preferred_element_type=jnp.float32)  4.29 us
    all_to_all x1, waiting for transfers between devices, spectral_by_modes(): lax.all_to_all(spectral_rows, 'lon', split_axis=1, concat_axis=0, tiled=T...  3.3 us
    ppermute x1, waiting for transfers between devices, lat_extend(): from_above = lax.ppermute(last_row, 'lat', lat_up)  2.67 us
    all_to_all x1, starting transfers between devices, spectral_by_modes(): lax.all_to_all(returned, both, split_axis=0, concat_axis=2, tiled=True)  2.58 us
  transfers between devices with their start and end apart: 6, of which 6 were waited for; matrix products, arithmetic and copies ran while one was open for 15% of the time, Pallas kernels for 21%

profile of v17, /device:TPU:0, one launch (start us, length us, event | category | flops | bytes accessed | tf_op | source)
XLA Modules:
  0.0 76.3 jit_solution(17441714819606836382)
XLA Ops:
  0.0 0.7 slice_bitcast_fusion.9
  0.7 1.3 %fusion.39 = (s32[1]{0:T(128)}, s32[1]{0:T(128)}) fusion(s32[8]{0:T(128)} %param.12, s32[]{:T(128)S(6)} %max.10, s32[]{:T(128)S(6)} %select_n.124), kind=kLoop, calls=%fused_computation.93 | loop fusion | bytes 24 | tf_op jit(solution)/shard_map/dynamic_slice | solution.py:116
  2.0 0.6 iota_compare_fusion.1
  2.6 1.1 %broadcast_select_fusion = (bf16[8,180,128]{2,1,0:T(8,128)(2,1)S(1)}, bf16[8,180,128]{2,1,0:T(8,128)(2,1)S(1)}) fusion(pred[8]{0:T(512)(128)(4,1)S(1)} %iota_compare_fusion.1, bf16[8,180,128]{2,0,1:T(8,128)(2,1)} %param.11), kind=kLoop, calls=%fused_computation.49 | loop fusion | flops 184320 | bytes 1105928 | tf_op jit(solution)/shard_map/jit(_where)/select_n | solution.py:298
  3.8 0.8 %pad_maximum_fusion.2 = bf16[4,376,128]{2,1,0:T(8,128)(2,1)} fusion(bf16[4,16,128]{2,1,0:T(8,128)(2,1)S(1)} %broadcast_in_dim.84, bf16[4,360,128]{2,1,0:T(8,128)(2,1)S(1)} %reshape.253), kind=kLoop, calls=%fused_computation.46 | loop fusion | flops 770048 | bytes 770048 | tf_op jit(solution)/shard_map/concatenate | solution.py:241
  4.5 6.3 %all-to-all-start = ((bf16[4,376,128]{2,1,0:T(8,128)(2,1)}), bf16[4,376,128]{2,1,0:T(8,128)(2,1)S(1)}, u32[]{:S(2)}, u32[]{:S(2)}) async-start(bf16[4,376,128]{2,1,0:T(8,128)(2,1)} %pad_maximum_fusion.2), calls=%async_computation | async-start | bytes 770048 | tf_op jit(solution)/shard_map/all_to_all | solution.py:240
  10.9 0.6 compare_select_fusion.2
  12.6 0.3 copy.119
  13.6 0.6 fusion.33
  14.2 0.1 copy.118
  14.3 0.1 reshape.260
  14.4 0.6 gather_fusion
  15.2 0.6 compare_or_fusion
  15.8 0.1 pad_add_fusion.1
  15.9 0.1 maximum_select_fusion
  16.0 0.1 copy.117
  16.0 0.7 reshape.254.src_ref
  16.7 0.7 select_n.133.coef_ref
  17.5 0.9 %copy.123 = bf16[128,9,128]{0,2,1:T(8,128)(2,1)} copy(bf16[128,9,128]{2,0,1:T(8,128)(2,1)S(1)} %copy-done.5) | data formatting | bytes 589824 | tf_op args[6]
  18.4 0.6 add_compare_fusion
  18.9 1.9 %fusion.21 = (bf16[6,360,64]{1,2,0:T(8,128)(2,1)}, bf16[6,360,64]{1,2,0:T(8,128)(2,1)S(1)}) fusion(f32[24,360,64]{1,2,0:T(8,128)} %param.13, s32[]{:T(128)S(6)} %select_n.126), kind=kLoop, calls=%fused_computation.43 | loop fusion | flops 552960 | bytes 1105924 | tf_op jit(solution)/shard_map/convert_element_type | solution.py:34
  20.8 0.3 fusion.19
  21.2 1.2 %all-to-all-done = bf16[4,376,128]{2,1,0:T(8,128)(2,1)S(1)} async-done(((bf16[4,376,128]{2,1,0:T(8,128)(2,1)}), bf16[4,376,128]{2,1,0:T(8,128)(2,1)S(1)}, u32[]{:S(2)}, u32[]{:S(2)}) %all-to-all-start) | async-done | bytes 385056 | tf_op jit(solution)/shard_map/all_to_all | solution.py:240
  22.5 0.1 select_bitcast_fusion
  22.6 0.5 copy-done.1
  23.2 0.3 fusion.41
  23.5 0.3 fusion.40
  23.8 0.1 slice-done
  24.0 0.3 fusion.9
  24.3 0.3 fusion.10
  24.6 0.1 pad_maximum_fusion.3
  24.7 0.9 %copy.131 = bf16[2,2,192,128]{3,0,1,2:T(2,128)(2,1)} copy(bf16[2,2,192,128]{3,2,0,1:T(8,128)(2,1)S(1)} %pad_maximum_fusion.4) | data formatting | bytes 393216 | tf_op jit(solution)/shard_map/optimization_barrier | solution.py:262
  25.6 4.9 %all-to-all-start.1 = ((bf16[2,2,192,128]{3,0,1,2:T(2,128)(2,1)}), bf16[2,2,192,128]{3,0,1,2:T(2,128)(2,1)S(1)}, u32[]{:S(2)}, u32[]{:S(2)}) async-start(bf16[2,2,192,128]{3,0,1,2:T(2,128)(2,1)} %copy.131), calls=%async_computation.1 | async-start | bytes 393216 | tf_op jit(solution)/shard_map/all_to_all | solution.py:265
  30.5 2.5 %collective-permute-start.1 = (bf16[1,182,128]{2,1,0:T(8,128)(2,1)S(1)}, bf16[1,182,128]{2,1,0:T(8,128)(2,1)S(1)}, u32[]{:S(2)}, u32[]{:S(2)}) collective-permute-start(bf16[1,182,128]{2,1,0:T(8,128)(2,1)S(1)} %get-tuple-element.44), channel_id=1, source_target_pairs={{4,0},{8,4},{12,8},{16,12},{20,16},{24,20},{28,24},{0,28},{5,1},{9... | collective-permute-start | bytes 139784 | tf_op jit(solution)/shard_map/ppermute | solution.py:137
  33.0 1.0 %slice_bitcast_fusion.1 = (f32[360,128]{1,0:T(8,128)S(1)}, f32[360,128]{1,0:T(8,128)S(1)}) fusion(f32[2,360,128]{2,1,0:T(8,128)} %param.15), kind=kLoop, calls=%fused_computation.59 | loop fusion | bytes 737280 | tf_op jit(solution)/shard_map/mul | solution.py:222
  34.0 0.7 collective-permute-done.1
  34.7 2.7 %collective-permute-done = bf16[1,182,128]{2,1,0:T(8,128)(2,1)S(1)} collective-permute-done((bf16[1,182,128]{2,1,0:T(8,128)(2,1)S(1)}, bf16[1,182,128]{2,1,0:T(8,128)(2,1)S(1)}, u32[]{:S(2)}, u32[]{:S(2)}) %collective-permute-start) | collective-permute-done | bytes 46624 | tf_op jit(solution)/shard_map/ppermute | solution.py:136
  37.4 0.8 %fusion.23.ext_ref = bf16[10,208,128]{2,1,0:T(8,128)(2,1)} fusion(bf16[1,182,128]{2,1,0:T(8,128)(2,1)S(1)} %collective-permute-done.1, bf16[8,182,128]{2,1,0:T(8,128)(2,1)S(1)} %pad_maximum_fusion.3, bf16[1,182,128]{2,1,0:T(8,128)(2,1)S(1)} %collective-permute-done), kind=kLoop, calls=%fused_computation.45 | loop fusion | flops 2662400 | bytes 998400 | tf_op jit(solution)/shard_map/concatenate | solution.py:138
  38.2 1.6 %all-to-all-done.1 = bf16[2,2,192,128]{3,0,1,2:T(2,128)(2,1)S(1)} async-done(((bf16[2,2,192,128]{3,0,1,2:T(2,128)(2,1)}), bf16[2,2,192,128]{3,0,1,2:T(2,128)(2,1)S(1)}, u32[]{:S(2)}, u32[]{:S(2)}) %all-to-all-start.1) | async-done | bytes 196640 | tf_op jit(solution)/shard_map/all_to_all | solution.py:265
  39.8 0.2 copy.133
  40.0 0.5 fusion.29
  40.5 0.5 copy-done.3
  40.9 0.5 add_bitcast_fusion
  41.4 0.2 multiply_add_fusion
  41.7 0.4 fusion.27
  42.1 0.4 convolution_add_fusion.3
  42.5 0.2 copy-done.11
  42.7 0.4 fusion.6
  43.1 0.9 %copy.134 = bf16[64,2,6,128]{3,1,2,0:T(2,128)(2,1)} copy(bf16[64,2,6,128]{3,0,1,2:T(8,128)(2,1)S(1)} %fusion.6) | data formatting | bytes 393216 | tf_op jit(solution)/shard_map/optimization_barrier | solution.py:270
  44.0 2.6 %all-to-all-start.2 = ((bf16[64,2,6,128]{3,1,2,0:T(2,128)(2,1)}), bf16[64,2,6,128]{3,1,2,0:T(2,128)(2,1)S(1)}, u32[]{:S(2)}, u32[]{:S(2)}) async-start(bf16[64,2,6,128]{3,1,2,0:T(2,128)(2,1)} %copy.134), calls=%async_computation.2 | async-start | bytes 393216 | tf_op jit(solution)/shard_map/all_to_all | solution.py:271
  46.6 0.9 %copy.136.w_ref = bf16[128,1152]{1,0:T(8,128)(2,1)} copy(bf16[128,1152]{0,1:T(8,128)(2,1)S(1)} %bitcast.126) | data formatting | bytes 589824 | tf_op jit(solution)/shard_map/optimization_barrier | solution.py:247
  47.5 8.1 %shard_map.109 = f32[4,192,128]{2,1,0:T(8,128)} custom-call(s32[24]{0:T(128)} %reshape.254.src_ref, f32[648]{0:T(1024)} %select_n.133.coef_ref, bf16[10,208,128]{2,1,0:T(8,128)(2,1)} %fusion.23.ext_ref, bf16[128,1152]{1,0:T(8,128)(2,1)} %copy.136.w_ref), custom_call_target="tpu_custom_call" | custom-call | tf_op jit(solution)/shard_map/pallas_call | solution.py:91
  55.6 0.3 all-to-all-done.2
  55.9 0.1 copy.135
  56.1 0.2 fusion.31
  56.3 0.2 fusion.32
  56.6 0.3 convolution_add_fusion.1
  56.8 0.3 fusion.4
  57.1 1.0 %copy.143 = bf16[2,720,128]{2,0,1:T(2,128)(2,1)} copy(bf16[2,720,128]{2,1,0:T(8,128)(2,1)S(1)} %fusion.4) | data formatting | bytes 737280 | tf_op jit(solution)/shard_map/optimization_barrier | solution.py:279
  58.1 4.6 %all-to-all-start.3 = ((bf16[2,720,128]{2,0,1:T(2,128)(2,1)}), bf16[2,720,128]{2,0,1:T(2,128)(2,1)S(1)}, u32[]{:S(2)}, u32[]{:S(2)}) async-start(bf16[2,720,128]{2,0,1:T(2,128)(2,1)} %copy.143), calls=%async_computation.3 | async-start | bytes 737280 | tf_op jit(solution)/shard_map/all_to_all | solution.py:280
  62.7 8.2 %shard_map.110 = f32[4,192,128]{2,1,0:T(8,128)} custom-call(s32[24]{0:T(128)} %reshape.254.src_ref, f32[648]{0:T(1024)} %select_n.133.coef_ref, bf16[10,208,128]{2,1,0:T(8,128)(2,1)} %fusion.23.ext_ref, bf16[128,1152]{1,0:T(8,128)(2,1)} %copy.136.w_ref), custom_call_target="tpu_custom_call" | custom-call | tf_op jit(solution)/shard_map/pallas_call | solution.py:91
  70.9 3.3 %all-to-all-done.3 = bf16[2,720,128]{2,0,1:T(2,128)(2,1)S(1)} async-done(((bf16[2,720,128]{2,0,1:T(2,128)(2,1)}), bf16[2,720,128]{2,0,1:T(2,128)(2,1)S(1)}, u32[]{:S(2)}, u32[]{:S(2)}) %all-to-all-start.3) | async-done | bytes 368672 | tf_op jit(solution)/shard_map/all_to_all | solution.py:280
  74.3 1.2 %fusion.18 = bf16[8,180,128]{2,1,0:T(8,128)(2,1)S(1)} fusion(f32[4,192,128]{2,1,0:T(8,128)} %shard_map.110, f32[4,192,128]{2,1,0:T(8,128)S(1)} %copy-done, bf16[8,180,128]{2,1,0:T(8,128)(2,1)S(1)} %bitcast.124, pred[8]{0:T(512)(128)(4,1)S(1)} %iota_compare_fusion.1, bf16[8,180,128]{2,0,1:T(8,128)(2,1)S(1)} %copy-done.2), kind=kLoop, calls=%fused_computation.38 | loop fusion | flops 1474560 | bytes 1892360 | tf_op jit(solution)/shard_map/convert_element_type | solution.py:323
  75.5 0.8 %copy.147 = bf16[8,180,128]{2,0,1:T(8,128)(2,1)} copy(bf16[8,180,128]{2,1,0:T(8,128)(2,1)S(1)} %fusion.18) | data formatting | bytes 737280 | tf_op jit(solution)/shard_map/convert_element_type | solution.py:323
  (47 shorter events, 0.7 us)
Async XLA Ops:
  3.7 9.0 %copy-start.6 = (f32[64,9,9]{0,2,1:T(8,128)S(1)}, f32[64,9,9]{0,2,1:T(8,128)}, u32[]{:S(2)}) copy-start(f32[64,9,9]{0,2,1:T(8,128)} %param.16) | copy-start | bytes 62212
  4.5 17.8 %all-to-all-start = ((bf16[4,376,128]{2,1,0:T(8,128)(2,1)}), bf16[4,376,128]{2,1,0:T(8,128)(2,1)S(1)}, u32[]{:S(2)}, u32[]{:S(2)}) async-start(bf16[4,376,128]{2,1,0:T(8,128)(2,1)} %pad_maximum_fusion.2), calls=%async_computation | async-start | bytes 770048 | tf_op jit(solution)/shard_map/all_to_all | solution.py:240
  10.9 6.6 %copy-start.5 = (bf16[128,9,128]{2,0,1:T(8,128)(2,1)S(1)}, bf16[128,9,128]{2,0,1:T(8,128)(2,1)}, u32[]{:S(2)}) copy-start(bf16[128,9,128]{2,0,1:T(8,128)(2,1)} %param.17) | copy-start | bytes 884740
  15.1 5.7 %copy-start.7 = (f32[45,192]{1,0:T(8,128)S(1)}, f32[45,192]{1,0:T(8,128)}, u32[]{:S(2)}) copy-start(f32[45,192]{1,0:T(8,128)} %constant.80.clone) | copy-start | bytes 103684
  15.1 5.7 %copy-start.8 = (f32[45,192]{1,0:T(8,128)S(1)}, f32[45,192]{1,0:T(8,128)}, u32[]{:S(2)}) copy-start(f32[45,192]{1,0:T(8,128)} %constant.79.clone) | copy-start | bytes 103684
  15.1 5.7 %copy-start.9 = (f32[16,192]{1,0:T(8,128)S(1)}, f32[16,192]{1,0:T(8,128)}, u32[]{:S(2)}) copy-start(f32[16,192]{1,0:T(8,128)} %constant.82.clone) | copy-start | bytes 36868
  15.1 5.7 %copy-start.10 = (f32[16,192]{1,0:T(8,128)S(1)}, f32[16,192]{1,0:T(8,128)}, u32[]{:S(2)}) copy-start(f32[16,192]{1,0:T(8,128)} %constant.81.clone) | copy-start | bytes 36868
  22.4 0.7 copy-start.1
  23.2 0.7 slice-start
  25.6 14.2 %all-to-all-start.1 = ((bf16[2,2,192,128]{3,0,1,2:T(2,128)(2,1)}), bf16[2,2,192,128]{3,0,1,2:T(2,128)(2,1)S(1)}, u32[]{:S(2)}, u32[]{:S(2)}) async-start(bf16[2,2,192,128]{3,0,1,2:T(2,128)(2,1)} %copy.131), calls=%async_computation.1 | async-start | bytes 393216 | tf_op jit(solution)/shard_map/all_to_all | solution.py:265
  30.5 4.2 %collective-permute-start.1 = (bf16[1,182,128]{2,1,0:T(8,128)(2,1)S(1)}, bf16[1,182,128]{2,1,0:T(8,128)(2,1)S(1)}, u32[]{:S(2)}, u32[]{:S(2)}) collective-permute-start(bf16[1,182,128]{2,1,0:T(8,128)(2,1)S(1)} %get-tuple-element.44), channel_id=1, source_target_pairs={{4,0},{8,4},{12,8},{16,12},{20,16},{24,20},{28,24},{0,28},{5,1},{9... | collective-permute-start | bytes 139784 | tf_op jit(solution)/shard_map/ppermute | solution.py:137
  33.0 4.4 %collective-permute-start = (bf16[1,182,128]{2,1,0:T(8,128)(2,1)S(1)}, bf16[1,182,128]{2,1,0:T(8,128)(2,1)S(1)}, u32[]{:S(2)}, u32[]{:S(2)}) collective-permute-start(bf16[1,182,128]{2,1,0:T(8,128)(2,1)S(1)} %get-tuple-element.43), channel_id=1, source_target_pairs={{0,4},{4,8},{8,12},{12,16},{16,20},{20,24},{24,28},{28,0},{1,5},{5... | collective-permute-start | bytes 139784 | tf_op jit(solution)/shard_map/ppermute | solution.py:136
  40.0 1.0 %copy-start.3 = (bf16[6,360,64]{1,2,0:T(8,128)(2,1)S(1)}, bf16[6,360,64]{1,2,0:T(8,128)(2,1)}, u32[]{:S(2)}) copy-start(bf16[6,360,64]{1,2,0:T(8,128)(2,1)} %get-tuple-element.25) | copy-start | bytes 829444
  42.1 0.7 copy-start.11
  42.7 3.8 %copy-start.4 = (bf16[128,9,128]{0,2,1:T(8,128)(2,1)S(1)}, bf16[128,9,128]{0,2,1:T(8,128)(2,1)}, u32[]{:S(2)}) copy-start(bf16[128,9,128]{0,2,1:T(8,128)(2,1)} %copy.123) | copy-start | bytes 884740
  44.0 11.9 %all-to-all-start.2 = ((bf16[64,2,6,128]{3,1,2,0:T(2,128)(2,1)}), bf16[64,2,6,128]{3,1,2,0:T(2,128)(2,1)S(1)}, u32[]{:S(2)}, u32[]{:S(2)}) async-start(bf16[64,2,6,128]{3,1,2,0:T(2,128)(2,1)} %copy.134), calls=%async_computation.2 | async-start | bytes 393216 | tf_op jit(solution)/shard_map/all_to_all | solution.py:271
  58.1 16.1 %all-to-all-start.3 = ((bf16[2,720,128]{2,0,1:T(2,128)(2,1)}), bf16[2,720,128]{2,0,1:T(2,128)(2,1)S(1)}, u32[]{:S(2)}, u32[]{:S(2)}) async-start(bf16[2,720,128]{2,0,1:T(2,128)(2,1)} %copy.143), calls=%async_computation.3 | async-start | bytes 737280 | tf_op jit(solution)/shard_map/all_to_all | solution.py:280
  62.7 11.5 %copy-start = (f32[4,192,128]{2,1,0:T(8,128)S(1)}, f32[4,192,128]{2,1,0:T(8,128)}, u32[]{:S(2)}) copy-start(f32[4,192,128]{2,1,0:T(8,128)} %shard_map.109) | copy-start | bytes 1179652
  62.7 11.6 %copy-start.2 = (bf16[8,180,128]{2,0,1:T(8,128)(2,1)S(1)}, bf16[8,180,128]{2,0,1:T(8,128)(2,1)}, u32[]{:S(2)}) copy-start(bf16[8,180,128]{2,0,1:T(8,128)(2,1)} %param.11) | copy-start | bytes 1105924

commit v18 on v16

--- a/solution.py
+++ b/solution.py
@@ -264,15 +264,13 @@
     ext = pad_lon(lat_extend(own, live_rows), lon_count)
     ext_now = ext
     columns = lax.all_to_all(spectra, both, split_axis=2, concat_axis=0, tiled=True)
-    disco_parts.append(disco_work(ext_now, 0, prep))
-    columns, disco_parts[0] = lax.optimization_barrier((columns, disco_parts[0]))
     coefficients = dot_split("mls,spmc->lpmc", legendre_parts, (columns,))
     filtered = filter_modes(coefficients, spectral_filter)
     returned = dot_split("mls,lpmc->spmc", legendre_parts, split_bf16(filtered))
     returned = (returned * quad_weights[:, None, None, None]).astype(jnp.bfloat16)
     returned, ext_now = lax.optimization_barrier((returned, ext))
     portion = lax.all_to_all(returned, both, split_axis=0, concat_axis=2, tiled=True)
-    disco_parts.append(disco_work(ext_now, 1, prep))
+    disco_parts.append(disco_work(ext_now, 0, prep))
     portion, disco_parts = lax.optimization_barrier((portion, disco_parts))
     spectral_rows = None
     for p, parts in enumerate(trig_parts):
@@ -281,7 +279,7 @@
     spectral_rows = spectral_rows.astype(jnp.bfloat16)
     spectral_rows, ext_now = lax.optimization_barrier((spectral_rows, ext))
     spectral = lax.all_to_all(spectral_rows, "lon", split_axis=1, concat_axis=0, tiled=True)
-    disco_parts.append(disco_work(ext_now, 2, prep))
+    disco_parts.append(disco_work(ext_now, 1, prep))
     spectral, disco_parts = lax.optimization_barrier((spectral, disco_parts))
     return spectral, disco_parts, masked
 
@@ -302,12 +300,12 @@
     trig_parts = make_trig(mode_count, point_count)
     src_rows, coef = disco_tables(band_rows, disco_kernel, band_index, band_total, row_count)
     weight_flat = disco_weight.reshape(channels, -1)
-    pieces = min(3, row_count)
+    by_modes = legendre.shape[0] % lon_total == 0 and row_count % lon_total == 0
+    pieces = min(2 if by_modes else 3, row_count)
 
     def disco_work(ext_now, piece, prep):
         return disco_piece(prep[0], prep[1], ext_now, prep[2], piece, pieces, lon_count)
 
-    by_modes = legendre.shape[0] % lon_total == 0 and row_count % lon_total == 0
     path = spectral_by_modes if by_modes else spectral_by_channels
     spectral, disco_parts, masked = path(
         masked,

time: 78.9 us -> 79.4 us (level)
  waiting for transfers between devices: 6.4 us -> 8.54 us
  starting transfers between devices: 24.1 us -> 22 us
  Pallas kernels: 18.3 us -> 16.3 us
  local copies, waits for them, and re-layouts: 13.5 us -> 15.5 us
    all_to_all x1, starting transfers between devices: 5.4 us -> 2.58 us  [spectral_by_modes(): lax.all_to_all(returned, both, split_axis=0, concat_axis=2, tiled=True)]
    all_to_all x1, waiting for transfers between devices: 2.61 us -> 0.29 us  [spectral_by_modes(): lax.all_to_all(returned, both, split_axis=0, concat_axis=2, tiled=True)]
    pallas_call x3 -> x2, Pallas kernels: 18.3 us -> 16.3 us  [disco_piece(): pl.pallas_call(functools.partial(disco_body, first, last), out_shape=jax....]
    ppermute x1, waiting for transfers between devices: 0.67 us -> 2.67 us  [lat_extend(): from_above = lax.ppermute(last_row, 'lat', lat_up)]
    select_n x2, local copies, waits for them, and re-layouts: 0.1 us -> 1.83 us  [spectral_by_modes(): jnp.where(portion_live[:, None, None], portion, jnp.zeros_like(portion))]
    all_to_all x1, waiting for transfers between devices: 0.01 us -> 1.59 us  [spectral_by_modes(): lax.all_to_all(spectra, both, split_axis=2, concat_axis=0, tiled=True)]
    select_n x1, other arithmetic: 0.1 us -> 1.09 us  [spectral_by_modes(): jnp.where(portion_live[:, None, None], portion, jnp.zeros_like(portion))]
    all_to_all x1, starting transfers between devices: 3.64 us -> 4.6 us  [spectral_by_modes(): lax.all_to_all(spectral_rows, 'lon', split_axis=1, concat_axis=0, tiled=T...]
  transfers between devices with their start and end apart: 6 -> 6, of which waited for: 3 -> 5; matrix products, arithmetic and copies ran while one was open for 17% -> 16% of each run, Pallas kernels for 23% -> 21%
where the time goes in v18:
time: 79.4 us; the launch traced here: 78.6 us
  starting transfers between devices  22 us (28%)
  Pallas kernels  16.3 us (21%)
  local copies, waits for them, and re-layouts  15.5 us (20%)
  other arithmetic  9.67 us (12%)
  waiting for transfers between devices  8.54 us (11%)
  matrix products  4.32 us (5%)
  between operations  2.24 us (3%)
    pallas_call x2, Pallas kernels, disco_piece(): pl.pallas_call(functools.partial(disco_body, first, last), out_shape=jax....  16.3 us
    all_to_all x1, starting transfers between devices, spectral_by_modes(): lax.all_to_all(send, 'lon', split_axis=0, concat_axis=0, tiled=True)  6.32 us
    all_to_all x1, starting transfers between devices, spectral_by_modes(): lax.all_to_all(spectra, both, split_axis=2, concat_axis=0, tiled=True)  6.07 us
    all_to_all x1, starting transfers between devices, spectral_by_modes(): lax.all_to_all(spectral_rows, 'lon', split_axis=1, concat_axis=0, tiled=T...  4.6 us
    dot_general x13, matrix products, dot_split(): term = jnp.einsum(spec, lp, rp, preferred_element_type=jnp.float32)  4.32 us
    all_to_all x1, waiting for transfers between devices, spectral_by_modes(): lax.all_to_all(spectral_rows, 'lon', split_axis=1, concat_axis=0, tiled=T...  3.3 us
    unnamed x29, local copies, waits for them, and re-layouts  2.98 us
    ppermute x1, waiting for transfers between devices, lat_extend(): from_above = lax.ppermute(last_row, 'lat', lat_up)  2.67 us
  transfers between devices with their start and end apart: 6, of which 5 were waited for; matrix products, arithmetic and copies ran while one was open for 16% of the time, Pallas kernels for 21%

profile of v18, /device:TPU:0, one launch (start us, length us, event | category | flops | bytes accessed | tf_op | source)
XLA Modules:
  0.0 78.6 jit_solution(18000682743874015984)
XLA Ops:
  0.0 0.7 slice_bitcast_fusion.9
  0.7 1.0 %copy.115 = bf16[8,180,128]{2,1,0:T(8,128)(2,1)S(1)} copy(bf16[8,180,128]{2,0,1:T(8,128)(2,1)} %param.11) | data formatting | bytes 737280 | tf_op args[0]
  1.9 0.8 pad_maximum_fusion.2
  2.6 6.3 %all-to-all-start = ((bf16[4,376,128]{2,1,0:T(8,128)(2,1)}), bf16[4,376,128]{2,1,0:T(8,128)(2,1)S(1)}, u32[]{:S(2)}, u32[]{:S(2)}) async-start(bf16[4,376,128]{2,1,0:T(8,128)(2,1)} %pad_maximum_fusion.2), calls=%async_computation | async-start | bytes 770048 | tf_op jit(solution)/shard_map/all_to_all | solution.py:241
  9.0 0.6 fusion.39
  9.6 0.6 compare_select_fusion.2
  10.1 0.6 iota_compare_fusion.1
  11.8 0.1 copy.117
  11.9 0.7 reshape.254.src_ref
  12.5 0.3 copy.119
  13.5 0.6 fusion.33
  14.1 0.1 copy.118
  14.2 0.1 reshape.260
  14.3 0.6 gather_fusion
  15.0 0.6 compare_or_fusion
  15.9 0.7 select_n.133.coef_ref
  16.6 0.9 %copy.123 = bf16[128,9,128]{0,2,1:T(8,128)(2,1)} copy(bf16[128,9,128]{2,0,1:T(8,128)(2,1)S(1)} %copy-done.5) | data formatting | bytes 589824 | tf_op args[6]
  17.5 1.9 %fusion.21 = (bf16[6,360,64]{1,2,0:T(8,128)(2,1)}, bf16[6,360,64]{1,2,0:T(8,128)(2,1)S(1)}) fusion(f32[24,360,64]{1,2,0:T(8,128)} %param.13, s32[]{:T(128)S(6)} %select_n.126), kind=kLoop, calls=%fused_computation.43 | loop fusion | flops 552960 | bytes 1105924 | tf_op jit(solution)/shard_map/convert_element_type | solution.py:34
  19.5 0.6 add_compare_fusion
  20.0 0.1 copy_select_fusion
  20.2 0.3 fusion.19
  20.6 0.8 %reshape.257 = bf16[4,2,180,128]{3,2,1,0:T(8,128)(2,1)} reshape(bf16[4,360,128]{2,1,0:T(8,128)(2,1)S(1)} %slice.59) | data formatting | bytes 737280 | tf_op jit(solution)/shard_map/reshape | solution.py:249
  21.4 1.1 %select_bitcast_fusion = bf16[2,4,180,128]{3,2,0,1:T(8,128)(2,1)S(1)} fusion(bf16[4,2,180,128]{3,2,1,0:T(8,128)(2,1)} %reshape.257, pred[2]{0:T(512)(128)(4,1)S(1)} %add_compare_fusion), kind=kLoop, calls=%fused_computation.49 | loop fusion | flops 184320 | bytes 737282 | tf_op jit(solution)/shard_map/jit(_where)/select_n | solution.py:252
  22.5 0.8 copy.124
  23.3 1.1 %select_n.136 = bf16[2,720,128]{2,1,0:T(8,128)(2,1)S(1)} reshape(bf16[2,4,180,128]{3,2,1,0:T(8,128)(2,1)} %copy.124) | data formatting | bytes 737280 | tf_op jit(solution)/shard_map/jit(_where)/select_n | solution.py:252
  24.4 0.3 fusion.41
  24.7 0.3 fusion.40
  25.0 0.1 slice-done
  25.1 0.3 fusion.9
  25.4 0.3 fusion.10
  25.7 0.1 pad_maximum_fusion.3
  25.8 0.9 %copy.131 = bf16[2,2,192,128]{3,0,1,2:T(2,128)(2,1)} copy(bf16[2,2,192,128]{3,2,0,1:T(8,128)(2,1)S(1)} %pad_maximum_fusion.4) | data formatting | bytes 393216 | tf_op jit(solution)/shard_map/optimization_barrier | solution.py:263
  26.7 6.1 %all-to-all-start.1 = ((bf16[2,2,192,128]{3,0,1,2:T(2,128)(2,1)}), bf16[2,2,192,128]{3,0,1,2:T(2,128)(2,1)S(1)}, u32[]{:S(2)}, u32[]{:S(2)}) async-start(bf16[2,2,192,128]{3,0,1,2:T(2,128)(2,1)} %copy.131), calls=%async_computation.1 | async-start | bytes 393216 | tf_op jit(solution)/shard_map/all_to_all | solution.py:266
  32.8 2.5 %collective-permute-start.1 = (bf16[1,182,128]{2,1,0:T(8,128)(2,1)S(1)}, bf16[1,182,128]{2,1,0:T(8,128)(2,1)S(1)}, u32[]{:S(2)}, u32[]{:S(2)}) collective-permute-start(bf16[1,182,128]{2,1,0:T(8,128)(2,1)S(1)} %get-tuple-element.48), channel_id=1, source_target_pairs={{4,0},{8,4},{12,8},{16,12},{20,16},{24,20},{28,24},{0,28},{5,1},{9... | collective-permute-start | bytes 139784 | tf_op jit(solution)/shard_map/ppermute | solution.py:137
  35.3 1.0 %slice_bitcast_fusion.1 = (f32[360,128]{1,0:T(8,128)S(1)}, f32[360,128]{1,0:T(8,128)S(1)}) fusion(f32[2,360,128]{2,1,0:T(8,128)} %param.15), kind=kLoop, calls=%fused_computation.59 | loop fusion | bytes 737280 | tf_op jit(solution)/shard_map/mul | solution.py:222
  36.3 0.7 collective-permute-done.1
  37.0 2.7 %collective-permute-done = bf16[1,182,128]{2,1,0:T(8,128)(2,1)S(1)} collective-permute-done((bf16[1,182,128]{2,1,0:T(8,128)(2,1)S(1)}, bf16[1,182,128]{2,1,0:T(8,128)(2,1)S(1)}, u32[]{:S(2)}, u32[]{:S(2)}) %collective-permute-start) | collective-permute-done | bytes 46624 | tf_op jit(solution)/shard_map/ppermute | solution.py:136
  39.7 0.8 %fusion.23.ext_ref = bf16[10,208,128]{2,1,0:T(8,128)(2,1)} fusion(bf16[1,182,128]{2,1,0:T(8,128)(2,1)S(1)} %collective-permute-done.1, bf16[8,182,128]{2,1,0:T(8,128)(2,1)S(1)} %pad_maximum_fusion.3, bf16[1,182,128]{2,1,0:T(8,128)(2,1)S(1)} %collective-permute-done), kind=kLoop, calls=%fused_computation.45 | loop fusion | flops 2662400 | bytes 998400 | tf_op jit(solution)/shard_map/concatenate | solution.py:138
  40.5 1.6 %all-to-all-done.1 = bf16[2,2,192,128]{3,0,1,2:T(2,128)(2,1)S(1)} async-done(((bf16[2,2,192,128]{3,0,1,2:T(2,128)(2,1)}), bf16[2,2,192,128]{3,0,1,2:T(2,128)(2,1)S(1)}, u32[]{:S(2)}, u32[]{:S(2)}) %all-to-all-start.1) | async-done | bytes 196640 | tf_op jit(solution)/shard_map/all_to_all | solution.py:266
  42.1 0.2 copy.133
  42.3 0.5 fusion.29
  42.8 0.4 copy-done.3
  43.3 0.5 add_bitcast_fusion
  43.8 0.2 multiply_add_fusion
  44.0 0.4 fusion.27
  44.4 0.4 convolution_add_fusion.3
  44.8 0.2 copy-done.12
  45.1 0.4 fusion.6
  45.4 0.9 %copy.134 = bf16[64,2,6,128]{3,1,2,0:T(2,128)(2,1)} copy(bf16[64,2,6,128]{3,0,1,2:T(8,128)(2,1)S(1)} %fusion.6) | data formatting | bytes 393216 | tf_op jit(solution)/shard_map/optimization_barrier | solution.py:271
  46.3 2.6 %all-to-all-start.2 = ((bf16[64,2,6,128]{3,1,2,0:T(2,128)(2,1)}), bf16[64,2,6,128]{3,1,2,0:T(2,128)(2,1)S(1)}, u32[]{:S(2)}, u32[]{:S(2)}) async-start(bf16[64,2,6,128]{3,1,2,0:T(2,128)(2,1)} %copy.134), calls=%async_computation.2 | async-start | bytes 393216 | tf_op jit(solution)/shard_map/all_to_all | solution.py:272
  48.9 0.9 %copy.136.w_ref = bf16[128,1152]{1,0:T(8,128)(2,1)} copy(bf16[128,1152]{0,1:T(8,128)(2,1)S(1)} %bitcast.126) | data formatting | bytes 589824 | tf_op jit(solution)/shard_map/optimization_barrier | solution.py:248
  49.8 8.1 %shard_map.109 = f32[4,192,128]{2,1,0:T(8,128)} custom-call(s32[24]{0:T(128)} %reshape.254.src_ref, f32[648]{0:T(1024)} %select_n.133.coef_ref, bf16[10,208,128]{2,1,0:T(8,128)(2,1)} %fusion.23.ext_ref, bf16[128,1152]{1,0:T(8,128)(2,1)} %copy.136.w_ref), custom_call_target="tpu_custom_call" | custom-call | tf_op jit(solution)/shard_map/pallas_call | solution.py:91
  57.9 0.3 all-to-all-done.2
  58.2 0.1 copy.135
  58.4 0.2 fusion.31
  58.6 0.2 fusion.32
  58.9 0.2 convolution_add_fusion.1
  59.1 0.3 fusion.4
  59.4 1.0 %copy.143 = bf16[2,720,128]{2,0,1:T(2,128)(2,1)} copy(bf16[2,720,128]{2,1,0:T(8,128)(2,1)S(1)} %fusion.4) | data formatting | bytes 737280 | tf_op jit(solution)/shard_map/optimization_barrier | solution.py:280
  60.5 4.6 %all-to-all-start.3 = ((bf16[2,720,128]{2,0,1:T(2,128)(2,1)}), bf16[2,720,128]{2,0,1:T(2,128)(2,1)S(1)}, u32[]{:S(2)}, u32[]{:S(2)}) async-start(bf16[2,720,128]{2,0,1:T(2,128)(2,1)} %copy.143), calls=%async_computation.3 | async-start | bytes 737280 | tf_op jit(solution)/shard_map/all_to_all | solution.py:281
  65.1 8.2 %shard_map.110 = f32[4,192,128]{2,1,0:T(8,128)} custom-call(s32[24]{0:T(128)} %reshape.254.src_ref, f32[648]{0:T(1024)} %select_n.133.coef_ref, bf16[10,208,128]{2,1,0:T(8,128)(2,1)} %fusion.23.ext_ref, bf16[128,1152]{1,0:T(8,128)(2,1)} %copy.136.w_ref), custom_call_target="tpu_custom_call" | custom-call | tf_op jit(solution)/shard_map/pallas_call | solution.py:91
  73.2 3.3 %all-to-all-done.3 = bf16[2,720,128]{2,0,1:T(2,128)(2,1)S(1)} async-done(((bf16[2,720,128]{2,0,1:T(2,128)(2,1)}), bf16[2,720,128]{2,0,1:T(2,128)(2,1)S(1)}, u32[]{:S(2)}, u32[]{:S(2)}) %all-to-all-start.3) | async-done | bytes 368672 | tf_op jit(solution)/shard_map/all_to_all | solution.py:281
  76.6 1.2 %fusion.18 = bf16[8,180,128]{2,1,0:T(8,128)(2,1)S(1)} fusion(f32[4,192,128]{2,1,0:T(8,128)} %shard_map.110, f32[4,192,128]{2,1,0:T(8,128)S(1)} %copy-done.1, bf16[8,180,128]{2,1,0:T(8,128)(2,1)S(1)} %bitcast.124, pred[8]{0:T(512)(128)(4,1)S(1)} %iota_compare_fusion.1, bf16[8,180,128]{2,0,1:T(8,128)(2,1)S(1)} %copy-done), kind=kLoop, calls=%fused_computation.38 | loop fusion | flops 1474560 | bytes 1892360 | tf_op jit(solution)/shard_map/convert_element_type | solution.py:324
  77.8 0.8 %copy.147 = bf16[8,180,128]{2,0,1:T(8,128)(2,1)} copy(bf16[8,180,128]{2,1,0:T(8,128)(2,1)S(1)} %fusion.18) | data formatting | bytes 737280 | tf_op jit(solution)/shard_map/convert_element_type | solution.py:324
  (50 shorter events, 0.7 us)
Async XLA Ops:
  1.7 7.2 %copy-start.11 = (s32[8]{0:T(128)S(1)}, s32[8]{0:T(128)}, u32[]{:S(2)}) copy-start(s32[8]{0:T(128)} %param.12) | copy-start | bytes 100
  1.8 10.8 %copy-start.6 = (f32[64,9,9]{0,2,1:T(8,128)S(1)}, f32[64,9,9]{0,2,1:T(8,128)}, u32[]{:S(2)}) copy-start(f32[64,9,9]{0,2,1:T(8,128)} %param.16) | copy-start | bytes 62212
  2.6 17.9 %all-to-all-start = ((bf16[4,376,128]{2,1,0:T(8,128)(2,1)}), bf16[4,376,128]{2,1,0:T(8,128)(2,1)S(1)}, u32[]{:S(2)}, u32[]{:S(2)}) async-start(bf16[4,376,128]{2,1,0:T(8,128)(2,1)} %pad_maximum_fusion.2), calls=%async_computation | async-start | bytes 770048 | tf_op jit(solution)/shard_map/all_to_all | solution.py:241
  9.0 7.7 %copy-start.5 = (bf16[128,9,128]{2,0,1:T(8,128)(2,1)S(1)}, bf16[128,9,128]{2,0,1:T(8,128)(2,1)}, u32[]{:S(2)}) copy-start(bf16[128,9,128]{2,0,1:T(8,128)(2,1)} %param.17) | copy-start | bytes 884740
  15.0 5.1 %copy-start = (bf16[8,180,128]{2,0,1:T(8,128)(2,1)S(1)}, bf16[8,180,128]{2,0,1:T(8,128)(2,1)}, u32[]{:S(2)}) copy-start(bf16[8,180,128]{2,0,1:T(8,128)(2,1)} %param.11) | copy-start | bytes 1105924
  17.5 2.6 %copy-start.7 = (f32[45,192]{1,0:T(8,128)S(1)}, f32[45,192]{1,0:T(8,128)}, u32[]{:S(2)}) copy-start(f32[45,192]{1,0:T(8,128)} %constant.80.clone) | copy-start | bytes 103684
  17.5 2.6 %copy-start.8 = (f32[45,192]{1,0:T(8,128)S(1)}, f32[45,192]{1,0:T(8,128)}, u32[]{:S(2)}) copy-start(f32[45,192]{1,0:T(8,128)} %constant.79.clone) | copy-start | bytes 103684
  17.5 2.6 %copy-start.9 = (f32[16,192]{1,0:T(8,128)S(1)}, f32[16,192]{1,0:T(8,128)}, u32[]{:S(2)}) copy-start(f32[16,192]{1,0:T(8,128)} %constant.82.clone) | copy-start | bytes 36868
  17.5 2.6 %copy-start.10 = (f32[16,192]{1,0:T(8,128)S(1)}, f32[16,192]{1,0:T(8,128)}, u32[]{:S(2)}) copy-start(f32[16,192]{1,0:T(8,128)} %constant.81.clone) | copy-start | bytes 36868
  20.5 2.0 %copy-start.2 = (bf16[4,376,128]{2,1,0:T(8,128)(2,1)}, bf16[4,376,128]{2,1,0:T(8,128)(2,1)S(1)}, u32[]{:S(2)}) copy-start(bf16[4,376,128]{2,1,0:T(8,128)(2,1)S(1)} %all-to-all-done) | copy-start | bytes 1155076
  24.4 0.7 slice-start
  26.7 15.4 %all-to-all-start.1 = ((bf16[2,2,192,128]{3,0,1,2:T(2,128)(2,1)}), bf16[2,2,192,128]{3,0,1,2:T(2,128)(2,1)S(1)}, u32[]{:S(2)}, u32[]{:S(2)}) async-start(bf16[2,2,192,128]{3,0,1,2:T(2,128)(2,1)} %copy.131), calls=%async_computation.1 | async-start | bytes 393216 | tf_op jit(solution)/shard_map/all_to_all | solution.py:266
  32.8 4.2 %collective-permute-start.1 = (bf16[1,182,128]{2,1,0:T(8,128)(2,1)S(1)}, bf16[1,182,128]{2,1,0:T(8,128)(2,1)S(1)}, u32[]{:S(2)}, u32[]{:S(2)}) collective-permute-start(bf16[1,182,128]{2,1,0:T(8,128)(2,1)S(1)} %get-tuple-element.48), channel_id=1, source_target_pairs={{4,0},{8,4},{12,8},{16,12},{20,16},{24,20},{28,24},{0,28},{5,1},{9... | collective-permute-start | bytes 139784 | tf_op jit(solution)/shard_map/ppermute | solution.py:137
  35.3 4.4 %collective-permute-start = (bf16[1,182,128]{2,1,0:T(8,128)(2,1)S(1)}, bf16[1,182,128]{2,1,0:T(8,128)(2,1)S(1)}, u32[]{:S(2)}, u32[]{:S(2)}) collective-permute-start(bf16[1,182,128]{2,1,0:T(8,128)(2,1)S(1)} %get-tuple-element.47), channel_id=1, source_target_pairs={{0,4},{4,8},{8,12},{12,16},{16,20},{20,24},{24,28},{28,0},{1,5},{5... | collective-permute-start | bytes 139784 | tf_op jit(solution)/shard_map/ppermute | solution.py:136
  42.3 1.0 %copy-start.3 = (bf16[6,360,64]{1,2,0:T(8,128)(2,1)S(1)}, bf16[6,360,64]{1,2,0:T(8,128)(2,1)}, u32[]{:S(2)}) copy-start(bf16[6,360,64]{1,2,0:T(8,128)(2,1)} %get-tuple-element.29) | copy-start | bytes 829444
  44.4 0.7 copy-start.12
  45.1 3.8 %copy-start.4 = (bf16[128,9,128]{0,2,1:T(8,128)(2,1)S(1)}, bf16[128,9,128]{0,2,1:T(8,128)(2,1)}, u32[]{:S(2)}) copy-start(bf16[128,9,128]{0,2,1:T(8,128)(2,1)} %copy.123) | copy-start | bytes 884740
  46.3 11.9 %all-to-all-start.2 = ((bf16[64,2,6,128]{3,1,2,0:T(2,128)(2,1)}), bf16[64,2,6,128]{3,1,2,0:T(2,128)(2,1)S(1)}, u32[]{:S(2)}, u32[]{:S(2)}) async-start(bf16[64,2,6,128]{3,1,2,0:T(2,128)(2,1)} %copy.134), calls=%async_computation.2 | async-start | bytes 393216 | tf_op jit(solution)/shard_map/all_to_all | solution.py:272
  60.5 16.1 %all-to-all-start.3 = ((bf16[2,720,128]{2,0,1:T(2,128)(2,1)}), bf16[2,720,128]{2,0,1:T(2,128)(2,1)S(1)}, u32[]{:S(2)}, u32[]{:S(2)}) async-start(bf16[2,720,128]{2,0,1:T(2,128)(2,1)} %copy.143), calls=%async_computation.3 | async-start | bytes 737280 | tf_op jit(solution)/shard_map/all_to_all | solution.py:281
  65.1 11.5 %copy-start.1 = (f32[4,192,128]{2,1,0:T(8,128)S(1)}, f32[4,192,128]{2,1,0:T(8,128)}, u32[]{:S(2)}) copy-start(f32[4,192,128]{2,1,0:T(8,128)} %shard_map.109) | copy-start | bytes 1179652

commit v19 on v17

--- a/solution.py
+++ b/solution.py
@@ -84,6 +84,8 @@
     bounds = [i * slot_total // pieces for i in range(pieces + 1)]
     if pieces == 3 and slot_total >= 8:
         bounds = [0, slot_total // 8, slot_total // 2, slot_total]
+    if pieces == 2 and slot_total >= 8:
+        bounds = [0, 3 * slot_total // 8, slot_total]
     first, last = bounds[piece], bounds[piece + 1]
     lon_pad, channels = ext.shape[1:]
     out_rows = round_up(lon_count, CHUNK)

time: 77.1 us -> 76 us (0.986)
  starting transfers between devices: 20.8 us -> 19.9 us
    all_to_all x1, waiting for transfers between devices: 3.3 us -> 1.55 us  [spectral_by_modes(): lax.all_to_all(spectral_rows, 'lon', split_axis=1, concat_axis=0, tiled=T...]
    all_to_all x1, waiting for transfers between devices: 0.29 us -> 1.79 us  [spectral_by_modes(): lax.all_to_all(returned, both, split_axis=0, concat_axis=2, tiled=True)]
    all_to_all x1, starting transfers between devices: 4.59 us -> 3.64 us  [spectral_by_modes(): lax.all_to_all(spectral_rows, 'lon', split_axis=1, concat_axis=0, tiled=T...]
  transfers between devices with their start and end apart: 6 -> 6, of which waited for: 6 -> 6; matrix products, arithmetic and copies ran while one was open for 15% -> 15% of each run, Pallas kernels for 21% -> 22%
where the time goes in v19:
time: 76 us; the launch traced here: 75.2 us
  starting transfers between devices  19.9 us (26%)
  Pallas kernels  16.4 us (22%)
  local copies, waits for them, and re-layouts  13.2 us (17%)
  other arithmetic  9.67 us (13%)
  waiting for transfers between devices  9.5 us (12%)
  matrix products  4.28 us (6%)
  between operations  2.28 us (3%)
    pallas_call x2, Pallas kernels, disco_piece(): pl.pallas_call(functools.partial(disco_body, first, last), out_shape=jax....  16.4 us
    all_to_all x1, starting transfers between devices, spectral_by_modes(): lax.all_to_all(jnp.concatenate([body, edges], axis=1), 'lon', split_axis=...  6.32 us
    all_to_all x1, starting transfers between devices, spectral_by_modes(): lax.all_to_all(spectra, both, split_axis=2, concat_axis=0, tiled=True)  4.87 us
    dot_general x13, matrix products, dot_split(): term = jnp.einsum(spec, lp, rp, preferred_element_type=jnp.float32)  4.28 us
    all_to_all x1, starting transfers between devices, spectral_by_modes(): lax.all_to_all(spectral_rows, 'lon', split_axis=1, concat_axis=0, tiled=T...  3.64 us
    ppermute x1, waiting for transfers between devices, lat_extend(): from_above = lax.ppermute(last_row, 'lat', lat_up)  2.67 us
    all_to_all x1, starting transfers between devices, spectral_by_modes(): lax.all_to_all(returned, both, split_axis=0, concat_axis=2, tiled=True)  2.58 us
    unnamed x26, local copies, waits for them, and re-layouts  2.49 us
  transfers between devices with their start and end apart: 6, of which 6 were waited for; matrix products, arithmetic and copies ran while one was open for 15% of the time, Pallas kernels for 22%

profile of v19, /device:TPU:0, one launch (start us, length us, event | category | flops | bytes accessed | tf_op | source)
XLA Modules:
  0.0 75.2 jit_solution(13840456035656075825)
XLA Ops:
  0.0 0.7 slice_bitcast_fusion.9
  0.7 1.3 %fusion.39 = (s32[1]{0:T(128)}, s32[1]{0:T(128)}) fusion(s32[8]{0:T(128)} %param.12, s32[]{:T(128)S(6)} %max.10, s32[]{:T(128)S(6)} %select_n.124), kind=kLoop, calls=%fused_computation.93 | loop fusion | bytes 24 | tf_op jit(solution)/shard_map/dynamic_slice | solution.py:118
  2.0 0.6 iota_compare_fusion.1
  2.6 1.1 %broadcast_select_fusion = (bf16[8,180,128]{2,1,0:T(8,128)(2,1)S(1)}, bf16[8,180,128]{2,1,0:T(8,128)(2,1)S(1)}) fusion(pred[8]{0:T(512)(128)(4,1)S(1)} %iota_compare_fusion.1, bf16[8,180,128]{2,0,1:T(8,128)(2,1)} %param.11), kind=kLoop, calls=%fused_computation.49 | loop fusion | flops 184320 | bytes 1105928 | tf_op jit(solution)/shard_map/jit(_where)/select_n | solution.py:300
  3.8 0.8 %pad_maximum_fusion.2 = bf16[4,376,128]{2,1,0:T(8,128)(2,1)} fusion(bf16[4,16,128]{2,1,0:T(8,128)(2,1)S(1)} %broadcast_in_dim.84, bf16[4,360,128]{2,1,0:T(8,128)(2,1)S(1)} %reshape.253), kind=kLoop, calls=%fused_computation.46 | loop fusion | flops 770048 | bytes 770048 | tf_op jit(solution)/shard_map/concatenate | solution.py:243
  4.5 6.3 %all-to-all-start = ((bf16[4,376,128]{2,1,0:T(8,128)(2,1)}), bf16[4,376,128]{2,1,0:T(8,128)(2,1)S(1)}, u32[]{:S(2)}, u32[]{:S(2)}) async-start(bf16[4,376,128]{2,1,0:T(8,128)(2,1)} %pad_maximum_fusion.2), calls=%async_computation | async-start | bytes 770048 | tf_op jit(solution)/shard_map/all_to_all | solution.py:242
  10.9 0.6 compare_select_fusion.2
  12.6 0.3 copy.119
  13.6 0.6 fusion.33
  14.2 0.1 copy.118
  14.3 0.1 reshape.260
  14.4 0.6 gather_fusion
  15.2 0.6 compare_or_fusion
  15.8 0.1 pad_add_fusion.1
  15.9 0.1 maximum_select_fusion
  16.0 0.1 copy.117
  16.0 0.7 reshape.254.src_ref
  16.7 0.7 select_n.133.coef_ref
  17.5 0.9 %copy.123 = bf16[128,9,128]{0,2,1:T(8,128)(2,1)} copy(bf16[128,9,128]{2,0,1:T(8,128)(2,1)S(1)} %copy-done.5) | data formatting | bytes 589824 | tf_op args[6]
  18.4 0.6 add_compare_fusion
  18.9 1.9 %fusion.21 = (bf16[6,360,64]{1,2,0:T(8,128)(2,1)}, bf16[6,360,64]{1,2,0:T(8,128)(2,1)S(1)}) fusion(f32[24,360,64]{1,2,0:T(8,128)} %param.13, s32[]{:T(128)S(6)} %select_n.126), kind=kLoop, calls=%fused_computation.43 | loop fusion | flops 552960 | bytes 1105924 | tf_op jit(solution)/shard_map/convert_element_type | solution.py:34
  20.8 0.3 fusion.19
  21.2 1.2 %all-to-all-done = bf16[4,376,128]{2,1,0:T(8,128)(2,1)S(1)} async-done(((bf16[4,376,128]{2,1,0:T(8,128)(2,1)}), bf16[4,376,128]{2,1,0:T(8,128)(2,1)S(1)}, u32[]{:S(2)}, u32[]{:S(2)}) %all-to-all-start) | async-done | bytes 385056 | tf_op jit(solution)/shard_map/all_to_all | solution.py:242
  22.5 0.1 select_bitcast_fusion
  22.6 0.5 copy-done
  23.2 0.3 fusion.41
  23.5 0.3 fusion.40
  23.8 0.1 slice-done
  24.0 0.3 fusion.9
  24.3 0.3 fusion.10
  24.6 0.1 pad_maximum_fusion.3
  24.7 0.9 %copy.131 = bf16[2,2,192,128]{3,0,1,2:T(2,128)(2,1)} copy(bf16[2,2,192,128]{3,2,0,1:T(8,128)(2,1)S(1)} %pad_maximum_fusion.4) | data formatting | bytes 393216 | tf_op jit(solution)/shard_map/optimization_barrier | solution.py:264
  25.6 4.9 %all-to-all-start.1 = ((bf16[2,2,192,128]{3,0,1,2:T(2,128)(2,1)}), bf16[2,2,192,128]{3,0,1,2:T(2,128)(2,1)S(1)}, u32[]{:S(2)}, u32[]{:S(2)}) async-start(bf16[2,2,192,128]{3,0,1,2:T(2,128)(2,1)} %copy.131), calls=%async_computation.1 | async-start | bytes 393216 | tf_op jit(solution)/shard_map/all_to_all | solution.py:267
  30.5 2.5 %collective-permute-start.1 = (bf16[1,182,128]{2,1,0:T(8,128)(2,1)S(1)}, bf16[1,182,128]{2,1,0:T(8,128)(2,1)S(1)}, u32[]{:S(2)}, u32[]{:S(2)}) collective-permute-start(bf16[1,182,128]{2,1,0:T(8,128)(2,1)S(1)} %get-tuple-element.44), channel_id=1, source_target_pairs={{4,0},{8,4},{12,8},{16,12},{20,16},{24,20},{28,24},{0,28},{5,1},{9... | collective-permute-start | bytes 139784 | tf_op jit(solution)/shard_map/ppermute | solution.py:139
  33.0 1.0 %slice_bitcast_fusion.1 = (f32[360,128]{1,0:T(8,128)S(1)}, f32[360,128]{1,0:T(8,128)S(1)}) fusion(f32[2,360,128]{2,1,0:T(8,128)} %param.15), kind=kLoop, calls=%fused_computation.59 | loop fusion | bytes 737280 | tf_op jit(solution)/shard_map/mul | solution.py:224
  34.0 0.7 collective-permute-done.1
  34.7 2.7 %collective-permute-done = bf16[1,182,128]{2,1,0:T(8,128)(2,1)S(1)} collective-permute-done((bf16[1,182,128]{2,1,0:T(8,128)(2,1)S(1)}, bf16[1,182,128]{2,1,0:T(8,128)(2,1)S(1)}, u32[]{:S(2)}, u32[]{:S(2)}) %collective-permute-start) | collective-permute-done | bytes 46624 | tf_op jit(solution)/shard_map/ppermute | solution.py:138
  37.4 0.8 %fusion.23.ext_ref = bf16[10,208,128]{2,1,0:T(8,128)(2,1)} fusion(bf16[1,182,128]{2,1,0:T(8,128)(2,1)S(1)} %collective-permute-done.1, bf16[8,182,128]{2,1,0:T(8,128)(2,1)S(1)} %pad_maximum_fusion.3, bf16[1,182,128]{2,1,0:T(8,128)(2,1)S(1)} %collective-permute-done), kind=kLoop, calls=%fused_computation.45 | loop fusion | flops 2662400 | bytes 998400 | tf_op jit(solution)/shard_map/concatenate | solution.py:140
  38.2 1.6 %all-to-all-done.1 = bf16[2,2,192,128]{3,0,1,2:T(2,128)(2,1)S(1)} async-done(((bf16[2,2,192,128]{3,0,1,2:T(2,128)(2,1)}), bf16[2,2,192,128]{3,0,1,2:T(2,128)(2,1)S(1)}, u32[]{:S(2)}, u32[]{:S(2)}) %all-to-all-start.1) | async-done | bytes 196640 | tf_op jit(solution)/shard_map/all_to_all | solution.py:267
  39.8 0.2 copy.133
  40.0 0.5 fusion.29
  40.5 0.5 copy-done.2
  40.9 0.5 add_bitcast_fusion
  41.4 0.2 multiply_add_fusion
  41.7 0.4 fusion.27
  42.1 0.4 convolution_add_fusion.3
  42.5 0.2 copy-done.11
  42.7 0.4 fusion.6
  43.1 0.9 %copy.134 = bf16[64,2,6,128]{3,1,2,0:T(2,128)(2,1)} copy(bf16[64,2,6,128]{3,0,1,2:T(8,128)(2,1)S(1)} %fusion.6) | data formatting | bytes 393216 | tf_op jit(solution)/shard_map/optimization_barrier | solution.py:272
  44.0 2.6 %all-to-all-start.2 = ((bf16[64,2,6,128]{3,1,2,0:T(2,128)(2,1)}), bf16[64,2,6,128]{3,1,2,0:T(2,128)(2,1)S(1)}, u32[]{:S(2)}, u32[]{:S(2)}) async-start(bf16[64,2,6,128]{3,1,2,0:T(2,128)(2,1)} %copy.134), calls=%async_computation.2 | async-start | bytes 393216 | tf_op jit(solution)/shard_map/all_to_all | solution.py:273
  46.6 0.9 %copy.136.w_ref = bf16[128,1152]{1,0:T(8,128)(2,1)} copy(bf16[128,1152]{0,1:T(8,128)(2,1)S(1)} %bitcast.126) | data formatting | bytes 589824 | tf_op jit(solution)/shard_map/optimization_barrier | solution.py:249
  47.5 6.6 %shard_map.109 = f32[3,192,128]{2,1,0:T(8,128)} custom-call(s32[24]{0:T(128)} %reshape.254.src_ref, f32[648]{0:T(1024)} %select_n.133.coef_ref, bf16[10,208,128]{2,1,0:T(8,128)(2,1)} %fusion.23.ext_ref, bf16[128,1152]{1,0:T(8,128)(2,1)} %copy.136.w_ref), custom_call_target="tpu_custom_call" | custom-call | tf_op jit(solution)/shard_map/pallas_call | solution.py:93
  54.1 1.8 %all-to-all-done.2 = bf16[64,2,6,128]{3,1,2,0:T(2,128)(2,1)S(1)} async-done(((bf16[64,2,6,128]{3,1,2,0:T(2,128)(2,1)}), bf16[64,2,6,128]{3,1,2,0:T(2,128)(2,1)S(1)}, u32[]{:S(2)}, u32[]{:S(2)}) %all-to-all-start.2) | async-done | bytes 196640 | tf_op jit(solution)/shard_map/all_to_all | solution.py:273
  55.9 0.1 copy.135
  56.1 0.2 fusion.31
  56.3 0.2 fusion.32
  56.6 0.2 convolution_add_fusion.1
  56.8 0.3 fusion.4
  57.1 1.0 %copy.143 = bf16[2,720,128]{2,0,1:T(2,128)(2,1)} copy(bf16[2,720,128]{2,1,0:T(8,128)(2,1)S(1)} %fusion.4) | data formatting | bytes 737280 | tf_op jit(solution)/shard_map/optimization_barrier | solution.py:281
  58.1 3.6 %all-to-all-start.3 = ((bf16[2,720,128]{2,0,1:T(2,128)(2,1)}), bf16[2,720,128]{2,0,1:T(2,128)(2,1)S(1)}, u32[]{:S(2)}, u32[]{:S(2)}) async-start(bf16[2,720,128]{2,0,1:T(2,128)(2,1)} %copy.143), calls=%async_computation.3 | async-start | bytes 737280 | tf_op jit(solution)/shard_map/all_to_all | solution.py:282
  61.8 9.7 %shard_map.110 = f32[5,192,128]{2,1,0:T(8,128)} custom-call(s32[24]{0:T(128)} %reshape.254.src_ref, f32[648]{0:T(1024)} %select_n.133.coef_ref, bf16[10,208,128]{2,1,0:T(8,128)(2,1)} %fusion.23.ext_ref, bf16[128,1152]{1,0:T(8,128)(2,1)} %copy.136.w_ref), custom_call_target="tpu_custom_call" | custom-call | tf_op jit(solution)/shard_map/pallas_call | solution.py:93
  71.5 1.6 %all-to-all-done.3 = bf16[2,720,128]{2,0,1:T(2,128)(2,1)S(1)} async-done(((bf16[2,720,128]{2,0,1:T(2,128)(2,1)}), bf16[2,720,128]{2,0,1:T(2,128)(2,1)S(1)}, u32[]{:S(2)}, u32[]{:S(2)}) %all-to-all-start.3) | async-done | bytes 368672 | tf_op jit(solution)/shard_map/all_to_all | solution.py:282
  73.2 1.3 %fusion.18 = bf16[8,180,128]{2,1,0:T(8,128)(2,1)S(1)} fusion(f32[5,192,128]{2,1,0:T(8,128)} %shard_map.110, f32[3,192,128]{2,1,0:T(8,128)S(1)} %copy-done.4, bf16[8,180,128]{2,1,0:T(8,128)(2,1)S(1)} %bitcast.124, pred[8]{0:T(512)(128)(4,1)S(1)} %iota_compare_fusion.1, bf16[8,180,128]{2,0,1:T(8,128)(2,1)S(1)} %copy-done.1), kind=kLoop, calls=%fused_computation.38 | loop fusion | flops 1474560 | bytes 1892360 | tf_op jit(solution)/shard_map/convert_element_type | solution.py:325
  74.4 0.8 %copy.147 = bf16[8,180,128]{2,0,1:T(8,128)(2,1)} copy(bf16[8,180,128]{2,1,0:T(8,128)(2,1)S(1)} %fusion.18) | data formatting | bytes 737280 | tf_op jit(solution)/shard_map/convert_element_type | solution.py:325
  (47 shorter events, 0.7 us)
Async XLA Ops:
  3.7 9.0 %copy-start.6 = (f32[64,9,9]{0,2,1:T(8,128)S(1)}, f32[64,9,9]{0,2,1:T(8,128)}, u32[]{:S(2)}) copy-start(f32[64,9,9]{0,2,1:T(8,128)} %param.16) | copy-start | bytes 62212
  4.5 17.8 %all-to-all-start = ((bf16[4,376,128]{2,1,0:T(8,128)(2,1)}), bf16[4,376,128]{2,1,0:T(8,128)(2,1)S(1)}, u32[]{:S(2)}, u32[]{:S(2)}) async-start(bf16[4,376,128]{2,1,0:T(8,128)(2,1)} %pad_maximum_fusion.2), calls=%async_computation | async-start | bytes 770048 | tf_op jit(solution)/shard_map/all_to_all | solution.py:242
  10.9 6.6 %copy-start.5 = (bf16[128,9,128]{2,0,1:T(8,128)(2,1)S(1)}, bf16[128,9,128]{2,0,1:T(8,128)(2,1)}, u32[]{:S(2)}) copy-start(bf16[128,9,128]{2,0,1:T(8,128)(2,1)} %param.17) | copy-start | bytes 884740
  15.1 5.7 %copy-start.7 = (f32[45,192]{1,0:T(8,128)S(1)}, f32[45,192]{1,0:T(8,128)}, u32[]{:S(2)}) copy-start(f32[45,192]{1,0:T(8,128)} %constant.80.clone) | copy-start | bytes 103684
  15.1 5.7 %copy-start.8 = (f32[45,192]{1,0:T(8,128)S(1)}, f32[45,192]{1,0:T(8,128)}, u32[]{:S(2)}) copy-start(f32[45,192]{1,0:T(8,128)} %constant.79.clone) | copy-start | bytes 103684
  15.1 5.7 %copy-start.9 = (f32[16,192]{1,0:T(8,128)S(1)}, f32[16,192]{1,0:T(8,128)}, u32[]{:S(2)}) copy-start(f32[16,192]{1,0:T(8,128)} %constant.82.clone) | copy-start | bytes 36868
  15.1 5.7 %copy-start.10 = (f32[16,192]{1,0:T(8,128)S(1)}, f32[16,192]{1,0:T(8,128)}, u32[]{:S(2)}) copy-start(f32[16,192]{1,0:T(8,128)} %constant.81.clone) | copy-start | bytes 36868
  22.4 0.7 copy-start
  23.2 0.7 slice-start
  25.6 14.2 %all-to-all-start.1 = ((bf16[2,2,192,128]{3,0,1,2:T(2,128)(2,1)}), bf16[2,2,192,128]{3,0,1,2:T(2,128)(2,1)S(1)}, u32[]{:S(2)}, u32[]{:S(2)}) async-start(bf16[2,2,192,128]{3,0,1,2:T(2,128)(2,1)} %copy.131), calls=%async_computation.1 | async-start | bytes 393216 | tf_op jit(solution)/shard_map/all_to_all | solution.py:267
  30.5 4.2 %collective-permute-start.1 = (bf16[1,182,128]{2,1,0:T(8,128)(2,1)S(1)}, bf16[1,182,128]{2,1,0:T(8,128)(2,1)S(1)}, u32[]{:S(2)}, u32[]{:S(2)}) collective-permute-start(bf16[1,182,128]{2,1,0:T(8,128)(2,1)S(1)} %get-tuple-element.44), channel_id=1, source_target_pairs={{4,0},{8,4},{12,8},{16,12},{20,16},{24,20},{28,24},{0,28},{5,1},{9... | collective-permute-start | bytes 139784 | tf_op jit(solution)/shard_map/ppermute | solution.py:139
  33.0 4.4 %collective-permute-start = (bf16[1,182,128]{2,1,0:T(8,128)(2,1)S(1)}, bf16[1,182,128]{2,1,0:T(8,128)(2,1)S(1)}, u32[]{:S(2)}, u32[]{:S(2)}) collective-permute-start(bf16[1,182,128]{2,1,0:T(8,128)(2,1)S(1)} %get-tuple-element.43), channel_id=1, source_target_pairs={{0,4},{4,8},{8,12},{12,16},{16,20},{20,24},{24,28},{28,0},{1,5},{5... | collective-permute-start | bytes 139784 | tf_op jit(solution)/shard_map/ppermute | solution.py:138
  40.0 1.0 %copy-start.2 = (bf16[6,360,64]{1,2,0:T(8,128)(2,1)S(1)}, bf16[6,360,64]{1,2,0:T(8,128)(2,1)}, u32[]{:S(2)}) copy-start(bf16[6,360,64]{1,2,0:T(8,128)(2,1)} %get-tuple-element.25) | copy-start | bytes 829444
  42.1 0.7 copy-start.11
  42.7 3.8 %copy-start.3 = (bf16[128,9,128]{0,2,1:T(8,128)(2,1)S(1)}, bf16[128,9,128]{0,2,1:T(8,128)(2,1)}, u32[]{:S(2)}) copy-start(bf16[128,9,128]{0,2,1:T(8,128)(2,1)} %copy.123) | copy-start | bytes 884740
  44.0 11.9 %all-to-all-start.2 = ((bf16[64,2,6,128]{3,1,2,0:T(2,128)(2,1)}), bf16[64,2,6,128]{3,1,2,0:T(2,128)(2,1)S(1)}, u32[]{:S(2)}, u32[]{:S(2)}) async-start(bf16[64,2,6,128]{3,1,2,0:T(2,128)(2,1)} %copy.134), calls=%async_computation.2 | async-start | bytes 393216 | tf_op jit(solution)/shard_map/all_to_all | solution.py:273
  58.1 15.0 %all-to-all-start.3 = ((bf16[2,720,128]{2,0,1:T(2,128)(2,1)}), bf16[2,720,128]{2,0,1:T(2,128)(2,1)S(1)}, u32[]{:S(2)}, u32[]{:S(2)}) async-start(bf16[2,720,128]{2,0,1:T(2,128)(2,1)} %copy.143), calls=%async_computation.3 | async-start | bytes 737280 | tf_op jit(solution)/shard_map/all_to_all | solution.py:282
  61.8 11.4 %copy-start.1 = (bf16[8,180,128]{2,0,1:T(8,128)(2,1)S(1)}, bf16[8,180,128]{2,0,1:T(8,128)(2,1)}, u32[]{:S(2)}) copy-start(bf16[8,180,128]{2,0,1:T(8,128)(2,1)} %param.11) | copy-start | bytes 1105924
  61.8 11.4 %copy-start.4 = (f32[3,192,128]{2,1,0:T(8,128)S(1)}, f32[3,192,128]{2,1,0:T(8,128)}, u32[]{:S(2)}) copy-start(f32[3,192,128]{2,1,0:T(8,128)} %shard_map.109) | copy-start | bytes 884740
